TPU v7x, 32 devices: a whole 2x2x4 slice. The times are simulated.
32 devices in a mesh: rows: 4 (over y, x), cols: 8 (over z, core).
Axes of the slice: x: 2, y: 2, z: 4, core: 2. Of those that a mesh axis runs over, the one named last changes fastest.
Arguments:
- frames: bfloat16 [2, 16, 8192], P(None, 'rows', 'cols'), may hold values from -6 to 6
- hidden_start: bfloat16 [16, 256, 128], P('rows', 'cols'), may hold values from -3 to 3
- cell_start: float32 [16, 256, 128], P('rows', 'cols'), may hold values from -6 to 6
- kernel: bfloat16 [1440, 512], replicated, may hold values from -0.15625 to 0.15625
- gate_bias: float32 [512], replicated, may hold values from -4 to 4
- cotangent: bfloat16 [2, 16, 256, 128], P(None, 'rows', 'cols'), may hold values from -6 to 6
Outputs:
- hidden_final: bfloat16 [16, 256, 128], P('rows', 'cols')
- grad_hidden_start: float32 [16, 256, 128], P('rows', 'cols')
- grad_cell_start: float32 [16, 256, 128], P('rows', 'cols')
- kernel_grad: float32 [1440, 512], replicated
- bias_grad: float32 [512], replicated
All inputs are finite; a program needn't handle non-finite values.
Results may differ from a plain program's by a relative error of at most 0.015.
Values may be sent and summed in bfloat16 or wider, within the bound.
No kernel may reach another device: no remote copies, remote signals or barrier semaphores. Data moves between devices by JAX's collectives and lax.ppermute only.
A program may use at most 64 MiB of HBM per device.

v0:
```python
import math

import jax
import jax.numpy as jnp
from jax import lax
from jax.sharding import PartitionSpec as P

HC = 128
CI = 32
KS = 3
STEPS = 2
GATES = 512
KIN = 1440


def extended(cells, sides, width):
    for axis, dim in sides:
        count = lax.axis_size(axis)
        ends = count - 1
        head = lax.slice_in_dim(cells, 0, width, axis=dim)
        tail = lax.slice_in_dim(cells, cells.shape[dim] - width, cells.shape[dim], axis=dim)
        cells = jnp.concatenate(
            [
                lax.ppermute(tail, axis, [(i, (i + 1) % count) for i in range(ends)]),
                cells,
                lax.ppermute(head, axis, [((i + 1) % count, i) for i in range(ends)]),
            ],
            axis=dim,
        )
    return cells


def tap_columns(padded, rows_dev, cols_dev, reverse):
    pieces = []
    for tap_row in range(KS):
        for tap_col in range(KS):
            if reverse:
                first_row = KS - 1 - tap_row
                first_col = KS - 1 - tap_col
            else:
                first_row = tap_row
                first_col = tap_col
            pieces.append(
                padded[first_row : first_row + rows_dev, first_col : first_col + cols_dev]
            )
    joined = jnp.concatenate(pieces, axis=-1)
    return joined.reshape(rows_dev * cols_dev, joined.shape[-1])


def shards(frames, hidden_start, cell_start, kernel, gate_bias, cotangent):
    rows_dev = hidden_start.shape[0]
    cols_dev = hidden_start.shape[1]
    chans = CI + HC
    taps = KS * KS
    cells = rows_dev * cols_dev
    hidden = hidden_start
    cell = cell_start
    saved = []
    for moment in range(STEPS):
        inputs = frames[moment].reshape(rows_dev, cols_dev, CI)
        stacked = jnp.concatenate([inputs, hidden], axis=-1)
        padded = extended(stacked, (("rows", 0), ("cols", 1)), 1)
        patches = tap_columns(padded, rows_dev, cols_dev, False)
        gates = jnp.dot(patches, kernel, preferred_element_type=jnp.float32) + gate_bias
        gates = gates.reshape(rows_dev, cols_dev, GATES)
        gate_in = jax.nn.sigmoid(gates[..., :HC])
        gate_forget = jax.nn.sigmoid(gates[..., HC : 2 * HC])
        gate_cand = jnp.tanh(gates[..., 2 * HC : 3 * HC])
        gate_out = jax.nn.sigmoid(gates[..., 3 * HC :])
        cell_prev = cell
        cell = gate_forget * cell_prev + gate_in * gate_cand
        hidden = (gate_out * jnp.tanh(cell)).astype(jnp.bfloat16)
        saved.append((patches, gate_in, gate_forget, gate_cand, gate_out, cell_prev, cell))
    blocks = kernel.reshape(taps, chans, GATES)
    adjoint_matrix = jnp.transpose(blocks, (0, 2, 1)).reshape(taps * GATES, chans)
    grad_hidden = cotangent[STEPS - 1].astype(jnp.float32)
    grad_cell = jnp.zeros((rows_dev, cols_dev, HC), jnp.float32)
    kernel_acc = jnp.zeros((KIN, GATES), jnp.float32)
    bias_acc = jnp.zeros((GATES,), jnp.float32)
    for moment in range(STEPS - 1, -1, -1):
        patches, gate_in, gate_forget, gate_cand, gate_out, cell_prev, cell_now = saved[moment]
        tanh_cell = jnp.tanh(cell_now)
        summed = grad_cell + grad_hidden * gate_out * (1.0 - tanh_cell * tanh_cell)
        pre_in = summed * gate_cand * gate_in * (1.0 - gate_in)
        pre_forget = summed * cell_prev * gate_forget * (1.0 - gate_forget)
        pre_cand = summed * gate_in * (1.0 - gate_cand * gate_cand)
        pre_out = grad_hidden * tanh_cell * gate_out * (1.0 - gate_out)
        grad_cell = summed * gate_forget
        grad_gates = jnp.concatenate([pre_in, pre_forget, pre_cand, pre_out], axis=-1).astype(
            jnp.bfloat16
        )
        flat_grads = grad_gates.reshape(cells, GATES)
        kernel_acc = kernel_acc + jnp.dot(patches.T, flat_grads, preferred_element_type=jnp.float32)
        bias_acc = bias_acc + jnp.sum(flat_grads.astype(jnp.float32), axis=0)
        grad_padded = extended(grad_gates, (("rows", 0), ("cols", 1)), 1)
        reversed_cols = tap_columns(grad_padded, rows_dev, cols_dev, True)
        grad_stacked = jnp.dot(reversed_cols, adjoint_matrix, preferred_element_type=jnp.float32)
        grad_stacked = grad_stacked.reshape(rows_dev, cols_dev, chans)
        grad_hidden = grad_stacked[..., CI:]
        if moment > 0:
            grad_hidden = grad_hidden + cotangent[moment - 1].astype(jnp.float32)
    kernel_total, bias_total = lax.psum((kernel_acc, bias_acc), ("rows", "cols"))
    total_cells = STEPS * rows_dev * lax.axis_size("rows") * cols_dev * lax.axis_size("cols")
    norm_scale = 1.0 / math.sqrt(total_cells)
    return (hidden, grad_hidden, grad_cell, kernel_total * norm_scale, bias_total * norm_scale)


def solution(mesh):
    placed = (
        P(None, "rows", "cols"),
        P("rows", "cols", None),
        P("rows", "cols", None),
        P(),
        P(),
        P(None, "rows", "cols", None),
    )
    return jax.shard_map(
        shards,
        mesh=mesh,
        in_specs=placed,
        out_specs=(
            P("rows", "cols", None),
            P("rows", "cols", None),
            P("rows", "cols", None),
            P(),
            P(),
        ),
        check_vma=False,
    )
```

profile of v0, /device:TPU:1, one launch (start us, length us, event | category | flops | bytes accessed | tf_op | source)
XLA Modules:
  0.0 273.0 jit_solution(14365913064977950264)
XLA Ops:
  8.8 3.9 %collective-permute-start = (bf16[1,32,160]{2,1,0:T(8,128)(2,1)S(1)}, bf16[1,32,160]{2,1,0:T(8,128)(2,1)S(1)}, u32[]{:S(2)}, u32[]{:S(2)}) collective-permute-start(bf16[1,32,160]{2,1,0:T(8,128)(2,1)S(1)} %get-tuple-element.60), channel_id=1, source_target_pairs={{0,8},{8,16},{16,24},{1,9},{9,17},{17,25},{2,10},{10,18},{18,26},{... | collective-permute-start | bytes 30728 | tf_op jit(solution)/shard_map/ppermute | solution.py:24
  12.8 1.3 collective-permute-start.1
  14.3 3.0 %collective-permute-done.1 = bf16[1,32,160]{2,1,0:T(8,128)(2,1)S(1)} collective-permute-done((bf16[1,32,160]{2,1,0:T(8,128)(2,1)S(1)}, bf16[1,32,160]{2,1,0:T(8,128)(2,1)S(1)}, u32[]{:S(2)}, u32[]{:S(2)}) %collective-permute-start.1) | collective-permute-done | bytes 10272 | tf_op jit(solution)/shard_map/ppermute | solution.py:26
  18.1 4.0 %collective-permute-start.3 = (bf16[6,1,160]{2,1,0:T(2,128)(2,1)S(1)}, bf16[6,1,160]{2,1,0:T(2,128)(2,1)S(1)}, u32[]{:S(2)}, u32[]{:S(2)}) collective-permute-start(bf16[6,1,160]{2,1,0:T(2,128)(2,1)S(1)} %get-tuple-element.52), channel_id=1, source_target_pairs={{1,0},{2,1},{3,2},{4,3},{5,4},{6,5},{7,6},{9,8},{10,9},{11,10},{12... | collective-permute-start | bytes 5768 | tf_op jit(solution)/shard_map/ppermute | solution.py:26
  22.1 3.2 %collective-permute-start.2 = (bf16[6,1,160]{2,1,0:T(2,128)(2,1)S(1)}, bf16[6,1,160]{2,1,0:T(2,128)(2,1)S(1)}, u32[]{:S(2)}, u32[]{:S(2)}) collective-permute-start(bf16[6,1,160]{2,1,0:T(2,128)(2,1)S(1)} %get-tuple-element.53), channel_id=1, source_target_pairs={{0,1},{1,2},{2,3},{3,4},{4,5},{5,6},{6,7},{8,9},{9,10},{10,11},{11... | collective-permute-start | bytes 5768 | tf_op jit(solution)/shard_map/ppermute | solution.py:24
  28.6 4.0 %collective-permute-start.4 = (bf16[1,32,160]{2,1,0:T(8,128)(2,1)S(1)}, bf16[1,32,160]{2,1,0:T(8,128)(2,1)S(1)}, u32[]{:S(2)}, u32[]{:S(2)}) collective-permute-start(bf16[1,32,160]{2,1,0:T(8,128)(2,1)S(1)} %get-tuple-element.56), channel_id=1, source_target_pairs={{0,8},{8,16},{16,24},{1,9},{9,17},{17,25},{2,10},{10,18},{18,26},{... | collective-permute-start | bytes 30728 | tf_op jit(solution)/shard_map/ppermute | solution.py:24
  34.0 3.5 %collective-permute-done.5 = bf16[1,32,160]{2,1,0:T(8,128)(2,1)S(1)} collective-permute-done((bf16[1,32,160]{2,1,0:T(8,128)(2,1)S(1)}, bf16[1,32,160]{2,1,0:T(8,128)(2,1)S(1)}, u32[]{:S(2)}, u32[]{:S(2)}) %collective-permute-start.5) | collective-permute-done | bytes 10272 | tf_op jit(solution)/shard_map/ppermute | solution.py:26
  37.6 2.4 collective-permute-start.7
  40.0 4.6 %collective-permute-start.6 = (bf16[6,1,160]{2,1,0:T(2,128)(2,1)S(1)}, bf16[6,1,160]{2,1,0:T(2,128)(2,1)S(1)}, u32[]{:S(2)}, u32[]{:S(2)}) collective-permute-start(bf16[6,1,160]{2,1,0:T(2,128)(2,1)S(1)} %get-tuple-element.49), channel_id=1, source_target_pairs={{0,1},{1,2},{2,3},{3,4},{4,5},{5,6},{6,7},{8,9},{9,10},{10,11},{11... | collective-permute-start | bytes 5768 | tf_op jit(solution)/shard_map/ppermute | solution.py:24
  48.1 3.1 %collective-permute-start.8 = (bf16[1,32,512]{2,1,0:T(8,128)(2,1)S(1)}, bf16[1,32,512]{2,1,0:T(8,128)(2,1)S(1)}, u32[]{:S(2)}, u32[]{:S(2)}) collective-permute-start(bf16[1,32,512]{2,1,0:T(8,128)(2,1)S(1)} %get-tuple-element.32), channel_id=1, source_target_pairs={{0,8},{8,16},{16,24},{1,9},{9,17},{17,25},{2,10},{10,18},{18,26},{... | collective-permute-start | bytes 98312 | tf_op jit(solution)/shard_map/ppermute | solution.py:24
  51.2 1.3 collective-permute-start.9
  52.5 2.5 copy.14
  55.0 4.0 %reshape.83 = bf16[4608,160,1]{0,1,2:T(8,128)(2,1)} reshape(bf16[9,512,160]{1,0,2:T(8,128)(2,1)} %bitcast.57) | data formatting | bytes 2949120 | tf_op jit(solution)/shard_map/reshape | solution.py:75
  59.3 4.5 %collective-permute-start.11 = (bf16[6,1,512]{2,1,0:T(2,128)(2,1)S(1)}, bf16[6,1,512]{2,1,0:T(2,128)(2,1)S(1)}, u32[]{:S(2)}, u32[]{:S(2)}) collective-permute-start(bf16[6,1,512]{2,1,0:T(2,128)(2,1)S(1)} %get-tuple-element.28), channel_id=1, source_target_pairs={{0,1},{1,2},{2,3},{3,4},{4,5},{5,6},{6,7},{8,9},{9,10},{10,11},{11... | collective-permute-start | bytes 18440 | tf_op jit(solution)/shard_map/ppermute | solution.py:24
  63.8 1.9 collective-permute-start.10
  66.0 2.7 collective-permute-done.10
  71.5 4.3 %collective-permute-start.12 = (bf16[1,32,512]{2,1,0:T(8,128)(2,1)S(1)}, bf16[1,32,512]{2,1,0:T(8,128)(2,1)S(1)}, u32[]{:S(2)}, u32[]{:S(2)}) collective-permute-start(bf16[1,32,512]{2,1,0:T(8,128)(2,1)S(1)} %get-tuple-element.30), channel_id=1, source_target_pairs={{0,8},{8,16},{16,24},{1,9},{9,17},{17,25},{2,10},{10,18},{18,26},{... | collective-permute-start | bytes 98312 | tf_op jit(solution)/shard_map/ppermute | solution.py:24
  77.6 2.2 fusion
  79.8 39.2 %psum.15 = f32[512]{0:T(512)S(1)} all-reduce(f32[512]{0:T(512)S(1)} %add.68), channel_id=1, replica_groups=mesh['rows'=4,'cols'=8] {'rows','cols'}, use_global_device_ids=true, to_apply=%region_3.0 | all-reduce | flops 512 | bytes 4096 | tf_op jit(solution)/shard_map/psum | solution.py:102
  119.1 3.6 %collective-permute-start.15 = (bf16[6,1,512]{2,1,0:T(2,128)(2,1)S(1)}, bf16[6,1,512]{2,1,0:T(2,128)(2,1)S(1)}, u32[]{:S(2)}, u32[]{:S(2)}) collective-permute-start(bf16[6,1,512]{2,1,0:T(2,128)(2,1)S(1)} %get-tuple-element.24), channel_id=1, source_target_pairs={{0,1},{1,2},{2,3},{3,4},{4,5},{5,6},{6,7},{8,9},{9,10},{10,11},{11... | collective-permute-start | bytes 18440 | tf_op jit(solution)/shard_map/ppermute | solution.py:24
  122.7 1.9 collective-permute-start.14
  125.3 2.5 collective-permute-done.14
  130.3 132.0 %all-reduce.2.cloned.1.call-done = f32[1440,512]{1,0:T(8,128)} async-done(((f32[1440,512]{1,0:T(8,128)}), f32[1440,512]{1,0:T(8,128)}) %all-reduce.2.cloned.1.call-update) | async-done | bytes 2949136 | tf_op jit(solution)/shard_map/psum | solution.py:102
  262.3 3.8 %broadcast_multiply_fusion = f32[1440,512]{1,0:T(8,128)} fusion(f32[1440,512]{1,0:T(8,128)} %all-reduce.2.cloned.1.call-done), kind=kLoop, calls=%fused_computation.4 | loop fusion | flops 737280 | bytes 5898240 | tf_op jit(solution)/shard_map/mul | solution.py:105
  (113 shorter events, 18.9 us)
Async XLA Ops:
  7.2 20.1 %copy-start.3 = (bf16[4,32,128]{2,1,0:T(8,128)(2,1)S(1)}, bf16[4,32,128]{2,1,0:T(8,128)(2,1)}, u32[]{:S(2)}) copy-start(bf16[4,32,128]{2,1,0:T(8,128)(2,1)} %param.7) | copy-start | bytes 98308
  7.2 255.2 %all-reduce.2.cloned.1.call-start = ((), (), s32[]{:S(2)}) async-start(), calls=%async_computation | async-start | bytes 5898240 | tf_op jit(solution)/shard_map/psum | solution.py:102
  8.8 5.4 %collective-permute-start = (bf16[1,32,160]{2,1,0:T(8,128)(2,1)S(1)}, bf16[1,32,160]{2,1,0:T(8,128)(2,1)S(1)}, u32[]{:S(2)}, u32[]{:S(2)}) collective-permute-start(bf16[1,32,160]{2,1,0:T(8,128)(2,1)S(1)} %get-tuple-element.60), channel_id=1, source_target_pairs={{0,8},{8,16},{16,24},{1,9},{9,17},{17,25},{2,10},{10,18},{18,26},{... | collective-permute-start | bytes 30728 | tf_op jit(solution)/shard_map/ppermute | solution.py:24
  12.8 4.5 %collective-permute-start.1 = (bf16[1,32,160]{2,1,0:T(8,128)(2,1)S(1)}, bf16[1,32,160]{2,1,0:T(8,128)(2,1)S(1)}, u32[]{:S(2)}, u32[]{:S(2)}) collective-permute-start(bf16[1,32,160]{2,1,0:T(8,128)(2,1)S(1)} %get-tuple-element.61), channel_id=1, source_target_pairs={{8,0},{16,8},{24,16},{9,1},{17,9},{25,17},{10,2},{18,10},{26,18},{... | collective-permute-start | bytes 30728 | tf_op jit(solution)/shard_map/ppermute | solution.py:26
  18.1 8.2 %collective-permute-start.3 = (bf16[6,1,160]{2,1,0:T(2,128)(2,1)S(1)}, bf16[6,1,160]{2,1,0:T(2,128)(2,1)S(1)}, u32[]{:S(2)}, u32[]{:S(2)}) collective-permute-start(bf16[6,1,160]{2,1,0:T(2,128)(2,1)S(1)} %get-tuple-element.52), channel_id=1, source_target_pairs={{1,0},{2,1},{3,2},{4,3},{5,4},{6,5},{7,6},{9,8},{10,9},{11,10},{12... | collective-permute-start | bytes 5768 | tf_op jit(solution)/shard_map/ppermute | solution.py:26
  22.1 5.5 %copy-start = (bf16[1440,512]{1,0:T(8,128)(2,1)S(1)}, bf16[1440,512]{1,0:T(8,128)(2,1)}, u32[]{:S(2)}) copy-start(bf16[1440,512]{1,0:T(8,128)(2,1)} %param.9) | copy-start | bytes 4423684
  22.1 5.5 %copy-start.16 = (f32[512]{0:T(512)S(1)}, f32[512]{0:T(512)}, u32[]{:S(2)}) copy-start(f32[512]{0:T(512)} %param.10) | copy-start | bytes 6148
  22.1 4.2 %collective-permute-start.2 = (bf16[6,1,160]{2,1,0:T(2,128)(2,1)S(1)}, bf16[6,1,160]{2,1,0:T(2,128)(2,1)S(1)}, u32[]{:S(2)}, u32[]{:S(2)}) collective-permute-start(bf16[6,1,160]{2,1,0:T(2,128)(2,1)S(1)} %get-tuple-element.53), channel_id=1, source_target_pairs={{0,1},{1,2},{2,3},{3,4},{4,5},{5,6},{6,7},{8,9},{9,10},{10,11},{11... | collective-permute-start | bytes 5768 | tf_op jit(solution)/shard_map/ppermute | solution.py:24
  28.6 5.4 %collective-permute-start.4 = (bf16[1,32,160]{2,1,0:T(8,128)(2,1)S(1)}, bf16[1,32,160]{2,1,0:T(8,128)(2,1)S(1)}, u32[]{:S(2)}, u32[]{:S(2)}) collective-permute-start(bf16[1,32,160]{2,1,0:T(8,128)(2,1)S(1)} %get-tuple-element.56), channel_id=1, source_target_pairs={{0,8},{8,16},{16,24},{1,9},{9,17},{17,25},{2,10},{10,18},{18,26},{... | collective-permute-start | bytes 30728 | tf_op jit(solution)/shard_map/ppermute | solution.py:24
  32.6 4.9 %collective-permute-start.5 = (bf16[1,32,160]{2,1,0:T(8,128)(2,1)S(1)}, bf16[1,32,160]{2,1,0:T(8,128)(2,1)S(1)}, u32[]{:S(2)}, u32[]{:S(2)}) collective-permute-start(bf16[1,32,160]{2,1,0:T(8,128)(2,1)S(1)} %get-tuple-element.57), channel_id=1, source_target_pairs={{8,0},{16,8},{24,16},{9,1},{17,9},{25,17},{10,2},{18,10},{26,18},{... | collective-permute-start | bytes 30728 | tf_op jit(solution)/shard_map/ppermute | solution.py:26
  37.6 7.1 %collective-permute-start.7 = (bf16[6,1,160]{2,1,0:T(2,128)(2,1)S(1)}, bf16[6,1,160]{2,1,0:T(2,128)(2,1)S(1)}, u32[]{:S(2)}, u32[]{:S(2)}) collective-permute-start(bf16[6,1,160]{2,1,0:T(2,128)(2,1)S(1)} %get-tuple-element.48), channel_id=1, source_target_pairs={{1,0},{2,1},{3,2},{4,3},{5,4},{6,5},{7,6},{9,8},{10,9},{11,10},{12... | collective-permute-start | bytes 5768 | tf_op jit(solution)/shard_map/ppermute | solution.py:26
  40.0 5.3 %collective-permute-start.6 = (bf16[6,1,160]{2,1,0:T(2,128)(2,1)S(1)}, bf16[6,1,160]{2,1,0:T(2,128)(2,1)S(1)}, u32[]{:S(2)}, u32[]{:S(2)}) collective-permute-start(bf16[6,1,160]{2,1,0:T(2,128)(2,1)S(1)} %get-tuple-element.49), channel_id=1, source_target_pairs={{0,1},{1,2},{2,3},{3,4},{4,5},{5,6},{6,7},{8,9},{9,10},{10,11},{11... | collective-permute-start | bytes 5768 | tf_op jit(solution)/shard_map/ppermute | solution.py:24
  48.1 11.1 %collective-permute-start.8 = (bf16[1,32,512]{2,1,0:T(8,128)(2,1)S(1)}, bf16[1,32,512]{2,1,0:T(8,128)(2,1)S(1)}, u32[]{:S(2)}, u32[]{:S(2)}) collective-permute-start(bf16[1,32,512]{2,1,0:T(8,128)(2,1)S(1)} %get-tuple-element.32), channel_id=1, source_target_pairs={{0,8},{8,16},{16,24},{1,9},{9,17},{17,25},{2,10},{10,18},{18,26},{... | collective-permute-start | bytes 98312 | tf_op jit(solution)/shard_map/ppermute | solution.py:24
  51.2 8.0 %collective-permute-start.9 = (bf16[1,32,512]{2,1,0:T(8,128)(2,1)S(1)}, bf16[1,32,512]{2,1,0:T(8,128)(2,1)S(1)}, u32[]{:S(2)}, u32[]{:S(2)}) collective-permute-start(bf16[1,32,512]{2,1,0:T(8,128)(2,1)S(1)} %get-tuple-element.33), channel_id=1, source_target_pairs={{8,0},{16,8},{24,16},{9,1},{17,9},{25,17},{10,2},{18,10},{26,18},{... | collective-permute-start | bytes 98312 | tf_op jit(solution)/shard_map/ppermute | solution.py:26
  58.9 6.8 %copy-start.5 = (bf16[4,32,160]{2,1,0:T(8,128)(2,1)S(1)}, bf16[4,32,160]{2,1,0:T(8,128)(2,1)}, u32[]{:S(2)}) copy-start(bf16[4,32,160]{2,1,0:T(8,128)(2,1)} %copy-done.4) | copy-start | bytes 122884
  58.9 6.8 %copy-start.7 = (bf16[4,32,160]{2,1,0:T(8,128)(2,1)S(1)}, bf16[4,32,160]{2,1,0:T(8,128)(2,1)}, u32[]{:S(2)}) copy-start(bf16[4,32,160]{2,1,0:T(8,128)(2,1)} %copy-done.6) | copy-start | bytes 122884
  58.9 6.8 %copy-start.9 = (bf16[4,32,160]{2,1,0:T(8,128)(2,1)S(1)}, bf16[4,32,160]{2,1,0:T(8,128)(2,1)}, u32[]{:S(2)}) copy-start(bf16[4,32,160]{2,1,0:T(8,128)(2,1)} %copy-done.8) | copy-start | bytes 122884
  58.9 6.8 %copy-start.11 = (bf16[4,32,160]{2,1,0:T(8,128)(2,1)S(1)}, bf16[4,32,160]{2,1,0:T(8,128)(2,1)}, u32[]{:S(2)}) copy-start(bf16[4,32,160]{2,1,0:T(8,128)(2,1)} %copy-done.10) | copy-start | bytes 122884
  59.3 6.8 %collective-permute-start.11 = (bf16[6,1,512]{2,1,0:T(2,128)(2,1)S(1)}, bf16[6,1,512]{2,1,0:T(2,128)(2,1)S(1)}, u32[]{:S(2)}, u32[]{:S(2)}) collective-permute-start(bf16[6,1,512]{2,1,0:T(2,128)(2,1)S(1)} %get-tuple-element.28), channel_id=1, source_target_pairs={{0,1},{1,2},{2,3},{3,4},{4,5},{5,6},{6,7},{8,9},{9,10},{10,11},{11... | collective-permute-start | bytes 18440 | tf_op jit(solution)/shard_map/ppermute | solution.py:24
  63.8 5.0 %collective-permute-start.10 = (bf16[6,1,512]{2,1,0:T(2,128)(2,1)S(1)}, bf16[6,1,512]{2,1,0:T(2,128)(2,1)S(1)}, u32[]{:S(2)}, u32[]{:S(2)}) collective-permute-start(bf16[6,1,512]{2,1,0:T(2,128)(2,1)S(1)} %get-tuple-element.29), channel_id=1, source_target_pairs={{1,0},{2,1},{3,2},{4,3},{5,4},{6,5},{7,6},{9,8},{10,9},{11,10},{12... | collective-permute-start | bytes 18440 | tf_op jit(solution)/shard_map/ppermute | solution.py:26
  71.5 47.6 %collective-permute-start.12 = (bf16[1,32,512]{2,1,0:T(8,128)(2,1)S(1)}, bf16[1,32,512]{2,1,0:T(8,128)(2,1)S(1)}, u32[]{:S(2)}, u32[]{:S(2)}) collective-permute-start(bf16[1,32,512]{2,1,0:T(8,128)(2,1)S(1)} %get-tuple-element.30), channel_id=1, source_target_pairs={{0,8},{8,16},{16,24},{1,9},{9,17},{17,25},{2,10},{10,18},{18,26},{... | collective-permute-start | bytes 98312 | tf_op jit(solution)/shard_map/ppermute | solution.py:24
  75.7 43.3 %collective-permute-start.13 = (bf16[1,32,512]{2,1,0:T(8,128)(2,1)S(1)}, bf16[1,32,512]{2,1,0:T(8,128)(2,1)S(1)}, u32[]{:S(2)}, u32[]{:S(2)}) collective-permute-start(bf16[1,32,512]{2,1,0:T(8,128)(2,1)S(1)} %get-tuple-element.31), channel_id=1, source_target_pairs={{8,0},{16,8},{24,16},{9,1},{17,9},{25,17},{10,2},{18,10},{26,18},{... | collective-permute-start | bytes 98312 | tf_op jit(solution)/shard_map/ppermute | solution.py:26
  119.1 6.2 %collective-permute-start.15 = (bf16[6,1,512]{2,1,0:T(2,128)(2,1)S(1)}, bf16[6,1,512]{2,1,0:T(2,128)(2,1)S(1)}, u32[]{:S(2)}, u32[]{:S(2)}) collective-permute-start(bf16[6,1,512]{2,1,0:T(2,128)(2,1)S(1)} %get-tuple-element.24), channel_id=1, source_target_pairs={{0,1},{1,2},{2,3},{3,4},{4,5},{5,6},{6,7},{8,9},{9,10},{10,11},{11... | collective-permute-start | bytes 18440 | tf_op jit(solution)/shard_map/ppermute | solution.py:24
  122.7 5.0 %collective-permute-start.14 = (bf16[6,1,512]{2,1,0:T(2,128)(2,1)S(1)}, bf16[6,1,512]{2,1,0:T(2,128)(2,1)S(1)}, u32[]{:S(2)}, u32[]{:S(2)}) collective-permute-start(bf16[6,1,512]{2,1,0:T(2,128)(2,1)S(1)} %get-tuple-element.25), channel_id=1, source_target_pairs={{1,0},{2,1},{3,2},{4,3},{5,4},{6,5},{7,6},{9,8},{10,9},{11,10},{12... | collective-permute-start | bytes 18440 | tf_op jit(solution)/shard_map/ppermute | solution.py:26
  (10 other events, 9.5 us)
Sparse Core Ops, SparseCore 0:
  125.4 136.9 all-reduce.1
where the time goes:
time: 276 us; the launch traced here: 273 us
  waiting for transfers between devices  144 us (52%)
  starting transfers between devices  46.7 us (17%)
  blocking collectives  39.2 us (14%)
  between operations  14.7 us (5%)
  local copies, waits for them, and re-layouts  12.7 us (5%)
  other arithmetic  9.56 us (3%)
  matrix products  5.7 us (2%)
    psum x1, waiting for transfers between devices, shards(): lax.psum((kernel_acc, bias_acc), ('rows', 'cols'))  132 us
    psum x1, blocking collectives, shards(): lax.psum((kernel_acc, bias_acc), ('rows', 'cols'))  39.2 us
    ppermute x8, starting transfers between devices, extended(): lax.ppermute(tail, axis, [(i, (i + 1) % count) for i in range(ends)])  31.2 us
    ppermute x8, starting transfers between devices, extended(): lax.ppermute(head, axis, [((i + 1) % count, i) for i in range(ends)])  15.4 us
    ppermute x8, waiting for transfers between devices, extended(): lax.ppermute(head, axis, [((i + 1) % count, i) for i in range(ends)])  11.7 us
  transfers between devices with their start and end apart: 17, of which 6 were waited for; matrix products, arithmetic and copies ran while one was open for 5% of the time, Pallas kernels for 0%

commit v1 on v0

--- a/solution.py
+++ b/solution.py
@@ -11,6 +11,8 @@
 STEPS = 2
 GATES = 512
 KIN = 1440
+SUM_ROWS = 1536
+SUM_WAYS = 3
 
 
 def extended(cells, sides, width):
@@ -29,6 +31,62 @@
         )
     return cells
 
+
+def flip_pairs(axis, bit):
+    count = lax.axis_size(axis)
+    return [(i, i ^ (1 << bit)) for i in range(count)]
+
+
+def summing_levels():
+    levels = []
+    for axis in ("cols", "rows"):
+        count = lax.axis_size(axis)
+        depth = count.bit_length() - 1
+        assert (1 << depth) == count
+        levels.extend((axis, bit) for bit in range(depth))
+    cols_levels = [lv for lv in levels if lv[0] == "cols"]
+    rows_levels = [lv for lv in levels if lv[0] == "rows"]
+    return cols_levels[:1], cols_levels[1:2] + rows_levels + cols_levels[2:]
+
+
+def halve(part, levels):
+    halved = []
+    for axis, bit in levels:
+        rows = part.shape[0]
+        if rows % 16 != 0:
+            break
+        half = rows // 2
+        upper = (lax.axis_index(axis) >> bit) & 1
+        keep = lax.dynamic_slice_in_dim(part, upper * half, half, 0)
+        send = lax.dynamic_slice_in_dim(part, (1 - upper) * half, half, 0)
+        part = keep + lax.ppermute(send, axis, flip_pairs(axis, bit))
+        halved.append((axis, bit))
+    for axis, bit in levels[len(halved):]:
+        part = part + lax.ppermute(part, axis, flip_pairs(axis, bit))
+    return part, halved
+
+
+def double(piece, halved):
+    for axis, bit in reversed(halved):
+        upper = (lax.axis_index(axis) >> bit) & 1
+        got = lax.ppermute(piece, axis, flip_pairs(axis, bit))
+        low = jnp.where(upper == 0, piece, got)
+        high = jnp.where(upper == 0, got, piece)
+        piece = jnp.concatenate([low, high], axis=0)
+    return piece
+
+
+def sum_everywhere(total):
+    first, rest = summing_levels()
+    part, first_halved = halve(total, first)
+    ways = min(SUM_WAYS, max(len(rest), 1))
+    width = part.shape[0] // ways
+    pieces = []
+    for way in range(ways):
+        order = rest[way:] + rest[:way]
+        chunk, halved = halve(part[way * width : (way + 1) * width], order)
+        pieces.append(double(chunk.astype(jnp.bfloat16), halved))
+    return double(jnp.concatenate(pieces, axis=0), first_halved).astype(jnp.float32)
 
 def tap_columns(padded, rows_dev, cols_dev, reverse):
     pieces = []
@@ -75,8 +133,9 @@
     adjoint_matrix = jnp.transpose(blocks, (0, 2, 1)).reshape(taps * GATES, chans)
     grad_hidden = cotangent[STEPS - 1].astype(jnp.float32)
     grad_cell = jnp.zeros((rows_dev, cols_dev, HC), jnp.float32)
-    kernel_acc = jnp.zeros((KIN, GATES), jnp.float32)
-    bias_acc = jnp.zeros((GATES,), jnp.float32)
+    spare = SUM_ROWS - KIN - 1
+    lifted = []
+    grads_seen = []
     for moment in range(STEPS - 1, -1, -1):
         patches, gate_in, gate_forget, gate_cand, gate_out, cell_prev, cell_now = saved[moment]
         tanh_cell = jnp.tanh(cell_now)
@@ -90,8 +149,17 @@
             jnp.bfloat16
         )
         flat_grads = grad_gates.reshape(cells, GATES)
-        kernel_acc = kernel_acc + jnp.dot(patches.T, flat_grads, preferred_element_type=jnp.float32)
-        bias_acc = bias_acc + jnp.sum(flat_grads.astype(jnp.float32), axis=0)
+        lifted.append(
+            jnp.concatenate(
+                [
+                    patches,
+                    jnp.ones((cells, 1), patches.dtype),
+                    jnp.zeros((cells, spare), patches.dtype),
+                ],
+                axis=1,
+            )
+        )
+        grads_seen.append(flat_grads)
         grad_padded = extended(grad_gates, (("rows", 0), ("cols", 1)), 1)
         reversed_cols = tap_columns(grad_padded, rows_dev, cols_dev, True)
         grad_stacked = jnp.dot(reversed_cols, adjoint_matrix, preferred_element_type=jnp.float32)
@@ -99,10 +167,15 @@
         grad_hidden = grad_stacked[..., CI:]
         if moment > 0:
             grad_hidden = grad_hidden + cotangent[moment - 1].astype(jnp.float32)
-    kernel_total, bias_total = lax.psum((kernel_acc, bias_acc), ("rows", "cols"))
     total_cells = STEPS * rows_dev * lax.axis_size("rows") * cols_dev * lax.axis_size("cols")
     norm_scale = 1.0 / math.sqrt(total_cells)
-    return (hidden, grad_hidden, grad_cell, kernel_total * norm_scale, bias_total * norm_scale)
+    joined = jnp.dot(
+        jnp.concatenate(lifted, axis=0).T,
+        jnp.concatenate(grads_seen, axis=0),
+        preferred_element_type=jnp.float32,
+    )
+    summed_all = sum_everywhere(joined * norm_scale)
+    return (hidden, grad_hidden, grad_cell, summed_all[:KIN], summed_all[KIN])
 
 
 def solution(mesh):

time: 276 us -> 147 us (0.53)
  waiting for transfers between devices: 144 us -> 41.4 us
  blocking collectives: 39.2 us -> 0 us
  starting transfers between devices: 46.7 us -> 74.5 us
  between operations: 14.7 us -> 1.75 us
    psum x1 -> x0, waiting for transfers between devices: 132 us -> none  [shards(): lax.psum((kernel_acc, bias_acc), ('rows', 'cols'))]
    psum x1 -> x0, blocking collectives: 39.2 us -> none  [shards(): lax.psum((kernel_acc, bias_acc), ('rows', 'cols'))]
    ppermute x0 -> x26, starting transfers between devices: none -> 27 us  [the longest x13 19.6 us: double(): got = lax.ppermute(piece, axis, flip_pairs(axis, bit))]
    ppermute x0 -> x26, waiting for transfers between devices: none -> 24.5 us  [the longest x13 17.7 us: halve(): part = keep + lax.ppermute(send, axis, flip_pairs(axis, bit))]
    ppermute x8, waiting for transfers between devices: 11.7 us -> 16.2 us  [extended(): lax.ppermute(head, axis, [((i + 1) % count, i) for i in range(ends)])]
    mul x2 -> x0, other arithmetic: 4.37 us -> none  [the longest x1 3.79 us: shards(): kernel_total * norm_scale]
  transfers between devices with their start and end apart: 17 -> 42, of which waited for: 6 -> 23; matrix products, arithmetic and copies ran while one was open for 5% -> 8% of each run, Pallas kernels for 0% -> 0%
where the time goes in v1:
time: 147 us; the launch traced here: 146 us
  starting transfers between devices  74.5 us (51%)
  waiting for transfers between devices  41.4 us (28%)
  local copies, waits for them, and re-layouts  15.4 us (10%)
  other arithmetic  9.33 us (6%)
  matrix products  3.57 us (2%)
  between operations  1.75 us (1%)
    ppermute x8, starting transfers between devices, extended(): lax.ppermute(tail, axis, [(i, (i + 1) % count) for i in range(ends)])  32.1 us
    ppermute x13, starting transfers between devices, double(): got = lax.ppermute(piece, axis, flip_pairs(axis, bit))  19.6 us
    ppermute x13, waiting for transfers between devices, halve(): part = keep + lax.ppermute(send, axis, flip_pairs(axis, bit))  17.7 us
    ppermute x8, waiting for transfers between devices, extended(): lax.ppermute(head, axis, [((i + 1) % count, i) for i in range(ends)])  16.2 us
    ppermute x8, starting transfers between devices, extended(): lax.ppermute(head, axis, [((i + 1) % count, i) for i in range(ends)])  15.4 us
    ppermute x13, starting transfers between devices, halve(): part = keep + lax.ppermute(send, axis, flip_pairs(axis, bit))  7.37 us
    ppermute x13, waiting for transfers between devices, double(): got = lax.ppermute(piece, axis, flip_pairs(axis, bit))  6.83 us
    concatenate x10, other arithmetic, extended(): jnp.concatenate([lax.ppermute(tail, axis, [(i, (i + 1) % count) for i in...  3.9 us
  transfers between devices with their start and end apart: 42, of which 23 were waited for; matrix products, arithmetic and copies ran while one was open for 8% of the time, Pallas kernels for 0%

profile of v1, /device:TPU:1, one launch (start us, length us, event | category | flops | bytes accessed | tf_op | source)
XLA Modules:
  0.0 145.9 jit_solution(4354436020355940070)
XLA Ops:
  2.3 3.9 %collective-permute-start = (bf16[1,32,160]{2,1,0:T(8,128)(2,1)S(1)}, bf16[1,32,160]{2,1,0:T(8,128)(2,1)S(1)}, u32[]{:S(2)}, u32[]{:S(2)}) collective-permute-start(bf16[1,32,160]{2,1,0:T(8,128)(2,1)S(1)} %get-tuple-element.77), channel_id=1, source_target_pairs={{0,8},{8,16},{16,24},{1,9},{9,17},{17,25},{2,10},{10,18},{18,26},{... | collective-permute-start | bytes 30728 | tf_op jit(solution)/shard_map/ppermute | solution.py:26
  7.7 3.0 %collective-permute-done.1 = bf16[1,32,160]{2,1,0:T(8,128)(2,1)S(1)} collective-permute-done((bf16[1,32,160]{2,1,0:T(8,128)(2,1)S(1)}, bf16[1,32,160]{2,1,0:T(8,128)(2,1)S(1)}, u32[]{:S(2)}, u32[]{:S(2)}) %collective-permute-start.1) | collective-permute-done | bytes 10272 | tf_op jit(solution)/shard_map/ppermute | solution.py:28
  11.5 4.0 %collective-permute-start.3 = (bf16[6,1,160]{2,1,0:T(2,128)(2,1)S(1)}, bf16[6,1,160]{2,1,0:T(2,128)(2,1)S(1)}, u32[]{:S(2)}, u32[]{:S(2)}) collective-permute-start(bf16[6,1,160]{2,1,0:T(2,128)(2,1)S(1)} %get-tuple-element.63), channel_id=1, source_target_pairs={{1,0},{2,1},{3,2},{4,3},{5,4},{6,5},{7,6},{9,8},{10,9},{11,10},{12... | collective-permute-start | bytes 5768 | tf_op jit(solution)/shard_map/ppermute | solution.py:28
  15.5 3.2 %collective-permute-start.2 = (bf16[6,1,160]{2,1,0:T(2,128)(2,1)S(1)}, bf16[6,1,160]{2,1,0:T(2,128)(2,1)S(1)}, u32[]{:S(2)}, u32[]{:S(2)}) collective-permute-start(bf16[6,1,160]{2,1,0:T(2,128)(2,1)S(1)} %get-tuple-element.64), channel_id=1, source_target_pairs={{0,1},{1,2},{2,3},{3,4},{4,5},{5,6},{6,7},{8,9},{9,10},{10,11},{11... | collective-permute-start | bytes 5768 | tf_op jit(solution)/shard_map/ppermute | solution.py:26
  22.0 4.0 %collective-permute-start.4 = (bf16[1,32,160]{2,1,0:T(8,128)(2,1)S(1)}, bf16[1,32,160]{2,1,0:T(8,128)(2,1)S(1)}, u32[]{:S(2)}, u32[]{:S(2)}) collective-permute-start(bf16[1,32,160]{2,1,0:T(8,128)(2,1)S(1)} %get-tuple-element.73), channel_id=1, source_target_pairs={{0,8},{8,16},{16,24},{1,9},{9,17},{17,25},{2,10},{10,18},{18,26},{... | collective-permute-start | bytes 30728 | tf_op jit(solution)/shard_map/ppermute | solution.py:26
  27.5 3.5 %collective-permute-done.5 = bf16[1,32,160]{2,1,0:T(8,128)(2,1)S(1)} collective-permute-done((bf16[1,32,160]{2,1,0:T(8,128)(2,1)S(1)}, bf16[1,32,160]{2,1,0:T(8,128)(2,1)S(1)}, u32[]{:S(2)}, u32[]{:S(2)}) %collective-permute-start.5) | collective-permute-done | bytes 10272 | tf_op jit(solution)/shard_map/ppermute | solution.py:28
  31.0 2.4 %collective-permute-start.7 = (bf16[6,1,160]{2,1,0:T(2,128)(2,1)S(1)}, bf16[6,1,160]{2,1,0:T(2,128)(2,1)S(1)}, u32[]{:S(2)}, u32[]{:S(2)}) collective-permute-start(bf16[6,1,160]{2,1,0:T(2,128)(2,1)S(1)} %get-tuple-element.59), channel_id=1, source_target_pairs={{1,0},{2,1},{3,2},{4,3},{5,4},{6,5},{7,6},{9,8},{10,9},{11,10},{12... | collective-permute-start | bytes 5768 | tf_op jit(solution)/shard_map/ppermute | solution.py:28
  33.4 4.6 %collective-permute-start.6 = (bf16[6,1,160]{2,1,0:T(2,128)(2,1)S(1)}, bf16[6,1,160]{2,1,0:T(2,128)(2,1)S(1)}, u32[]{:S(2)}, u32[]{:S(2)}) collective-permute-start(bf16[6,1,160]{2,1,0:T(2,128)(2,1)S(1)} %get-tuple-element.60), channel_id=1, source_target_pairs={{0,1},{1,2},{2,3},{3,4},{4,5},{5,6},{6,7},{8,9},{9,10},{10,11},{11... | collective-permute-start | bytes 5768 | tf_op jit(solution)/shard_map/ppermute | solution.py:26
  41.5 3.1 %collective-permute-start.8 = (bf16[1,32,512]{2,1,0:T(8,128)(2,1)S(1)}, bf16[1,32,512]{2,1,0:T(8,128)(2,1)S(1)}, u32[]{:S(2)}, u32[]{:S(2)}) collective-permute-start(bf16[1,32,512]{2,1,0:T(8,128)(2,1)S(1)} %get-tuple-element.43), channel_id=1, source_target_pairs={{0,8},{8,16},{16,24},{1,9},{9,17},{17,25},{2,10},{10,18},{18,26},{... | collective-permute-start | bytes 98312 | tf_op jit(solution)/shard_map/ppermute | solution.py:26
  46.0 3.3 %collective-permute-done.9 = bf16[1,32,512]{2,1,0:T(8,128)(2,1)S(1)} collective-permute-done((bf16[1,32,512]{2,1,0:T(8,128)(2,1)S(1)}, bf16[1,32,512]{2,1,0:T(8,128)(2,1)S(1)}, u32[]{:S(2)}, u32[]{:S(2)}) %collective-permute-start.9) | collective-permute-done | bytes 32800 | tf_op jit(solution)/shard_map/ppermute | solution.py:28
  49.3 5.6 %collective-permute-start.11 = (bf16[6,1,512]{2,1,0:T(2,128)(2,1)S(1)}, bf16[6,1,512]{2,1,0:T(2,128)(2,1)S(1)}, u32[]{:S(2)}, u32[]{:S(2)}) collective-permute-start(bf16[6,1,512]{2,1,0:T(2,128)(2,1)S(1)} %get-tuple-element.33), channel_id=1, source_target_pairs={{0,1},{1,2},{2,3},{3,4},{4,5},{5,6},{6,7},{8,9},{9,10},{10,11},{11... | collective-permute-start | bytes 18440 | tf_op jit(solution)/shard_map/ppermute | solution.py:26
  55.0 1.9 %collective-permute-start.10 = (bf16[6,1,512]{2,1,0:T(2,128)(2,1)S(1)}, bf16[6,1,512]{2,1,0:T(2,128)(2,1)}, u32[]{:S(2)}, u32[]{:S(2)}) collective-permute-start(bf16[6,1,512]{2,1,0:T(2,128)(2,1)S(1)} %get-tuple-element.34), channel_id=1, source_target_pairs={{1,0},{2,1},{3,2},{4,3},{5,4},{6,5},{7,6},{9,8},{10,9},{11,10},{12... | collective-permute-start | bytes 18440 | tf_op jit(solution)/shard_map/ppermute | solution.py:28
  56.9 2.5 %copy.14 = bf16[9,160,512]{2,0,1:T(8,128)(2,1)} copy(bf16[9,160,512]{2,1,0:T(8,128)(2,1)S(1)} %bitcast.49) | data formatting | bytes 2949120 | tf_op jit(solution)/shard_map/reshape | solution.py:132
  59.4 3.0 %reshape.83 = bf16[4608,160,1]{0,1,2:T(8,128)(2,1)S(1)} reshape(bf16[9,512,160]{1,0,2:T(8,128)(2,1)} %bitcast.50) | data formatting | bytes 2949120 | tf_op jit(solution)/shard_map/reshape | solution.py:133
  69.5 2.5 %collective-permute-start.12 = (bf16[1,32,512]{2,1,0:T(8,128)(2,1)S(1)}, bf16[1,32,512]{2,1,0:T(8,128)(2,1)S(1)}, u32[]{:S(2)}, u32[]{:S(2)}) collective-permute-start(bf16[1,32,512]{2,1,0:T(8,128)(2,1)S(1)} %get-tuple-element.41), channel_id=1, source_target_pairs={{0,8},{8,16},{16,24},{1,9},{9,17},{17,25},{2,10},{10,18},{18,26},{... | collective-permute-start | bytes 98312 | tf_op jit(solution)/shard_map/ppermute | solution.py:26
  73.3 3.3 %collective-permute-done.13 = bf16[1,32,512]{2,1,0:T(8,128)(2,1)S(1)} collective-permute-done((bf16[1,32,512]{2,1,0:T(8,128)(2,1)S(1)}, bf16[1,32,512]{2,1,0:T(8,128)(2,1)S(1)}, u32[]{:S(2)}, u32[]{:S(2)}) %collective-permute-start.13) | collective-permute-done | bytes 32800 | tf_op jit(solution)/shard_map/ppermute | solution.py:28
  76.7 5.1 %collective-permute-start.15 = (bf16[6,1,512]{2,1,0:T(2,128)(2,1)S(1)}, bf16[6,1,512]{2,1,0:T(2,128)(2,1)S(1)}, u32[]{:S(2)}, u32[]{:S(2)}) collective-permute-start(bf16[6,1,512]{2,1,0:T(2,128)(2,1)S(1)} %get-tuple-element.29), channel_id=1, source_target_pairs={{0,1},{1,2},{2,3},{3,4},{4,5},{5,6},{6,7},{8,9},{9,10},{10,11},{11... | collective-permute-start | bytes 18440 | tf_op jit(solution)/shard_map/ppermute | solution.py:26
  83.8 3.0 %collective-permute-done.14 = bf16[6,1,512]{2,1,0:T(2,128)(2,1)S(1)} collective-permute-done((bf16[6,1,512]{2,1,0:T(2,128)(2,1)S(1)}, bf16[6,1,512]{2,1,0:T(2,128)(2,1)S(1)}, u32[]{:S(2)}, u32[]{:S(2)}) %collective-permute-start.14) | collective-permute-done | bytes 6176 | tf_op jit(solution)/shard_map/ppermute | solution.py:28
  91.3 5.0 %collective-permute-done.17 = f32[128,512]{1,0:T(8,128)S(1)} collective-permute-done((f32[128,512]{1,0:T(8,128)S(1)}, f32[128,512]{1,0:T(8,128)S(1)}, u32[]{:S(2)}, u32[]{:S(2)}) %collective-permute-start.17) | collective-permute-done | bytes 262176 | tf_op jit(solution)/shard_map/ppermute | solution.py:62
  101.7 2.0 %collective-permute-done.26 = f32[64,512]{1,0:T(8,128)S(1)} collective-permute-done((f32[64,512]{1,0:T(8,128)S(1)}, f32[64,512]{1,0:T(8,128)S(1)}, u32[]{:S(2)}, u32[]{:S(2)}) %collective-permute-start.26) | collective-permute-done | bytes 131104 | tf_op jit(solution)/shard_map/ppermute | solution.py:62
  104.7 5.1 %collective-permute-done.34 = f32[64,512]{1,0:T(8,128)S(1)} collective-permute-done((f32[64,512]{1,0:T(8,128)S(1)}, f32[64,512]{1,0:T(8,128)S(1)}, u32[]{:S(2)}, u32[]{:S(2)}) %collective-permute-start.34) | collective-permute-done | bytes 131104 | tf_op jit(solution)/shard_map/ppermute | solution.py:62
  117.9 2.1 %collective-permute-start.30 = (bf16[32,512]{1,0:T(8,128)(2,1)S(1)}, bf16[32,512]{1,0:T(8,128)(2,1)S(1)}, u32[]{:S(2)}, u32[]{:S(2)}) collective-permute-start(bf16[32,512]{1,0:T(8,128)(2,1)S(1)} %pad_maximum_fusion.43), channel_id=1, source_target_pairs={{0,4},{1,5},{2,6},{3,7},{4,0},{5,1},{6,2},{7,3},{8,12},{9,13},{10,... | collective-permute-start | bytes 98312 | tf_op jit(solution)/shard_map/ppermute | solution.py:72
  130.1 2.7 %collective-permute-done.40 = bf16[128,512]{1,0:T(8,128)(2,1)S(1)} collective-permute-done((bf16[128,512]{1,0:T(8,128)(2,1)S(1)}, bf16[128,512]{1,0:T(8,128)(2,1)S(1)}, u32[]{:S(2)}, u32[]{:S(2)}) %collective-permute-start.40) | collective-permute-done | bytes 131104 | tf_op jit(solution)/shard_map/ppermute | solution.py:72
  132.9 8.0 %collective-permute-start.41 = (bf16[768,512]{1,0:T(8,128)(2,1)S(1)}, bf16[768,512]{1,0:T(8,128)(2,1)S(1)}, u32[]{:S(2)}, u32[]{:S(2)}) collective-permute-start(bf16[768,512]{1,0:T(8,128)(2,1)S(1)} %select_dynamic-update-slice_fusion), channel_id=1, source_target_pairs={{0,1},{1,0},{2,3},{3,2},{4,5},{5,4},{6,7},{7,6},{8,9},{9,8},{10,11... | collective-permute-start | bytes 2359304 | tf_op jit(solution)/shard_map/ppermute | solution.py:72
  (224 shorter events, 57.1 us)
Async XLA Ops:
  2.3 5.4 %collective-permute-start = (bf16[1,32,160]{2,1,0:T(8,128)(2,1)S(1)}, bf16[1,32,160]{2,1,0:T(8,128)(2,1)S(1)}, u32[]{:S(2)}, u32[]{:S(2)}) collective-permute-start(bf16[1,32,160]{2,1,0:T(8,128)(2,1)S(1)} %get-tuple-element.77), channel_id=1, source_target_pairs={{0,8},{8,16},{16,24},{1,9},{9,17},{17,25},{2,10},{10,18},{18,26},{... | collective-permute-start | bytes 30728 | tf_op jit(solution)/shard_map/ppermute | solution.py:26
  11.5 8.2 %collective-permute-start.3 = (bf16[6,1,160]{2,1,0:T(2,128)(2,1)S(1)}, bf16[6,1,160]{2,1,0:T(2,128)(2,1)S(1)}, u32[]{:S(2)}, u32[]{:S(2)}) collective-permute-start(bf16[6,1,160]{2,1,0:T(2,128)(2,1)S(1)} %get-tuple-element.63), channel_id=1, source_target_pairs={{1,0},{2,1},{3,2},{4,3},{5,4},{6,5},{7,6},{9,8},{10,9},{11,10},{12... | collective-permute-start | bytes 5768 | tf_op jit(solution)/shard_map/ppermute | solution.py:28
  22.0 5.4 %collective-permute-start.4 = (bf16[1,32,160]{2,1,0:T(8,128)(2,1)S(1)}, bf16[1,32,160]{2,1,0:T(8,128)(2,1)S(1)}, u32[]{:S(2)}, u32[]{:S(2)}) collective-permute-start(bf16[1,32,160]{2,1,0:T(8,128)(2,1)S(1)} %get-tuple-element.73), channel_id=1, source_target_pairs={{0,8},{8,16},{16,24},{1,9},{9,17},{17,25},{2,10},{10,18},{18,26},{... | collective-permute-start | bytes 30728 | tf_op jit(solution)/shard_map/ppermute | solution.py:26
  26.1 4.9 %collective-permute-start.5 = (bf16[1,32,160]{2,1,0:T(8,128)(2,1)S(1)}, bf16[1,32,160]{2,1,0:T(8,128)(2,1)S(1)}, u32[]{:S(2)}, u32[]{:S(2)}) collective-permute-start(bf16[1,32,160]{2,1,0:T(8,128)(2,1)S(1)} %get-tuple-element.74), channel_id=1, source_target_pairs={{8,0},{16,8},{24,16},{9,1},{17,9},{25,17},{10,2},{18,10},{26,18},{... | collective-permute-start | bytes 30728 | tf_op jit(solution)/shard_map/ppermute | solution.py:28
  31.0 7.1 %collective-permute-start.7 = (bf16[6,1,160]{2,1,0:T(2,128)(2,1)S(1)}, bf16[6,1,160]{2,1,0:T(2,128)(2,1)S(1)}, u32[]{:S(2)}, u32[]{:S(2)}) collective-permute-start(bf16[6,1,160]{2,1,0:T(2,128)(2,1)S(1)} %get-tuple-element.59), channel_id=1, source_target_pairs={{1,0},{2,1},{3,2},{4,3},{5,4},{6,5},{7,6},{9,8},{10,9},{11,10},{12... | collective-permute-start | bytes 5768 | tf_op jit(solution)/shard_map/ppermute | solution.py:28
  33.4 5.3 %collective-permute-start.6 = (bf16[6,1,160]{2,1,0:T(2,128)(2,1)S(1)}, bf16[6,1,160]{2,1,0:T(2,128)(2,1)S(1)}, u32[]{:S(2)}, u32[]{:S(2)}) collective-permute-start(bf16[6,1,160]{2,1,0:T(2,128)(2,1)S(1)} %get-tuple-element.60), channel_id=1, source_target_pairs={{0,1},{1,2},{2,3},{3,4},{4,5},{5,6},{6,7},{8,9},{9,10},{10,11},{11... | collective-permute-start | bytes 5768 | tf_op jit(solution)/shard_map/ppermute | solution.py:26
  44.6 4.7 %collective-permute-start.9 = (bf16[1,32,512]{2,1,0:T(8,128)(2,1)S(1)}, bf16[1,32,512]{2,1,0:T(8,128)(2,1)S(1)}, u32[]{:S(2)}, u32[]{:S(2)}) collective-permute-start(bf16[1,32,512]{2,1,0:T(8,128)(2,1)S(1)} %get-tuple-element.44), channel_id=1, source_target_pairs={{8,0},{16,8},{24,16},{9,1},{17,9},{25,17},{10,2},{18,10},{26,18},{... | collective-permute-start | bytes 98312 | tf_op jit(solution)/shard_map/ppermute | solution.py:28
  49.3 15.3 %collective-permute-start.11 = (bf16[6,1,512]{2,1,0:T(2,128)(2,1)S(1)}, bf16[6,1,512]{2,1,0:T(2,128)(2,1)S(1)}, u32[]{:S(2)}, u32[]{:S(2)}) collective-permute-start(bf16[6,1,512]{2,1,0:T(2,128)(2,1)S(1)} %get-tuple-element.33), channel_id=1, source_target_pairs={{0,1},{1,2},{2,3},{3,4},{4,5},{5,6},{6,7},{8,9},{9,10},{10,11},{11... | collective-permute-start | bytes 18440 | tf_op jit(solution)/shard_map/ppermute | solution.py:26
  55.0 9.7 %collective-permute-start.10 = (bf16[6,1,512]{2,1,0:T(2,128)(2,1)S(1)}, bf16[6,1,512]{2,1,0:T(2,128)(2,1)}, u32[]{:S(2)}, u32[]{:S(2)}) collective-permute-start(bf16[6,1,512]{2,1,0:T(2,128)(2,1)S(1)} %get-tuple-element.34), channel_id=1, source_target_pairs={{1,0},{2,1},{3,2},{4,3},{5,4},{6,5},{7,6},{9,8},{10,9},{11,10},{12... | collective-permute-start | bytes 18440 | tf_op jit(solution)/shard_map/ppermute | solution.py:28
  69.5 17.7 %collective-permute-start.16 = (f32[768,512]{1,0:T(8,128)}, f32[768,512]{1,0:T(8,128)}, u32[]{:S(2)}, u32[]{:S(2)}) collective-permute-start(f32[768,512]{1,0:T(8,128)} %constant_dynamic-slice_fusion.12), channel_id=1, source_target_pairs={{0,1},{1,0},{2,3},{3,2},{4,5},{5,4},{6,7},{7,6},{8,9},{9,8},{10,11... | collective-permute-start | bytes 4718600 | tf_op jit(solution)/shard_map/ppermute | solution.py:62
  72.0 4.7 %collective-permute-start.13 = (bf16[1,32,512]{2,1,0:T(8,128)(2,1)S(1)}, bf16[1,32,512]{2,1,0:T(8,128)(2,1)S(1)}, u32[]{:S(2)}, u32[]{:S(2)}) collective-permute-start(bf16[1,32,512]{2,1,0:T(8,128)(2,1)S(1)} %get-tuple-element.42), channel_id=1, source_target_pairs={{8,0},{16,8},{24,16},{9,1},{17,9},{25,17},{10,2},{18,10},{26,18},{... | collective-permute-start | bytes 98312 | tf_op jit(solution)/shard_map/ppermute | solution.py:28
  76.7 7.0 %collective-permute-start.15 = (bf16[6,1,512]{2,1,0:T(2,128)(2,1)S(1)}, bf16[6,1,512]{2,1,0:T(2,128)(2,1)S(1)}, u32[]{:S(2)}, u32[]{:S(2)}) collective-permute-start(bf16[6,1,512]{2,1,0:T(2,128)(2,1)S(1)} %get-tuple-element.29), channel_id=1, source_target_pairs={{0,1},{1,2},{2,3},{3,4},{4,5},{5,6},{6,7},{8,9},{9,10},{10,11},{11... | collective-permute-start | bytes 18440 | tf_op jit(solution)/shard_map/ppermute | solution.py:26
  81.8 5.0 %collective-permute-start.14 = (bf16[6,1,512]{2,1,0:T(2,128)(2,1)S(1)}, bf16[6,1,512]{2,1,0:T(2,128)(2,1)S(1)}, u32[]{:S(2)}, u32[]{:S(2)}) collective-permute-start(bf16[6,1,512]{2,1,0:T(2,128)(2,1)S(1)} %get-tuple-element.30), channel_id=1, source_target_pairs={{1,0},{2,1},{3,2},{4,3},{5,4},{6,5},{7,6},{9,8},{10,9},{11,10},{12... | collective-permute-start | bytes 18440 | tf_op jit(solution)/shard_map/ppermute | solution.py:28
  89.0 7.3 %collective-permute-start.17 = (f32[128,512]{1,0:T(8,128)S(1)}, f32[128,512]{1,0:T(8,128)S(1)}, u32[]{:S(2)}, u32[]{:S(2)}) collective-permute-start(f32[128,512]{1,0:T(8,128)S(1)} %constant_dynamic-slice_fusion.11), channel_id=1, source_target_pairs={{0,2},{1,3},{2,0},{3,1},{4,6},{5,7},{6,4},{7,5},{8,10},{9,11},{10,... | collective-permute-start | bytes 786440 | tf_op jit(solution)/shard_map/ppermute | solution.py:62
  90.5 8.0 %collective-permute-start.25 = (f32[128,512]{1,0:T(8,128)S(1)}, f32[128,512]{1,0:T(8,128)S(1)}, u32[]{:S(2)}, u32[]{:S(2)}) collective-permute-start(f32[128,512]{1,0:T(8,128)S(1)} %constant_dynamic-slice_fusion.7), channel_id=1, source_target_pairs={{0,8},{8,0},{16,24},{24,16},{1,9},{9,1},{17,25},{25,17},{2,10},{10... | collective-permute-start | bytes 786440 | tf_op jit(solution)/shard_map/ppermute | solution.py:62
  91.2 8.3 %collective-permute-start.33 = (f32[128,512]{1,0:T(8,128)S(1)}, f32[128,512]{1,0:T(8,128)S(1)}, u32[]{:S(2)}, u32[]{:S(2)}) collective-permute-start(f32[128,512]{1,0:T(8,128)S(1)} %constant_dynamic-slice_fusion.3), channel_id=1, source_target_pairs={{0,16},{8,24},{16,0},{24,8},{1,17},{9,25},{17,1},{25,9},{2,18},{10... | collective-permute-start | bytes 786440 | tf_op jit(solution)/shard_map/ppermute | solution.py:62
  96.4 5.1 %collective-permute-start.18 = (f32[64,512]{1,0:T(8,128)S(1)}, f32[64,512]{1,0:T(8,128)S(1)}, u32[]{:S(2)}, u32[]{:S(2)}) collective-permute-start(f32[64,512]{1,0:T(8,128)S(1)} %constant_dynamic-slice_fusion.10), channel_id=1, source_target_pairs={{0,8},{8,0},{16,24},{24,16},{1,9},{9,1},{17,25},{25,17},{2,10},{10... | collective-permute-start | bytes 393224 | tf_op jit(solution)/shard_map/ppermute | solution.py:62
  98.5 5.1 %collective-permute-start.26 = (f32[64,512]{1,0:T(8,128)S(1)}, f32[64,512]{1,0:T(8,128)S(1)}, u32[]{:S(2)}, u32[]{:S(2)}) collective-permute-start(f32[64,512]{1,0:T(8,128)S(1)} %constant_dynamic-slice_fusion.6), channel_id=1, source_target_pairs={{0,16},{8,24},{16,0},{24,8},{1,17},{9,25},{17,1},{25,9},{2,18},{10... | collective-permute-start | bytes 393224 | tf_op jit(solution)/shard_map/ppermute | solution.py:62
  99.5 10.3 %collective-permute-start.34 = (f32[64,512]{1,0:T(8,128)S(1)}, f32[64,512]{1,0:T(8,128)S(1)}, u32[]{:S(2)}, u32[]{:S(2)}) collective-permute-start(f32[64,512]{1,0:T(8,128)S(1)} %constant_dynamic-slice_fusion.2), channel_id=1, source_target_pairs={{0,4},{1,5},{2,6},{3,7},{4,0},{5,1},{6,2},{7,3},{8,12},{9,13},{10,... | collective-permute-start | bytes 393224 | tf_op jit(solution)/shard_map/ppermute | solution.py:62
  101.5 8.5 %collective-permute-start.19 = (f32[32,512]{1,0:T(8,128)S(1)}, f32[32,512]{1,0:T(8,128)S(1)}, u32[]{:S(2)}, u32[]{:S(2)}) collective-permute-start(f32[32,512]{1,0:T(8,128)S(1)} %constant_dynamic-slice_fusion.9), channel_id=1, source_target_pairs={{0,16},{8,24},{16,0},{24,8},{1,17},{9,25},{17,1},{25,9},{2,18},{10... | collective-permute-start | bytes 196616 | tf_op jit(solution)/shard_map/ppermute | solution.py:62
  103.7 7.7 %collective-permute-start.27 = (f32[32,512]{1,0:T(8,128)S(1)}, f32[32,512]{1,0:T(8,128)S(1)}, u32[]{:S(2)}, u32[]{:S(2)}) collective-permute-start(f32[32,512]{1,0:T(8,128)S(1)} %constant_dynamic-slice_fusion.5), channel_id=1, source_target_pairs={{0,4},{1,5},{2,6},{3,7},{4,0},{5,1},{6,2},{7,3},{8,12},{9,13},{10,... | collective-permute-start | bytes 196616 | tf_op jit(solution)/shard_map/ppermute | solution.py:62
  123.2 5.0 %collective-permute-start.39 = (bf16[64,512]{1,0:T(8,128)(2,1)S(1)}, bf16[64,512]{1,0:T(8,128)(2,1)S(1)}, u32[]{:S(2)}, u32[]{:S(2)}) collective-permute-start(bf16[64,512]{1,0:T(8,128)(2,1)S(1)} %pad_maximum_fusion.33), channel_id=1, source_target_pairs={{0,4},{1,5},{2,6},{3,7},{4,0},{5,1},{6,2},{7,3},{8,12},{9,13},{10,... | collective-permute-start | bytes 196616 | tf_op jit(solution)/shard_map/ppermute | solution.py:72
  124.5 5.1 %collective-permute-start.24 = (bf16[128,512]{1,0:T(8,128)(2,1)S(1)}, bf16[128,512]{1,0:T(8,128)(2,1)S(1)}, u32[]{:S(2)}, u32[]{:S(2)}) collective-permute-start(bf16[128,512]{1,0:T(8,128)(2,1)S(1)} %pad_maximum_fusion.18), channel_id=1, source_target_pairs={{0,2},{1,3},{2,0},{3,1},{4,6},{5,7},{6,4},{7,5},{8,10},{9,11},{10,... | collective-permute-start | bytes 393224 | tf_op jit(solution)/shard_map/ppermute | solution.py:72
  132.9 9.9 %collective-permute-start.41 = (bf16[768,512]{1,0:T(8,128)(2,1)S(1)}, bf16[768,512]{1,0:T(8,128)(2,1)S(1)}, u32[]{:S(2)}, u32[]{:S(2)}) collective-permute-start(bf16[768,512]{1,0:T(8,128)(2,1)S(1)} %select_dynamic-update-slice_fusion), channel_id=1, source_target_pairs={{0,1},{1,0},{2,3},{3,2},{4,5},{5,4},{6,7},{7,6},{8,9},{9,8},{10,11... | collective-permute-start | bytes 2359304 | tf_op jit(solution)/shard_map/ppermute | solution.py:72
  (41 other events, 187.2 us)

commit v2 on v1

v2 whole, which is shorter than its diff:
```python
import math

import jax
import jax.numpy as jnp
from jax import lax
from jax.sharding import PartitionSpec as P

HC = 128
CI = 32
KS = 3
STEPS = 2
GATES = 512
KIN = 1440
SUM_ROWS = 1536
SUM_WAYS = 3


def flip_pairs(axis, bit):
    count = lax.axis_size(axis)
    return [(i, i ^ (1 << bit)) for i in range(count)]


def summing_levels():
    levels = []
    for axis in ("cols", "rows"):
        count = lax.axis_size(axis)
        depth = count.bit_length() - 1
        assert (1 << depth) == count
        levels.extend((axis, bit) for bit in range(depth))
    cols_levels = [lv for lv in levels if lv[0] == "cols"]
    rows_levels = [lv for lv in levels if lv[0] == "rows"]
    return cols_levels[:1], cols_levels[1:2] + rows_levels + cols_levels[2:]


def halve(part, levels):
    halved = []
    for axis, bit in levels:
        rows = part.shape[0]
        if rows % 16 != 0:
            break
        half = rows // 2
        upper = (lax.axis_index(axis) >> bit) & 1
        keep = lax.dynamic_slice_in_dim(part, upper * half, half, 0)
        send = lax.dynamic_slice_in_dim(part, (1 - upper) * half, half, 0)
        part = keep + lax.ppermute(send, axis, flip_pairs(axis, bit))
        halved.append((axis, bit))
    for axis, bit in levels[len(halved):]:
        part = part + lax.ppermute(part, axis, flip_pairs(axis, bit))
    return part, halved


def double(piece, halved):
    for axis, bit in reversed(halved):
        upper = (lax.axis_index(axis) >> bit) & 1
        got = lax.ppermute(piece, axis, flip_pairs(axis, bit))
        low = jnp.where(upper == 0, piece, got)
        high = jnp.where(upper == 0, got, piece)
        piece = jnp.concatenate([low, high], axis=0)
    return piece


def sum_everywhere(total):
    first, rest = summing_levels()
    part, first_halved = halve(total, first)
    ways = min(SUM_WAYS, max(len(rest), 1))
    width = part.shape[0] // ways
    pieces = []
    for way in range(ways):
        order = rest[way:] + rest[:way]
        chunk, halved = halve(part[way * width : (way + 1) * width], order)
        pieces.append(double(chunk.astype(jnp.bfloat16), halved))
    return double(jnp.concatenate(pieces, axis=0), first_halved).astype(jnp.float32)

def tap_columns(padded, rows_dev, cols_dev, reverse):
    pieces = []
    for tap_row in range(KS):
        for tap_col in range(KS):
            if reverse:
                first_row = KS - 1 - tap_row
                first_col = KS - 1 - tap_col
            else:
                first_row = tap_row
                first_col = tap_col
            pieces.append(
                padded[first_row : first_row + rows_dev, first_col : first_col + cols_dev]
            )
    joined = jnp.concatenate(pieces, axis=-1)
    return joined.reshape(rows_dev * cols_dev, joined.shape[-1])


def widen(cells, axis, dim, width):
    count = lax.axis_size(axis)
    size = cells.shape[dim]
    before, after = [], []
    need, dist = width, 1
    while need > 0:
        take = min(need, size)
        if dist < count:
            tail = lax.slice_in_dim(cells, size - take, size, axis=dim)
            head = lax.slice_in_dim(cells, 0, take, axis=dim)
            before.insert(0, lax.ppermute(tail, axis, [(i, i + dist) for i in range(count - dist)]))
            after.append(lax.ppermute(head, axis, [(i + dist, i) for i in range(count - dist)]))
        else:
            blank = list(cells.shape)
            blank[dim] = take
            before.insert(0, jnp.zeros(blank, cells.dtype))
            after.append(jnp.zeros(blank, cells.dtype))
        need -= take
        dist += 1
    return jnp.concatenate(before + [cells] + after, axis=dim)


def surround(cells, width):
    return widen(widen(cells, "rows", 0, width), "cols", 1, width)


def inner(cells, outer, inner_width):
    cut = outer - inner_width
    return cells[cut : cells.shape[0] - cut, cut : cells.shape[1] - cut]


def inside(rows_dev, cols_dev, width):
    rows_all = rows_dev * lax.axis_size("rows")
    cols_all = cols_dev * lax.axis_size("cols")
    row_at = lax.axis_index("rows") * rows_dev - width + jnp.arange(rows_dev + 2 * width)
    col_at = lax.axis_index("cols") * cols_dev - width + jnp.arange(cols_dev + 2 * width)
    row_ok = (row_at >= 0) & (row_at < rows_all)
    col_ok = (col_at >= 0) & (col_at < cols_all)
    return (row_ok[:, None] & col_ok[None, :])[..., None]


def cell_step(patches, kernel, gate_bias, cell_prev, shape):
    gates = jnp.dot(patches, kernel, preferred_element_type=jnp.float32) + gate_bias
    gates = gates.reshape(shape + (GATES,))
    gate_in = jax.nn.sigmoid(gates[..., :HC])
    gate_forget = jax.nn.sigmoid(gates[..., HC : 2 * HC])
    gate_cand = jnp.tanh(gates[..., 2 * HC : 3 * HC])
    gate_out = jax.nn.sigmoid(gates[..., 3 * HC :])
    cell = gate_forget * cell_prev + gate_in * gate_cand
    hidden = (gate_out * jnp.tanh(cell)).astype(jnp.bfloat16)
    return (gate_in, gate_forget, gate_cand, gate_out), cell, hidden


def cell_grads(grad_cell, grad_hidden, gates, cell_prev, cell_now):
    gate_in, gate_forget, gate_cand, gate_out = gates
    tanh_cell = jnp.tanh(cell_now)
    summed = grad_hidden * gate_out * (1.0 - tanh_cell * tanh_cell)
    if grad_cell is not None:
        summed = grad_cell + summed
    pre_in = summed * gate_cand * gate_in * (1.0 - gate_in)
    pre_forget = summed * cell_prev * gate_forget * (1.0 - gate_forget)
    pre_cand = summed * gate_in * (1.0 - gate_cand * gate_cand)
    pre_out = grad_hidden * tanh_cell * gate_out * (1.0 - gate_out)
    grad_gates = jnp.concatenate([pre_in, pre_forget, pre_cand, pre_out], axis=-1).astype(
        jnp.bfloat16
    )
    return grad_gates, summed * gate_forget


def shards(frames, hidden_start, cell_start, kernel, gate_bias, cotangent):
    rows_dev = hidden_start.shape[0]
    cols_dev = hidden_start.shape[1]
    chans = CI + HC
    taps = KS * KS
    cells = rows_dev * cols_dev
    reach = 2 * STEPS
    pack = jnp.concatenate(
        [
            frames[0].reshape(rows_dev, cols_dev, CI),
            frames[1].reshape(rows_dev, cols_dev, CI),
            hidden_start,
            cotangent[0],
            cotangent[1],
        ],
        axis=-1,
    )
    pack = surround(pack, reach)
    cell_zero = surround(cell_start, reach - 1)
    inputs_one = pack[..., :CI]
    inputs_two = pack[..., CI : 2 * CI]
    hidden_zero = pack[..., 2 * CI : 2 * CI + HC]
    cot_zero = pack[..., 2 * CI + HC : 2 * CI + 2 * HC]
    cot_one = pack[..., 2 * CI + 2 * HC :]

    def dims(width):
        return (rows_dev + 2 * width, cols_dev + 2 * width)

    stacked_one = jnp.concatenate([inputs_one, hidden_zero], axis=-1)
    patches_one = tap_columns(stacked_one, *dims(reach - 1), False)
    gates_one, cell_one, hidden_one = cell_step(
        patches_one, kernel, gate_bias, cell_zero, dims(reach - 1)
    )
    hidden_one = jnp.where(inside(rows_dev, cols_dev, reach - 1), hidden_one, 0)

    stacked_two = jnp.concatenate([inner(inputs_two, reach, reach - 1), hidden_one], axis=-1)
    patches_two = tap_columns(stacked_two, *dims(reach - 2), False)
    cell_one_two = inner(cell_one, reach - 1, reach - 2)
    gates_two, cell_two, hidden_two = cell_step(
        patches_two, kernel, gate_bias, cell_one_two, dims(reach - 2)
    )
    hidden_final = inner(hidden_two, reach - 2, 0)

    blocks = kernel.reshape(taps, chans, GATES)
    adjoint_matrix = jnp.transpose(blocks[:, CI:, :], (0, 2, 1)).reshape(taps * GATES, HC)

    grad_gates_two, grad_cell = cell_grads(
        None, inner(cot_one, reach, reach - 2).astype(jnp.float32), gates_two, cell_one_two, cell_two
    )
    masked_two = jnp.where(inside(rows_dev, cols_dev, reach - 2), grad_gates_two, 0)
    reversed_two = tap_columns(masked_two, *dims(reach - 3), True)
    grad_hidden = jnp.dot(reversed_two, adjoint_matrix, preferred_element_type=jnp.float32)
    grad_hidden = grad_hidden.reshape(dims(reach - 3) + (HC,))
    grad_hidden = grad_hidden + inner(cot_zero, reach, reach - 3).astype(jnp.float32)

    def near(values, width):
        return inner(values, width, reach - 3)

    gates_near = tuple(near(g, reach - 1) for g in gates_one)
    grad_gates_one, grad_cell = cell_grads(
        near(grad_cell, reach - 2),
        grad_hidden,
        gates_near,
        near(cell_zero, reach - 1),
        near(cell_one, reach - 1),
    )
    grad_cell_start = inner(grad_cell, reach - 3, 0)
    masked_one = jnp.where(inside(rows_dev, cols_dev, reach - 3), grad_gates_one, 0)
    reversed_one = tap_columns(masked_one, rows_dev, cols_dev, True)
    grad_hidden_start = jnp.dot(reversed_one, adjoint_matrix, preferred_element_type=jnp.float32)
    grad_hidden_start = grad_hidden_start.reshape(rows_dev, cols_dev, HC)

    spare = SUM_ROWS - KIN - 1
    lifted = []
    for stacked, width in ((stacked_two, reach - 1), (stacked_one, reach)):
        patches = tap_columns(inner(stacked, width, 1), rows_dev, cols_dev, False)
        lifted.append(
            jnp.concatenate(
                [
                    patches,
                    jnp.ones((cells, 1), patches.dtype),
                    jnp.zeros((cells, spare), patches.dtype),
                ],
                axis=1,
            )
        )
    grads_seen = [
        inner(grad_gates_two, reach - 2, 0).reshape(cells, GATES),
        inner(grad_gates_one, reach - 3, 0).reshape(cells, GATES),
    ]
    total_cells = STEPS * rows_dev * lax.axis_size("rows") * cols_dev * lax.axis_size("cols")
    norm_scale = 1.0 / math.sqrt(total_cells)
    joined = jnp.dot(
        jnp.concatenate(lifted, axis=0).T,
        jnp.concatenate(grads_seen, axis=0),
        preferred_element_type=jnp.float32,
    )
    summed_all = sum_everywhere(joined * norm_scale)
    return (
        hidden_final,
        grad_hidden_start,
        grad_cell_start,
        summed_all[:KIN],
        summed_all[KIN],
    )


def solution(mesh):
    placed = (
        P(None, "rows", "cols"),
        P("rows", "cols", None),
        P("rows", "cols", None),
        P(),
        P(),
        P(None, "rows", "cols", None),
    )
    return jax.shard_map(
        shards,
        mesh=mesh,
        in_specs=placed,
        out_specs=(
            P("rows", "cols", None),
            P("rows", "cols", None),
            P("rows", "cols", None),
            P(),
            P(),
        ),
        check_vma=False,
    )
```

time: 147 us -> 134 us (0.912)
  waiting for transfers between devices: 41.4 us -> 20.5 us
  starting transfers between devices: 74.5 us -> 58.9 us
  local copies, waits for them, and re-layouts: 15.4 us -> 25.3 us
  matrix products: 3.57 us -> 10.8 us
  other arithmetic: 9.33 us -> 15.6 us
    ppermute x16 -> x8, starting transfers between devices: 47.5 us -> 24.5 us  [the longest x4 15.6 us: widen(): lax.ppermute(tail, axis, [(i, i + dist) for i in range(count - dist)])]
    ppermute x16 -> x8, waiting for transfers between devices: 16.9 us -> 0.43 us  [the longest x4 0.42 us: widen(): lax.ppermute(tail, axis, [(i, i + dist) for i in range(count - dist)])]
    dot_general x4, matrix products: 2.97 us -> 10.2 us  [the longest x2 6.53 us: cell_step(): jnp.dot(patches, kernel, preferred_element_type=jnp.float32) + gate_bias]
    concatenate x6, local copies, waits for them, and re-layouts: 0.72 us -> 7.23 us  [tap_columns(): joined = jnp.concatenate(pieces, axis=-1)]
    ppermute x13, starting transfers between devices: 7.37 us -> 12.3 us  [halve(): part = keep + lax.ppermute(send, axis, flip_pairs(axis, bit))]
    slice x5 -> x10, local copies, waits for them, and re-layouts: 2.69 us -> 6.1 us  [the longest x1 1.88 us: shards(): summed_all[:KIN]]
    concatenate x10 -> x8, other arithmetic: 3.9 us -> 7.26 us  [the longest x2 2.81 us: shards(): stacked_one = jnp.concatenate([inputs_one, hidden_zero], axis=-1)]
    ppermute x13, waiting for transfers between devices: 17.7 us -> 14.6 us  [halve(): part = keep + lax.ppermute(send, axis, flip_pairs(axis, bit))]
  transfers between devices with their start and end apart: 42 -> 34, of which waited for: 23 -> 11; matrix products, arithmetic and copies ran while one was open for 8% -> 7% of each run, Pallas kernels for 0% -> 0%
where the time goes in v2:
time: 134 us; the launch traced here: 133 us
  starting transfers between devices  58.9 us (44%)
  local copies, waits for them, and re-layouts  25.3 us (19%)
  waiting for transfers between devices  20.5 us (15%)
  other arithmetic  15.6 us (12%)
  matrix products  10.8 us (8%)
  between operations  1.73 us (1%)
    ppermute x13, starting transfers between devices, double(): got = lax.ppermute(piece, axis, flip_pairs(axis, bit))  22.1 us
    ppermute x4, starting transfers between devices, widen(): lax.ppermute(tail, axis, [(i, i + dist) for i in range(count - dist)])  15.6 us
    ppermute x13, waiting for transfers between devices, halve(): part = keep + lax.ppermute(send, axis, flip_pairs(axis, bit))  14.6 us
    ppermute x13, starting transfers between devices, halve(): part = keep + lax.ppermute(send, axis, flip_pairs(axis, bit))  12.3 us
    ppermute x4, starting transfers between devices, widen(): lax.ppermute(head, axis, [(i + dist, i) for i in range(count - dist)])  8.89 us
    concatenate x6, local copies, waits for them, and re-layouts, tap_columns(): joined = jnp.concatenate(pieces, axis=-1)  7.23 us
    dot_general x2, matrix products, cell_step(): jnp.dot(patches, kernel, preferred_element_type=jnp.float32) + gate_bias  6.53 us
    ppermute x13, waiting for transfers between devices, double(): got = lax.ppermute(piece, axis, flip_pairs(axis, bit))  5.47 us
  transfers between devices with their start and end apart: 34, of which 11 were waited for; matrix products, arithmetic and copies ran while one was open for 7% of the time, Pallas kernels for 0%

profile of v2, /device:TPU:1, one launch (start us, length us, event | category | flops | bytes accessed | tf_op | source)
XLA Modules:
  0.0 132.8 jit_solution(12424175162997292671)
XLA Ops:
  4.5 4.6 %collective-permute-start = (bf16[4,32,448]{2,1,0:T(8,128)(2,1)S(1)}, bf16[4,32,448]{2,1,0:T(8,128)(2,1)S(1)}, u32[]{:S(2)}, u32[]{:S(2)}) collective-permute-start(bf16[4,32,448]{2,1,0:T(8,128)(2,1)S(1)} %concatenate.92), channel_id=1, source_target_pairs={{0,8},{8,16},{16,24},{1,9},{9,17},{17,25},{2,10},{10,18},{18,26},{... | collective-permute-start | bytes 344072 | tf_op jit(solution)/shard_map/ppermute | solution.py:101
  10.0 4.2 %collective-permute-start.4 = (f32[3,32,128]{2,1,0:T(8,128)S(1)}, f32[3,32,128]{2,1,0:T(8,128)S(1)}, u32[]{:S(2)}, u32[]{:S(2)}) collective-permute-start(f32[3,32,128]{2,1,0:T(8,128)S(1)} %get-tuple-element.90), channel_id=1, source_target_pairs={{0,8},{8,16},{16,24},{1,9},{9,17},{17,25},{2,10},{10,18},{18,26},{... | collective-permute-start | bytes 147464 | tf_op jit(solution)/shard_map/ppermute | solution.py:101
  19.3 4.4 %collective-permute-start.7 = (f32[10,3,128]{2,1,0:T(4,128)S(1)}, f32[10,3,128]{2,1,0:T(4,128)S(1)}, u32[]{:S(2)}, u32[]{:S(2)}) collective-permute-start(f32[10,3,128]{2,1,0:T(4,128)S(1)} %get-tuple-element.75), channel_id=1, source_target_pairs={{1,0},{2,1},{3,2},{4,3},{5,4},{6,5},{7,6},{9,8},{10,9},{11,10},{12... | collective-permute-start | bytes 46088 | tf_op jit(solution)/shard_map/ppermute | solution.py:102
  23.7 3.1 %collective-permute-start.6 = (f32[10,3,128]{2,1,0:T(4,128)S(1)}, f32[10,3,128]{2,1,0:T(4,128)S(1)}, u32[]{:S(2)}, u32[]{:S(2)}) collective-permute-start(f32[10,3,128]{2,1,0:T(4,128)S(1)} %get-tuple-element.74), channel_id=1, source_target_pairs={{0,1},{1,2},{2,3},{3,4},{4,5},{5,6},{6,7},{8,9},{9,10},{10,11},{11... | collective-permute-start | bytes 46088 | tf_op jit(solution)/shard_map/ppermute | solution.py:101
  26.9 1.9 %collective-permute-start.3 = (bf16[12,4,448]{2,1,0:T(4,128)(2,1)S(1)}, bf16[12,4,448]{2,1,0:T(4,128)(2,1)S(1)}, u32[]{:S(2)}, u32[]{:S(2)}) collective-permute-start(bf16[12,4,448]{2,1,0:T(4,128)(2,1)S(1)} %get-tuple-element.31), channel_id=1, source_target_pairs={{1,0},{2,1},{3,2},{4,3},{5,4},{6,5},{7,6},{9,8},{10,9},{11,10},{12... | collective-permute-start | bytes 129032 | tf_op jit(solution)/shard_map/ppermute | solution.py:102
  28.8 3.6 %collective-permute-start.2 = (bf16[12,4,448]{2,1,0:T(4,128)(2,1)S(1)}, bf16[12,4,448]{2,1,0:T(4,128)(2,1)S(1)}, u32[]{:S(2)}, u32[]{:S(2)}) collective-permute-start(bf16[12,4,448]{2,1,0:T(4,128)(2,1)S(1)} %get-tuple-element.30), channel_id=1, source_target_pairs={{0,1},{1,2},{2,3},{3,4},{4,5},{5,6},{6,7},{8,9},{9,10},{10,11},{11... | collective-permute-start | bytes 129032 | tf_op jit(solution)/shard_map/ppermute | solution.py:101
  34.0 1.8 %fusion.14 = (bf16[10,38,160]{2,1,0:T(8,128)(2,1)S(1)}, bf16[10,38,160]{2,1,0:T(8,128)(2,1)S(1)}, bf16[10,38,160]{2,1,0:T(8,128)(2,1)}, bf16[10,38,160]{2,1,0:T(...) fusion(bf16[12,40,32]{2,1,0:T(8,128)(2,1)S(1)} %slice.407, ...), kind=kLoop, calls=%fused_computation.106 | loop fusion | flops 2188800 | bytes 1248000 | tf_op jit(solution)/shard_map/concatenate | solution.py:188
  36.8 2.9 %concatenate.96 = bf16[10,38,1440]{2,1,0:T(8,128)(2,1)S(1)} concatenate(bf16[10,38,160]{2,1,0:T(8,128)(2,1)S(1)} %get-tuple-element.46, bf16[10,38,160]{2,1,0:T(8,128)(2,1)} %get-tuple-element.47, bf16[10,38,160]{2,1,0:T(8,128)(2,1)} %get-tuple-element.48, bf16[10,38,160]{2,1,0:T(8,128)(2,1)} %get-tuple-element.49, bf16[10,38,160]{2,1,0:T(8,128)(2,1)} %get-tuple-element.50, ...), dimensions={2} | concatenate | bytes 2188800 | tf_op jit(solution)/shard_map/concatenate | solution.py:87
  41.3 3.4 %convolution_add_fusion = f32[380,512]{1,0:T(8,128)} fusion(bf16[380,1440]{1,0:T(8,128)(2,1)} %reshape.172, bf16[1440,512]{1,0:T(8,128)(2,1)} %param.9, f32[512]{0:T(512)S(1)} %copy-done.25), kind=kOutput, calls=%fused_computation.3 | convolution fusion | flops 560527360 | bytes 3349248 | tf_op jit(solution)/shard_map/dot_general | solution.py:133
  49.8 2.7 %concatenate.100 = bf16[8,36,1440]{2,1,0:T(8,128)(2,1)S(1)} concatenate(bf16[8,36,160]{2,1,0:T(8,128)(2,1)} %get-tuple-element.66, bf16[8,36,160]{2,1,0:T(8,128)(2,1)} %get-tuple-element.67, bf16[8,36,160]{2,1,0:T(8,128)(2,1)} %get-tuple-element.68, bf16[8,36,160]{2,1,0:T(8,128)(2,1)} %get-tuple-element.69, bf16[8,36,160]{2,1,0:T(8,128)(2,1)} %get-tuple-element.70, ...), dimensions={2} | concatenate | bytes 1658880 | tf_op jit(solution)/shard_map/concatenate | solution.py:87
  53.9 3.1 %convolution_add_fusion.1 = f32[288,512]{1,0:T(8,128)} fusion(bf16[288,1440]{1,0:T(8,128)(2,1)} %reshape.174, bf16[1440,512]{1,0:T(8,128)(2,1)} %param.9, f32[512]{0:T(512)S(1)} %copy-done.25), kind=kOutput, calls=%fused_computation.4 | convolution fusion | flops 424820736 | bytes 2895872 | tf_op jit(solution)/shard_map/dot_general | solution.py:133
  65.3 2.6 %multiply_convert_fusion.6 = (bf16[6,34,128]{2,1,0:T(8,128)(2,1)S(1)}, f32[6,34,128]{2,1,0:T(8,128)S(1)}, bf16[6,34,128]{2,1,0:T(8,128)(2,1)S(1)}, f32[6,34,128]{2,1,0:T(8,128)S(1)}) fusion(f32[10,38,128]{2,1,0:T(8,128)S(1)} %get-tuple-element.21, f32[10,38,128]{2,1,0:T(8,128)S(1)} %get-tuple-element.20, f32[10,38,128]{2,1,0:T(8,128)S(1)} %get-tuple-element.13, ...), kind=kOutput, calls=%fused_computation.185 | convolution fusion | flops 241248768 | bytes 4429824 | tf_op jit(solution)/shard_map/dot_general | solution.py:211
  70.3 3.1 %collective-permute-done.8 = f32[768,512]{1,0:T(8,128)S(1)} collective-permute-done((f32[768,512]{1,0:T(8,128)S(1)}, f32[768,512]{1,0:T(8,128)S(1)}, u32[]{:S(2)}, u32[]{:S(2)}) %collective-permute-start.8) | collective-permute-done | bytes 1572896 | tf_op jit(solution)/shard_map/ppermute | solution.py:45
  73.9 2.1 %collective-permute-start.9 = (f32[128,512]{1,0:T(8,128)S(1)}, f32[128,512]{1,0:T(8,128)S(1)}, u32[]{:S(2)}, u32[]{:S(2)}) collective-permute-start(f32[128,512]{1,0:T(8,128)S(1)} %constant_dynamic-slice_fusion.11), channel_id=1, source_target_pairs={{0,2},{1,3},{2,0},{3,1},{4,6},{5,7},{6,4},{7,5},{8,10},{9,11},{10,... | collective-permute-start | bytes 786440 | tf_op jit(solution)/shard_map/ppermute | solution.py:45
  78.3 4.1 %collective-permute-done.9 = f32[128,512]{1,0:T(8,128)S(1)} collective-permute-done((f32[128,512]{1,0:T(8,128)S(1)}, f32[128,512]{1,0:T(8,128)S(1)}, u32[]{:S(2)}, u32[]{:S(2)}) %collective-permute-start.9) | collective-permute-done | bytes 262176 | tf_op jit(solution)/shard_map/ppermute | solution.py:45
  85.6 2.4 %collective-permute-start.26 = (f32[64,512]{1,0:T(8,128)S(1)}, f32[64,512]{1,0:T(8,128)S(1)}, u32[]{:S(2)}, u32[]{:S(2)}) collective-permute-start(f32[64,512]{1,0:T(8,128)S(1)} %constant_dynamic-slice_fusion.2), channel_id=1, source_target_pairs={{0,4},{1,5},{2,6},{3,7},{4,0},{5,1},{6,2},{7,3},{8,12},{9,13},{10,... | collective-permute-start | bytes 393224 | tf_op jit(solution)/shard_map/ppermute | solution.py:45
  88.3 2.3 %collective-permute-start.19 = (f32[32,512]{1,0:T(8,128)S(1)}, f32[32,512]{1,0:T(8,128)S(1)}, u32[]{:S(2)}, u32[]{:S(2)}) collective-permute-start(f32[32,512]{1,0:T(8,128)S(1)} %constant_dynamic-slice_fusion.5), channel_id=1, source_target_pairs={{0,4},{1,5},{2,6},{3,7},{4,0},{5,1},{6,2},{7,3},{8,12},{9,13},{10,... | collective-permute-start | bytes 196616 | tf_op jit(solution)/shard_map/ppermute | solution.py:45
  90.6 4.4 %collective-permute-done.26 = f32[64,512]{1,0:T(8,128)S(1)} collective-permute-done((f32[64,512]{1,0:T(8,128)S(1)}, f32[64,512]{1,0:T(8,128)S(1)}, u32[]{:S(2)}, u32[]{:S(2)}) %collective-permute-start.26) | collective-permute-done | bytes 131104 | tf_op jit(solution)/shard_map/ppermute | solution.py:45
  95.2 1.8 %collective-permute-done.19 = f32[32,512]{1,0:T(8,128)S(1)} collective-permute-done((f32[32,512]{1,0:T(8,128)S(1)}, f32[32,512]{1,0:T(8,128)S(1)}, u32[]{:S(2)}, u32[]{:S(2)}) %collective-permute-start.19) | collective-permute-done | bytes 65568 | tf_op jit(solution)/shard_map/ppermute | solution.py:45
  103.6 2.3 %collective-permute-start.22 = (bf16[32,512]{1,0:T(8,128)(2,1)S(1)}, bf16[32,512]{1,0:T(8,128)(2,1)S(1)}, u32[]{:S(2)}, u32[]{:S(2)}) collective-permute-start(bf16[32,512]{1,0:T(8,128)(2,1)S(1)} %pad_maximum_fusion.18), channel_id=1, source_target_pairs={{0,4},{1,5},{2,6},{3,7},{4,0},{5,1},{6,2},{7,3},{8,12},{9,13},{10,... | collective-permute-start | bytes 98312 | tf_op jit(solution)/shard_map/ppermute | solution.py:55
  112.6 1.7 %collective-permute-done.31 = bf16[64,512]{1,0:T(8,128)(2,1)S(1)} collective-permute-done((bf16[64,512]{1,0:T(8,128)(2,1)S(1)}, bf16[64,512]{1,0:T(8,128)(2,1)S(1)}, u32[]{:S(2)}, u32[]{:S(2)}) %collective-permute-start.31) | collective-permute-done | bytes 65568 | tf_op jit(solution)/shard_map/ppermute | solution.py:55
  116.4 2.3 %collective-permute-done.32 = bf16[128,512]{1,0:T(8,128)(2,1)S(1)} collective-permute-done((bf16[128,512]{1,0:T(8,128)(2,1)S(1)}, bf16[128,512]{1,0:T(8,128)(2,1)S(1)}, u32[]{:S(2)}, u32[]{:S(2)}) %collective-permute-start.32) | collective-permute-done | bytes 131104 | tf_op jit(solution)/shard_map/ppermute | solution.py:55
  118.7 8.3 %collective-permute-start.33 = (bf16[768,512]{1,0:T(8,128)(2,1)S(1)}, bf16[768,512]{1,0:T(8,128)(2,1)S(1)}, u32[]{:S(2)}, u32[]{:S(2)}) collective-permute-start(bf16[768,512]{1,0:T(8,128)(2,1)S(1)} %select_dynamic-update-slice_fusion), channel_id=1, source_target_pairs={{0,1},{1,0},{2,3},{3,2},{4,5},{5,4},{6,7},{7,6},{8,9},{9,8},{10,11... | collective-permute-start | bytes 2359304 | tf_op jit(solution)/shard_map/ppermute | solution.py:55
  130.9 1.9 %slice.524 = f32[1440,512]{1,0:T(8,128)} slice(f32[1536,512]{1,0:T(8,128)S(1)} %maximum_convert_fusion), slice={[0:1440], [0:512]} | slice | bytes 5898240 | tf_op jit(solution)/shard_map/slice | solution.py:262
  (228 shorter events, 56.0 us)
Async XLA Ops:
  3.2 23.6 %collective-permute-start.1 = (bf16[4,32,448]{2,1,0:T(8,128)(2,1)S(1)}, bf16[4,32,448]{2,1,0:T(8,128)(2,1)S(1)}, u32[]{:S(2)}, u32[]{:S(2)}) collective-permute-start(bf16[4,32,448]{2,1,0:T(8,128)(2,1)S(1)} %concatenate.92), channel_id=1, source_target_pairs={{8,0},{16,8},{24,16},{9,1},{17,9},{25,17},{10,2},{18,10},{26,18},{... | collective-permute-start | bytes 344072 | tf_op jit(solution)/shard_map/ppermute | solution.py:102
  4.5 22.3 %collective-permute-start = (bf16[4,32,448]{2,1,0:T(8,128)(2,1)S(1)}, bf16[4,32,448]{2,1,0:T(8,128)(2,1)S(1)}, u32[]{:S(2)}, u32[]{:S(2)}) collective-permute-start(bf16[4,32,448]{2,1,0:T(8,128)(2,1)S(1)} %concatenate.92), channel_id=1, source_target_pairs={{0,8},{8,16},{16,24},{1,9},{9,17},{17,25},{2,10},{10,18},{18,26},{... | collective-permute-start | bytes 344072 | tf_op jit(solution)/shard_map/ppermute | solution.py:101
  10.0 9.2 %collective-permute-start.4 = (f32[3,32,128]{2,1,0:T(8,128)S(1)}, f32[3,32,128]{2,1,0:T(8,128)S(1)}, u32[]{:S(2)}, u32[]{:S(2)}) collective-permute-start(f32[3,32,128]{2,1,0:T(8,128)S(1)} %get-tuple-element.90), channel_id=1, source_target_pairs={{0,8},{8,16},{16,24},{1,9},{9,17},{17,25},{2,10},{10,18},{18,26},{... | collective-permute-start | bytes 147464 | tf_op jit(solution)/shard_map/ppermute | solution.py:101
  14.2 5.0 %collective-permute-start.5 = (f32[3,32,128]{2,1,0:T(8,128)S(1)}, f32[3,32,128]{2,1,0:T(8,128)S(1)}, u32[]{:S(2)}, u32[]{:S(2)}) collective-permute-start(f32[3,32,128]{2,1,0:T(8,128)S(1)} %get-tuple-element.89), channel_id=1, source_target_pairs={{8,0},{16,8},{24,16},{9,1},{17,9},{25,17},{10,2},{18,10},{26,18},{... | collective-permute-start | bytes 147464 | tf_op jit(solution)/shard_map/ppermute | solution.py:102
  19.3 13.2 %collective-permute-start.7 = (f32[10,3,128]{2,1,0:T(4,128)S(1)}, f32[10,3,128]{2,1,0:T(4,128)S(1)}, u32[]{:S(2)}, u32[]{:S(2)}) collective-permute-start(f32[10,3,128]{2,1,0:T(4,128)S(1)} %get-tuple-element.75), channel_id=1, source_target_pairs={{1,0},{2,1},{3,2},{4,3},{5,4},{6,5},{7,6},{9,8},{10,9},{11,10},{12... | collective-permute-start | bytes 46088 | tf_op jit(solution)/shard_map/ppermute | solution.py:102
  23.7 8.8 %collective-permute-start.6 = (f32[10,3,128]{2,1,0:T(4,128)S(1)}, f32[10,3,128]{2,1,0:T(4,128)S(1)}, u32[]{:S(2)}, u32[]{:S(2)}) collective-permute-start(f32[10,3,128]{2,1,0:T(4,128)S(1)} %get-tuple-element.74), channel_id=1, source_target_pairs={{0,1},{1,2},{2,3},{3,4},{4,5},{5,6},{6,7},{8,9},{9,10},{10,11},{11... | collective-permute-start | bytes 46088 | tf_op jit(solution)/shard_map/ppermute | solution.py:101
  26.9 6.3 %collective-permute-start.3 = (bf16[12,4,448]{2,1,0:T(4,128)(2,1)S(1)}, bf16[12,4,448]{2,1,0:T(4,128)(2,1)S(1)}, u32[]{:S(2)}, u32[]{:S(2)}) collective-permute-start(bf16[12,4,448]{2,1,0:T(4,128)(2,1)S(1)} %get-tuple-element.31), channel_id=1, source_target_pairs={{1,0},{2,1},{3,2},{4,3},{5,4},{6,5},{7,6},{9,8},{10,9},{11,10},{12... | collective-permute-start | bytes 129032 | tf_op jit(solution)/shard_map/ppermute | solution.py:102
  28.8 4.8 %collective-permute-start.2 = (bf16[12,4,448]{2,1,0:T(4,128)(2,1)S(1)}, bf16[12,4,448]{2,1,0:T(4,128)(2,1)S(1)}, u32[]{:S(2)}, u32[]{:S(2)}) collective-permute-start(bf16[12,4,448]{2,1,0:T(4,128)(2,1)S(1)} %get-tuple-element.30), channel_id=1, source_target_pairs={{0,1},{1,2},{2,3},{3,4},{4,5},{5,6},{6,7},{8,9},{9,10},{10,11},{11... | collective-permute-start | bytes 129032 | tf_op jit(solution)/shard_map/ppermute | solution.py:101
  73.9 8.5 %collective-permute-start.9 = (f32[128,512]{1,0:T(8,128)S(1)}, f32[128,512]{1,0:T(8,128)S(1)}, u32[]{:S(2)}, u32[]{:S(2)}) collective-permute-start(f32[128,512]{1,0:T(8,128)S(1)} %constant_dynamic-slice_fusion.11), channel_id=1, source_target_pairs={{0,2},{1,3},{2,0},{3,1},{4,6},{5,7},{6,4},{7,5},{8,10},{9,11},{10,... | collective-permute-start | bytes 786440 | tf_op jit(solution)/shard_map/ppermute | solution.py:45
  76.7 7.3 %collective-permute-start.17 = (f32[128,512]{1,0:T(8,128)S(1)}, f32[128,512]{1,0:T(8,128)S(1)}, u32[]{:S(2)}, u32[]{:S(2)}) collective-permute-start(f32[128,512]{1,0:T(8,128)S(1)} %constant_dynamic-slice_fusion.7), channel_id=1, source_target_pairs={{0,8},{8,0},{16,24},{24,16},{1,9},{9,1},{17,25},{25,17},{2,10},{10... | collective-permute-start | bytes 786440 | tf_op jit(solution)/shard_map/ppermute | solution.py:45
  78.2 7.3 %collective-permute-start.25 = (f32[128,512]{1,0:T(8,128)S(1)}, f32[128,512]{1,0:T(8,128)S(1)}, u32[]{:S(2)}, u32[]{:S(2)}) collective-permute-start(f32[128,512]{1,0:T(8,128)S(1)} %constant_dynamic-slice_fusion.3), channel_id=1, source_target_pairs={{0,16},{8,24},{16,0},{24,8},{1,17},{9,25},{17,1},{25,9},{2,18},{10... | collective-permute-start | bytes 786440 | tf_op jit(solution)/shard_map/ppermute | solution.py:45
  82.5 5.5 %collective-permute-start.10 = (f32[64,512]{1,0:T(8,128)S(1)}, f32[64,512]{1,0:T(8,128)S(1)}, u32[]{:S(2)}, u32[]{:S(2)}) collective-permute-start(f32[64,512]{1,0:T(8,128)S(1)} %constant_dynamic-slice_fusion.10), channel_id=1, source_target_pairs={{0,8},{8,0},{16,24},{24,16},{1,9},{9,1},{17,25},{25,17},{2,10},{10... | collective-permute-start | bytes 393224 | tf_op jit(solution)/shard_map/ppermute | solution.py:45
  84.0 4.2 %collective-permute-start.18 = (f32[64,512]{1,0:T(8,128)S(1)}, f32[64,512]{1,0:T(8,128)S(1)}, u32[]{:S(2)}, u32[]{:S(2)}) collective-permute-start(f32[64,512]{1,0:T(8,128)S(1)} %constant_dynamic-slice_fusion.6), channel_id=1, source_target_pairs={{0,16},{8,24},{16,0},{24,8},{1,17},{9,25},{17,1},{25,9},{2,18},{10... | collective-permute-start | bytes 393224 | tf_op jit(solution)/shard_map/ppermute | solution.py:45
  85.6 9.3 %collective-permute-start.26 = (f32[64,512]{1,0:T(8,128)S(1)}, f32[64,512]{1,0:T(8,128)S(1)}, u32[]{:S(2)}, u32[]{:S(2)}) collective-permute-start(f32[64,512]{1,0:T(8,128)S(1)} %constant_dynamic-slice_fusion.2), channel_id=1, source_target_pairs={{0,4},{1,5},{2,6},{3,7},{4,0},{5,1},{6,2},{7,3},{8,12},{9,13},{10,... | collective-permute-start | bytes 393224 | tf_op jit(solution)/shard_map/ppermute | solution.py:45
  88.0 7.0 %collective-permute-start.11 = (f32[32,512]{1,0:T(8,128)S(1)}, f32[32,512]{1,0:T(8,128)S(1)}, u32[]{:S(2)}, u32[]{:S(2)}) collective-permute-start(f32[32,512]{1,0:T(8,128)S(1)} %constant_dynamic-slice_fusion.9), channel_id=1, source_target_pairs={{0,16},{8,24},{16,0},{24,8},{1,17},{9,25},{17,1},{25,9},{2,18},{10... | collective-permute-start | bytes 196616 | tf_op jit(solution)/shard_map/ppermute | solution.py:45
  88.3 8.8 %collective-permute-start.19 = (f32[32,512]{1,0:T(8,128)S(1)}, f32[32,512]{1,0:T(8,128)S(1)}, u32[]{:S(2)}, u32[]{:S(2)}) collective-permute-start(f32[32,512]{1,0:T(8,128)S(1)} %constant_dynamic-slice_fusion.5), channel_id=1, source_target_pairs={{0,4},{1,5},{2,6},{3,7},{4,0},{5,1},{6,2},{7,3},{8,12},{9,13},{10,... | collective-permute-start | bytes 196616 | tf_op jit(solution)/shard_map/ppermute | solution.py:45
  101.7 4.1 %collective-permute-start.29 = (bf16[16,512]{1,0:T(8,128)(2,1)S(1)}, bf16[16,512]{1,0:T(8,128)(2,1)S(1)}, u32[]{:S(2)}, u32[]{:S(2)}) collective-permute-start(bf16[16,512]{1,0:T(8,128)(2,1)S(1)} %add_convert_fusion), channel_id=1, source_target_pairs={{0,8},{8,0},{16,24},{24,16},{1,9},{9,1},{17,25},{25,17},{2,10},{10... | collective-permute-start | bytes 49160 | tf_op jit(solution)/shard_map/ppermute | solution.py:55
  106.1 4.2 %collective-permute-start.15 = (bf16[64,512]{1,0:T(8,128)(2,1)S(1)}, bf16[64,512]{1,0:T(8,128)(2,1)S(1)}, u32[]{:S(2)}, u32[]{:S(2)}) collective-permute-start(bf16[64,512]{1,0:T(8,128)(2,1)S(1)} %pad_maximum_fusion.10), channel_id=1, source_target_pairs={{0,8},{8,0},{16,24},{24,16},{1,9},{9,1},{17,25},{25,17},{2,10},{10... | collective-permute-start | bytes 196616 | tf_op jit(solution)/shard_map/ppermute | solution.py:55
  107.4 4.3 %collective-permute-start.23 = (bf16[64,512]{1,0:T(8,128)(2,1)S(1)}, bf16[64,512]{1,0:T(8,128)(2,1)S(1)}, u32[]{:S(2)}, u32[]{:S(2)}) collective-permute-start(bf16[64,512]{1,0:T(8,128)(2,1)S(1)} %pad_maximum_fusion.11), channel_id=1, source_target_pairs={{0,16},{8,24},{16,0},{24,8},{1,17},{9,25},{17,1},{25,9},{2,18},{10... | collective-permute-start | bytes 196616 | tf_op jit(solution)/shard_map/ppermute | solution.py:55
  108.7 5.5 %collective-permute-start.31 = (bf16[64,512]{1,0:T(8,128)(2,1)S(1)}, bf16[64,512]{1,0:T(8,128)(2,1)S(1)}, u32[]{:S(2)}, u32[]{:S(2)}) collective-permute-start(bf16[64,512]{1,0:T(8,128)(2,1)S(1)} %pad_maximum_fusion.12), channel_id=1, source_target_pairs={{0,4},{1,5},{2,6},{3,7},{4,0},{5,1},{6,2},{7,3},{8,12},{9,13},{10,... | collective-permute-start | bytes 196616 | tf_op jit(solution)/shard_map/ppermute | solution.py:55
  110.3 4.8 %collective-permute-start.16 = (bf16[128,512]{1,0:T(8,128)(2,1)S(1)}, bf16[128,512]{1,0:T(8,128)(2,1)S(1)}, u32[]{:S(2)}, u32[]{:S(2)}) collective-permute-start(bf16[128,512]{1,0:T(8,128)(2,1)S(1)} %pad_maximum_fusion.4), channel_id=1, source_target_pairs={{0,2},{1,3},{2,0},{3,1},{4,6},{5,7},{6,4},{7,5},{8,10},{9,11},{10,... | collective-permute-start | bytes 393224 | tf_op jit(solution)/shard_map/ppermute | solution.py:55
  111.7 4.6 %collective-permute-start.24 = (bf16[128,512]{1,0:T(8,128)(2,1)S(1)}, bf16[128,512]{1,0:T(8,128)(2,1)S(1)}, u32[]{:S(2)}, u32[]{:S(2)}) collective-permute-start(bf16[128,512]{1,0:T(8,128)(2,1)S(1)} %pad_maximum_fusion.5), channel_id=1, source_target_pairs={{0,8},{8,0},{16,24},{24,16},{1,9},{9,1},{17,25},{25,17},{2,10},{10... | collective-permute-start | bytes 393224 | tf_op jit(solution)/shard_map/ppermute | solution.py:55
  114.3 4.4 %collective-permute-start.32 = (bf16[128,512]{1,0:T(8,128)(2,1)S(1)}, bf16[128,512]{1,0:T(8,128)(2,1)S(1)}, u32[]{:S(2)}, u32[]{:S(2)}) collective-permute-start(bf16[128,512]{1,0:T(8,128)(2,1)S(1)} %pad_maximum_fusion.6), channel_id=1, source_target_pairs={{0,16},{8,24},{16,0},{24,8},{1,17},{9,25},{17,1},{25,9},{2,18},{10... | collective-permute-start | bytes 393224 | tf_op jit(solution)/shard_map/ppermute | solution.py:55
  118.7 11.0 %collective-permute-start.33 = (bf16[768,512]{1,0:T(8,128)(2,1)S(1)}, bf16[768,512]{1,0:T(8,128)(2,1)S(1)}, u32[]{:S(2)}, u32[]{:S(2)}) collective-permute-start(bf16[768,512]{1,0:T(8,128)(2,1)S(1)} %select_dynamic-update-slice_fusion), channel_id=1, source_target_pairs={{0,1},{1,0},{2,3},{3,2},{4,5},{5,4},{6,7},{7,6},{8,9},{9,8},{10,11... | collective-permute-start | bytes 2359304 | tf_op jit(solution)/shard_map/ppermute | solution.py:55
  (36 other events, 85.1 us)

commit v3 on v2

--- a/solution.py
+++ b/solution.py
@@ -129,9 +129,17 @@
     return (row_ok[:, None] & col_ok[None, :])[..., None]
 
 
-def cell_step(patches, kernel, gate_bias, cell_prev, shape):
-    gates = jnp.dot(patches, kernel, preferred_element_type=jnp.float32) + gate_bias
-    gates = gates.reshape(shape + (GATES,))
+def convolve(field, weights):
+    numbers = ("NHWC", "HWIO", "NHWC")
+    result = lax.conv_general_dilated(
+        field[None], weights, (1, 1), "VALID", dimension_numbers=numbers,
+        preferred_element_type=jnp.float32,
+    )
+    return result[0]
+
+
+def cell_step(stacked, weights, gate_bias, cell_prev):
+    gates = convolve(stacked, weights) + gate_bias
     gate_in = jax.nn.sigmoid(gates[..., :HC])
     gate_forget = jax.nn.sigmoid(gates[..., HC : 2 * HC])
     gate_cand = jnp.tanh(gates[..., 2 * HC : 3 * HC])
@@ -161,7 +169,6 @@
     rows_dev = hidden_start.shape[0]
     cols_dev = hidden_start.shape[1]
     chans = CI + HC
-    taps = KS * KS
     cells = rows_dev * cols_dev
     reach = 2 * STEPS
     pack = jnp.concatenate(
@@ -182,35 +189,22 @@
     cot_zero = pack[..., 2 * CI + HC : 2 * CI + 2 * HC]
     cot_one = pack[..., 2 * CI + 2 * HC :]
 
-    def dims(width):
-        return (rows_dev + 2 * width, cols_dev + 2 * width)
-
+    weights = kernel.reshape(KS, KS, chans, GATES)
+    flipped = jnp.transpose(weights[::-1, ::-1, CI:, :], (0, 1, 3, 2))
     stacked_one = jnp.concatenate([inputs_one, hidden_zero], axis=-1)
-    patches_one = tap_columns(stacked_one, *dims(reach - 1), False)
-    gates_one, cell_one, hidden_one = cell_step(
-        patches_one, kernel, gate_bias, cell_zero, dims(reach - 1)
-    )
+    gates_one, cell_one, hidden_one = cell_step(stacked_one, weights, gate_bias, cell_zero)
     hidden_one = jnp.where(inside(rows_dev, cols_dev, reach - 1), hidden_one, 0)
 
     stacked_two = jnp.concatenate([inner(inputs_two, reach, reach - 1), hidden_one], axis=-1)
-    patches_two = tap_columns(stacked_two, *dims(reach - 2), False)
     cell_one_two = inner(cell_one, reach - 1, reach - 2)
-    gates_two, cell_two, hidden_two = cell_step(
-        patches_two, kernel, gate_bias, cell_one_two, dims(reach - 2)
-    )
+    gates_two, cell_two, hidden_two = cell_step(stacked_two, weights, gate_bias, cell_one_two)
     hidden_final = inner(hidden_two, reach - 2, 0)
-
-    blocks = kernel.reshape(taps, chans, GATES)
-    adjoint_matrix = jnp.transpose(blocks[:, CI:, :], (0, 2, 1)).reshape(taps * GATES, HC)
 
     grad_gates_two, grad_cell = cell_grads(
         None, inner(cot_one, reach, reach - 2).astype(jnp.float32), gates_two, cell_one_two, cell_two
     )
     masked_two = jnp.where(inside(rows_dev, cols_dev, reach - 2), grad_gates_two, 0)
-    reversed_two = tap_columns(masked_two, *dims(reach - 3), True)
-    grad_hidden = jnp.dot(reversed_two, adjoint_matrix, preferred_element_type=jnp.float32)
-    grad_hidden = grad_hidden.reshape(dims(reach - 3) + (HC,))
-    grad_hidden = grad_hidden + inner(cot_zero, reach, reach - 3).astype(jnp.float32)
+    grad_hidden = convolve(masked_two, flipped) + inner(cot_zero, reach, reach - 3).astype(jnp.float32)
 
     def near(values, width):
         return inner(values, width, reach - 3)
@@ -225,9 +219,7 @@
     )
     grad_cell_start = inner(grad_cell, reach - 3, 0)
     masked_one = jnp.where(inside(rows_dev, cols_dev, reach - 3), grad_gates_one, 0)
-    reversed_one = tap_columns(masked_one, rows_dev, cols_dev, True)
-    grad_hidden_start = jnp.dot(reversed_one, adjoint_matrix, preferred_element_type=jnp.float32)
-    grad_hidden_start = grad_hidden_start.reshape(rows_dev, cols_dev, HC)
+    grad_hidden_start = convolve(masked_one, flipped)
 
     spare = SUM_ROWS - KIN - 1
     lifted = []

time: 134 us -> 122 us (0.910)
  local copies, waits for them, and re-layouts: 25.3 us -> 16.6 us
  matrix products: 10.8 us -> 4.84 us
  waiting for transfers between devices: 20.5 us -> 24 us
  other arithmetic: 15.6 us -> 12.5 us
  starting transfers between devices: 58.9 us -> 61 us
    dot_general x4 -> x0, matrix products: 10.2 us -> none  [the longest x2 6.53 us: cell_step(): jnp.dot(patches, kernel, preferred_element_type=jnp.float32) + gate_bias]
    ppermute x13, starting transfers between devices: 12.3 us -> 19.5 us  [halve(): part = keep + lax.ppermute(send, axis, flip_pairs(axis, bit))]
    concatenate x6 -> x2, local copies, waits for them, and re-layouts: 7.23 us -> 1.39 us  [tap_columns(): joined = jnp.concatenate(pieces, axis=-1)]
    ppermute x13, starting transfers between devices: 22.1 us -> 16.8 us  [double(): got = lax.ppermute(piece, axis, flip_pairs(axis, bit))]
    reshape x4 -> x0, local copies, waits for them, and re-layouts: 5.19 us -> none  [the longest x2 2.84 us: tap_columns(): return joined.reshape(rows_dev * cols_dev, joined.shape[-1])]
    ppermute x13, waiting for transfers between devices: 5.47 us -> 10 us  [double(): got = lax.ppermute(piece, axis, flip_pairs(axis, bit))]
    ppermute x13, waiting for transfers between devices: 14.6 us -> 10.3 us  [halve(): part = keep + lax.ppermute(send, axis, flip_pairs(axis, bit))]
    conv_general_dilated x0 -> x4, matrix products: none -> 4.24 us  [convolve(): lax.conv_general_dilated(field[None], weights, (1, 1), 'VALID', dimension...]
  transfers between devices with their start and end apart: 34 -> 34, of which waited for: 11 -> 15; matrix products, arithmetic and copies ran while one was open for 7% -> 6% of each run, Pallas kernels for 0% -> 0%
where the time goes in v3:
time: 122 us; the launch traced here: 121 us
  starting transfers between devices  61 us (50%)
  waiting for transfers between devices  24 us (20%)
  local copies, waits for them, and re-layouts  16.6 us (14%)
  other arithmetic  12.5 us (10%)
  matrix products  4.84 us (4%)
  between operations  1.71 us (1%)
    ppermute x13, starting transfers between devices, halve(): part = keep + lax.ppermute(send, axis, flip_pairs(axis, bit))  19.5 us
    ppermute x4, starting transfers between devices, widen(): lax.ppermute(tail, axis, [(i, i + dist) for i in range(count - dist)])  18.3 us
    ppermute x13, starting transfers between devices, double(): got = lax.ppermute(piece, axis, flip_pairs(axis, bit))  16.8 us
    ppermute x13, waiting for transfers between devices, halve(): part = keep + lax.ppermute(send, axis, flip_pairs(axis, bit))  10.3 us
    ppermute x13, waiting for transfers between devices, double(): got = lax.ppermute(piece, axis, flip_pairs(axis, bit))  10 us
    ppermute x4, starting transfers between devices, widen(): lax.ppermute(head, axis, [(i + dist, i) for i in range(count - dist)])  6.41 us
    unnamed x63, local copies, waits for them, and re-layouts  5.23 us
    conv_general_dilated x4, matrix products, convolve(): lax.conv_general_dilated(field[None], weights, (1, 1), 'VALID', dimension...  4.24 us
  transfers between devices with their start and end apart: 34, of which 15 were waited for; matrix products, arithmetic and copies ran while one was open for 6% of the time, Pallas kernels for 0%

profile of v3, /device:TPU:1, one launch (start us, length us, event | category | flops | bytes accessed | tf_op | source)
XLA Modules:
  0.0 120.7 jit_solution(15551138355351492144)
XLA Ops:
  4.5 4.6 %collective-permute-start = (bf16[4,32,448]{2,1,0:T(8,128)(2,1)S(1)}, bf16[4,32,448]{2,1,0:T(8,128)(2,1)S(1)}, u32[]{:S(2)}, u32[]{:S(2)}) collective-permute-start(bf16[4,32,448]{2,1,0:T(8,128)(2,1)S(1)} %concatenate.116), channel_id=1, source_target_pairs={{0,8},{8,16},{16,24},{1,9},{9,17},{17,25},{2,10},{10,18},{18,26},{... | collective-permute-start | bytes 344072 | tf_op jit(solution)/shard_map/ppermute | solution.py:101
  11.3 4.9 %collective-permute-start.4 = (f32[3,32,128]{2,1,0:T(8,128)S(1)}, f32[3,32,128]{2,1,0:T(8,128)S(1)}, u32[]{:S(2)}, u32[]{:S(2)}) collective-permute-start(f32[3,32,128]{2,1,0:T(8,128)S(1)} %get-tuple-element.73), channel_id=1, source_target_pairs={{0,8},{8,16},{16,24},{1,9},{9,17},{17,25},{2,10},{10,18},{18,26},{... | collective-permute-start | bytes 147464 | tf_op jit(solution)/shard_map/ppermute | solution.py:101
  18.2 5.2 %collective-permute-start.6 = (f32[10,3,128]{2,1,0:T(4,128)S(1)}, f32[10,3,128]{2,1,0:T(4,128)S(1)}, u32[]{:S(2)}, u32[]{:S(2)}) collective-permute-start(f32[10,3,128]{2,1,0:T(4,128)S(1)} %get-tuple-element.57), channel_id=1, source_target_pairs={{0,1},{1,2},{2,3},{3,4},{4,5},{5,6},{6,7},{8,9},{9,10},{10,11},{11... | collective-permute-start | bytes 46088 | tf_op jit(solution)/shard_map/ppermute | solution.py:101
  23.4 1.9 %collective-permute-start.7 = (f32[10,3,128]{2,1,0:T(4,128)S(1)}, f32[10,3,128]{2,1,0:T(4,128)S(1)}, u32[]{:S(2)}, u32[]{:S(2)}) collective-permute-start(f32[10,3,128]{2,1,0:T(4,128)S(1)} %get-tuple-element.58), channel_id=1, source_target_pairs={{1,0},{2,1},{3,2},{4,3},{5,4},{6,5},{7,6},{9,8},{10,9},{11,10},{12... | collective-permute-start | bytes 46088 | tf_op jit(solution)/shard_map/ppermute | solution.py:102
  25.4 3.6 %collective-permute-start.2 = (bf16[12,4,448]{2,1,0:T(4,128)(2,1)S(1)}, bf16[12,4,448]{2,1,0:T(4,128)(2,1)S(1)}, u32[]{:S(2)}, u32[]{:S(2)}) collective-permute-start(bf16[12,4,448]{2,1,0:T(4,128)(2,1)S(1)} %get-tuple-element.35), channel_id=1, source_target_pairs={{0,1},{1,2},{2,3},{3,4},{4,5},{5,6},{6,7},{8,9},{9,10},{10,11},{11... | collective-permute-start | bytes 129032 | tf_op jit(solution)/shard_map/ppermute | solution.py:101
  29.0 1.9 %collective-permute-start.3 = (bf16[12,4,448]{2,1,0:T(4,128)(2,1)S(1)}, bf16[12,4,448]{2,1,0:T(4,128)(2,1)S(1)}, u32[]{:S(2)}, u32[]{:S(2)}) collective-permute-start(bf16[12,4,448]{2,1,0:T(4,128)(2,1)S(1)} %get-tuple-element.36), channel_id=1, source_target_pairs={{1,0},{2,1},{3,2},{4,3},{5,4},{6,5},{7,6},{9,8},{10,9},{11,10},{12... | collective-permute-start | bytes 129032 | tf_op jit(solution)/shard_map/ppermute | solution.py:102
  31.7 2.7 %collective-permute-done.3 = bf16[12,4,448]{2,1,0:T(4,128)(2,1)S(1)} collective-permute-done((bf16[12,4,448]{2,1,0:T(4,128)(2,1)S(1)}, bf16[12,4,448]{2,1,0:T(4,128)(2,1)S(1)}, u32[]{:S(2)}, u32[]{:S(2)}) %collective-permute-start.3) | collective-permute-done | bytes 43040 | tf_op jit(solution)/shard_map/ppermute | solution.py:102
  40.8 2.1 %convolution_select_fusion.1 = f32[8,8,5,512]{3,1,2,0:T(8,128)S(1)} fusion(bf16[3,3,160,512]{3,2,1,0:T(8,128)(2,1)} %bitcast.86, pred[8,5]{0,1:T(8,128)(4,1)S(1)} %copy-done.27, bf16[10,1,7,2,160]{4,2,3,0,1:T(8,128)(2,1)S(1)} %slice.281, bf16[10,1,8,5,160]{4,2,3,0,1:T(8,128)(2,1)S(1)} %copy.16), kind=kOutput, calls=%fused_computation.4 | convolution fusion | flops 472560640 | bytes 2302760 | tf_op jit(solution)/shard_map/conv_general_dilated | solution.py:134
  54.0 3.6 %collective-permute-done.8 = f32[768,512]{1,0:T(8,128)} collective-permute-done((f32[768,512]{1,0:T(8,128)}, f32[768,512]{1,0:T(8,128)}, u32[]{:S(2)}, u32[]{:S(2)}) %collective-permute-start.8) | collective-permute-done | bytes 1572896 | tf_op jit(solution)/shard_map/ppermute | solution.py:45
  61.4 2.7 %collective-permute-start.17 = (f32[128,512]{1,0:T(8,128)S(1)}, f32[128,512]{1,0:T(8,128)S(1)}, u32[]{:S(2)}, u32[]{:S(2)}) collective-permute-start(f32[128,512]{1,0:T(8,128)S(1)} %constant_dynamic-slice_fusion.7), channel_id=1, source_target_pairs={{0,8},{8,0},{16,24},{24,16},{1,9},{9,1},{17,25},{25,17},{2,10},{10... | collective-permute-start | bytes 786440 | tf_op jit(solution)/shard_map/ppermute | solution.py:45
  64.1 1.9 %collective-permute-start.25 = (f32[128,512]{1,0:T(8,128)S(1)}, f32[128,512]{1,0:T(8,128)S(1)}, u32[]{:S(2)}, u32[]{:S(2)}) collective-permute-start(f32[128,512]{1,0:T(8,128)S(1)} %constant_dynamic-slice_fusion.3), channel_id=1, source_target_pairs={{0,16},{8,24},{16,0},{24,8},{1,17},{9,25},{17,1},{25,9},{2,18},{10... | collective-permute-start | bytes 786440 | tf_op jit(solution)/shard_map/ppermute | solution.py:45
  67.5 2.7 %collective-permute-start.10 = (f32[64,512]{1,0:T(8,128)S(1)}, f32[64,512]{1,0:T(8,128)S(1)}, u32[]{:S(2)}, u32[]{:S(2)}) collective-permute-start(f32[64,512]{1,0:T(8,128)S(1)} %constant_dynamic-slice_fusion.10), channel_id=1, source_target_pairs={{0,8},{8,0},{16,24},{24,16},{1,9},{9,1},{17,25},{25,17},{2,10},{10... | collective-permute-start | bytes 393224 | tf_op jit(solution)/shard_map/ppermute | solution.py:45
  70.5 3.0 %collective-permute-start.18 = (f32[64,512]{1,0:T(8,128)S(1)}, f32[64,512]{1,0:T(8,128)S(1)}, u32[]{:S(2)}, u32[]{:S(2)}) collective-permute-start(f32[64,512]{1,0:T(8,128)S(1)} %constant_dynamic-slice_fusion.6), channel_id=1, source_target_pairs={{0,16},{8,24},{16,0},{24,8},{1,17},{9,25},{17,1},{25,9},{2,18},{10... | collective-permute-start | bytes 393224 | tf_op jit(solution)/shard_map/ppermute | solution.py:45
  73.5 2.0 %collective-permute-start.26 = (f32[64,512]{1,0:T(8,128)S(1)}, f32[64,512]{1,0:T(8,128)S(1)}, u32[]{:S(2)}, u32[]{:S(2)}) collective-permute-start(f32[64,512]{1,0:T(8,128)S(1)} %constant_dynamic-slice_fusion.2), channel_id=1, source_target_pairs={{0,4},{1,5},{2,6},{3,7},{4,0},{5,1},{6,2},{7,3},{8,12},{9,13},{10,... | collective-permute-start | bytes 393224 | tf_op jit(solution)/shard_map/ppermute | solution.py:45
  76.0 2.5 %collective-permute-start.19 = (f32[32,512]{1,0:T(8,128)S(1)}, f32[32,512]{1,0:T(8,128)S(1)}, u32[]{:S(2)}, u32[]{:S(2)}) collective-permute-start(f32[32,512]{1,0:T(8,128)S(1)} %constant_dynamic-slice_fusion.5), channel_id=1, source_target_pairs={{0,4},{1,5},{2,6},{3,7},{4,0},{5,1},{6,2},{7,3},{8,12},{9,13},{10,... | collective-permute-start | bytes 196616 | tf_op jit(solution)/shard_map/ppermute | solution.py:45
  78.4 4.2 %collective-permute-done.26 = f32[64,512]{1,0:T(8,128)S(1)} collective-permute-done((f32[64,512]{1,0:T(8,128)S(1)}, f32[64,512]{1,0:T(8,128)S(1)}, u32[]{:S(2)}, u32[]{:S(2)}) %collective-permute-start.26) | collective-permute-done | bytes 131104 | tf_op jit(solution)/shard_map/ppermute | solution.py:45
  82.9 2.5 %collective-permute-start.12 = (f32[16,512]{1,0:T(8,128)S(1)}, f32[16,512]{1,0:T(8,128)S(1)}, u32[]{:S(2)}, u32[]{:S(2)}) collective-permute-start(f32[16,512]{1,0:T(8,128)S(1)} %constant_dynamic-slice_fusion.8), channel_id=1, source_target_pairs={{0,4},{1,5},{2,6},{3,7},{4,0},{5,1},{6,2},{7,3},{8,12},{9,13},{10,... | collective-permute-start | bytes 98312 | tf_op jit(solution)/shard_map/ppermute | solution.py:45
  86.7 2.5 %collective-permute-start.13 = (bf16[16,512]{1,0:T(8,128)(2,1)S(1)}, bf16[16,512]{1,0:T(8,128)(2,1)S(1)}, u32[]{:S(2)}, u32[]{:S(2)}) collective-permute-start(bf16[16,512]{1,0:T(8,128)(2,1)S(1)} %add_convert_fusion.2), channel_id=1, source_target_pairs={{0,4},{1,5},{2,6},{3,7},{4,0},{5,1},{6,2},{7,3},{8,12},{9,13},{10,... | collective-permute-start | bytes 49160 | tf_op jit(solution)/shard_map/ppermute | solution.py:55
  94.5 2.0 %collective-permute-done.22 = bf16[32,512]{1,0:T(8,128)(2,1)S(1)} collective-permute-done((bf16[32,512]{1,0:T(8,128)(2,1)S(1)}, bf16[32,512]{1,0:T(8,128)(2,1)S(1)}, u32[]{:S(2)}, u32[]{:S(2)}) %collective-permute-start.22) | collective-permute-done | bytes 32800 | tf_op jit(solution)/shard_map/ppermute | solution.py:55
  96.6 1.9 %collective-permute-start.31 = (bf16[64,512]{1,0:T(8,128)(2,1)S(1)}, bf16[64,512]{1,0:T(8,128)(2,1)S(1)}, u32[]{:S(2)}, u32[]{:S(2)}) collective-permute-start(bf16[64,512]{1,0:T(8,128)(2,1)S(1)} %pad_maximum_fusion.16), channel_id=1, source_target_pairs={{0,4},{1,5},{2,6},{3,7},{4,0},{5,1},{6,2},{7,3},{8,12},{9,13},{10,... | collective-permute-start | bytes 196616 | tf_op jit(solution)/shard_map/ppermute | solution.py:55
  100.3 2.0 %collective-permute-done.31 = bf16[64,512]{1,0:T(8,128)(2,1)S(1)} collective-permute-done((bf16[64,512]{1,0:T(8,128)(2,1)S(1)}, bf16[64,512]{1,0:T(8,128)(2,1)S(1)}, u32[]{:S(2)}, u32[]{:S(2)}) %collective-permute-start.31) | collective-permute-done | bytes 65568 | tf_op jit(solution)/shard_map/ppermute | solution.py:55
  104.6 2.2 %collective-permute-done.32 = bf16[128,512]{1,0:T(8,128)(2,1)S(1)} collective-permute-done((bf16[128,512]{1,0:T(8,128)(2,1)S(1)}, bf16[128,512]{1,0:T(8,128)(2,1)S(1)}, u32[]{:S(2)}, u32[]{:S(2)}) %collective-permute-start.32) | collective-permute-done | bytes 131104 | tf_op jit(solution)/shard_map/ppermute | solution.py:55
  106.9 7.3 %collective-permute-start.33 = (bf16[768,512]{1,0:T(8,128)(2,1)S(1)}, bf16[768,512]{1,0:T(8,128)(2,1)S(1)}, u32[]{:S(2)}, u32[]{:S(2)}) collective-permute-start(bf16[768,512]{1,0:T(8,128)(2,1)S(1)} %select_dynamic-update-slice_fusion), channel_id=1, source_target_pairs={{0,1},{1,0},{2,3},{3,2},{4,5},{5,4},{6,7},{7,6},{8,9},{9,8},{10,11... | collective-permute-start | bytes 2359304 | tf_op jit(solution)/shard_map/ppermute | solution.py:55
  118.8 1.9 %slice.344 = f32[1440,512]{1,0:T(8,128)} slice(f32[1536,512]{1,0:T(8,128)S(1)} %maximum_convert_fusion), slice={[0:1440], [0:512]} | slice | bytes 5898240 | tf_op jit(solution)/shard_map/slice | solution.py:254
  (235 shorter events, 47.1 us)
Async XLA Ops:
  3.2 22.1 %collective-permute-start.1 = (bf16[4,32,448]{2,1,0:T(8,128)(2,1)S(1)}, bf16[4,32,448]{2,1,0:T(8,128)(2,1)S(1)}, u32[]{:S(2)}, u32[]{:S(2)}) collective-permute-start(bf16[4,32,448]{2,1,0:T(8,128)(2,1)S(1)} %concatenate.116), channel_id=1, source_target_pairs={{8,0},{16,8},{24,16},{9,1},{17,9},{25,17},{10,2},{18,10},{26,18},{... | collective-permute-start | bytes 344072 | tf_op jit(solution)/shard_map/ppermute | solution.py:102
  4.5 20.8 %collective-permute-start = (bf16[4,32,448]{2,1,0:T(8,128)(2,1)S(1)}, bf16[4,32,448]{2,1,0:T(8,128)(2,1)S(1)}, u32[]{:S(2)}, u32[]{:S(2)}) collective-permute-start(bf16[4,32,448]{2,1,0:T(8,128)(2,1)S(1)} %concatenate.116), channel_id=1, source_target_pairs={{0,8},{8,16},{16,24},{1,9},{9,17},{17,25},{2,10},{10,18},{18,26},{... | collective-permute-start | bytes 344072 | tf_op jit(solution)/shard_map/ppermute | solution.py:101
  10.0 8.2 %collective-permute-start.5 = (f32[3,32,128]{2,1,0:T(8,128)S(1)}, f32[3,32,128]{2,1,0:T(8,128)S(1)}, u32[]{:S(2)}, u32[]{:S(2)}) collective-permute-start(f32[3,32,128]{2,1,0:T(8,128)S(1)} %get-tuple-element.72), channel_id=1, source_target_pairs={{8,0},{16,8},{24,16},{9,1},{17,9},{25,17},{10,2},{18,10},{26,18},{... | collective-permute-start | bytes 147464 | tf_op jit(solution)/shard_map/ppermute | solution.py:102
  11.3 6.0 %collective-permute-start.4 = (f32[3,32,128]{2,1,0:T(8,128)S(1)}, f32[3,32,128]{2,1,0:T(8,128)S(1)}, u32[]{:S(2)}, u32[]{:S(2)}) collective-permute-start(f32[3,32,128]{2,1,0:T(8,128)S(1)} %get-tuple-element.73), channel_id=1, source_target_pairs={{0,8},{8,16},{16,24},{1,9},{9,17},{17,25},{2,10},{10,18},{18,26},{... | collective-permute-start | bytes 147464 | tf_op jit(solution)/shard_map/ppermute | solution.py:101
  18.2 12.8 %collective-permute-start.6 = (f32[10,3,128]{2,1,0:T(4,128)S(1)}, f32[10,3,128]{2,1,0:T(4,128)S(1)}, u32[]{:S(2)}, u32[]{:S(2)}) collective-permute-start(f32[10,3,128]{2,1,0:T(4,128)S(1)} %get-tuple-element.57), channel_id=1, source_target_pairs={{0,1},{1,2},{2,3},{3,4},{4,5},{5,6},{6,7},{8,9},{9,10},{10,11},{11... | collective-permute-start | bytes 46088 | tf_op jit(solution)/shard_map/ppermute | solution.py:101
  23.4 7.6 %collective-permute-start.7 = (f32[10,3,128]{2,1,0:T(4,128)S(1)}, f32[10,3,128]{2,1,0:T(4,128)S(1)}, u32[]{:S(2)}, u32[]{:S(2)}) collective-permute-start(f32[10,3,128]{2,1,0:T(4,128)S(1)} %get-tuple-element.58), channel_id=1, source_target_pairs={{1,0},{2,1},{3,2},{4,3},{5,4},{6,5},{7,6},{9,8},{10,9},{11,10},{12... | collective-permute-start | bytes 46088 | tf_op jit(solution)/shard_map/ppermute | solution.py:102
  25.4 6.3 %collective-permute-start.2 = (bf16[12,4,448]{2,1,0:T(4,128)(2,1)S(1)}, bf16[12,4,448]{2,1,0:T(4,128)(2,1)S(1)}, u32[]{:S(2)}, u32[]{:S(2)}) collective-permute-start(bf16[12,4,448]{2,1,0:T(4,128)(2,1)S(1)} %get-tuple-element.35), channel_id=1, source_target_pairs={{0,1},{1,2},{2,3},{3,4},{4,5},{5,6},{6,7},{8,9},{9,10},{10,11},{11... | collective-permute-start | bytes 129032 | tf_op jit(solution)/shard_map/ppermute | solution.py:101
  29.0 5.4 %collective-permute-start.3 = (bf16[12,4,448]{2,1,0:T(4,128)(2,1)S(1)}, bf16[12,4,448]{2,1,0:T(4,128)(2,1)S(1)}, u32[]{:S(2)}, u32[]{:S(2)}) collective-permute-start(bf16[12,4,448]{2,1,0:T(4,128)(2,1)S(1)} %get-tuple-element.36), channel_id=1, source_target_pairs={{1,0},{2,1},{3,2},{4,3},{5,4},{6,5},{7,6},{9,8},{10,9},{11,10},{12... | collective-permute-start | bytes 129032 | tf_op jit(solution)/shard_map/ppermute | solution.py:102
  59.6 7.8 %collective-permute-start.9 = (f32[128,512]{1,0:T(8,128)S(1)}, f32[128,512]{1,0:T(8,128)S(1)}, u32[]{:S(2)}, u32[]{:S(2)}) collective-permute-start(f32[128,512]{1,0:T(8,128)S(1)} %constant_dynamic-slice_fusion.11), channel_id=1, source_target_pairs={{0,2},{1,3},{2,0},{3,1},{4,6},{5,7},{6,4},{7,5},{8,10},{9,11},{10,... | collective-permute-start | bytes 786440 | tf_op jit(solution)/shard_map/ppermute | solution.py:45
  61.4 9.0 %collective-permute-start.17 = (f32[128,512]{1,0:T(8,128)S(1)}, f32[128,512]{1,0:T(8,128)S(1)}, u32[]{:S(2)}, u32[]{:S(2)}) collective-permute-start(f32[128,512]{1,0:T(8,128)S(1)} %constant_dynamic-slice_fusion.7), channel_id=1, source_target_pairs={{0,8},{8,0},{16,24},{24,16},{1,9},{9,1},{17,25},{25,17},{2,10},{10... | collective-permute-start | bytes 786440 | tf_op jit(solution)/shard_map/ppermute | solution.py:45
  64.1 9.3 %collective-permute-start.25 = (f32[128,512]{1,0:T(8,128)S(1)}, f32[128,512]{1,0:T(8,128)S(1)}, u32[]{:S(2)}, u32[]{:S(2)}) collective-permute-start(f32[128,512]{1,0:T(8,128)S(1)} %constant_dynamic-slice_fusion.3), channel_id=1, source_target_pairs={{0,16},{8,24},{16,0},{24,8},{1,17},{9,25},{17,1},{25,9},{2,18},{10... | collective-permute-start | bytes 786440 | tf_op jit(solution)/shard_map/ppermute | solution.py:45
  67.5 8.1 %collective-permute-start.10 = (f32[64,512]{1,0:T(8,128)S(1)}, f32[64,512]{1,0:T(8,128)S(1)}, u32[]{:S(2)}, u32[]{:S(2)}) collective-permute-start(f32[64,512]{1,0:T(8,128)S(1)} %constant_dynamic-slice_fusion.10), channel_id=1, source_target_pairs={{0,8},{8,0},{16,24},{24,16},{1,9},{9,1},{17,25},{25,17},{2,10},{10... | collective-permute-start | bytes 393224 | tf_op jit(solution)/shard_map/ppermute | solution.py:45
  70.5 5.4 %collective-permute-start.18 = (f32[64,512]{1,0:T(8,128)S(1)}, f32[64,512]{1,0:T(8,128)S(1)}, u32[]{:S(2)}, u32[]{:S(2)}) collective-permute-start(f32[64,512]{1,0:T(8,128)S(1)} %constant_dynamic-slice_fusion.6), channel_id=1, source_target_pairs={{0,16},{8,24},{16,0},{24,8},{1,17},{9,25},{17,1},{25,9},{2,18},{10... | collective-permute-start | bytes 393224 | tf_op jit(solution)/shard_map/ppermute | solution.py:45
  73.5 9.2 %collective-permute-start.26 = (f32[64,512]{1,0:T(8,128)S(1)}, f32[64,512]{1,0:T(8,128)S(1)}, u32[]{:S(2)}, u32[]{:S(2)}) collective-permute-start(f32[64,512]{1,0:T(8,128)S(1)} %constant_dynamic-slice_fusion.2), channel_id=1, source_target_pairs={{0,4},{1,5},{2,6},{3,7},{4,0},{5,1},{6,2},{7,3},{8,12},{9,13},{10,... | collective-permute-start | bytes 393224 | tf_op jit(solution)/shard_map/ppermute | solution.py:45
  75.6 7.2 %collective-permute-start.11 = (f32[32,512]{1,0:T(8,128)S(1)}, f32[32,512]{1,0:T(8,128)S(1)}, u32[]{:S(2)}, u32[]{:S(2)}) collective-permute-start(f32[32,512]{1,0:T(8,128)S(1)} %constant_dynamic-slice_fusion.9), channel_id=1, source_target_pairs={{0,16},{8,24},{16,0},{24,8},{1,17},{9,25},{17,1},{25,9},{2,18},{10... | collective-permute-start | bytes 196616 | tf_op jit(solution)/shard_map/ppermute | solution.py:45
  76.0 9.4 %collective-permute-start.19 = (f32[32,512]{1,0:T(8,128)S(1)}, f32[32,512]{1,0:T(8,128)S(1)}, u32[]{:S(2)}, u32[]{:S(2)}) collective-permute-start(f32[32,512]{1,0:T(8,128)S(1)} %constant_dynamic-slice_fusion.5), channel_id=1, source_target_pairs={{0,4},{1,5},{2,6},{3,7},{4,0},{5,1},{6,2},{7,3},{8,12},{9,13},{10,... | collective-permute-start | bytes 196616 | tf_op jit(solution)/shard_map/ppermute | solution.py:45
  82.9 3.8 %collective-permute-start.12 = (f32[16,512]{1,0:T(8,128)S(1)}, f32[16,512]{1,0:T(8,128)S(1)}, u32[]{:S(2)}, u32[]{:S(2)}) collective-permute-start(f32[16,512]{1,0:T(8,128)S(1)} %constant_dynamic-slice_fusion.8), channel_id=1, source_target_pairs={{0,4},{1,5},{2,6},{3,7},{4,0},{5,1},{6,2},{7,3},{8,12},{9,13},{10,... | collective-permute-start | bytes 98312 | tf_op jit(solution)/shard_map/ppermute | solution.py:45
  92.4 4.1 %collective-permute-start.22 = (bf16[32,512]{1,0:T(8,128)(2,1)S(1)}, bf16[32,512]{1,0:T(8,128)(2,1)S(1)}, u32[]{:S(2)}, u32[]{:S(2)}) collective-permute-start(bf16[32,512]{1,0:T(8,128)(2,1)S(1)} %pad_maximum_fusion.22), channel_id=1, source_target_pairs={{0,4},{1,5},{2,6},{3,7},{4,0},{5,1},{6,2},{7,3},{8,12},{9,13},{10,... | collective-permute-start | bytes 98312 | tf_op jit(solution)/shard_map/ppermute | solution.py:55
  93.9 4.6 %collective-permute-start.15 = (bf16[64,512]{1,0:T(8,128)(2,1)S(1)}, bf16[64,512]{1,0:T(8,128)(2,1)S(1)}, u32[]{:S(2)}, u32[]{:S(2)}) collective-permute-start(bf16[64,512]{1,0:T(8,128)(2,1)S(1)} %pad_maximum_fusion.14), channel_id=1, source_target_pairs={{0,8},{8,0},{16,24},{24,16},{1,9},{9,1},{17,25},{25,17},{2,10},{10... | collective-permute-start | bytes 196616 | tf_op jit(solution)/shard_map/ppermute | solution.py:55
  96.6 5.6 %collective-permute-start.31 = (bf16[64,512]{1,0:T(8,128)(2,1)S(1)}, bf16[64,512]{1,0:T(8,128)(2,1)S(1)}, u32[]{:S(2)}, u32[]{:S(2)}) collective-permute-start(bf16[64,512]{1,0:T(8,128)(2,1)S(1)} %pad_maximum_fusion.16), channel_id=1, source_target_pairs={{0,4},{1,5},{2,6},{3,7},{4,0},{5,1},{6,2},{7,3},{8,12},{9,13},{10,... | collective-permute-start | bytes 196616 | tf_op jit(solution)/shard_map/ppermute | solution.py:55
  98.5 5.1 %collective-permute-start.16 = (bf16[128,512]{1,0:T(8,128)(2,1)S(1)}, bf16[128,512]{1,0:T(8,128)(2,1)S(1)}, u32[]{:S(2)}, u32[]{:S(2)}) collective-permute-start(bf16[128,512]{1,0:T(8,128)(2,1)S(1)} %pad_maximum_fusion.10), channel_id=1, source_target_pairs={{0,2},{1,3},{2,0},{3,1},{4,6},{5,7},{6,4},{7,5},{8,10},{9,11},{10,... | collective-permute-start | bytes 393224 | tf_op jit(solution)/shard_map/ppermute | solution.py:55
  99.8 4.8 %collective-permute-start.24 = (bf16[128,512]{1,0:T(8,128)(2,1)S(1)}, bf16[128,512]{1,0:T(8,128)(2,1)S(1)}, u32[]{:S(2)}, u32[]{:S(2)}) collective-permute-start(bf16[128,512]{1,0:T(8,128)(2,1)S(1)} %pad_maximum_fusion.11), channel_id=1, source_target_pairs={{0,8},{8,0},{16,24},{24,16},{1,9},{9,1},{17,25},{25,17},{2,10},{10... | collective-permute-start | bytes 393224 | tf_op jit(solution)/shard_map/ppermute | solution.py:55
  102.3 4.5 %collective-permute-start.32 = (bf16[128,512]{1,0:T(8,128)(2,1)S(1)}, bf16[128,512]{1,0:T(8,128)(2,1)S(1)}, u32[]{:S(2)}, u32[]{:S(2)}) collective-permute-start(bf16[128,512]{1,0:T(8,128)(2,1)S(1)} %pad_maximum_fusion.12), channel_id=1, source_target_pairs={{0,16},{8,24},{16,0},{24,8},{1,17},{9,25},{17,1},{25,9},{2,18},{10... | collective-permute-start | bytes 393224 | tf_op jit(solution)/shard_map/ppermute | solution.py:55
  106.9 10.8 %collective-permute-start.33 = (bf16[768,512]{1,0:T(8,128)(2,1)S(1)}, bf16[768,512]{1,0:T(8,128)(2,1)S(1)}, u32[]{:S(2)}, u32[]{:S(2)}) collective-permute-start(bf16[768,512]{1,0:T(8,128)(2,1)S(1)} %select_dynamic-update-slice_fusion), channel_id=1, source_target_pairs={{0,1},{1,0},{2,3},{3,2},{4,5},{5,4},{6,7},{7,6},{8,9},{9,8},{10,11... | collective-permute-start | bytes 2359304 | tf_op jit(solution)/shard_map/ppermute | solution.py:55
  (39 other events, 124.6 us)

commit v4 on v3

--- a/solution.py
+++ b/solution.py
@@ -12,7 +12,6 @@
 GATES = 512
 KIN = 1440
 SUM_ROWS = 1536
-SUM_WAYS = 3
 
 
 def flip_pairs(axis, bit):
@@ -62,14 +61,25 @@
 def sum_everywhere(total):
     first, rest = summing_levels()
     part, first_halved = halve(total, first)
-    ways = min(SUM_WAYS, max(len(rest), 1))
-    width = part.shape[0] // ways
-    pieces = []
-    for way in range(ways):
-        order = rest[way:] + rest[:way]
-        chunk, halved = halve(part[way * width : (way + 1) * width], order)
-        pieces.append(double(chunk.astype(jnp.bfloat16), halved))
-    return double(jnp.concatenate(pieces, axis=0), first_halved).astype(jnp.float32)
+    if len(rest) >= 2:
+        width = part.shape[0] // 2
+        orders = (rest[:2], [rest[1], rest[0]])
+        chunks, halves = [], []
+        for way, order in enumerate(orders):
+            chunk, halved = halve(part[way * width : (way + 1) * width], order)
+            chunks.append(chunk)
+            halves.append(halved)
+        merged, merged_halved = halve(jnp.concatenate(chunks, axis=0), rest[2:])
+        merged = double(merged.astype(jnp.bfloat16), merged_halved)
+        size = merged.shape[0] // 2
+        pieces = [
+            double(merged[way * size : (way + 1) * size], halves[way]) for way in range(2)
+        ]
+        piece = jnp.concatenate(pieces, axis=0)
+    else:
+        chunk, halved = halve(part, rest)
+        piece = double(chunk.astype(jnp.bfloat16), halved)
+    return double(piece, first_halved).astype(jnp.float32)
 
 def tap_columns(padded, rows_dev, cols_dev, reverse):
     pieces = []

time: 122 us -> 124 us (1.016)
  waiting for transfers between devices: 24 us -> 36.6 us
  starting transfers between devices: 61 us -> 51.3 us
    ppermute x13 -> x7, waiting for transfers between devices: 10.3 us -> 20.8 us  [halve(): part = keep + lax.ppermute(send, axis, flip_pairs(axis, bit))]
    ppermute x13 -> x7, starting transfers between devices: 19.5 us -> 12.7 us  [halve(): part = keep + lax.ppermute(send, axis, flip_pairs(axis, bit))]
    ppermute x13 -> x7, starting transfers between devices: 16.8 us -> 14 us  [double(): got = lax.ppermute(piece, axis, flip_pairs(axis, bit))]
    ppermute x13 -> x7, waiting for transfers between devices: 10 us -> 12.1 us  [double(): got = lax.ppermute(piece, axis, flip_pairs(axis, bit))]
  transfers between devices with their start and end apart: 34 -> 22, of which waited for: 15 -> 14; matrix products, arithmetic and copies ran while one was open for 6% -> 6% of each run, Pallas kernels for 0% -> 0%
where the time goes in v4:
time: 124 us; the launch traced here: 123 us
  starting transfers between devices  51.3 us (41%)
  waiting for transfers between devices  36.6 us (30%)
  local copies, waits for them, and re-layouts  16.5 us (13%)
  other arithmetic  12.6 us (10%)
  matrix products  4.84 us (4%)
  between operations  1.53 us (1%)
    ppermute x7, waiting for transfers between devices, halve(): part = keep + lax.ppermute(send, axis, flip_pairs(axis, bit))  20.8 us
    ppermute x4, starting transfers between devices, widen(): lax.ppermute(tail, axis, [(i, i + dist) for i in range(count - dist)])  18.3 us
    ppermute x7, starting transfers between devices, double(): got = lax.ppermute(piece, axis, flip_pairs(axis, bit))  14 us
    ppermute x7, starting transfers between devices, halve(): part = keep + lax.ppermute(send, axis, flip_pairs(axis, bit))  12.7 us
    ppermute x7, waiting for transfers between devices, double(): got = lax.ppermute(piece, axis, flip_pairs(axis, bit))  12.1 us
    ppermute x4, starting transfers between devices, widen(): lax.ppermute(head, axis, [(i + dist, i) for i in range(count - dist)])  6.41 us
    unnamed x63, local copies, waits for them, and re-layouts  5.23 us
    conv_general_dilated x4, matrix products, convolve(): lax.conv_general_dilated(field[None], weights, (1, 1), 'VALID', dimension...  4.24 us
  transfers between devices with their start and end apart: 22, of which 14 were waited for; matrix products, arithmetic and copies ran while one was open for 6% of the time, Pallas kernels for 0%

profile of v4, /device:TPU:1, one launch (start us, length us, event | category | flops | bytes accessed | tf_op | source)
XLA Modules:
  0.0 123.4 jit_solution(15765200262406810552)
XLA Ops:
  4.5 4.6 %collective-permute-start = (bf16[4,32,448]{2,1,0:T(8,128)(2,1)S(1)}, bf16[4,32,448]{2,1,0:T(8,128)(2,1)S(1)}, u32[]{:S(2)}, u32[]{:S(2)}) collective-permute-start(bf16[4,32,448]{2,1,0:T(8,128)(2,1)S(1)} %concatenate.101), channel_id=1, source_target_pairs={{0,8},{8,16},{16,24},{1,9},{9,17},{17,25},{2,10},{10,18},{18,26},{... | collective-permute-start | bytes 344072 | tf_op jit(solution)/shard_map/ppermute | solution.py:111
  11.3 4.9 %collective-permute-start.4 = (f32[3,32,128]{2,1,0:T(8,128)S(1)}, f32[3,32,128]{2,1,0:T(8,128)S(1)}, u32[]{:S(2)}, u32[]{:S(2)}) collective-permute-start(f32[3,32,128]{2,1,0:T(8,128)S(1)} %get-tuple-element.72), channel_id=1, source_target_pairs={{0,8},{8,16},{16,24},{1,9},{9,17},{17,25},{2,10},{10,18},{18,26},{... | collective-permute-start | bytes 147464 | tf_op jit(solution)/shard_map/ppermute | solution.py:111
  18.2 5.2 %collective-permute-start.6 = (f32[10,3,128]{2,1,0:T(4,128)S(1)}, f32[10,3,128]{2,1,0:T(4,128)S(1)}, u32[]{:S(2)}, u32[]{:S(2)}) collective-permute-start(f32[10,3,128]{2,1,0:T(4,128)S(1)} %get-tuple-element.66), channel_id=1, source_target_pairs={{0,1},{1,2},{2,3},{3,4},{4,5},{5,6},{6,7},{8,9},{9,10},{10,11},{11... | collective-permute-start | bytes 46088 | tf_op jit(solution)/shard_map/ppermute | solution.py:111
  23.4 1.9 %collective-permute-start.7 = (f32[10,3,128]{2,1,0:T(4,128)S(1)}, f32[10,3,128]{2,1,0:T(4,128)S(1)}, u32[]{:S(2)}, u32[]{:S(2)}) collective-permute-start(f32[10,3,128]{2,1,0:T(4,128)S(1)} %get-tuple-element.67), channel_id=1, source_target_pairs={{1,0},{2,1},{3,2},{4,3},{5,4},{6,5},{7,6},{9,8},{10,9},{11,10},{12... | collective-permute-start | bytes 46088 | tf_op jit(solution)/shard_map/ppermute | solution.py:112
  25.4 3.6 %collective-permute-start.2 = (bf16[12,4,448]{2,1,0:T(4,128)(2,1)S(1)}, bf16[12,4,448]{2,1,0:T(4,128)(2,1)S(1)}, u32[]{:S(2)}, u32[]{:S(2)}) collective-permute-start(bf16[12,4,448]{2,1,0:T(4,128)(2,1)S(1)} %get-tuple-element.38), channel_id=1, source_target_pairs={{0,1},{1,2},{2,3},{3,4},{4,5},{5,6},{6,7},{8,9},{9,10},{10,11},{11... | collective-permute-start | bytes 129032 | tf_op jit(solution)/shard_map/ppermute | solution.py:111
  29.0 1.9 %collective-permute-start.3 = (bf16[12,4,448]{2,1,0:T(4,128)(2,1)S(1)}, bf16[12,4,448]{2,1,0:T(4,128)(2,1)S(1)}, u32[]{:S(2)}, u32[]{:S(2)}) collective-permute-start(bf16[12,4,448]{2,1,0:T(4,128)(2,1)S(1)} %get-tuple-element.39), channel_id=1, source_target_pairs={{1,0},{2,1},{3,2},{4,3},{5,4},{6,5},{7,6},{9,8},{10,9},{11,10},{12... | collective-permute-start | bytes 129032 | tf_op jit(solution)/shard_map/ppermute | solution.py:112
  31.7 2.8 %collective-permute-done.3 = bf16[12,4,448]{2,1,0:T(4,128)(2,1)S(1)} collective-permute-done((bf16[12,4,448]{2,1,0:T(4,128)(2,1)S(1)}, bf16[12,4,448]{2,1,0:T(4,128)(2,1)S(1)}, u32[]{:S(2)}, u32[]{:S(2)}) %collective-permute-start.3) | collective-permute-done | bytes 43040 | tf_op jit(solution)/shard_map/ppermute | solution.py:112
  40.8 2.1 %convolution_select_fusion.1 = f32[8,8,5,512]{3,1,2,0:T(8,128)S(1)} fusion(bf16[3,3,160,512]{3,2,1,0:T(8,128)(2,1)} %bitcast.86, pred[8,5]{0,1:T(8,128)(4,1)S(1)} %copy-done.27, bf16[10,1,7,2,160]{4,2,3,0,1:T(8,128)(2,1)S(1)} %slice.277, bf16[10,1,8,5,160]{4,2,3,0,1:T(8,128)(2,1)S(1)} %copy.16), kind=kOutput, calls=%fused_computation.4 | convolution fusion | flops 472560640 | bytes 2302760 | tf_op jit(solution)/shard_map/conv_general_dilated | solution.py:144
  53.9 3.7 %collective-permute-done.8 = f32[768,512]{1,0:T(8,128)} collective-permute-done((f32[768,512]{1,0:T(8,128)}, f32[768,512]{1,0:T(8,128)}, u32[]{:S(2)}, u32[]{:S(2)}) %collective-permute-start.8) | collective-permute-done | bytes 1572896 | tf_op jit(solution)/shard_map/ppermute | solution.py:44
  61.0 2.7 %collective-permute-start.11 = (f32[192,512]{1,0:T(8,128)S(1)}, f32[192,512]{1,0:T(8,128)S(1)}, u32[]{:S(2)}, u32[]{:S(2)}) collective-permute-start(f32[192,512]{1,0:T(8,128)S(1)} %constant_dynamic-slice_fusion.2), channel_id=1, source_target_pairs={{0,8},{8,0},{16,24},{24,16},{1,9},{9,1},{17,25},{25,17},{2,10},{10... | collective-permute-start | bytes 1179656 | tf_op jit(solution)/shard_map/ppermute | solution.py:44
  63.7 6.6 %collective-permute-done.9 = f32[192,512]{1,0:T(8,128)S(1)} collective-permute-done((f32[192,512]{1,0:T(8,128)S(1)}, f32[192,512]{1,0:T(8,128)S(1)}, u32[]{:S(2)}, u32[]{:S(2)}) %collective-permute-start.9) | collective-permute-done | bytes 393248 | tf_op jit(solution)/shard_map/ppermute | solution.py:44
  70.3 2.7 %collective-permute-start.10 = (f32[96,512]{1,0:T(8,128)S(1)}, f32[96,512]{1,0:T(8,128)S(1)}, u32[]{:S(2)}, u32[]{:S(2)}) collective-permute-start(f32[96,512]{1,0:T(8,128)S(1)} %constant_dynamic-slice_fusion.3), channel_id=1, source_target_pairs={{0,8},{8,0},{16,24},{24,16},{1,9},{9,1},{17,25},{25,17},{2,10},{10... | collective-permute-start | bytes 589832 | tf_op jit(solution)/shard_map/ppermute | solution.py:44
  74.5 2.8 %collective-permute-done.10 = f32[96,512]{1,0:T(8,128)S(1)} collective-permute-done((f32[96,512]{1,0:T(8,128)S(1)}, f32[96,512]{1,0:T(8,128)S(1)}, u32[]{:S(2)}, u32[]{:S(2)}) %collective-permute-start.10) | collective-permute-done | bytes 196640 | tf_op jit(solution)/shard_map/ppermute | solution.py:44
  78.4 2.7 %collective-permute-start.13 = (f32[96,512]{1,0:T(8,128)S(1)}, f32[96,512]{1,0:T(8,128)S(1)}, u32[]{:S(2)}, u32[]{:S(2)}) collective-permute-start(f32[96,512]{1,0:T(8,128)S(1)} %fusion.51), channel_id=1, source_target_pairs={{0,16},{8,24},{16,0},{24,8},{1,17},{9,25},{17,1},{25,9},{2,18},{10... | collective-permute-start | bytes 589832 | tf_op jit(solution)/shard_map/ppermute | solution.py:44
  81.1 3.1 %collective-permute-done.13 = f32[96,512]{1,0:T(8,128)S(1)} collective-permute-done((f32[96,512]{1,0:T(8,128)S(1)}, f32[96,512]{1,0:T(8,128)S(1)}, u32[]{:S(2)}, u32[]{:S(2)}) %collective-permute-start.13) | collective-permute-done | bytes 196640 | tf_op jit(solution)/shard_map/ppermute | solution.py:44
  84.3 1.8 %collective-permute-start.14 = (f32[48,512]{1,0:T(8,128)S(1)}, f32[48,512]{1,0:T(8,128)S(1)}, u32[]{:S(2)}, u32[]{:S(2)}) collective-permute-start(f32[48,512]{1,0:T(8,128)S(1)} %constant_dynamic-slice_fusion), channel_id=1, source_target_pairs={{0,4},{1,5},{2,6},{3,7},{4,0},{5,1},{6,2},{7,3},{8,12},{9,13},{10,... | collective-permute-start | bytes 294920 | tf_op jit(solution)/shard_map/ppermute | solution.py:44
  86.1 3.7 %collective-permute-done.14 = f32[48,512]{1,0:T(8,128)S(1)} collective-permute-done((f32[48,512]{1,0:T(8,128)S(1)}, f32[48,512]{1,0:T(8,128)S(1)}, u32[]{:S(2)}, u32[]{:S(2)}) %collective-permute-start.14) | collective-permute-done | bytes 98336 | tf_op jit(solution)/shard_map/ppermute | solution.py:44
  90.7 3.7 %collective-permute-done.15 = bf16[48,512]{1,0:T(8,128)(2,1)S(1)} collective-permute-done((bf16[48,512]{1,0:T(8,128)(2,1)S(1)}, bf16[48,512]{1,0:T(8,128)(2,1)S(1)}, u32[]{:S(2)}, u32[]{:S(2)}) %collective-permute-start.15) | collective-permute-done | bytes 49184 | tf_op jit(solution)/shard_map/ppermute | solution.py:54
  94.4 2.1 %collective-permute-start.16 = (bf16[96,512]{1,0:T(8,128)(2,1)S(1)}, bf16[96,512]{1,0:T(8,128)(2,1)S(1)}, u32[]{:S(2)}, u32[]{:S(2)}) collective-permute-start(bf16[96,512]{1,0:T(8,128)(2,1)S(1)} %pad_maximum_fusion.13), channel_id=1, source_target_pairs={{0,16},{8,24},{16,0},{24,8},{1,17},{9,25},{17,1},{25,9},{2,18},{10... | collective-permute-start | bytes 294920 | tf_op jit(solution)/shard_map/ppermute | solution.py:54
  96.5 1.9 %collective-permute-done.16 = bf16[96,512]{1,0:T(8,128)(2,1)S(1)} collective-permute-done((bf16[96,512]{1,0:T(8,128)(2,1)S(1)}, bf16[96,512]{1,0:T(8,128)(2,1)S(1)}, u32[]{:S(2)}, u32[]{:S(2)}) %collective-permute-start.16) | collective-permute-done | bytes 98336 | tf_op jit(solution)/shard_map/ppermute | solution.py:54
  99.5 2.5 %collective-permute-done.17 = bf16[96,512]{1,0:T(8,128)(2,1)S(1)} collective-permute-done((bf16[96,512]{1,0:T(8,128)(2,1)S(1)}, bf16[96,512]{1,0:T(8,128)(2,1)S(1)}, u32[]{:S(2)}, u32[]{:S(2)}) %collective-permute-start.17) | collective-permute-done | bytes 98336 | tf_op jit(solution)/shard_map/ppermute | solution.py:54
  104.4 2.3 %collective-permute-done.18 = bf16[192,512]{1,0:T(8,128)(2,1)S(1)} collective-permute-done((bf16[192,512]{1,0:T(8,128)(2,1)S(1)}, bf16[192,512]{1,0:T(8,128)(2,1)S(1)}, u32[]{:S(2)}, u32[]{:S(2)}) %collective-permute-start.18) | collective-permute-done | bytes 196640 | tf_op jit(solution)/shard_map/ppermute | solution.py:54
  107.8 9.0 %collective-permute-start.21 = (bf16[768,512]{1,0:T(8,128)(2,1)S(1)}, bf16[768,512]{1,0:T(8,128)(2,1)S(1)}, u32[]{:S(2)}, u32[]{:S(2)}) collective-permute-start(bf16[768,512]{1,0:T(8,128)(2,1)S(1)} %pad_maximum_fusion), channel_id=1, source_target_pairs={{0,1},{1,0},{2,3},{3,2},{4,5},{5,4},{6,7},{7,6},{8,9},{9,8},{10,11... | collective-permute-start | bytes 2359304 | tf_op jit(solution)/shard_map/ppermute | solution.py:54
  121.5 1.9 %slice.339 = f32[1440,512]{1,0:T(8,128)} slice(f32[1536,512]{1,0:T(8,128)S(1)} %maximum_convert_fusion), slice={[0:1440], [0:512]} | slice | bytes 5898240 | tf_op jit(solution)/shard_map/slice | solution.py:264
  (185 shorter events, 41.7 us)
Async XLA Ops:
  3.2 22.1 %collective-permute-start.1 = (bf16[4,32,448]{2,1,0:T(8,128)(2,1)S(1)}, bf16[4,32,448]{2,1,0:T(8,128)(2,1)S(1)}, u32[]{:S(2)}, u32[]{:S(2)}) collective-permute-start(bf16[4,32,448]{2,1,0:T(8,128)(2,1)S(1)} %concatenate.101), channel_id=1, source_target_pairs={{8,0},{16,8},{24,16},{9,1},{17,9},{25,17},{10,2},{18,10},{26,18},{... | collective-permute-start | bytes 344072 | tf_op jit(solution)/shard_map/ppermute | solution.py:112
  4.5 20.8 %collective-permute-start = (bf16[4,32,448]{2,1,0:T(8,128)(2,1)S(1)}, bf16[4,32,448]{2,1,0:T(8,128)(2,1)S(1)}, u32[]{:S(2)}, u32[]{:S(2)}) collective-permute-start(bf16[4,32,448]{2,1,0:T(8,128)(2,1)S(1)} %concatenate.101), channel_id=1, source_target_pairs={{0,8},{8,16},{16,24},{1,9},{9,17},{17,25},{2,10},{10,18},{18,26},{... | collective-permute-start | bytes 344072 | tf_op jit(solution)/shard_map/ppermute | solution.py:111
  10.0 8.2 %collective-permute-start.5 = (f32[3,32,128]{2,1,0:T(8,128)S(1)}, f32[3,32,128]{2,1,0:T(8,128)S(1)}, u32[]{:S(2)}, u32[]{:S(2)}) collective-permute-start(f32[3,32,128]{2,1,0:T(8,128)S(1)} %get-tuple-element.71), channel_id=1, source_target_pairs={{8,0},{16,8},{24,16},{9,1},{17,9},{25,17},{10,2},{18,10},{26,18},{... | collective-permute-start | bytes 147464 | tf_op jit(solution)/shard_map/ppermute | solution.py:112
  11.3 6.0 %collective-permute-start.4 = (f32[3,32,128]{2,1,0:T(8,128)S(1)}, f32[3,32,128]{2,1,0:T(8,128)S(1)}, u32[]{:S(2)}, u32[]{:S(2)}) collective-permute-start(f32[3,32,128]{2,1,0:T(8,128)S(1)} %get-tuple-element.72), channel_id=1, source_target_pairs={{0,8},{8,16},{16,24},{1,9},{9,17},{17,25},{2,10},{10,18},{18,26},{... | collective-permute-start | bytes 147464 | tf_op jit(solution)/shard_map/ppermute | solution.py:111
  18.2 12.8 %collective-permute-start.6 = (f32[10,3,128]{2,1,0:T(4,128)S(1)}, f32[10,3,128]{2,1,0:T(4,128)S(1)}, u32[]{:S(2)}, u32[]{:S(2)}) collective-permute-start(f32[10,3,128]{2,1,0:T(4,128)S(1)} %get-tuple-element.66), channel_id=1, source_target_pairs={{0,1},{1,2},{2,3},{3,4},{4,5},{5,6},{6,7},{8,9},{9,10},{10,11},{11... | collective-permute-start | bytes 46088 | tf_op jit(solution)/shard_map/ppermute | solution.py:111
  23.4 7.6 %collective-permute-start.7 = (f32[10,3,128]{2,1,0:T(4,128)S(1)}, f32[10,3,128]{2,1,0:T(4,128)S(1)}, u32[]{:S(2)}, u32[]{:S(2)}) collective-permute-start(f32[10,3,128]{2,1,0:T(4,128)S(1)} %get-tuple-element.67), channel_id=1, source_target_pairs={{1,0},{2,1},{3,2},{4,3},{5,4},{6,5},{7,6},{9,8},{10,9},{11,10},{12... | collective-permute-start | bytes 46088 | tf_op jit(solution)/shard_map/ppermute | solution.py:112
  25.4 6.3 %collective-permute-start.2 = (bf16[12,4,448]{2,1,0:T(4,128)(2,1)S(1)}, bf16[12,4,448]{2,1,0:T(4,128)(2,1)S(1)}, u32[]{:S(2)}, u32[]{:S(2)}) collective-permute-start(bf16[12,4,448]{2,1,0:T(4,128)(2,1)S(1)} %get-tuple-element.38), channel_id=1, source_target_pairs={{0,1},{1,2},{2,3},{3,4},{4,5},{5,6},{6,7},{8,9},{9,10},{10,11},{11... | collective-permute-start | bytes 129032 | tf_op jit(solution)/shard_map/ppermute | solution.py:111
  29.0 5.4 %collective-permute-start.3 = (bf16[12,4,448]{2,1,0:T(4,128)(2,1)S(1)}, bf16[12,4,448]{2,1,0:T(4,128)(2,1)S(1)}, u32[]{:S(2)}, u32[]{:S(2)}) collective-permute-start(bf16[12,4,448]{2,1,0:T(4,128)(2,1)S(1)} %get-tuple-element.39), channel_id=1, source_target_pairs={{1,0},{2,1},{3,2},{4,3},{5,4},{6,5},{7,6},{9,8},{10,9},{11,10},{12... | collective-permute-start | bytes 129032 | tf_op jit(solution)/shard_map/ppermute | solution.py:112
  53.9 3.8 %collective-permute-start.8 = (f32[768,512]{1,0:T(8,128)}, f32[768,512]{1,0:T(8,128)}, u32[]{:S(2)}, u32[]{:S(2)}) collective-permute-start(f32[768,512]{1,0:T(8,128)} %constant_dynamic-slice_fusion.5), channel_id=1, source_target_pairs={{0,1},{1,0},{2,3},{3,2},{4,5},{5,4},{6,7},{7,6},{8,9},{9,8},{10,11... | collective-permute-start | bytes 4718600 | tf_op jit(solution)/shard_map/ppermute | solution.py:44
  59.6 10.6 %collective-permute-start.9 = (f32[192,512]{1,0:T(8,128)S(1)}, f32[192,512]{1,0:T(8,128)S(1)}, u32[]{:S(2)}, u32[]{:S(2)}) collective-permute-start(f32[192,512]{1,0:T(8,128)S(1)} %constant_dynamic-slice_fusion.4), channel_id=1, source_target_pairs={{0,2},{1,3},{2,0},{3,1},{4,6},{5,7},{6,4},{7,5},{8,10},{9,11},{10,... | collective-permute-start | bytes 1179656 | tf_op jit(solution)/shard_map/ppermute | solution.py:44
  61.0 12.0 %collective-permute-start.11 = (f32[192,512]{1,0:T(8,128)S(1)}, f32[192,512]{1,0:T(8,128)S(1)}, u32[]{:S(2)}, u32[]{:S(2)}) collective-permute-start(f32[192,512]{1,0:T(8,128)S(1)} %constant_dynamic-slice_fusion.2), channel_id=1, source_target_pairs={{0,8},{8,0},{16,24},{24,16},{1,9},{9,1},{17,25},{25,17},{2,10},{10... | collective-permute-start | bytes 1179656 | tf_op jit(solution)/shard_map/ppermute | solution.py:44
  70.3 7.0 %collective-permute-start.10 = (f32[96,512]{1,0:T(8,128)S(1)}, f32[96,512]{1,0:T(8,128)S(1)}, u32[]{:S(2)}, u32[]{:S(2)}) collective-permute-start(f32[96,512]{1,0:T(8,128)S(1)} %constant_dynamic-slice_fusion.3), channel_id=1, source_target_pairs={{0,8},{8,0},{16,24},{24,16},{1,9},{9,1},{17,25},{25,17},{2,10},{10... | collective-permute-start | bytes 589832 | tf_op jit(solution)/shard_map/ppermute | solution.py:44
  73.1 5.2 %collective-permute-start.12 = (f32[96,512]{1,0:T(8,128)S(1)}, f32[96,512]{1,0:T(8,128)S(1)}, u32[]{:S(2)}, u32[]{:S(2)}) collective-permute-start(f32[96,512]{1,0:T(8,128)S(1)} %constant_dynamic-slice_fusion.1), channel_id=1, source_target_pairs={{0,2},{1,3},{2,0},{3,1},{4,6},{5,7},{6,4},{7,5},{8,10},{9,11},{10,... | collective-permute-start | bytes 589832 | tf_op jit(solution)/shard_map/ppermute | solution.py:44
  77.4 21.7 %copy-start.5 = (bf16[6,34,128]{2,1,0:T(8,128)(2,1)S(1)}, bf16[6,34,128]{2,1,0:T(8,128)(2,1)}, u32[]{:S(2)}) copy-start(bf16[6,34,128]{2,1,0:T(8,128)(2,1)} %copy-done.4) | copy-start | bytes 156676
  77.4 21.6 %copy-start.7 = (bf16[6,34,128]{2,1,0:T(8,128)(2,1)S(1)}, bf16[6,34,128]{2,1,0:T(8,128)(2,1)}, u32[]{:S(2)}) copy-start(bf16[6,34,128]{2,1,0:T(8,128)(2,1)} %copy-done.6) | copy-start | bytes 156676
  78.4 5.8 %collective-permute-start.13 = (f32[96,512]{1,0:T(8,128)S(1)}, f32[96,512]{1,0:T(8,128)S(1)}, u32[]{:S(2)}, u32[]{:S(2)}) collective-permute-start(f32[96,512]{1,0:T(8,128)S(1)} %fusion.51), channel_id=1, source_target_pairs={{0,16},{8,24},{16,0},{24,8},{1,17},{9,25},{17,1},{25,9},{2,18},{10... | collective-permute-start | bytes 589832 | tf_op jit(solution)/shard_map/ppermute | solution.py:44
  84.3 5.5 %collective-permute-start.14 = (f32[48,512]{1,0:T(8,128)S(1)}, f32[48,512]{1,0:T(8,128)S(1)}, u32[]{:S(2)}, u32[]{:S(2)}) collective-permute-start(f32[48,512]{1,0:T(8,128)S(1)} %constant_dynamic-slice_fusion), channel_id=1, source_target_pairs={{0,4},{1,5},{2,6},{3,7},{4,0},{5,1},{6,2},{7,3},{8,12},{9,13},{10,... | collective-permute-start | bytes 294920 | tf_op jit(solution)/shard_map/ppermute | solution.py:44
  89.8 4.6 %collective-permute-start.15 = (bf16[48,512]{1,0:T(8,128)(2,1)S(1)}, bf16[48,512]{1,0:T(8,128)(2,1)S(1)}, u32[]{:S(2)}, u32[]{:S(2)}) collective-permute-start(bf16[48,512]{1,0:T(8,128)(2,1)S(1)} %add_convert_fusion), channel_id=1, source_target_pairs={{0,4},{1,5},{2,6},{3,7},{4,0},{5,1},{6,2},{7,3},{8,12},{9,13},{10,... | collective-permute-start | bytes 147464 | tf_op jit(solution)/shard_map/ppermute | solution.py:54
  94.4 4.1 %collective-permute-start.16 = (bf16[96,512]{1,0:T(8,128)(2,1)S(1)}, bf16[96,512]{1,0:T(8,128)(2,1)S(1)}, u32[]{:S(2)}, u32[]{:S(2)}) collective-permute-start(bf16[96,512]{1,0:T(8,128)(2,1)S(1)} %pad_maximum_fusion.13), channel_id=1, source_target_pairs={{0,16},{8,24},{16,0},{24,8},{1,17},{9,25},{17,1},{25,9},{2,18},{10... | collective-permute-start | bytes 294920 | tf_op jit(solution)/shard_map/ppermute | solution.py:54
  98.5 3.5 %collective-permute-start.17 = (bf16[96,512]{1,0:T(8,128)(2,1)S(1)}, bf16[96,512]{1,0:T(8,128)(2,1)S(1)}, u32[]{:S(2)}, u32[]{:S(2)}) collective-permute-start(bf16[96,512]{1,0:T(8,128)(2,1)S(1)} %get-tuple-element.62), channel_id=1, source_target_pairs={{0,8},{8,0},{16,24},{24,16},{1,9},{9,1},{17,25},{25,17},{2,10},{10... | collective-permute-start | bytes 294920 | tf_op jit(solution)/shard_map/ppermute | solution.py:54
  99.4 3.5 %collective-permute-start.19 = (bf16[96,512]{1,0:T(8,128)(2,1)S(1)}, bf16[96,512]{1,0:T(8,128)(2,1)S(1)}, u32[]{:S(2)}, u32[]{:S(2)}) collective-permute-start(bf16[96,512]{1,0:T(8,128)(2,1)S(1)} %get-tuple-element.63), channel_id=1, source_target_pairs={{0,2},{1,3},{2,0},{3,1},{4,6},{5,7},{6,4},{7,5},{8,10},{9,11},{10,... | collective-permute-start | bytes 294920 | tf_op jit(solution)/shard_map/ppermute | solution.py:54
  102.1 4.6 %collective-permute-start.18 = (bf16[192,512]{1,0:T(8,128)(2,1)S(1)}, bf16[192,512]{1,0:T(8,128)(2,1)S(1)}, u32[]{:S(2)}, u32[]{:S(2)}) collective-permute-start(bf16[192,512]{1,0:T(8,128)(2,1)S(1)} %pad_maximum_fusion.5), channel_id=1, source_target_pairs={{0,2},{1,3},{2,0},{3,1},{4,6},{5,7},{6,4},{7,5},{8,10},{9,11},{10,... | collective-permute-start | bytes 589832 | tf_op jit(solution)/shard_map/ppermute | solution.py:54
  103.0 4.6 %collective-permute-start.20 = (bf16[192,512]{1,0:T(8,128)(2,1)S(1)}, bf16[192,512]{1,0:T(8,128)(2,1)S(1)}, u32[]{:S(2)}, u32[]{:S(2)}) collective-permute-start(bf16[192,512]{1,0:T(8,128)(2,1)S(1)} %pad_maximum_fusion.6), channel_id=1, source_target_pairs={{0,8},{8,0},{16,24},{24,16},{1,9},{9,1},{17,25},{25,17},{2,10},{10... | collective-permute-start | bytes 589832 | tf_op jit(solution)/shard_map/ppermute | solution.py:54
  107.8 12.5 %collective-permute-start.21 = (bf16[768,512]{1,0:T(8,128)(2,1)S(1)}, bf16[768,512]{1,0:T(8,128)(2,1)S(1)}, u32[]{:S(2)}, u32[]{:S(2)}) collective-permute-start(bf16[768,512]{1,0:T(8,128)(2,1)S(1)} %pad_maximum_fusion), channel_id=1, source_target_pairs={{0,1},{1,0},{2,3},{3,2},{4,5},{5,4},{6,7},{7,6},{8,9},{9,8},{10,11... | collective-permute-start | bytes 2359304 | tf_op jit(solution)/shard_map/ppermute | solution.py:54
  (27 other events, 128.7 us)

commit v5 on v3

--- a/solution.py
+++ b/solution.py
@@ -69,7 +69,18 @@
         order = rest[way:] + rest[:way]
         chunk, halved = halve(part[way * width : (way + 1) * width], order)
         pieces.append(double(chunk.astype(jnp.bfloat16), halved))
-    return double(jnp.concatenate(pieces, axis=0), first_halved).astype(jnp.float32)
+    piece = jnp.concatenate(pieces, axis=0)
+    if len(first_halved) == 1:
+        axis, bit = first_halved[0]
+        upper = (lax.axis_index(axis) >> bit) & 1
+        got = lax.ppermute(piece, axis, flip_pairs(axis, bit))
+        low = jnp.where(upper == 0, piece, got)
+        high = jnp.where(upper == 0, got, piece)
+        split = KIN - low.shape[0]
+        kernel_part = jnp.concatenate([low, high[:split]], axis=0).astype(jnp.float32)
+        return kernel_part, high[split].astype(jnp.float32)
+    summed = double(piece, first_halved).astype(jnp.float32)
+    return summed[:KIN], summed[KIN]
 
 def tap_columns(padded, rows_dev, cols_dev, reverse):
     pieces = []
@@ -246,14 +257,8 @@
         jnp.concatenate(grads_seen, axis=0),
         preferred_element_type=jnp.float32,
     )
-    summed_all = sum_everywhere(joined * norm_scale)
-    return (
-        hidden_final,
-        grad_hidden_start,
-        grad_cell_start,
-        summed_all[:KIN],
-        summed_all[KIN],
-    )
+    kernel_grad, bias_grad = sum_everywhere(joined * norm_scale)
+    return (hidden_final, grad_hidden_start, grad_cell_start, kernel_grad, bias_grad)
 
 
 def solution(mesh):

time: 122 us -> 119 us (0.975)
  local copies, waits for them, and re-layouts: 16.6 us -> 13.3 us
  other arithmetic: 12.5 us -> 15.4 us
  waiting for transfers between devices: 24 us -> 22.7 us
    ppermute x0 -> x1, starting transfers between devices: none -> 7.85 us  [sum_everywhere(): got = lax.ppermute(piece, axis, flip_pairs(axis, bit))]
    ppermute x13, starting transfers between devices: 19.5 us -> 14.7 us  [halve(): part = keep + lax.ppermute(send, axis, flip_pairs(axis, bit))]
    ppermute x13 -> x12, starting transfers between devices: 16.8 us -> 13.3 us  [double(): got = lax.ppermute(piece, axis, flip_pairs(axis, bit))]
    ppermute x13 -> x12, waiting for transfers between devices: 10 us -> 6.71 us  [double(): got = lax.ppermute(piece, axis, flip_pairs(axis, bit))]
    ppermute x13, waiting for transfers between devices: 10.3 us -> 13.1 us  [halve(): part = keep + lax.ppermute(send, axis, flip_pairs(axis, bit))]
    ppermute x4, starting transfers between devices: 18.3 us -> 15.6 us  [widen(): lax.ppermute(tail, axis, [(i, i + dist) for i in range(count - dist)])]
    ppermute x4, starting transfers between devices: 6.41 us -> 9.08 us  [widen(): lax.ppermute(head, axis, [(i + dist, i) for i in range(count - dist)])]
    convert_element_type x1 -> x2, other arithmetic: 0.43 us -> 2.6 us  [the longest x1 2.02 us: sum_everywhere(): jnp.concatenate([low, high[:split]], axis=0).astype(jnp.float32)]
  transfers between devices with their start and end apart: 34 -> 34, of which waited for: 15 -> 14; matrix products, arithmetic and copies ran while one was open for 6% -> 6% of each run, Pallas kernels for 0% -> 0%
where the time goes in v5:
time: 119 us; the launch traced here: 118 us
  starting transfers between devices  60.4 us (51%)
  waiting for transfers between devices  22.7 us (19%)
  other arithmetic  15.4 us (13%)
  local copies, waits for them, and re-layouts  13.3 us (11%)
  matrix products  4.84 us (4%)
  between operations  1.72 us (1%)
    ppermute x4, starting transfers between devices, widen(): lax.ppermute(tail, axis, [(i, i + dist) for i in range(count - dist)])  15.6 us
    ppermute x13, starting transfers between devices, halve(): part = keep + lax.ppermute(send, axis, flip_pairs(axis, bit))  14.7 us
    ppermute x12, starting transfers between devices, double(): got = lax.ppermute(piece, axis, flip_pairs(axis, bit))  13.3 us
    ppermute x13, waiting for transfers between devices, halve(): part = keep + lax.ppermute(send, axis, flip_pairs(axis, bit))  13.1 us
    ppermute x4, starting transfers between devices, widen(): lax.ppermute(head, axis, [(i + dist, i) for i in range(count - dist)])  9.08 us
    ppermute x1, starting transfers between devices, sum_everywhere(): got = lax.ppermute(piece, axis, flip_pairs(axis, bit))  7.85 us
    ppermute x12, waiting for transfers between devices, double(): got = lax.ppermute(piece, axis, flip_pairs(axis, bit))  6.71 us
    conv_general_dilated x4, matrix products, convolve(): lax.conv_general_dilated(field[None], weights, (1, 1), 'VALID', dimension...  4.25 us
  transfers between devices with their start and end apart: 34, of which 14 were waited for; matrix products, arithmetic and copies ran while one was open for 6% of the time, Pallas kernels for 0%

profile of v5, /device:TPU:1, one launch (start us, length us, event | category | flops | bytes accessed | tf_op | source)
XLA Modules:
  0.0 118.4 jit_solution(18029076530869158478)
XLA Ops:
  4.5 4.6 %collective-permute-start = (bf16[4,32,448]{2,1,0:T(8,128)(2,1)S(1)}, bf16[4,32,448]{2,1,0:T(8,128)(2,1)S(1)}, u32[]{:S(2)}, u32[]{:S(2)}) collective-permute-start(bf16[4,32,448]{2,1,0:T(8,128)(2,1)S(1)} %concatenate.116), channel_id=1, source_target_pairs={{0,8},{8,16},{16,24},{1,9},{9,17},{17,25},{2,10},{10,18},{18,26},{... | collective-permute-start | bytes 344072 | tf_op jit(solution)/shard_map/ppermute | solution.py:112
  10.0 4.2 %collective-permute-start.4 = (f32[3,32,128]{2,1,0:T(8,128)S(1)}, f32[3,32,128]{2,1,0:T(8,128)S(1)}, u32[]{:S(2)}, u32[]{:S(2)}) collective-permute-start(f32[3,32,128]{2,1,0:T(8,128)S(1)} %get-tuple-element.73), channel_id=1, source_target_pairs={{0,8},{8,16},{16,24},{1,9},{9,17},{17,25},{2,10},{10,18},{18,26},{... | collective-permute-start | bytes 147464 | tf_op jit(solution)/shard_map/ppermute | solution.py:112
  16.6 2.5 %collective-permute-done.5 = f32[3,32,128]{2,1,0:T(8,128)S(1)} collective-permute-done((f32[3,32,128]{2,1,0:T(8,128)S(1)}, f32[3,32,128]{2,1,0:T(8,128)S(1)}, u32[]{:S(2)}, u32[]{:S(2)}) %collective-permute-start.5) | collective-permute-done | bytes 49184 | tf_op jit(solution)/shard_map/ppermute | solution.py:113
  19.1 4.6 %collective-permute-start.7 = (f32[10,3,128]{2,1,0:T(4,128)S(1)}, f32[10,3,128]{2,1,0:T(4,128)S(1)}, u32[]{:S(2)}, u32[]{:S(2)}) collective-permute-start(f32[10,3,128]{2,1,0:T(4,128)S(1)} %get-tuple-element.58), channel_id=1, source_target_pairs={{1,0},{2,1},{3,2},{4,3},{5,4},{6,5},{7,6},{9,8},{10,9},{11,10},{12... | collective-permute-start | bytes 46088 | tf_op jit(solution)/shard_map/ppermute | solution.py:113
  23.7 3.1 %collective-permute-start.6 = (f32[10,3,128]{2,1,0:T(4,128)S(1)}, f32[10,3,128]{2,1,0:T(4,128)S(1)}, u32[]{:S(2)}, u32[]{:S(2)}) collective-permute-start(f32[10,3,128]{2,1,0:T(4,128)S(1)} %get-tuple-element.57), channel_id=1, source_target_pairs={{0,1},{1,2},{2,3},{3,4},{4,5},{5,6},{6,7},{8,9},{9,10},{10,11},{11... | collective-permute-start | bytes 46088 | tf_op jit(solution)/shard_map/ppermute | solution.py:112
  26.9 1.9 %collective-permute-start.3 = (bf16[12,4,448]{2,1,0:T(4,128)(2,1)S(1)}, bf16[12,4,448]{2,1,0:T(4,128)(2,1)S(1)}, u32[]{:S(2)}, u32[]{:S(2)}) collective-permute-start(bf16[12,4,448]{2,1,0:T(4,128)(2,1)S(1)} %get-tuple-element.36), channel_id=1, source_target_pairs={{1,0},{2,1},{3,2},{4,3},{5,4},{6,5},{7,6},{9,8},{10,9},{11,10},{12... | collective-permute-start | bytes 129032 | tf_op jit(solution)/shard_map/ppermute | solution.py:113
  28.8 3.6 %collective-permute-start.2 = (bf16[12,4,448]{2,1,0:T(4,128)(2,1)S(1)}, bf16[12,4,448]{2,1,0:T(4,128)(2,1)S(1)}, u32[]{:S(2)}, u32[]{:S(2)}) collective-permute-start(bf16[12,4,448]{2,1,0:T(4,128)(2,1)S(1)} %get-tuple-element.35), channel_id=1, source_target_pairs={{0,1},{1,2},{2,3},{3,4},{4,5},{5,6},{6,7},{8,9},{9,10},{10,11},{11... | collective-permute-start | bytes 129032 | tf_op jit(solution)/shard_map/ppermute | solution.py:112
  40.1 2.1 %convolution_select_fusion.1 = f32[8,8,5,512]{3,1,2,0:T(8,128)S(1)} fusion(bf16[3,3,160,512]{3,2,1,0:T(8,128)(2,1)} %bitcast.86, pred[8,5]{0,1:T(8,128)(4,1)S(1)} %copy-done.32, bf16[10,1,7,2,160]{4,2,3,0,1:T(8,128)(2,1)S(1)} %slice.281, bf16[10,1,8,5,160]{4,2,3,0,1:T(8,128)(2,1)S(1)} %copy.16), kind=kOutput, calls=%fused_computation.4 | convolution fusion | flops 472560640 | bytes 2302760 | tf_op jit(solution)/shard_map/conv_general_dilated | solution.py:145
  53.1 3.6 %collective-permute-done.8 = f32[768,512]{1,0:T(8,128)} collective-permute-done((f32[768,512]{1,0:T(8,128)}, f32[768,512]{1,0:T(8,128)}, u32[]{:S(2)}, u32[]{:S(2)}) %collective-permute-start.8) | collective-permute-done | bytes 1572896 | tf_op jit(solution)/shard_map/ppermute | solution.py:45
  56.7 1.8 %dynamic-slice_add_fusion = f32[768,512]{1,0:T(8,128)S(1)} fusion(f32[768,512]{1,0:T(8,128)} %collective-permute-done.8, f32[1536,512]{1,0:T(8,128)S(1)} %convolution_multiply_fusion, s32[]{:T(128)S(6)} %select_n.252), kind=kLoop, calls=%fused_computation.1 | loop fusion | flops 393216 | bytes 4718596 | tf_op jit(solution)/shard_map/add | solution.py:45
  58.7 2.1 %collective-permute-start.9 = (f32[128,512]{1,0:T(8,128)S(1)}, f32[128,512]{1,0:T(8,128)S(1)}, u32[]{:S(2)}, u32[]{:S(2)}) collective-permute-start(f32[128,512]{1,0:T(8,128)S(1)} %constant_dynamic-slice_fusion.11), channel_id=1, source_target_pairs={{0,2},{1,3},{2,0},{3,1},{4,6},{5,7},{6,4},{7,5},{8,10},{9,11},{10,... | collective-permute-start | bytes 786440 | tf_op jit(solution)/shard_map/ppermute | solution.py:45
  62.6 4.6 %collective-permute-done.9 = f32[128,512]{1,0:T(8,128)S(1)} collective-permute-done((f32[128,512]{1,0:T(8,128)S(1)}, f32[128,512]{1,0:T(8,128)S(1)}, u32[]{:S(2)}, u32[]{:S(2)}) %collective-permute-start.9) | collective-permute-done | bytes 262176 | tf_op jit(solution)/shard_map/ppermute | solution.py:45
  69.6 2.4 %collective-permute-start.26 = (f32[64,512]{1,0:T(8,128)S(1)}, f32[64,512]{1,0:T(8,128)S(1)}, u32[]{:S(2)}, u32[]{:S(2)}) collective-permute-start(f32[64,512]{1,0:T(8,128)S(1)} %constant_dynamic-slice_fusion.2), channel_id=1, source_target_pairs={{0,4},{1,5},{2,6},{3,7},{4,0},{5,1},{6,2},{7,3},{8,12},{9,13},{10,... | collective-permute-start | bytes 393224 | tf_op jit(solution)/shard_map/ppermute | solution.py:45
  72.8 2.3 %collective-permute-start.19 = (f32[32,512]{1,0:T(8,128)S(1)}, f32[32,512]{1,0:T(8,128)S(1)}, u32[]{:S(2)}, u32[]{:S(2)}) collective-permute-start(f32[32,512]{1,0:T(8,128)S(1)} %constant_dynamic-slice_fusion.5), channel_id=1, source_target_pairs={{0,4},{1,5},{2,6},{3,7},{4,0},{5,1},{6,2},{7,3},{8,12},{9,13},{10,... | collective-permute-start | bytes 196616 | tf_op jit(solution)/shard_map/ppermute | solution.py:45
  75.2 3.4 %collective-permute-done.26 = f32[64,512]{1,0:T(8,128)S(1)} collective-permute-done((f32[64,512]{1,0:T(8,128)S(1)}, f32[64,512]{1,0:T(8,128)S(1)}, u32[]{:S(2)}, u32[]{:S(2)}) %collective-permute-start.26) | collective-permute-done | bytes 131104 | tf_op jit(solution)/shard_map/ppermute | solution.py:45
  79.2 3.2 %collective-permute-start.12 = (f32[16,512]{1,0:T(8,128)S(1)}, f32[16,512]{1,0:T(8,128)S(1)}, u32[]{:S(2)}, u32[]{:S(2)}) collective-permute-start(f32[16,512]{1,0:T(8,128)S(1)} %constant_dynamic-slice_fusion.8), channel_id=1, source_target_pairs={{0,4},{1,5},{2,6},{3,7},{4,0},{5,1},{6,2},{7,3},{8,12},{9,13},{10,... | collective-permute-start | bytes 98312 | tf_op jit(solution)/shard_map/ppermute | solution.py:45
  83.7 2.4 %collective-permute-start.13 = (bf16[16,512]{1,0:T(8,128)(2,1)S(1)}, bf16[16,512]{1,0:T(8,128)(2,1)S(1)}, u32[]{:S(2)}, u32[]{:S(2)}) collective-permute-start(bf16[16,512]{1,0:T(8,128)(2,1)S(1)} %add_convert_fusion.2), channel_id=1, source_target_pairs={{0,4},{1,5},{2,6},{3,7},{4,0},{5,1},{6,2},{7,3},{8,12},{9,13},{10,... | collective-permute-start | bytes 49160 | tf_op jit(solution)/shard_map/ppermute | solution.py:55
  88.8 2.0 %collective-permute-start.22 = (bf16[32,512]{1,0:T(8,128)(2,1)S(1)}, bf16[32,512]{1,0:T(8,128)(2,1)S(1)}, u32[]{:S(2)}, u32[]{:S(2)}) collective-permute-start(bf16[32,512]{1,0:T(8,128)(2,1)S(1)} %pad_maximum_fusion.22), channel_id=1, source_target_pairs={{0,4},{1,5},{2,6},{3,7},{4,0},{5,1},{6,2},{7,3},{8,12},{9,13},{10,... | collective-permute-start | bytes 98312 | tf_op jit(solution)/shard_map/ppermute | solution.py:55
  92.6 1.5 %collective-permute-start.23 = (bf16[64,512]{1,0:T(8,128)(2,1)S(1)}, bf16[64,512]{1,0:T(8,128)(2,1)S(1)}, u32[]{:S(2)}, u32[]{:S(2)}) collective-permute-start(bf16[64,512]{1,0:T(8,128)(2,1)S(1)} %pad_maximum_fusion.15), channel_id=1, source_target_pairs={{0,16},{8,24},{16,0},{24,8},{1,17},{9,25},{17,1},{25,9},{2,18},{10... | collective-permute-start | bytes 196616 | tf_op jit(solution)/shard_map/ppermute | solution.py:55
  97.0 2.2 %collective-permute-done.31 = bf16[64,512]{1,0:T(8,128)(2,1)S(1)} collective-permute-done((bf16[64,512]{1,0:T(8,128)(2,1)S(1)}, bf16[64,512]{1,0:T(8,128)(2,1)S(1)}, u32[]{:S(2)}, u32[]{:S(2)}) %collective-permute-start.31) | collective-permute-done | bytes 65568 | tf_op jit(solution)/shard_map/ppermute | solution.py:55
  101.1 3.1 %collective-permute-done.32 = bf16[128,512]{1,0:T(8,128)(2,1)S(1)} collective-permute-done((bf16[128,512]{1,0:T(8,128)(2,1)S(1)}, bf16[128,512]{1,0:T(8,128)(2,1)S(1)}, u32[]{:S(2)}, u32[]{:S(2)}) %collective-permute-start.32) | collective-permute-done | bytes 131104 | tf_op jit(solution)/shard_map/ppermute | solution.py:55
  104.3 7.8 %collective-permute-start.33 = (bf16[768,512]{1,0:T(8,128)(2,1)S(1)}, bf16[768,512]{1,0:T(8,128)(2,1)S(1)}, u32[]{:S(2)}, u32[]{:S(2)}) collective-permute-start(bf16[768,512]{1,0:T(8,128)(2,1)S(1)} %select_dynamic-update-slice_fusion), channel_id=1, source_target_pairs={{0,1},{1,0},{2,3},{3,2},{4,5},{5,4},{6,7},{7,6},{8,9},{9,8},{10,11... | collective-permute-start | bytes 2359304 | tf_op jit(solution)/shard_map/ppermute | solution.py:76
  113.4 1.6 %fusion.91 = bf16[4,32,128]{2,1,0:T(8,128)(2,1)} fusion(f32[8,36,128]{2,1,0:T(8,128)} %copy-done.2, f32[8,36,128]{2,1,0:T(8,128)} %get-tuple-element.34), kind=kLoop, calls=%fused_computation.192 | loop fusion | flops 32768 | bytes 163840 | tf_op jit(solution)/shard_map/convert_element_type | solution.py:159
  116.4 2.0 %maximum_convert_fusion = f32[1440,512]{1,0:T(8,128)} fusion(bf16[672,512]{1,0:T(8,128)(2,1)S(1)} %slice.344, bf16[768,512]{1,0:T(8,128)(2,1)S(1)} %get-tuple-element.19), kind=kLoop, calls=%fused_computation.2 | loop fusion | flops 2949120 | bytes 4423680 | tf_op jit(solution)/shard_map/convert_element_type | solution.py:80
  (245 shorter events, 44.0 us)
Async XLA Ops:
  3.2 23.6 %collective-permute-start.1 = (bf16[4,32,448]{2,1,0:T(8,128)(2,1)S(1)}, bf16[4,32,448]{2,1,0:T(8,128)(2,1)S(1)}, u32[]{:S(2)}, u32[]{:S(2)}) collective-permute-start(bf16[4,32,448]{2,1,0:T(8,128)(2,1)S(1)} %concatenate.116), channel_id=1, source_target_pairs={{8,0},{16,8},{24,16},{9,1},{17,9},{25,17},{10,2},{18,10},{26,18},{... | collective-permute-start | bytes 344072 | tf_op jit(solution)/shard_map/ppermute | solution.py:113
  4.5 22.3 %collective-permute-start = (bf16[4,32,448]{2,1,0:T(8,128)(2,1)S(1)}, bf16[4,32,448]{2,1,0:T(8,128)(2,1)S(1)}, u32[]{:S(2)}, u32[]{:S(2)}) collective-permute-start(bf16[4,32,448]{2,1,0:T(8,128)(2,1)S(1)} %concatenate.116), channel_id=1, source_target_pairs={{0,8},{8,16},{16,24},{1,9},{9,17},{17,25},{2,10},{10,18},{18,26},{... | collective-permute-start | bytes 344072 | tf_op jit(solution)/shard_map/ppermute | solution.py:112
  10.0 5.8 %collective-permute-start.4 = (f32[3,32,128]{2,1,0:T(8,128)S(1)}, f32[3,32,128]{2,1,0:T(8,128)S(1)}, u32[]{:S(2)}, u32[]{:S(2)}) collective-permute-start(f32[3,32,128]{2,1,0:T(8,128)S(1)} %get-tuple-element.73), channel_id=1, source_target_pairs={{0,8},{8,16},{16,24},{1,9},{9,17},{17,25},{2,10},{10,18},{18,26},{... | collective-permute-start | bytes 147464 | tf_op jit(solution)/shard_map/ppermute | solution.py:112
  14.2 4.8 %collective-permute-start.5 = (f32[3,32,128]{2,1,0:T(8,128)S(1)}, f32[3,32,128]{2,1,0:T(8,128)S(1)}, u32[]{:S(2)}, u32[]{:S(2)}) collective-permute-start(f32[3,32,128]{2,1,0:T(8,128)S(1)} %get-tuple-element.72), channel_id=1, source_target_pairs={{8,0},{16,8},{24,16},{9,1},{17,9},{25,17},{10,2},{18,10},{26,18},{... | collective-permute-start | bytes 147464 | tf_op jit(solution)/shard_map/ppermute | solution.py:113
  19.1 13.3 %collective-permute-start.7 = (f32[10,3,128]{2,1,0:T(4,128)S(1)}, f32[10,3,128]{2,1,0:T(4,128)S(1)}, u32[]{:S(2)}, u32[]{:S(2)}) collective-permute-start(f32[10,3,128]{2,1,0:T(4,128)S(1)} %get-tuple-element.58), channel_id=1, source_target_pairs={{1,0},{2,1},{3,2},{4,3},{5,4},{6,5},{7,6},{9,8},{10,9},{11,10},{12... | collective-permute-start | bytes 46088 | tf_op jit(solution)/shard_map/ppermute | solution.py:113
  23.7 8.8 %collective-permute-start.6 = (f32[10,3,128]{2,1,0:T(4,128)S(1)}, f32[10,3,128]{2,1,0:T(4,128)S(1)}, u32[]{:S(2)}, u32[]{:S(2)}) collective-permute-start(f32[10,3,128]{2,1,0:T(4,128)S(1)} %get-tuple-element.57), channel_id=1, source_target_pairs={{0,1},{1,2},{2,3},{3,4},{4,5},{5,6},{6,7},{8,9},{9,10},{10,11},{11... | collective-permute-start | bytes 46088 | tf_op jit(solution)/shard_map/ppermute | solution.py:112
  26.9 6.3 %collective-permute-start.3 = (bf16[12,4,448]{2,1,0:T(4,128)(2,1)S(1)}, bf16[12,4,448]{2,1,0:T(4,128)(2,1)S(1)}, u32[]{:S(2)}, u32[]{:S(2)}) collective-permute-start(bf16[12,4,448]{2,1,0:T(4,128)(2,1)S(1)} %get-tuple-element.36), channel_id=1, source_target_pairs={{1,0},{2,1},{3,2},{4,3},{5,4},{6,5},{7,6},{9,8},{10,9},{11,10},{12... | collective-permute-start | bytes 129032 | tf_op jit(solution)/shard_map/ppermute | solution.py:113
  28.8 4.8 %collective-permute-start.2 = (bf16[12,4,448]{2,1,0:T(4,128)(2,1)S(1)}, bf16[12,4,448]{2,1,0:T(4,128)(2,1)S(1)}, u32[]{:S(2)}, u32[]{:S(2)}) collective-permute-start(bf16[12,4,448]{2,1,0:T(4,128)(2,1)S(1)} %get-tuple-element.35), channel_id=1, source_target_pairs={{0,1},{1,2},{2,3},{3,4},{4,5},{5,6},{6,7},{8,9},{9,10},{10,11},{11... | collective-permute-start | bytes 129032 | tf_op jit(solution)/shard_map/ppermute | solution.py:112
  58.7 8.5 %collective-permute-start.9 = (f32[128,512]{1,0:T(8,128)S(1)}, f32[128,512]{1,0:T(8,128)S(1)}, u32[]{:S(2)}, u32[]{:S(2)}) collective-permute-start(f32[128,512]{1,0:T(8,128)S(1)} %constant_dynamic-slice_fusion.11), channel_id=1, source_target_pairs={{0,2},{1,3},{2,0},{3,1},{4,6},{5,7},{6,4},{7,5},{8,10},{9,11},{10,... | collective-permute-start | bytes 786440 | tf_op jit(solution)/shard_map/ppermute | solution.py:45
  61.2 7.3 %collective-permute-start.17 = (f32[128,512]{1,0:T(8,128)S(1)}, f32[128,512]{1,0:T(8,128)S(1)}, u32[]{:S(2)}, u32[]{:S(2)}) collective-permute-start(f32[128,512]{1,0:T(8,128)S(1)} %constant_dynamic-slice_fusion.7), channel_id=1, source_target_pairs={{0,8},{8,0},{16,24},{24,16},{1,9},{9,1},{17,25},{25,17},{2,10},{10... | collective-permute-start | bytes 786440 | tf_op jit(solution)/shard_map/ppermute | solution.py:45
  62.5 6.9 %collective-permute-start.25 = (f32[128,512]{1,0:T(8,128)S(1)}, f32[128,512]{1,0:T(8,128)S(1)}, u32[]{:S(2)}, u32[]{:S(2)}) collective-permute-start(f32[128,512]{1,0:T(8,128)S(1)} %constant_dynamic-slice_fusion.3), channel_id=1, source_target_pairs={{0,16},{8,24},{16,0},{24,8},{1,17},{9,25},{17,1},{25,9},{2,18},{10... | collective-permute-start | bytes 786440 | tf_op jit(solution)/shard_map/ppermute | solution.py:45
  67.3 4.7 %collective-permute-start.10 = (f32[64,512]{1,0:T(8,128)S(1)}, f32[64,512]{1,0:T(8,128)S(1)}, u32[]{:S(2)}, u32[]{:S(2)}) collective-permute-start(f32[64,512]{1,0:T(8,128)S(1)} %constant_dynamic-slice_fusion.10), channel_id=1, source_target_pairs={{0,8},{8,0},{16,24},{24,16},{1,9},{9,1},{17,25},{25,17},{2,10},{10... | collective-permute-start | bytes 393224 | tf_op jit(solution)/shard_map/ppermute | solution.py:45
  68.6 4.2 %collective-permute-start.18 = (f32[64,512]{1,0:T(8,128)S(1)}, f32[64,512]{1,0:T(8,128)S(1)}, u32[]{:S(2)}, u32[]{:S(2)}) collective-permute-start(f32[64,512]{1,0:T(8,128)S(1)} %constant_dynamic-slice_fusion.6), channel_id=1, source_target_pairs={{0,16},{8,24},{16,0},{24,8},{1,17},{9,25},{17,1},{25,9},{2,18},{10... | collective-permute-start | bytes 393224 | tf_op jit(solution)/shard_map/ppermute | solution.py:45
  69.6 9.0 %collective-permute-start.26 = (f32[64,512]{1,0:T(8,128)S(1)}, f32[64,512]{1,0:T(8,128)S(1)}, u32[]{:S(2)}, u32[]{:S(2)}) collective-permute-start(f32[64,512]{1,0:T(8,128)S(1)} %constant_dynamic-slice_fusion.2), channel_id=1, source_target_pairs={{0,4},{1,5},{2,6},{3,7},{4,0},{5,1},{6,2},{7,3},{8,12},{9,13},{10,... | collective-permute-start | bytes 393224 | tf_op jit(solution)/shard_map/ppermute | solution.py:45
  72.0 7.2 %collective-permute-start.11 = (f32[32,512]{1,0:T(8,128)S(1)}, f32[32,512]{1,0:T(8,128)S(1)}, u32[]{:S(2)}, u32[]{:S(2)}) collective-permute-start(f32[32,512]{1,0:T(8,128)S(1)} %constant_dynamic-slice_fusion.9), channel_id=1, source_target_pairs={{0,16},{8,24},{16,0},{24,8},{1,17},{9,25},{17,1},{25,9},{2,18},{10... | collective-permute-start | bytes 196616 | tf_op jit(solution)/shard_map/ppermute | solution.py:45
  72.8 9.5 %collective-permute-start.19 = (f32[32,512]{1,0:T(8,128)S(1)}, f32[32,512]{1,0:T(8,128)S(1)}, u32[]{:S(2)}, u32[]{:S(2)}) collective-permute-start(f32[32,512]{1,0:T(8,128)S(1)} %constant_dynamic-slice_fusion.5), channel_id=1, source_target_pairs={{0,4},{1,5},{2,6},{3,7},{4,0},{5,1},{6,2},{7,3},{8,12},{9,13},{10,... | collective-permute-start | bytes 196616 | tf_op jit(solution)/shard_map/ppermute | solution.py:45
  79.2 4.5 %collective-permute-start.12 = (f32[16,512]{1,0:T(8,128)S(1)}, f32[16,512]{1,0:T(8,128)S(1)}, u32[]{:S(2)}, u32[]{:S(2)}) collective-permute-start(f32[16,512]{1,0:T(8,128)S(1)} %constant_dynamic-slice_fusion.8), channel_id=1, source_target_pairs={{0,4},{1,5},{2,6},{3,7},{4,0},{5,1},{6,2},{7,3},{8,12},{9,13},{10,... | collective-permute-start | bytes 98312 | tf_op jit(solution)/shard_map/ppermute | solution.py:45
  86.2 4.5 %collective-permute-start.29 = (bf16[16,512]{1,0:T(8,128)(2,1)S(1)}, bf16[16,512]{1,0:T(8,128)(2,1)S(1)}, u32[]{:S(2)}, u32[]{:S(2)}) collective-permute-start(bf16[16,512]{1,0:T(8,128)(2,1)S(1)} %add_convert_fusion), channel_id=1, source_target_pairs={{0,8},{8,0},{16,24},{24,16},{1,9},{9,1},{17,25},{25,17},{2,10},{10... | collective-permute-start | bytes 49160 | tf_op jit(solution)/shard_map/ppermute | solution.py:55
  91.2 4.2 %collective-permute-start.15 = (bf16[64,512]{1,0:T(8,128)(2,1)S(1)}, bf16[64,512]{1,0:T(8,128)(2,1)S(1)}, u32[]{:S(2)}, u32[]{:S(2)}) collective-permute-start(bf16[64,512]{1,0:T(8,128)(2,1)S(1)} %pad_maximum_fusion.14), channel_id=1, source_target_pairs={{0,8},{8,0},{16,24},{24,16},{1,9},{9,1},{17,25},{25,17},{2,10},{10... | collective-permute-start | bytes 196616 | tf_op jit(solution)/shard_map/ppermute | solution.py:55
  94.1 5.2 %collective-permute-start.31 = (bf16[64,512]{1,0:T(8,128)(2,1)S(1)}, bf16[64,512]{1,0:T(8,128)(2,1)S(1)}, u32[]{:S(2)}, u32[]{:S(2)}) collective-permute-start(bf16[64,512]{1,0:T(8,128)(2,1)S(1)} %pad_maximum_fusion.16), channel_id=1, source_target_pairs={{0,4},{1,5},{2,6},{3,7},{4,0},{5,1},{6,2},{7,3},{8,12},{9,13},{10,... | collective-permute-start | bytes 196616 | tf_op jit(solution)/shard_map/ppermute | solution.py:55
  95.5 5.4 %collective-permute-start.16 = (bf16[128,512]{1,0:T(8,128)(2,1)S(1)}, bf16[128,512]{1,0:T(8,128)(2,1)S(1)}, u32[]{:S(2)}, u32[]{:S(2)}) collective-permute-start(bf16[128,512]{1,0:T(8,128)(2,1)S(1)} %pad_maximum_fusion.10), channel_id=1, source_target_pairs={{0,2},{1,3},{2,0},{3,1},{4,6},{5,7},{6,4},{7,5},{8,10},{9,11},{10,... | collective-permute-start | bytes 393224 | tf_op jit(solution)/shard_map/ppermute | solution.py:55
  96.0 5.0 %collective-permute-start.24 = (bf16[128,512]{1,0:T(8,128)(2,1)S(1)}, bf16[128,512]{1,0:T(8,128)(2,1)S(1)}, u32[]{:S(2)}, u32[]{:S(2)}) collective-permute-start(bf16[128,512]{1,0:T(8,128)(2,1)S(1)} %pad_maximum_fusion.11), channel_id=1, source_target_pairs={{0,8},{8,0},{16,24},{24,16},{1,9},{9,1},{17,25},{25,17},{2,10},{10... | collective-permute-start | bytes 393224 | tf_op jit(solution)/shard_map/ppermute | solution.py:55
  99.3 4.9 %collective-permute-start.32 = (bf16[128,512]{1,0:T(8,128)(2,1)S(1)}, bf16[128,512]{1,0:T(8,128)(2,1)S(1)}, u32[]{:S(2)}, u32[]{:S(2)}) collective-permute-start(bf16[128,512]{1,0:T(8,128)(2,1)S(1)} %pad_maximum_fusion.12), channel_id=1, source_target_pairs={{0,16},{8,24},{16,0},{24,8},{1,17},{9,25},{17,1},{25,9},{2,18},{10... | collective-permute-start | bytes 393224 | tf_op jit(solution)/shard_map/ppermute | solution.py:55
  104.3 11.3 %collective-permute-start.33 = (bf16[768,512]{1,0:T(8,128)(2,1)S(1)}, bf16[768,512]{1,0:T(8,128)(2,1)S(1)}, u32[]{:S(2)}, u32[]{:S(2)}) collective-permute-start(bf16[768,512]{1,0:T(8,128)(2,1)S(1)} %select_dynamic-update-slice_fusion), channel_id=1, source_target_pairs={{0,1},{1,0},{2,3},{3,2},{4,5},{5,4},{6,7},{7,6},{8,9},{9,8},{10,11... | collective-permute-start | bytes 2359304 | tf_op jit(solution)/shard_map/ppermute | solution.py:76
  (44 other events, 151.4 us)

commit v6 on v5

--- a/solution.py
+++ b/solution.py
@@ -59,9 +59,7 @@
     return piece
 
 
-def sum_everywhere(total):
-    first, rest = summing_levels()
-    part, first_halved = halve(total, first)
+def sum_everywhere(part, first_halved, rest):
     ways = min(SUM_WAYS, max(len(rest), 1))
     width = part.shape[0] // ways
     pieces = []
@@ -233,9 +231,20 @@
     grad_hidden_start = convolve(masked_one, flipped)
 
     spare = SUM_ROWS - KIN - 1
+    near = [inner(stacked_two, reach - 1, 1), inner(stacked_one, reach, 1)]
+    grads_seen = [
+        inner(grad_gates_two, reach - 2, 0).reshape(cells, GATES),
+        inner(grad_gates_one, reach - 3, 0).reshape(cells, GATES),
+    ]
+    first, rest = summing_levels()
+    axis, bit = first[0]
+    pairs = flip_pairs(axis, bit)
+    upper = (lax.axis_index(axis) >> bit) & 1
+    near = near + [lax.ppermute(s, axis, pairs) for s in near]
+    grads_seen = grads_seen + [lax.ppermute(g, axis, pairs) for g in grads_seen]
     lifted = []
-    for stacked, width in ((stacked_two, reach - 1), (stacked_one, reach)):
-        patches = tap_columns(inner(stacked, width, 1), rows_dev, cols_dev, False)
+    for stacked in near:
+        patches = tap_columns(stacked, rows_dev, cols_dev, False)
         lifted.append(
             jnp.concatenate(
                 [
@@ -246,18 +255,14 @@
                 axis=1,
             )
         )
-    grads_seen = [
-        inner(grad_gates_two, reach - 2, 0).reshape(cells, GATES),
-        inner(grad_gates_one, reach - 3, 0).reshape(cells, GATES),
-    ]
+    half = SUM_ROWS // 2
+    lifted = lax.dynamic_slice_in_dim(jnp.concatenate(lifted, axis=0), upper * half, half, 1)
     total_cells = STEPS * rows_dev * lax.axis_size("rows") * cols_dev * lax.axis_size("cols")
     norm_scale = 1.0 / math.sqrt(total_cells)
     joined = jnp.dot(
-        jnp.concatenate(lifted, axis=0).T,
-        jnp.concatenate(grads_seen, axis=0),
-        preferred_element_type=jnp.float32,
-    )
-    kernel_grad, bias_grad = sum_everywhere(joined * norm_scale)
+        lifted.T, jnp.concatenate(grads_seen, axis=0), preferred_element_type=jnp.float32
+    )
+    kernel_grad, bias_grad = sum_everywhere(joined * norm_scale, first, rest)
     return (hidden_final, grad_hidden_start, grad_cell_start, kernel_grad, bias_grad)
 
 

time: 119 us -> 118 us (level)
  waiting for transfers between devices: 22.7 us -> 20.6 us
  other arithmetic: 15.4 us -> 14 us
    ppermute x13 -> x12, waiting for transfers between devices: 13.1 us -> 6.31 us  [halve(): part = keep + lax.ppermute(send, axis, flip_pairs(axis, bit))]
    ppermute x13 -> x12, starting transfers between devices: 14.7 us -> 19.4 us  [halve(): part = keep + lax.ppermute(send, axis, flip_pairs(axis, bit))]
    ppermute x12, starting transfers between devices: 13.3 us -> 9.47 us  [double(): got = lax.ppermute(piece, axis, flip_pairs(axis, bit))]
    ppermute x12, waiting for transfers between devices: 6.71 us -> 10.2 us  [double(): got = lax.ppermute(piece, axis, flip_pairs(axis, bit))]
    ppermute x4, starting transfers between devices: 15.6 us -> 18.3 us  [widen(): lax.ppermute(tail, axis, [(i, i + dist) for i in range(count - dist)])]
    ppermute x4, starting transfers between devices: 9.08 us -> 6.41 us  [widen(): lax.ppermute(head, axis, [(i + dist, i) for i in range(count - dist)])]
    add x10 -> x9, other arithmetic: 1.96 us -> 0.2 us  [halve(): part = keep + lax.ppermute(send, axis, flip_pairs(axis, bit))]
    dynamic_slice x13 -> x12, local copies, waits for them, and re-layouts: 1.49 us -> 0.22 us  [halve(): send = lax.dynamic_slice_in_dim(part, (1 - upper) * half, half, 0)]
  transfers between devices with their start and end apart: 34 -> 37, of which waited for: 14 -> 16; matrix products, arithmetic and copies ran while one was open for 6% -> 15% of each run, Pallas kernels for 0% -> 0%
where the time goes in v6:
time: 118 us
  starting transfers between devices  61.5 us (52%)
  waiting for transfers between devices  20.6 us (17%)
  other arithmetic  14 us (12%)
  local copies, waits for them, and re-layouts  13.9 us (12%)
  matrix products  5.75 us (5%)
  between operations  1.79 us (2%)
    ppermute x12, starting transfers between devices, halve(): part = keep + lax.ppermute(send, axis, flip_pairs(axis, bit))  19.4 us
    ppermute x4, starting transfers between devices, widen(): lax.ppermute(tail, axis, [(i, i + dist) for i in range(count - dist)])  18.3 us
    ppermute x12, waiting for transfers between devices, double(): got = lax.ppermute(piece, axis, flip_pairs(axis, bit))  10.2 us
    ppermute x12, starting transfers between devices, double(): got = lax.ppermute(piece, axis, flip_pairs(axis, bit))  9.47 us
    ppermute x1, starting transfers between devices, sum_everywhere(): got = lax.ppermute(piece, axis, flip_pairs(axis, bit))  7.14 us
    ppermute x4, starting transfers between devices, widen(): lax.ppermute(head, axis, [(i + dist, i) for i in range(count - dist)])  6.41 us
    ppermute x12, waiting for transfers between devices, halve(): part = keep + lax.ppermute(send, axis, flip_pairs(axis, bit))  6.31 us
    conv_general_dilated x4, matrix products, convolve(): lax.conv_general_dilated(field[None], weights, (1, 1), 'VALID', dimension...  4.24 us
  transfers between devices with their start and end apart: 37, of which 16 were waited for; matrix products, arithmetic and copies ran while one was open for 15% of the time, Pallas kernels for 0%

profile of v6, /device:TPU:1, one launch (start us, length us, event | category | flops | bytes accessed | tf_op | source)
XLA Modules:
  0.0 117.5 jit_solution(17771299479367118956)
XLA Ops:
  4.5 4.6 %collective-permute-start = (bf16[4,32,448]{2,1,0:T(8,128)(2,1)S(1)}, bf16[4,32,448]{2,1,0:T(8,128)(2,1)S(1)}, u32[]{:S(2)}, u32[]{:S(2)}) collective-permute-start(bf16[4,32,448]{2,1,0:T(8,128)(2,1)S(1)} %concatenate.128), channel_id=1, source_target_pairs={{0,8},{8,16},{16,24},{1,9},{9,17},{17,25},{2,10},{10,18},{18,26},{... | collective-permute-start | bytes 344072 | tf_op jit(solution)/shard_map/ppermute | solution.py:110
  11.3 4.9 %collective-permute-start.4 = (f32[3,32,128]{2,1,0:T(8,128)S(1)}, f32[3,32,128]{2,1,0:T(8,128)S(1)}, u32[]{:S(2)}, u32[]{:S(2)}) collective-permute-start(f32[3,32,128]{2,1,0:T(8,128)S(1)} %get-tuple-element.91), channel_id=1, source_target_pairs={{0,8},{8,16},{16,24},{1,9},{9,17},{17,25},{2,10},{10,18},{18,26},{... | collective-permute-start | bytes 147464 | tf_op jit(solution)/shard_map/ppermute | solution.py:110
  18.2 5.2 %collective-permute-start.6 = (f32[10,3,128]{2,1,0:T(4,128)S(1)}, f32[10,3,128]{2,1,0:T(4,128)S(1)}, u32[]{:S(2)}, u32[]{:S(2)}) collective-permute-start(f32[10,3,128]{2,1,0:T(4,128)S(1)} %get-tuple-element.57), channel_id=1, source_target_pairs={{0,1},{1,2},{2,3},{3,4},{4,5},{5,6},{6,7},{8,9},{9,10},{10,11},{11... | collective-permute-start | bytes 46088 | tf_op jit(solution)/shard_map/ppermute | solution.py:110
  23.4 1.9 %collective-permute-start.7 = (f32[10,3,128]{2,1,0:T(4,128)S(1)}, f32[10,3,128]{2,1,0:T(4,128)S(1)}, u32[]{:S(2)}, u32[]{:S(2)}) collective-permute-start(f32[10,3,128]{2,1,0:T(4,128)S(1)} %get-tuple-element.58), channel_id=1, source_target_pairs={{1,0},{2,1},{3,2},{4,3},{5,4},{6,5},{7,6},{9,8},{10,9},{11,10},{12... | collective-permute-start | bytes 46088 | tf_op jit(solution)/shard_map/ppermute | solution.py:111
  25.4 3.6 %collective-permute-start.2 = (bf16[12,4,448]{2,1,0:T(4,128)(2,1)S(1)}, bf16[12,4,448]{2,1,0:T(4,128)(2,1)S(1)}, u32[]{:S(2)}, u32[]{:S(2)}) collective-permute-start(bf16[12,4,448]{2,1,0:T(4,128)(2,1)S(1)} %get-tuple-element.35), channel_id=1, source_target_pairs={{0,1},{1,2},{2,3},{3,4},{4,5},{5,6},{6,7},{8,9},{9,10},{10,11},{11... | collective-permute-start | bytes 129032 | tf_op jit(solution)/shard_map/ppermute | solution.py:110
  29.0 1.9 %collective-permute-start.3 = (bf16[12,4,448]{2,1,0:T(4,128)(2,1)S(1)}, bf16[12,4,448]{2,1,0:T(4,128)(2,1)S(1)}, u32[]{:S(2)}, u32[]{:S(2)}) collective-permute-start(bf16[12,4,448]{2,1,0:T(4,128)(2,1)S(1)} %get-tuple-element.36), channel_id=1, source_target_pairs={{1,0},{2,1},{3,2},{4,3},{5,4},{6,5},{7,6},{9,8},{10,9},{11,10},{12... | collective-permute-start | bytes 129032 | tf_op jit(solution)/shard_map/ppermute | solution.py:111
  31.7 2.7 %collective-permute-done.3 = bf16[12,4,448]{2,1,0:T(4,128)(2,1)S(1)} collective-permute-done((bf16[12,4,448]{2,1,0:T(4,128)(2,1)S(1)}, bf16[12,4,448]{2,1,0:T(4,128)(2,1)S(1)}, u32[]{:S(2)}, u32[]{:S(2)}) %collective-permute-start.3) | collective-permute-done | bytes 43040 | tf_op jit(solution)/shard_map/ppermute | solution.py:111
  43.0 2.1 %convolution_select_fusion.1 = f32[8,8,5,512]{3,1,2,0:T(8,128)S(1)} fusion(bf16[3,3,160,512]{3,2,1,0:T(8,128)(2,1)} %bitcast.92, pred[8,5]{0,1:T(8,128)(4,1)S(1)} %copy-done.23, bf16[10,1,7,2,160]{4,2,3,0,1:T(8,128)(2,1)S(1)} %slice.359, bf16[10,1,8,5,160]{4,2,3,0,1:T(8,128)(2,1)S(1)} %copy.16), kind=kOutput, calls=%fused_computation.7 | convolution fusion | flops 472560640 | bytes 2302760 | tf_op jit(solution)/shard_map/conv_general_dilated | solution.py:143
  59.0 2.7 %collective-permute-start.20 = (f32[128,512]{1,0:T(8,128)S(1)}, f32[128,512]{1,0:T(8,128)S(1)}, u32[]{:S(2)}, u32[]{:S(2)}) collective-permute-start(f32[128,512]{1,0:T(8,128)S(1)} %constant_dynamic-slice_fusion.7), channel_id=1, source_target_pairs={{0,8},{8,0},{16,24},{24,16},{1,9},{9,1},{17,25},{25,17},{2,10},{10... | collective-permute-start | bytes 786440 | tf_op jit(solution)/shard_map/ppermute | solution.py:45
  61.8 1.9 %collective-permute-start.28 = (f32[128,512]{1,0:T(8,128)S(1)}, f32[128,512]{1,0:T(8,128)S(1)}, u32[]{:S(2)}, u32[]{:S(2)}) collective-permute-start(f32[128,512]{1,0:T(8,128)S(1)} %constant_dynamic-slice_fusion.3), channel_id=1, source_target_pairs={{0,16},{8,24},{16,0},{24,8},{1,17},{9,25},{17,1},{25,9},{2,18},{10... | collective-permute-start | bytes 786440 | tf_op jit(solution)/shard_map/ppermute | solution.py:45
  64.8 2.7 %collective-permute-start.13 = (f32[64,512]{1,0:T(8,128)S(1)}, f32[64,512]{1,0:T(8,128)S(1)}, u32[]{:S(2)}, u32[]{:S(2)}) collective-permute-start(f32[64,512]{1,0:T(8,128)S(1)} %constant_dynamic-slice_fusion.10), channel_id=1, source_target_pairs={{0,8},{8,0},{16,24},{24,16},{1,9},{9,1},{17,25},{25,17},{2,10},{10... | collective-permute-start | bytes 393224 | tf_op jit(solution)/shard_map/ppermute | solution.py:45
  67.8 3.0 %collective-permute-start.21 = (f32[64,512]{1,0:T(8,128)S(1)}, f32[64,512]{1,0:T(8,128)S(1)}, u32[]{:S(2)}, u32[]{:S(2)}) collective-permute-start(f32[64,512]{1,0:T(8,128)S(1)} %constant_dynamic-slice_fusion.6), channel_id=1, source_target_pairs={{0,16},{8,24},{16,0},{24,8},{1,17},{9,25},{17,1},{25,9},{2,18},{10... | collective-permute-start | bytes 393224 | tf_op jit(solution)/shard_map/ppermute | solution.py:45
  73.3 2.4 %collective-permute-start.22 = (f32[32,512]{1,0:T(8,128)S(1)}, f32[32,512]{1,0:T(8,128)S(1)}, u32[]{:S(2)}, u32[]{:S(2)}) collective-permute-start(f32[32,512]{1,0:T(8,128)S(1)} %constant_dynamic-slice_fusion.5), channel_id=1, source_target_pairs={{0,4},{1,5},{2,6},{3,7},{4,0},{5,1},{6,2},{7,3},{8,12},{9,13},{10,... | collective-permute-start | bytes 196616 | tf_op jit(solution)/shard_map/ppermute | solution.py:45
  75.6 3.9 %collective-permute-done.29 = f32[64,512]{1,0:T(8,128)S(1)} collective-permute-done((f32[64,512]{1,0:T(8,128)S(1)}, f32[64,512]{1,0:T(8,128)S(1)}, u32[]{:S(2)}, u32[]{:S(2)}) %collective-permute-start.29) | collective-permute-done | bytes 131104 | tf_op jit(solution)/shard_map/ppermute | solution.py:45
  79.8 2.9 %collective-permute-start.15 = (f32[16,512]{1,0:T(8,128)S(1)}, f32[16,512]{1,0:T(8,128)S(1)}, u32[]{:S(2)}, u32[]{:S(2)}) collective-permute-start(f32[16,512]{1,0:T(8,128)S(1)} %constant_dynamic-slice_fusion.8), channel_id=1, source_target_pairs={{0,4},{1,5},{2,6},{3,7},{4,0},{5,1},{6,2},{7,3},{8,12},{9,13},{10,... | collective-permute-start | bytes 98312 | tf_op jit(solution)/shard_map/ppermute | solution.py:45
  83.9 2.6 %collective-permute-start.16 = (bf16[16,512]{1,0:T(8,128)(2,1)S(1)}, bf16[16,512]{1,0:T(8,128)(2,1)S(1)}, u32[]{:S(2)}, u32[]{:S(2)}) collective-permute-start(bf16[16,512]{1,0:T(8,128)(2,1)S(1)} %add_convert_fusion.2), channel_id=1, source_target_pairs={{0,4},{1,5},{2,6},{3,7},{4,0},{5,1},{6,2},{7,3},{8,12},{9,13},{10,... | collective-permute-start | bytes 49160 | tf_op jit(solution)/shard_map/ppermute | solution.py:55
  88.0 1.6 %collective-permute-done.24 = bf16[16,512]{1,0:T(8,128)(2,1)S(1)} collective-permute-done((bf16[16,512]{1,0:T(8,128)(2,1)S(1)}, bf16[16,512]{1,0:T(8,128)(2,1)S(1)}, u32[]{:S(2)}, u32[]{:S(2)}) %collective-permute-start.24) | collective-permute-done | bytes 16416 | tf_op jit(solution)/shard_map/ppermute | solution.py:55
  91.8 1.9 %collective-permute-done.25 = bf16[32,512]{1,0:T(8,128)(2,1)S(1)} collective-permute-done((bf16[32,512]{1,0:T(8,128)(2,1)S(1)}, bf16[32,512]{1,0:T(8,128)(2,1)S(1)}, u32[]{:S(2)}, u32[]{:S(2)}) %collective-permute-start.25) | collective-permute-done | bytes 32800 | tf_op jit(solution)/shard_map/ppermute | solution.py:55
  93.9 1.8 %collective-permute-start.34 = (bf16[64,512]{1,0:T(8,128)(2,1)S(1)}, bf16[64,512]{1,0:T(8,128)(2,1)S(1)}, u32[]{:S(2)}, u32[]{:S(2)}) collective-permute-start(bf16[64,512]{1,0:T(8,128)(2,1)S(1)} %pad_maximum_fusion.16), channel_id=1, source_target_pairs={{0,4},{1,5},{2,6},{3,7},{4,0},{5,1},{6,2},{7,3},{8,12},{9,13},{10,... | collective-permute-start | bytes 196616 | tf_op jit(solution)/shard_map/ppermute | solution.py:55
  97.6 2.0 %collective-permute-done.34 = bf16[64,512]{1,0:T(8,128)(2,1)S(1)} collective-permute-done((bf16[64,512]{1,0:T(8,128)(2,1)S(1)}, bf16[64,512]{1,0:T(8,128)(2,1)S(1)}, u32[]{:S(2)}, u32[]{:S(2)}) %collective-permute-start.34) | collective-permute-done | bytes 65568 | tf_op jit(solution)/shard_map/ppermute | solution.py:55
  101.6 2.5 %collective-permute-done.35 = bf16[128,512]{1,0:T(8,128)(2,1)S(1)} collective-permute-done((bf16[128,512]{1,0:T(8,128)(2,1)S(1)}, bf16[128,512]{1,0:T(8,128)(2,1)S(1)}, u32[]{:S(2)}, u32[]{:S(2)}) %collective-permute-start.35) | collective-permute-done | bytes 131104 | tf_op jit(solution)/shard_map/ppermute | solution.py:55
  104.2 7.1 %collective-permute-start.36 = (bf16[768,512]{1,0:T(8,128)(2,1)S(1)}, bf16[768,512]{1,0:T(8,128)(2,1)S(1)}, u32[]{:S(2)}, u32[]{:S(2)}) collective-permute-start(bf16[768,512]{1,0:T(8,128)(2,1)S(1)} %select_dynamic-update-slice_fusion), channel_id=1, source_target_pairs={{0,1},{1,0},{2,3},{3,2},{4,5},{5,4},{6,7},{7,6},{8,9},{9,8},{10,11... | collective-permute-start | bytes 2359304 | tf_op jit(solution)/shard_map/ppermute | solution.py:74
  112.6 1.5 %fusion.98 = bf16[4,32,128]{2,1,0:T(8,128)(2,1)} fusion(f32[8,36,128]{2,1,0:T(8,128)S(1)} %get-tuple-element.16, f32[8,36,128]{2,1,0:T(8,128)} %get-tuple-element.34), kind=kLoop, calls=%fused_computation.205 | loop fusion | flops 32768 | bytes 163840 | tf_op jit(solution)/shard_map/convert_element_type | solution.py:157
  115.5 2.0 %maximum_convert_fusion = f32[1440,512]{1,0:T(8,128)} fusion(bf16[672,512]{1,0:T(8,128)(2,1)S(1)} %slice.444, bf16[768,512]{1,0:T(8,128)(2,1)S(1)} %get-tuple-element.19), kind=kLoop, calls=%fused_computation.5 | loop fusion | flops 2949120 | bytes 4423680 | tf_op jit(solution)/shard_map/convert_element_type | solution.py:78
  (239 shorter events, 46.4 us)
Async XLA Ops:
  3.2 22.1 %collective-permute-start.1 = (bf16[4,32,448]{2,1,0:T(8,128)(2,1)S(1)}, bf16[4,32,448]{2,1,0:T(8,128)(2,1)S(1)}, u32[]{:S(2)}, u32[]{:S(2)}) collective-permute-start(bf16[4,32,448]{2,1,0:T(8,128)(2,1)S(1)} %concatenate.128), channel_id=1, source_target_pairs={{8,0},{16,8},{24,16},{9,1},{17,9},{25,17},{10,2},{18,10},{26,18},{... | collective-permute-start | bytes 344072 | tf_op jit(solution)/shard_map/ppermute | solution.py:111
  4.5 20.8 %collective-permute-start = (bf16[4,32,448]{2,1,0:T(8,128)(2,1)S(1)}, bf16[4,32,448]{2,1,0:T(8,128)(2,1)S(1)}, u32[]{:S(2)}, u32[]{:S(2)}) collective-permute-start(bf16[4,32,448]{2,1,0:T(8,128)(2,1)S(1)} %concatenate.128), channel_id=1, source_target_pairs={{0,8},{8,16},{16,24},{1,9},{9,17},{17,25},{2,10},{10,18},{18,26},{... | collective-permute-start | bytes 344072 | tf_op jit(solution)/shard_map/ppermute | solution.py:110
  10.0 8.2 %collective-permute-start.5 = (f32[3,32,128]{2,1,0:T(8,128)S(1)}, f32[3,32,128]{2,1,0:T(8,128)S(1)}, u32[]{:S(2)}, u32[]{:S(2)}) collective-permute-start(f32[3,32,128]{2,1,0:T(8,128)S(1)} %get-tuple-element.90), channel_id=1, source_target_pairs={{8,0},{16,8},{24,16},{9,1},{17,9},{25,17},{10,2},{18,10},{26,18},{... | collective-permute-start | bytes 147464 | tf_op jit(solution)/shard_map/ppermute | solution.py:111
  11.3 6.0 %collective-permute-start.4 = (f32[3,32,128]{2,1,0:T(8,128)S(1)}, f32[3,32,128]{2,1,0:T(8,128)S(1)}, u32[]{:S(2)}, u32[]{:S(2)}) collective-permute-start(f32[3,32,128]{2,1,0:T(8,128)S(1)} %get-tuple-element.91), channel_id=1, source_target_pairs={{0,8},{8,16},{16,24},{1,9},{9,17},{17,25},{2,10},{10,18},{18,26},{... | collective-permute-start | bytes 147464 | tf_op jit(solution)/shard_map/ppermute | solution.py:110
  18.2 12.8 %collective-permute-start.6 = (f32[10,3,128]{2,1,0:T(4,128)S(1)}, f32[10,3,128]{2,1,0:T(4,128)S(1)}, u32[]{:S(2)}, u32[]{:S(2)}) collective-permute-start(f32[10,3,128]{2,1,0:T(4,128)S(1)} %get-tuple-element.57), channel_id=1, source_target_pairs={{0,1},{1,2},{2,3},{3,4},{4,5},{5,6},{6,7},{8,9},{9,10},{10,11},{11... | collective-permute-start | bytes 46088 | tf_op jit(solution)/shard_map/ppermute | solution.py:110
  23.4 7.6 %collective-permute-start.7 = (f32[10,3,128]{2,1,0:T(4,128)S(1)}, f32[10,3,128]{2,1,0:T(4,128)S(1)}, u32[]{:S(2)}, u32[]{:S(2)}) collective-permute-start(f32[10,3,128]{2,1,0:T(4,128)S(1)} %get-tuple-element.58), channel_id=1, source_target_pairs={{1,0},{2,1},{3,2},{4,3},{5,4},{6,5},{7,6},{9,8},{10,9},{11,10},{12... | collective-permute-start | bytes 46088 | tf_op jit(solution)/shard_map/ppermute | solution.py:111
  25.4 6.3 %collective-permute-start.2 = (bf16[12,4,448]{2,1,0:T(4,128)(2,1)S(1)}, bf16[12,4,448]{2,1,0:T(4,128)(2,1)S(1)}, u32[]{:S(2)}, u32[]{:S(2)}) collective-permute-start(bf16[12,4,448]{2,1,0:T(4,128)(2,1)S(1)} %get-tuple-element.35), channel_id=1, source_target_pairs={{0,1},{1,2},{2,3},{3,4},{4,5},{5,6},{6,7},{8,9},{9,10},{10,11},{11... | collective-permute-start | bytes 129032 | tf_op jit(solution)/shard_map/ppermute | solution.py:110
  29.0 5.4 %collective-permute-start.3 = (bf16[12,4,448]{2,1,0:T(4,128)(2,1)S(1)}, bf16[12,4,448]{2,1,0:T(4,128)(2,1)S(1)}, u32[]{:S(2)}, u32[]{:S(2)}) collective-permute-start(bf16[12,4,448]{2,1,0:T(4,128)(2,1)S(1)} %get-tuple-element.36), channel_id=1, source_target_pairs={{1,0},{2,1},{3,2},{4,3},{5,4},{6,5},{7,6},{9,8},{10,9},{11,10},{12... | collective-permute-start | bytes 129032 | tf_op jit(solution)/shard_map/ppermute | solution.py:111
  42.3 11.8 %collective-permute-start.9 = (bf16[6,34,160]{2,1,0:T(8,128)(2,1)}, bf16[6,34,160]{2,1,0:T(8,128)(2,1)S(1)}, u32[]{:S(2)}, u32[]{:S(2)}) collective-permute-start(bf16[6,34,160]{2,1,0:T(8,128)(2,1)} %fusion.73), channel_id=1, source_target_pairs={{0,1},{1,0},{2,3},{3,2},{4,5},{5,4},{6,7},{7,6},{8,9},{9,8},{10,11... | collective-permute-start | bytes 195848 | tf_op jit(solution)/shard_map/ppermute | solution.py:243
  42.3 12.2 %collective-permute-start.8 = (bf16[6,34,160]{2,1,0:T(8,128)(2,1)}, bf16[6,34,160]{2,1,0:T(8,128)(2,1)S(1)}, u32[]{:S(2)}, u32[]{:S(2)}) collective-permute-start(bf16[6,34,160]{2,1,0:T(8,128)(2,1)} %fusion.72), channel_id=1, source_target_pairs={{0,1},{1,0},{2,3},{3,2},{4,5},{5,4},{6,7},{7,6},{8,9},{9,8},{10,11... | collective-permute-start | bytes 195848 | tf_op jit(solution)/shard_map/ppermute | solution.py:243
  57.3 7.5 %collective-permute-start.12 = (f32[128,512]{1,0:T(8,128)S(1)}, f32[128,512]{1,0:T(8,128)S(1)}, u32[]{:S(2)}, u32[]{:S(2)}) collective-permute-start(f32[128,512]{1,0:T(8,128)S(1)} %constant_dynamic-slice_fusion.11), channel_id=1, source_target_pairs={{0,2},{1,3},{2,0},{3,1},{4,6},{5,7},{6,4},{7,5},{8,10},{9,11},{10,... | collective-permute-start | bytes 786440 | tf_op jit(solution)/shard_map/ppermute | solution.py:45
  59.0 8.7 %collective-permute-start.20 = (f32[128,512]{1,0:T(8,128)S(1)}, f32[128,512]{1,0:T(8,128)S(1)}, u32[]{:S(2)}, u32[]{:S(2)}) collective-permute-start(f32[128,512]{1,0:T(8,128)S(1)} %constant_dynamic-slice_fusion.7), channel_id=1, source_target_pairs={{0,8},{8,0},{16,24},{24,16},{1,9},{9,1},{17,25},{25,17},{2,10},{10... | collective-permute-start | bytes 786440 | tf_op jit(solution)/shard_map/ppermute | solution.py:45
  61.8 9.0 %collective-permute-start.28 = (f32[128,512]{1,0:T(8,128)S(1)}, f32[128,512]{1,0:T(8,128)S(1)}, u32[]{:S(2)}, u32[]{:S(2)}) collective-permute-start(f32[128,512]{1,0:T(8,128)S(1)} %constant_dynamic-slice_fusion.3), channel_id=1, source_target_pairs={{0,16},{8,24},{16,0},{24,8},{1,17},{9,25},{17,1},{25,9},{2,18},{10... | collective-permute-start | bytes 786440 | tf_op jit(solution)/shard_map/ppermute | solution.py:45
  64.8 7.5 %collective-permute-start.13 = (f32[64,512]{1,0:T(8,128)S(1)}, f32[64,512]{1,0:T(8,128)S(1)}, u32[]{:S(2)}, u32[]{:S(2)}) collective-permute-start(f32[64,512]{1,0:T(8,128)S(1)} %constant_dynamic-slice_fusion.10), channel_id=1, source_target_pairs={{0,8},{8,0},{16,24},{24,16},{1,9},{9,1},{17,25},{25,17},{2,10},{10... | collective-permute-start | bytes 393224 | tf_op jit(solution)/shard_map/ppermute | solution.py:45
  67.8 5.5 %collective-permute-start.21 = (f32[64,512]{1,0:T(8,128)S(1)}, f32[64,512]{1,0:T(8,128)S(1)}, u32[]{:S(2)}, u32[]{:S(2)}) collective-permute-start(f32[64,512]{1,0:T(8,128)S(1)} %constant_dynamic-slice_fusion.6), channel_id=1, source_target_pairs={{0,16},{8,24},{16,0},{24,8},{1,17},{9,25},{17,1},{25,9},{2,18},{10... | collective-permute-start | bytes 393224 | tf_op jit(solution)/shard_map/ppermute | solution.py:45
  70.8 8.8 %collective-permute-start.29 = (f32[64,512]{1,0:T(8,128)S(1)}, f32[64,512]{1,0:T(8,128)S(1)}, u32[]{:S(2)}, u32[]{:S(2)}) collective-permute-start(f32[64,512]{1,0:T(8,128)S(1)} %constant_dynamic-slice_fusion.2), channel_id=1, source_target_pairs={{0,4},{1,5},{2,6},{3,7},{4,0},{5,1},{6,2},{7,3},{8,12},{9,13},{10,... | collective-permute-start | bytes 393224 | tf_op jit(solution)/shard_map/ppermute | solution.py:45
  72.3 7.4 %collective-permute-start.14 = (f32[32,512]{1,0:T(8,128)S(1)}, f32[32,512]{1,0:T(8,128)S(1)}, u32[]{:S(2)}, u32[]{:S(2)}) collective-permute-start(f32[32,512]{1,0:T(8,128)S(1)} %constant_dynamic-slice_fusion.9), channel_id=1, source_target_pairs={{0,16},{8,24},{16,0},{24,8},{1,17},{9,25},{17,1},{25,9},{2,18},{10... | collective-permute-start | bytes 196616 | tf_op jit(solution)/shard_map/ppermute | solution.py:45
  73.3 9.4 %collective-permute-start.22 = (f32[32,512]{1,0:T(8,128)S(1)}, f32[32,512]{1,0:T(8,128)S(1)}, u32[]{:S(2)}, u32[]{:S(2)}) collective-permute-start(f32[32,512]{1,0:T(8,128)S(1)} %constant_dynamic-slice_fusion.5), channel_id=1, source_target_pairs={{0,4},{1,5},{2,6},{3,7},{4,0},{5,1},{6,2},{7,3},{8,12},{9,13},{10,... | collective-permute-start | bytes 196616 | tf_op jit(solution)/shard_map/ppermute | solution.py:45
  91.3 4.4 %collective-permute-start.18 = (bf16[64,512]{1,0:T(8,128)(2,1)S(1)}, bf16[64,512]{1,0:T(8,128)(2,1)S(1)}, u32[]{:S(2)}, u32[]{:S(2)}) collective-permute-start(bf16[64,512]{1,0:T(8,128)(2,1)S(1)} %pad_maximum_fusion.14), channel_id=1, source_target_pairs={{0,8},{8,0},{16,24},{24,16},{1,9},{9,1},{17,25},{25,17},{2,10},{10... | collective-permute-start | bytes 196616 | tf_op jit(solution)/shard_map/ppermute | solution.py:55
  93.9 5.7 %collective-permute-start.34 = (bf16[64,512]{1,0:T(8,128)(2,1)S(1)}, bf16[64,512]{1,0:T(8,128)(2,1)S(1)}, u32[]{:S(2)}, u32[]{:S(2)}) collective-permute-start(bf16[64,512]{1,0:T(8,128)(2,1)S(1)} %pad_maximum_fusion.16), channel_id=1, source_target_pairs={{0,4},{1,5},{2,6},{3,7},{4,0},{5,1},{6,2},{7,3},{8,12},{9,13},{10,... | collective-permute-start | bytes 196616 | tf_op jit(solution)/shard_map/ppermute | solution.py:55
  95.7 5.2 %collective-permute-start.19 = (bf16[128,512]{1,0:T(8,128)(2,1)S(1)}, bf16[128,512]{1,0:T(8,128)(2,1)S(1)}, u32[]{:S(2)}, u32[]{:S(2)}) collective-permute-start(bf16[128,512]{1,0:T(8,128)(2,1)S(1)} %pad_maximum_fusion.10), channel_id=1, source_target_pairs={{0,2},{1,3},{2,0},{3,1},{4,6},{5,7},{6,4},{7,5},{8,10},{9,11},{10,... | collective-permute-start | bytes 393224 | tf_op jit(solution)/shard_map/ppermute | solution.py:55
  97.0 4.6 %collective-permute-start.27 = (bf16[128,512]{1,0:T(8,128)(2,1)S(1)}, bf16[128,512]{1,0:T(8,128)(2,1)S(1)}, u32[]{:S(2)}, u32[]{:S(2)}) collective-permute-start(bf16[128,512]{1,0:T(8,128)(2,1)S(1)} %pad_maximum_fusion.11), channel_id=1, source_target_pairs={{0,8},{8,0},{16,24},{24,16},{1,9},{9,1},{17,25},{25,17},{2,10},{10... | collective-permute-start | bytes 393224 | tf_op jit(solution)/shard_map/ppermute | solution.py:55
  99.6 4.6 %collective-permute-start.35 = (bf16[128,512]{1,0:T(8,128)(2,1)S(1)}, bf16[128,512]{1,0:T(8,128)(2,1)S(1)}, u32[]{:S(2)}, u32[]{:S(2)}) collective-permute-start(bf16[128,512]{1,0:T(8,128)(2,1)S(1)} %pad_maximum_fusion.12), channel_id=1, source_target_pairs={{0,16},{8,24},{16,0},{24,8},{1,17},{9,25},{17,1},{25,9},{2,18},{10... | collective-permute-start | bytes 393224 | tf_op jit(solution)/shard_map/ppermute | solution.py:55
  104.2 10.6 %collective-permute-start.36 = (bf16[768,512]{1,0:T(8,128)(2,1)S(1)}, bf16[768,512]{1,0:T(8,128)(2,1)S(1)}, u32[]{:S(2)}, u32[]{:S(2)}) collective-permute-start(bf16[768,512]{1,0:T(8,128)(2,1)S(1)} %select_dynamic-update-slice_fusion), channel_id=1, source_target_pairs={{0,1},{1,0},{2,3},{3,2},{4,5},{5,4},{6,7},{7,6},{8,9},{9,8},{10,11... | collective-permute-start | bytes 2359304 | tf_op jit(solution)/shard_map/ppermute | solution.py:74
  (38 other events, 104.5 us)

commit v7 on v6

--- a/solution.py
+++ b/solution.py
@@ -13,6 +13,7 @@
 KIN = 1440
 SUM_ROWS = 1536
 SUM_WAYS = 3
+SUM_SHARED = 2
 
 
 def flip_pairs(axis, bit):
@@ -32,11 +33,11 @@
     return cols_levels[:1], cols_levels[1:2] + rows_levels + cols_levels[2:]
 
 
-def halve(part, levels):
+def halve(part, levels, limit=None):
     halved = []
     for axis, bit in levels:
         rows = part.shape[0]
-        if rows % 16 != 0:
+        if rows % 16 != 0 or len(halved) == limit:
             break
         half = rows // 2
         upper = (lax.axis_index(axis) >> bit) & 1
@@ -65,7 +66,9 @@
     pieces = []
     for way in range(ways):
         order = rest[way:] + rest[:way]
-        chunk, halved = halve(part[way * width : (way + 1) * width], order)
+        chunk, halved = halve(
+            part[way * width : (way + 1) * width], order, max(len(order) - SUM_SHARED, 0)
+        )
         pieces.append(double(chunk.astype(jnp.bfloat16), halved))
     piece = jnp.concatenate(pieces, axis=0)
     if len(first_halved) == 1:

time: 118 us -> 116 us (0.983)
  waiting for transfers between devices: 20.6 us -> 15 us
  starting transfers between devices: 61.5 us -> 64.1 us
    ppermute x0 -> x6, starting transfers between devices: none -> 10.9 us  [halve(): part = part + lax.ppermute(part, axis, flip_pairs(axis, bit))]
    ppermute x12 -> x6, waiting for transfers between devices: 10.2 us -> 2.64 us  [double(): got = lax.ppermute(piece, axis, flip_pairs(axis, bit))]
    ppermute x12 -> x6, starting transfers between devices: 19.4 us -> 12.9 us  [halve(): part = keep + lax.ppermute(send, axis, flip_pairs(axis, bit))]
    ppermute x0 -> x6, waiting for transfers between devices: none -> 6 us  [halve(): part = part + lax.ppermute(part, axis, flip_pairs(axis, bit))]
    ppermute x12 -> x6, waiting for transfers between devices: 6.31 us -> 2.21 us  [halve(): part = keep + lax.ppermute(send, axis, flip_pairs(axis, bit))]
    ppermute x12 -> x6, starting transfers between devices: 9.47 us -> 7.39 us  [double(): got = lax.ppermute(piece, axis, flip_pairs(axis, bit))]
  transfers between devices with their start and end apart: 37 -> 31, of which waited for: 16 -> 12; matrix products, arithmetic and copies ran while one was open for 15% -> 16% of each run, Pallas kernels for 0% -> 0%
where the time goes in v7:
time: 116 us; the launch traced here: 115 us
  starting transfers between devices  64.1 us (55%)
  waiting for transfers between devices  15 us (13%)
  other arithmetic  14.8 us (13%)
  local copies, waits for them, and re-layouts  13.9 us (12%)
  matrix products  5.79 us (5%)
  between operations  1.68 us (1%)
    ppermute x4, starting transfers between devices, widen(): lax.ppermute(tail, axis, [(i, i + dist) for i in range(count - dist)])  18.3 us
    ppermute x6, starting transfers between devices, halve(): part = keep + lax.ppermute(send, axis, flip_pairs(axis, bit))  12.9 us
    ppermute x6, starting transfers between devices, halve(): part = part + lax.ppermute(part, axis, flip_pairs(axis, bit))  10.9 us
    ppermute x1, starting transfers between devices, sum_everywhere(): got = lax.ppermute(piece, axis, flip_pairs(axis, bit))  7.48 us
    ppermute x6, starting transfers between devices, double(): got = lax.ppermute(piece, axis, flip_pairs(axis, bit))  7.39 us
    ppermute x4, starting transfers between devices, widen(): lax.ppermute(head, axis, [(i + dist, i) for i in range(count - dist)])  6.41 us
    ppermute x6, waiting for transfers between devices, halve(): part = part + lax.ppermute(part, axis, flip_pairs(axis, bit))  6 us
    conv_general_dilated x4, matrix products, convolve(): lax.conv_general_dilated(field[None], weights, (1, 1), 'VALID', dimension...  4.27 us
  transfers between devices with their start and end apart: 31, of which 12 were waited for; matrix products, arithmetic and copies ran while one was open for 16% of the time, Pallas kernels for 0%

profile of v7, /device:TPU:1, one launch (start us, length us, event | category | flops | bytes accessed | tf_op | source)
XLA Modules:
  0.0 115.3 jit_solution(3829875412891693274)
XLA Ops:
  4.5 4.6 %collective-permute-start = (bf16[4,32,448]{2,1,0:T(8,128)(2,1)S(1)}, bf16[4,32,448]{2,1,0:T(8,128)(2,1)S(1)}, u32[]{:S(2)}, u32[]{:S(2)}) collective-permute-start(bf16[4,32,448]{2,1,0:T(8,128)(2,1)S(1)} %concatenate.110), channel_id=1, source_target_pairs={{0,8},{8,16},{16,24},{1,9},{9,17},{17,25},{2,10},{10,18},{18,26},{... | collective-permute-start | bytes 344072 | tf_op jit(solution)/shard_map/ppermute | solution.py:113
  11.3 4.9 %collective-permute-start.4 = (f32[3,32,128]{2,1,0:T(8,128)S(1)}, f32[3,32,128]{2,1,0:T(8,128)S(1)}, u32[]{:S(2)}, u32[]{:S(2)}) collective-permute-start(f32[3,32,128]{2,1,0:T(8,128)S(1)} %get-tuple-element.85), channel_id=1, source_target_pairs={{0,8},{8,16},{16,24},{1,9},{9,17},{17,25},{2,10},{10,18},{18,26},{... | collective-permute-start | bytes 147464 | tf_op jit(solution)/shard_map/ppermute | solution.py:113
  18.2 5.2 %collective-permute-start.6 = (f32[10,3,128]{2,1,0:T(4,128)S(1)}, f32[10,3,128]{2,1,0:T(4,128)S(1)}, u32[]{:S(2)}, u32[]{:S(2)}) collective-permute-start(f32[10,3,128]{2,1,0:T(4,128)S(1)} %get-tuple-element.57), channel_id=1, source_target_pairs={{0,1},{1,2},{2,3},{3,4},{4,5},{5,6},{6,7},{8,9},{9,10},{10,11},{11... | collective-permute-start | bytes 46088 | tf_op jit(solution)/shard_map/ppermute | solution.py:113
  23.4 1.9 %collective-permute-start.7 = (f32[10,3,128]{2,1,0:T(4,128)S(1)}, f32[10,3,128]{2,1,0:T(4,128)S(1)}, u32[]{:S(2)}, u32[]{:S(2)}) collective-permute-start(f32[10,3,128]{2,1,0:T(4,128)S(1)} %get-tuple-element.58), channel_id=1, source_target_pairs={{1,0},{2,1},{3,2},{4,3},{5,4},{6,5},{7,6},{9,8},{10,9},{11,10},{12... | collective-permute-start | bytes 46088 | tf_op jit(solution)/shard_map/ppermute | solution.py:114
  25.4 3.6 %collective-permute-start.2 = (bf16[12,4,448]{2,1,0:T(4,128)(2,1)S(1)}, bf16[12,4,448]{2,1,0:T(4,128)(2,1)S(1)}, u32[]{:S(2)}, u32[]{:S(2)}) collective-permute-start(bf16[12,4,448]{2,1,0:T(4,128)(2,1)S(1)} %get-tuple-element.35), channel_id=1, source_target_pairs={{0,1},{1,2},{2,3},{3,4},{4,5},{5,6},{6,7},{8,9},{9,10},{10,11},{11... | collective-permute-start | bytes 129032 | tf_op jit(solution)/shard_map/ppermute | solution.py:113
  29.1 1.9 %collective-permute-start.3 = (bf16[12,4,448]{2,1,0:T(4,128)(2,1)S(1)}, bf16[12,4,448]{2,1,0:T(4,128)(2,1)S(1)}, u32[]{:S(2)}, u32[]{:S(2)}) collective-permute-start(bf16[12,4,448]{2,1,0:T(4,128)(2,1)S(1)} %get-tuple-element.36), channel_id=1, source_target_pairs={{1,0},{2,1},{3,2},{4,3},{5,4},{6,5},{7,6},{9,8},{10,9},{11,10},{12... | collective-permute-start | bytes 129032 | tf_op jit(solution)/shard_map/ppermute | solution.py:114
  31.7 2.7 %collective-permute-done.3 = bf16[12,4,448]{2,1,0:T(4,128)(2,1)S(1)} collective-permute-done((bf16[12,4,448]{2,1,0:T(4,128)(2,1)S(1)}, bf16[12,4,448]{2,1,0:T(4,128)(2,1)S(1)}, u32[]{:S(2)}, u32[]{:S(2)}) %collective-permute-start.3) | collective-permute-done | bytes 43040 | tf_op jit(solution)/shard_map/ppermute | solution.py:114
  43.0 2.1 %convolution_select_fusion.1 = f32[8,8,5,512]{3,1,2,0:T(8,128)S(1)} fusion(bf16[3,3,160,512]{3,2,1,0:T(8,128)(2,1)} %bitcast.92, pred[8,5]{0,1:T(8,128)(4,1)S(1)} %copy-done.23, bf16[10,1,7,2,160]{4,2,3,0,1:T(8,128)(2,1)S(1)} %slice.359, bf16[10,1,8,5,160]{4,2,3,0,1:T(8,128)(2,1)S(1)} %copy.16), kind=kOutput, calls=%fused_computation.7 | convolution fusion | flops 472560640 | bytes 2302760 | tf_op jit(solution)/shard_map/conv_general_dilated | solution.py:146
  55.7 1.5 %convolution_multiply_fusion = f32[768,512]{1,0:T(8,128)S(1)} fusion(s32[]{:T(128)S(6)} %select_n.147, bf16[128,1536]{1,0:T(8,128)(2,1)S(1)} %copy-done.3, bf16[128,1536]{1,0:T(8,128)(2,1)S(1)} %copy-done.2, bf16[128,1536]{1,0:T(8,128)(2,1)S(1)} %concatenate.132, bf16[128,1536]{1,0:T(8,128)(2,1)S(1)} %concatenate.134, ...), kind=kOutput, calls=%fused_computation.4 | convolution fusion | flops 408289280 | bytes 3670020 | tf_op jit(solution)/shard_map/dot_general | solution.py:265
  58.8 2.7 %collective-permute-start.18 = (f32[128,512]{1,0:T(8,128)S(1)}, f32[128,512]{1,0:T(8,128)S(1)}, u32[]{:S(2)}, u32[]{:S(2)}) collective-permute-start(f32[128,512]{1,0:T(8,128)S(1)} %constant_dynamic-slice_fusion.3), channel_id=1, source_target_pairs={{0,8},{8,0},{16,24},{24,16},{1,9},{9,1},{17,25},{25,17},{2,10},{10... | collective-permute-start | bytes 786440 | tf_op jit(solution)/shard_map/ppermute | solution.py:46
  61.5 1.9 %collective-permute-start.24 = (f32[128,512]{1,0:T(8,128)S(1)}, f32[128,512]{1,0:T(8,128)S(1)}, u32[]{:S(2)}, u32[]{:S(2)}) collective-permute-start(f32[128,512]{1,0:T(8,128)S(1)} %constant_dynamic-slice_fusion.1), channel_id=1, source_target_pairs={{0,16},{8,24},{16,0},{24,8},{1,17},{9,25},{17,1},{25,9},{2,18},{10... | collective-permute-start | bytes 786440 | tf_op jit(solution)/shard_map/ppermute | solution.py:46
  63.4 1.6 %collective-permute-done.12 = f32[128,512]{1,0:T(8,128)} collective-permute-done((f32[128,512]{1,0:T(8,128)S(1)}, f32[128,512]{1,0:T(8,128)}, u32[]{:S(2)}, u32[]{:S(2)}) %collective-permute-start.12) | collective-permute-done | bytes 262176 | tf_op jit(solution)/shard_map/ppermute | solution.py:46
  66.0 2.7 %collective-permute-start.13 = (f32[64,512]{1,0:T(8,128)S(1)}, f32[64,512]{1,0:T(8,128)S(1)}, u32[]{:S(2)}, u32[]{:S(2)}) collective-permute-start(f32[64,512]{1,0:T(8,128)S(1)} %constant_dynamic-slice_fusion.4), channel_id=1, source_target_pairs={{0,8},{8,0},{16,24},{24,16},{1,9},{9,1},{17,25},{25,17},{2,10},{10... | collective-permute-start | bytes 393224 | tf_op jit(solution)/shard_map/ppermute | solution.py:46
  68.7 1.9 %collective-permute-start.19 = (f32[64,512]{1,0:T(8,128)S(1)}, f32[64,512]{1,0:T(8,128)S(1)}, u32[]{:S(2)}, u32[]{:S(2)}) collective-permute-start(f32[64,512]{1,0:T(8,128)S(1)} %constant_dynamic-slice_fusion.2), channel_id=1, source_target_pairs={{0,16},{8,24},{16,0},{24,8},{1,17},{9,25},{17,1},{25,9},{2,18},{10... | collective-permute-start | bytes 393224 | tf_op jit(solution)/shard_map/ppermute | solution.py:46
  70.7 2.4 %collective-permute-start.25 = (f32[64,512]{1,0:T(8,128)S(1)}, f32[64,512]{1,0:T(8,128)S(1)}, u32[]{:S(2)}, u32[]{:S(2)}) collective-permute-start(f32[64,512]{1,0:T(8,128)S(1)} %constant_dynamic-slice_fusion), channel_id=1, source_target_pairs={{0,4},{1,5},{2,6},{3,7},{4,0},{5,1},{6,2},{7,3},{8,12},{9,13},{10,... | collective-permute-start | bytes 393224 | tf_op jit(solution)/shard_map/ppermute | solution.py:46
  74.4 2.4 %collective-permute-start.20 = (f32[64,512]{1,0:T(8,128)S(1)}, f32[64,512]{1,0:T(8,128)S(1)}, u32[]{:S(2)}, u32[]{:S(2)}) collective-permute-start(f32[64,512]{1,0:T(8,128)S(1)} %dynamic-slice_add_fusion.4), channel_id=1, source_target_pairs={{0,4},{1,5},{2,6},{3,7},{4,0},{5,1},{6,2},{7,3},{8,12},{9,13},{10,... | collective-permute-start | bytes 393224 | tf_op jit(solution)/shard_map/ppermute | solution.py:49
  77.5 5.8 %collective-permute-start.15 = (f32[64,512]{1,0:T(8,128)S(1)}, f32[64,512]{1,0:T(8,128)S(1)}, u32[]{:S(2)}, u32[]{:S(2)}) collective-permute-start(f32[64,512]{1,0:T(8,128)S(1)} %add.220), channel_id=1, source_target_pairs={{0,4},{1,5},{2,6},{3,7},{4,0},{5,1},{6,2},{7,3},{8,12},{9,13},{10,... | collective-permute-start | bytes 393224 | tf_op jit(solution)/shard_map/ppermute | solution.py:49
  86.0 2.2 %collective-permute-done.15 = f32[64,512]{1,0:T(8,128)S(1)} collective-permute-done((f32[64,512]{1,0:T(8,128)S(1)}, f32[64,512]{1,0:T(8,128)S(1)}, u32[]{:S(2)}, u32[]{:S(2)}) %collective-permute-start.15) | collective-permute-done | bytes 131104 | tf_op jit(solution)/shard_map/ppermute | solution.py:49
  89.7 2.9 %collective-permute-done.21 = f32[64,512]{1,0:T(8,128)S(1)} collective-permute-done((f32[64,512]{1,0:T(8,128)S(1)}, f32[64,512]{1,0:T(8,128)S(1)}, u32[]{:S(2)}, u32[]{:S(2)}) %collective-permute-start.21) | collective-permute-done | bytes 131104 | tf_op jit(solution)/shard_map/ppermute | solution.py:49
  93.5 2.3 %collective-permute-start.17 = (bf16[128,512]{1,0:T(8,128)(2,1)S(1)}, bf16[128,512]{1,0:T(8,128)(2,1)S(1)}, u32[]{:S(2)}, u32[]{:S(2)}) collective-permute-start(bf16[128,512]{1,0:T(8,128)(2,1)S(1)} %pad_maximum_fusion.10), channel_id=1, source_target_pairs={{0,2},{1,3},{2,0},{3,1},{4,6},{5,7},{6,4},{7,5},{8,10},{9,11},{10,... | collective-permute-start | bytes 393224 | tf_op jit(solution)/shard_map/ppermute | solution.py:56
  100.0 1.6 %collective-permute-done.29 = bf16[128,512]{1,0:T(8,128)(2,1)S(1)} collective-permute-done((bf16[128,512]{1,0:T(8,128)(2,1)S(1)}, bf16[128,512]{1,0:T(8,128)(2,1)S(1)}, u32[]{:S(2)}, u32[]{:S(2)}) %collective-permute-start.29) | collective-permute-done | bytes 131104 | tf_op jit(solution)/shard_map/ppermute | solution.py:56
  101.7 7.5 %collective-permute-start.30 = (bf16[768,512]{1,0:T(8,128)(2,1)S(1)}, bf16[768,512]{1,0:T(8,128)(2,1)S(1)}, u32[]{:S(2)}, u32[]{:S(2)}) collective-permute-start(bf16[768,512]{1,0:T(8,128)(2,1)S(1)} %select_dynamic-update-slice_fusion), channel_id=1, source_target_pairs={{0,1},{1,0},{2,3},{3,2},{4,5},{5,4},{6,7},{7,6},{8,9},{9,8},{10,11... | collective-permute-start | bytes 2359304 | tf_op jit(solution)/shard_map/ppermute | solution.py:77
  110.4 1.5 %fusion.98 = bf16[4,32,128]{2,1,0:T(8,128)(2,1)} fusion(f32[8,36,128]{2,1,0:T(8,128)S(1)} %get-tuple-element.16, f32[8,36,128]{2,1,0:T(8,128)} %get-tuple-element.34), kind=kLoop, calls=%fused_computation.208 | loop fusion | flops 32768 | bytes 163840 | tf_op jit(solution)/shard_map/convert_element_type | solution.py:160
  113.3 2.0 %maximum_convert_fusion = f32[1440,512]{1,0:T(8,128)} fusion(bf16[672,512]{1,0:T(8,128)(2,1)S(1)} %slice.444, bf16[768,512]{1,0:T(8,128)(2,1)S(1)} %get-tuple-element.19), kind=kLoop, calls=%fused_computation.5 | loop fusion | flops 2949120 | bytes 4423680 | tf_op jit(solution)/shard_map/convert_element_type | solution.py:81
  (209 shorter events, 43.9 us)
Async XLA Ops:
  3.2 22.1 %collective-permute-start.1 = (bf16[4,32,448]{2,1,0:T(8,128)(2,1)S(1)}, bf16[4,32,448]{2,1,0:T(8,128)(2,1)S(1)}, u32[]{:S(2)}, u32[]{:S(2)}) collective-permute-start(bf16[4,32,448]{2,1,0:T(8,128)(2,1)S(1)} %concatenate.110), channel_id=1, source_target_pairs={{8,0},{16,8},{24,16},{9,1},{17,9},{25,17},{10,2},{18,10},{26,18},{... | collective-permute-start | bytes 344072 | tf_op jit(solution)/shard_map/ppermute | solution.py:114
  4.5 20.8 %collective-permute-start = (bf16[4,32,448]{2,1,0:T(8,128)(2,1)S(1)}, bf16[4,32,448]{2,1,0:T(8,128)(2,1)S(1)}, u32[]{:S(2)}, u32[]{:S(2)}) collective-permute-start(bf16[4,32,448]{2,1,0:T(8,128)(2,1)S(1)} %concatenate.110), channel_id=1, source_target_pairs={{0,8},{8,16},{16,24},{1,9},{9,17},{17,25},{2,10},{10,18},{18,26},{... | collective-permute-start | bytes 344072 | tf_op jit(solution)/shard_map/ppermute | solution.py:113
  10.0 8.2 %collective-permute-start.5 = (f32[3,32,128]{2,1,0:T(8,128)S(1)}, f32[3,32,128]{2,1,0:T(8,128)S(1)}, u32[]{:S(2)}, u32[]{:S(2)}) collective-permute-start(f32[3,32,128]{2,1,0:T(8,128)S(1)} %get-tuple-element.84), channel_id=1, source_target_pairs={{8,0},{16,8},{24,16},{9,1},{17,9},{25,17},{10,2},{18,10},{26,18},{... | collective-permute-start | bytes 147464 | tf_op jit(solution)/shard_map/ppermute | solution.py:114
  11.3 6.0 %collective-permute-start.4 = (f32[3,32,128]{2,1,0:T(8,128)S(1)}, f32[3,32,128]{2,1,0:T(8,128)S(1)}, u32[]{:S(2)}, u32[]{:S(2)}) collective-permute-start(f32[3,32,128]{2,1,0:T(8,128)S(1)} %get-tuple-element.85), channel_id=1, source_target_pairs={{0,8},{8,16},{16,24},{1,9},{9,17},{17,25},{2,10},{10,18},{18,26},{... | collective-permute-start | bytes 147464 | tf_op jit(solution)/shard_map/ppermute | solution.py:113
  18.2 12.8 %collective-permute-start.6 = (f32[10,3,128]{2,1,0:T(4,128)S(1)}, f32[10,3,128]{2,1,0:T(4,128)S(1)}, u32[]{:S(2)}, u32[]{:S(2)}) collective-permute-start(f32[10,3,128]{2,1,0:T(4,128)S(1)} %get-tuple-element.57), channel_id=1, source_target_pairs={{0,1},{1,2},{2,3},{3,4},{4,5},{5,6},{6,7},{8,9},{9,10},{10,11},{11... | collective-permute-start | bytes 46088 | tf_op jit(solution)/shard_map/ppermute | solution.py:113
  23.4 7.6 %collective-permute-start.7 = (f32[10,3,128]{2,1,0:T(4,128)S(1)}, f32[10,3,128]{2,1,0:T(4,128)S(1)}, u32[]{:S(2)}, u32[]{:S(2)}) collective-permute-start(f32[10,3,128]{2,1,0:T(4,128)S(1)} %get-tuple-element.58), channel_id=1, source_target_pairs={{1,0},{2,1},{3,2},{4,3},{5,4},{6,5},{7,6},{9,8},{10,9},{11,10},{12... | collective-permute-start | bytes 46088 | tf_op jit(solution)/shard_map/ppermute | solution.py:114
  25.4 6.3 %collective-permute-start.2 = (bf16[12,4,448]{2,1,0:T(4,128)(2,1)S(1)}, bf16[12,4,448]{2,1,0:T(4,128)(2,1)S(1)}, u32[]{:S(2)}, u32[]{:S(2)}) collective-permute-start(bf16[12,4,448]{2,1,0:T(4,128)(2,1)S(1)} %get-tuple-element.35), channel_id=1, source_target_pairs={{0,1},{1,2},{2,3},{3,4},{4,5},{5,6},{6,7},{8,9},{9,10},{10,11},{11... | collective-permute-start | bytes 129032 | tf_op jit(solution)/shard_map/ppermute | solution.py:113
  29.1 5.4 %collective-permute-start.3 = (bf16[12,4,448]{2,1,0:T(4,128)(2,1)S(1)}, bf16[12,4,448]{2,1,0:T(4,128)(2,1)S(1)}, u32[]{:S(2)}, u32[]{:S(2)}) collective-permute-start(bf16[12,4,448]{2,1,0:T(4,128)(2,1)S(1)} %get-tuple-element.36), channel_id=1, source_target_pairs={{1,0},{2,1},{3,2},{4,3},{5,4},{6,5},{7,6},{9,8},{10,9},{11,10},{12... | collective-permute-start | bytes 129032 | tf_op jit(solution)/shard_map/ppermute | solution.py:114
  42.3 11.8 %collective-permute-start.9 = (bf16[6,34,160]{2,1,0:T(8,128)(2,1)}, bf16[6,34,160]{2,1,0:T(8,128)(2,1)S(1)}, u32[]{:S(2)}, u32[]{:S(2)}) collective-permute-start(bf16[6,34,160]{2,1,0:T(8,128)(2,1)} %fusion.73), channel_id=1, source_target_pairs={{0,1},{1,0},{2,3},{3,2},{4,5},{5,4},{6,7},{7,6},{8,9},{9,8},{10,11... | collective-permute-start | bytes 195848 | tf_op jit(solution)/shard_map/ppermute | solution.py:246
  42.3 12.3 %collective-permute-start.8 = (bf16[6,34,160]{2,1,0:T(8,128)(2,1)}, bf16[6,34,160]{2,1,0:T(8,128)(2,1)S(1)}, u32[]{:S(2)}, u32[]{:S(2)}) collective-permute-start(bf16[6,34,160]{2,1,0:T(8,128)(2,1)} %fusion.72), channel_id=1, source_target_pairs={{0,1},{1,0},{2,3},{3,2},{4,5},{5,4},{6,7},{7,6},{8,9},{9,8},{10,11... | collective-permute-start | bytes 195848 | tf_op jit(solution)/shard_map/ppermute | solution.py:246
  57.3 7.6 %collective-permute-start.12 = (f32[128,512]{1,0:T(8,128)S(1)}, f32[128,512]{1,0:T(8,128)}, u32[]{:S(2)}, u32[]{:S(2)}) collective-permute-start(f32[128,512]{1,0:T(8,128)S(1)} %constant_dynamic-slice_fusion.5), channel_id=1, source_target_pairs={{0,2},{1,3},{2,0},{3,1},{4,6},{5,7},{6,4},{7,5},{8,10},{9,11},{10,... | collective-permute-start | bytes 786440 | tf_op jit(solution)/shard_map/ppermute | solution.py:46
  58.8 9.9 %collective-permute-start.18 = (f32[128,512]{1,0:T(8,128)S(1)}, f32[128,512]{1,0:T(8,128)S(1)}, u32[]{:S(2)}, u32[]{:S(2)}) collective-permute-start(f32[128,512]{1,0:T(8,128)S(1)} %constant_dynamic-slice_fusion.3), channel_id=1, source_target_pairs={{0,8},{8,0},{16,24},{24,16},{1,9},{9,1},{17,25},{25,17},{2,10},{10... | collective-permute-start | bytes 786440 | tf_op jit(solution)/shard_map/ppermute | solution.py:46
  61.5 9.1 %collective-permute-start.24 = (f32[128,512]{1,0:T(8,128)S(1)}, f32[128,512]{1,0:T(8,128)S(1)}, u32[]{:S(2)}, u32[]{:S(2)}) collective-permute-start(f32[128,512]{1,0:T(8,128)S(1)} %constant_dynamic-slice_fusion.1), channel_id=1, source_target_pairs={{0,16},{8,24},{16,0},{24,8},{1,17},{9,25},{17,1},{25,9},{2,18},{10... | collective-permute-start | bytes 786440 | tf_op jit(solution)/shard_map/ppermute | solution.py:46
  66.0 7.1 %collective-permute-start.13 = (f32[64,512]{1,0:T(8,128)S(1)}, f32[64,512]{1,0:T(8,128)S(1)}, u32[]{:S(2)}, u32[]{:S(2)}) collective-permute-start(f32[64,512]{1,0:T(8,128)S(1)} %constant_dynamic-slice_fusion.4), channel_id=1, source_target_pairs={{0,8},{8,0},{16,24},{24,16},{1,9},{9,1},{17,25},{25,17},{2,10},{10... | collective-permute-start | bytes 393224 | tf_op jit(solution)/shard_map/ppermute | solution.py:46
  68.7 5.6 %collective-permute-start.19 = (f32[64,512]{1,0:T(8,128)S(1)}, f32[64,512]{1,0:T(8,128)S(1)}, u32[]{:S(2)}, u32[]{:S(2)}) collective-permute-start(f32[64,512]{1,0:T(8,128)S(1)} %constant_dynamic-slice_fusion.2), channel_id=1, source_target_pairs={{0,16},{8,24},{16,0},{24,8},{1,17},{9,25},{17,1},{25,9},{2,18},{10... | collective-permute-start | bytes 393224 | tf_op jit(solution)/shard_map/ppermute | solution.py:46
  70.7 6.7 %collective-permute-start.25 = (f32[64,512]{1,0:T(8,128)S(1)}, f32[64,512]{1,0:T(8,128)S(1)}, u32[]{:S(2)}, u32[]{:S(2)}) collective-permute-start(f32[64,512]{1,0:T(8,128)S(1)} %constant_dynamic-slice_fusion), channel_id=1, source_target_pairs={{0,4},{1,5},{2,6},{3,7},{4,0},{5,1},{6,2},{7,3},{8,12},{9,13},{10,... | collective-permute-start | bytes 393224 | tf_op jit(solution)/shard_map/ppermute | solution.py:46
  74.4 10.2 %collective-permute-start.20 = (f32[64,512]{1,0:T(8,128)S(1)}, f32[64,512]{1,0:T(8,128)S(1)}, u32[]{:S(2)}, u32[]{:S(2)}) collective-permute-start(f32[64,512]{1,0:T(8,128)S(1)} %dynamic-slice_add_fusion.4), channel_id=1, source_target_pairs={{0,4},{1,5},{2,6},{3,7},{4,0},{5,1},{6,2},{7,3},{8,12},{9,13},{10,... | collective-permute-start | bytes 393224 | tf_op jit(solution)/shard_map/ppermute | solution.py:49
  77.4 7.2 %collective-permute-start.26 = (f32[64,512]{1,0:T(8,128)S(1)}, f32[64,512]{1,0:T(8,128)S(1)}, u32[]{:S(2)}, u32[]{:S(2)}) collective-permute-start(f32[64,512]{1,0:T(8,128)S(1)} %dynamic-slice_add_fusion.3), channel_id=1, source_target_pairs={{0,2},{1,3},{2,0},{3,1},{4,6},{5,7},{6,4},{7,5},{8,10},{9,11},{10,... | collective-permute-start | bytes 393224 | tf_op jit(solution)/shard_map/ppermute | solution.py:49
  77.5 10.7 %collective-permute-start.15 = (f32[64,512]{1,0:T(8,128)S(1)}, f32[64,512]{1,0:T(8,128)S(1)}, u32[]{:S(2)}, u32[]{:S(2)}) collective-permute-start(f32[64,512]{1,0:T(8,128)S(1)} %add.220), channel_id=1, source_target_pairs={{0,4},{1,5},{2,6},{3,7},{4,0},{5,1},{6,2},{7,3},{8,12},{9,13},{10,... | collective-permute-start | bytes 393224 | tf_op jit(solution)/shard_map/ppermute | solution.py:49
  84.6 8.1 %collective-permute-start.21 = (f32[64,512]{1,0:T(8,128)S(1)}, f32[64,512]{1,0:T(8,128)S(1)}, u32[]{:S(2)}, u32[]{:S(2)}) collective-permute-start(f32[64,512]{1,0:T(8,128)S(1)} %add.228), channel_id=1, source_target_pairs={{0,2},{1,3},{2,0},{3,1},{4,6},{5,7},{6,4},{7,5},{8,10},{9,11},{10,... | collective-permute-start | bytes 393224 | tf_op jit(solution)/shard_map/ppermute | solution.py:49
  84.7 8.1 %collective-permute-start.27 = (f32[64,512]{1,0:T(8,128)S(1)}, f32[64,512]{1,0:T(8,128)S(1)}, u32[]{:S(2)}, u32[]{:S(2)}) collective-permute-start(f32[64,512]{1,0:T(8,128)S(1)} %add.236), channel_id=1, source_target_pairs={{0,8},{8,0},{16,24},{24,16},{1,9},{9,1},{17,25},{25,17},{2,10},{10... | collective-permute-start | bytes 393224 | tf_op jit(solution)/shard_map/ppermute | solution.py:49
  88.3 5.2 %collective-permute-start.16 = (bf16[64,512]{1,0:T(8,128)(2,1)S(1)}, bf16[64,512]{1,0:T(8,128)(2,1)S(1)}, u32[]{:S(2)}, u32[]{:S(2)}) collective-permute-start(bf16[64,512]{1,0:T(8,128)(2,1)S(1)} %add_convert_fusion.2), channel_id=1, source_target_pairs={{0,8},{8,0},{16,24},{24,16},{1,9},{9,1},{17,25},{25,17},{2,10},{10... | collective-permute-start | bytes 196616 | tf_op jit(solution)/shard_map/ppermute | solution.py:56
  93.5 5.7 %collective-permute-start.17 = (bf16[128,512]{1,0:T(8,128)(2,1)S(1)}, bf16[128,512]{1,0:T(8,128)(2,1)S(1)}, u32[]{:S(2)}, u32[]{:S(2)}) collective-permute-start(bf16[128,512]{1,0:T(8,128)(2,1)S(1)} %pad_maximum_fusion.10), channel_id=1, source_target_pairs={{0,2},{1,3},{2,0},{3,1},{4,6},{5,7},{6,4},{7,5},{8,10},{9,11},{10,... | collective-permute-start | bytes 393224 | tf_op jit(solution)/shard_map/ppermute | solution.py:56
  101.7 10.9 %collective-permute-start.30 = (bf16[768,512]{1,0:T(8,128)(2,1)S(1)}, bf16[768,512]{1,0:T(8,128)(2,1)S(1)}, u32[]{:S(2)}, u32[]{:S(2)}) collective-permute-start(bf16[768,512]{1,0:T(8,128)(2,1)S(1)} %select_dynamic-update-slice_fusion), channel_id=1, source_target_pairs={{0,1},{1,0},{2,3},{3,2},{4,5},{5,4},{6,7},{7,6},{8,9},{9,8},{10,11... | collective-permute-start | bytes 2359304 | tf_op jit(solution)/shard_map/ppermute | solution.py:77
  (32 other events, 82.8 us)

commit v8 on v7

--- a/solution.py
+++ b/solution.py
@@ -122,6 +122,21 @@
     return jnp.concatenate(before + [cells] + after, axis=dim)
 
 
+def split_exact(values):
+    high = lax.reduce_precision(values, exponent_bits=8, mantissa_bits=7)
+    rest = values - high
+    middle = lax.reduce_precision(rest, exponent_bits=8, mantissa_bits=7)
+    low = rest - middle
+    parts = [high, middle, low]
+    return jnp.concatenate([p.astype(jnp.bfloat16) for p in parts], axis=-1)
+
+
+def join_exact(parts):
+    width = parts.shape[-1] // 3
+    pieces = [parts[..., k * width : (k + 1) * width].astype(jnp.float32) for k in range(3)]
+    return (pieces[0] + pieces[1]) + pieces[2]
+
+
 def surround(cells, width):
     return widen(widen(cells, "rows", 0, width), "cols", 1, width)
 
@@ -190,11 +205,13 @@
             hidden_start,
             cotangent[0],
             cotangent[1],
+            split_exact(cell_start),
         ],
         axis=-1,
     )
     pack = surround(pack, reach)
-    cell_zero = surround(cell_start, reach - 1)
+    cell_zero = inner(join_exact(pack[..., 2 * CI + 3 * HC :]), reach, reach - 1)
+    pack = pack[..., : 2 * CI + 3 * HC]
     inputs_one = pack[..., :CI]
     inputs_two = pack[..., CI : 2 * CI]
     hidden_zero = pack[..., 2 * CI : 2 * CI + HC]

time: 116 us -> 105 us (0.905)
  starting transfers between devices: 64.1 us -> 54.8 us
  local copies, waits for them, and re-layouts: 13.9 us -> 10.3 us
  waiting for transfers between devices: 15 us -> 16.7 us
    ppermute x4 -> x2, starting transfers between devices: 18.3 us -> 9.47 us  [widen(): lax.ppermute(tail, axis, [(i, i + dist) for i in range(count - dist)])]
    ppermute x6, starting transfers between devices: 12.9 us -> 16.2 us  [halve(): part = keep + lax.ppermute(send, axis, flip_pairs(axis, bit))]
    ppermute x4 -> x2, waiting for transfers between devices: 2.74 us -> 5.99 us  [widen(): lax.ppermute(head, axis, [(i + dist, i) for i in range(count - dist)])]
    ppermute x4 -> x2, starting transfers between devices: 6.41 us -> 3.21 us  [widen(): lax.ppermute(head, axis, [(i + dist, i) for i in range(count - dist)])]
    ppermute x6, waiting for transfers between devices: 6 us -> 4.3 us  [halve(): part = part + lax.ppermute(part, axis, flip_pairs(axis, bit))]
    unnamed x55 -> x43, local copies, waits for them, and re-layouts: 4.05 us -> 2.35 us
    concatenate x2 -> x1, other arithmetic: 1.8 us -> 0.19 us  [shards(): jnp.concatenate([inner(inputs_two, reach, reach - 1), hidden_one], axis=-1)]
    concatenate x4, local copies, waits for them, and re-layouts: 1.95 us -> 0.42 us  [shards(): jnp.concatenate([patches, jnp.ones((cells, 1), patches.dtype), jnp.zeros(...]
  transfers between devices with their start and end apart: 31 -> 27, of which waited for: 12 -> 10; matrix products, arithmetic and copies ran while one was open for 16% -> 15% of each run, Pallas kernels for 0% -> 0%
where the time goes in v8:
time: 105 us; the launch traced here: 104 us
  starting transfers between devices  54.8 us (52%)
  waiting for transfers between devices  16.7 us (16%)
  other arithmetic  14.9 us (14%)
  local copies, waits for them, and re-layouts  10.3 us (10%)
  matrix products  5.95 us (6%)
  between operations  1.53 us (1%)
    ppermute x6, starting transfers between devices, halve(): part = keep + lax.ppermute(send, axis, flip_pairs(axis, bit))  16.2 us
    ppermute x6, starting transfers between devices, halve(): part = part + lax.ppermute(part, axis, flip_pairs(axis, bit))  11.7 us
    ppermute x2, starting transfers between devices, widen(): lax.ppermute(tail, axis, [(i, i + dist) for i in range(count - dist)])  9.47 us
    ppermute x1, starting transfers between devices, sum_everywhere(): got = lax.ppermute(piece, axis, flip_pairs(axis, bit))  7.01 us
    ppermute x6, starting transfers between devices, double(): got = lax.ppermute(piece, axis, flip_pairs(axis, bit))  6.44 us
    ppermute x2, waiting for transfers between devices, widen(): lax.ppermute(head, axis, [(i + dist, i) for i in range(count - dist)])  5.99 us
    ppermute x6, waiting for transfers between devices, halve(): part = part + lax.ppermute(part, axis, flip_pairs(axis, bit))  4.3 us
    conv_general_dilated x4, matrix products, convolve(): lax.conv_general_dilated(field[None], weights, (1, 1), 'VALID', dimension...  4.23 us
  transfers between devices with their start and end apart: 27, of which 10 were waited for; matrix products, arithmetic and copies ran while one was open for 15% of the time, Pallas kernels for 0%

profile of v8, /device:TPU:1, one launch (start us, length us, event | category | flops | bytes accessed | tf_op | source)
XLA Modules:
  0.0 104.2 jit_solution(18289516262032452003)
XLA Ops:
  4.2 1.3 %collective-permute-start.1 = (bf16[4,32,832]{2,1,0:T(8,128)(2,1)S(1)}, bf16[4,32,832]{2,1,0:T(8,128)(2,1)S(1)}, u32[]{:S(2)}, u32[]{:S(2)}) collective-permute-start(bf16[4,32,832]{2,1,0:T(8,128)(2,1)S(1)} %concatenate.104), channel_id=1, source_target_pairs={{8,0},{16,8},{24,16},{9,1},{17,9},{25,17},{10,2},{18,10},{26,18},{... | collective-permute-start | bytes 638984 | tf_op jit(solution)/shard_map/ppermute | solution.py:114
  5.5 4.6 %collective-permute-start = (bf16[4,32,832]{2,1,0:T(8,128)(2,1)S(1)}, bf16[4,32,832]{2,1,0:T(8,128)(2,1)S(1)}, u32[]{:S(2)}, u32[]{:S(2)}) collective-permute-start(bf16[4,32,832]{2,1,0:T(8,128)(2,1)S(1)} %concatenate.104), channel_id=1, source_target_pairs={{0,8},{8,16},{16,24},{1,9},{9,17},{17,25},{2,10},{10,18},{18,26},{... | collective-permute-start | bytes 638984 | tf_op jit(solution)/shard_map/ppermute | solution.py:113
  10.8 2.6 %collective-permute-done.1 = bf16[4,32,832]{2,1,0:T(8,128)(2,1)S(1)} collective-permute-done((bf16[4,32,832]{2,1,0:T(8,128)(2,1)S(1)}, bf16[4,32,832]{2,1,0:T(8,128)(2,1)S(1)}, u32[]{:S(2)}, u32[]{:S(2)}) %collective-permute-start.1) | collective-permute-done | bytes 213024 | tf_op jit(solution)/shard_map/ppermute | solution.py:114
  14.4 4.9 %collective-permute-start.2 = (bf16[12,4,832]{2,1,0:T(4,128)(2,1)S(1)}, bf16[12,4,832]{2,1,0:T(4,128)(2,1)S(1)}, u32[]{:S(2)}, u32[]{:S(2)}) collective-permute-start(bf16[12,4,832]{2,1,0:T(4,128)(2,1)S(1)} %get-tuple-element.30), channel_id=1, source_target_pairs={{0,1},{1,2},{2,3},{3,4},{4,5},{5,6},{6,7},{8,9},{9,10},{10,11},{11... | collective-permute-start | bytes 239624 | tf_op jit(solution)/shard_map/ppermute | solution.py:113
  19.2 1.9 %collective-permute-start.3 = (bf16[12,4,832]{2,1,0:T(4,128)(2,1)S(1)}, bf16[12,4,832]{2,1,0:T(4,128)(2,1)S(1)}, u32[]{:S(2)}, u32[]{:S(2)}) collective-permute-start(bf16[12,4,832]{2,1,0:T(4,128)(2,1)S(1)} %get-tuple-element.31), channel_id=1, source_target_pairs={{1,0},{2,1},{3,2},{4,3},{5,4},{6,5},{7,6},{9,8},{10,9},{11,10},{12... | collective-permute-start | bytes 239624 | tf_op jit(solution)/shard_map/ppermute | solution.py:114
  21.7 3.4 %collective-permute-done.3 = bf16[12,4,832]{2,1,0:T(4,128)(2,1)S(1)} collective-permute-done((bf16[12,4,832]{2,1,0:T(4,128)(2,1)S(1)}, bf16[12,4,832]{2,1,0:T(4,128)(2,1)S(1)}, u32[]{:S(2)}, u32[]{:S(2)}) %collective-permute-start.3) | collective-permute-done | bytes 79904 | tf_op jit(solution)/shard_map/ppermute | solution.py:114
  32.6 2.1 %convolution_select_fusion.1 = f32[8,8,5,512]{3,1,2,0:T(8,128)S(1)} fusion(bf16[3,3,160,512]{3,2,1,0:T(8,128)(2,1)} %bitcast.88, pred[8,5]{0,1:T(8,128)(4,1)S(1)} %copy-done.18, bf16[10,1,7,2,160]{4,2,3,0,1:T(8,128)(2,1)S(1)} %slice.371, bf16[10,1,8,5,160]{4,2,3,0,1:T(8,128)(2,1)S(1)} %copy.16), kind=kOutput, calls=%fused_computation.7 | convolution fusion | flops 472560640 | bytes 2302760 | tf_op jit(solution)/shard_map/conv_general_dilated | solution.py:161
  43.4 1.7 %convolution_multiply_fusion = f32[768,512]{1,0:T(8,128)S(1)} fusion(s32[]{:T(128)S(6)} %select_n.147, bf16[128,1536]{1,0:T(8,128)(2,1)S(1)} %concatenate.120, bf16[128,1536]{1,0:T(8,128)(2,1)S(1)} %concatenate.122, bf16[128,1536]{1,0:T(8,128)(2,1)S(1)} %concatenate.124, bf16[128,1536]{1,0:T(8,128)(2,1)S(1)} %concatenate.126, ...), kind=kOutput, calls=%fused_computation.4 | convolution fusion | flops 408289280 | bytes 3670020 | tf_op jit(solution)/shard_map/dot_general | solution.py:282
  45.3 1.4 %collective-permute-start.8 = (f32[128,512]{1,0:T(8,128)S(1)}, f32[128,512]{1,0:T(8,128)S(1)}, u32[]{:S(2)}, u32[]{:S(2)}) collective-permute-start(f32[128,512]{1,0:T(8,128)S(1)} %constant_dynamic-slice_fusion.5), channel_id=1, source_target_pairs={{0,2},{1,3},{2,0},{3,1},{4,6},{5,7},{6,4},{7,5},{8,10},{9,11},{10,... | collective-permute-start | bytes 786440 | tf_op jit(solution)/shard_map/ppermute | solution.py:46
  46.8 3.1 %collective-permute-start.14 = (f32[128,512]{1,0:T(8,128)S(1)}, f32[128,512]{1,0:T(8,128)S(1)}, u32[]{:S(2)}, u32[]{:S(2)}) collective-permute-start(f32[128,512]{1,0:T(8,128)S(1)} %constant_dynamic-slice_fusion.3), channel_id=1, source_target_pairs={{0,8},{8,0},{16,24},{24,16},{1,9},{9,1},{17,25},{25,17},{2,10},{10... | collective-permute-start | bytes 786440 | tf_op jit(solution)/shard_map/ppermute | solution.py:46
  49.9 3.2 %collective-permute-start.20 = (f32[128,512]{1,0:T(8,128)S(1)}, f32[128,512]{1,0:T(8,128)S(1)}, u32[]{:S(2)}, u32[]{:S(2)}) collective-permute-start(f32[128,512]{1,0:T(8,128)S(1)} %constant_dynamic-slice_fusion.1), channel_id=1, source_target_pairs={{0,16},{8,24},{16,0},{24,8},{1,17},{9,25},{17,1},{25,9},{2,18},{10... | collective-permute-start | bytes 786440 | tf_op jit(solution)/shard_map/ppermute | solution.py:46
  53.2 3.0 %collective-permute-start.9 = (f32[64,512]{1,0:T(8,128)S(1)}, f32[64,512]{1,0:T(8,128)S(1)}, u32[]{:S(2)}, u32[]{:S(2)}) collective-permute-start(f32[64,512]{1,0:T(8,128)S(1)} %constant_dynamic-slice_fusion.4), channel_id=1, source_target_pairs={{0,8},{8,0},{16,24},{24,16},{1,9},{9,1},{17,25},{25,17},{2,10},{10... | collective-permute-start | bytes 393224 | tf_op jit(solution)/shard_map/ppermute | solution.py:46
  56.2 3.2 %collective-permute-start.15 = (f32[64,512]{1,0:T(8,128)S(1)}, f32[64,512]{1,0:T(8,128)S(1)}, u32[]{:S(2)}, u32[]{:S(2)}) collective-permute-start(f32[64,512]{1,0:T(8,128)S(1)} %constant_dynamic-slice_fusion.2), channel_id=1, source_target_pairs={{0,16},{8,24},{16,0},{24,8},{1,17},{9,25},{17,1},{25,9},{2,18},{10... | collective-permute-start | bytes 393224 | tf_op jit(solution)/shard_map/ppermute | solution.py:46
  59.5 2.4 %collective-permute-start.21 = (f32[64,512]{1,0:T(8,128)S(1)}, f32[64,512]{1,0:T(8,128)S(1)}, u32[]{:S(2)}, u32[]{:S(2)}) collective-permute-start(f32[64,512]{1,0:T(8,128)S(1)} %constant_dynamic-slice_fusion), channel_id=1, source_target_pairs={{0,4},{1,5},{2,6},{3,7},{4,0},{5,1},{6,2},{7,3},{8,12},{9,13},{10,... | collective-permute-start | bytes 393224 | tf_op jit(solution)/shard_map/ppermute | solution.py:46
  62.1 2.3 %collective-permute-start.16 = (f32[64,512]{1,0:T(8,128)S(1)}, f32[64,512]{1,0:T(8,128)S(1)}, u32[]{:S(2)}, u32[]{:S(2)}) collective-permute-start(f32[64,512]{1,0:T(8,128)S(1)} %dynamic-slice_add_fusion.4), channel_id=1, source_target_pairs={{0,4},{1,5},{2,6},{3,7},{4,0},{5,1},{6,2},{7,3},{8,12},{9,13},{10,... | collective-permute-start | bytes 393224 | tf_op jit(solution)/shard_map/ppermute | solution.py:49
  64.4 1.8 %collective-permute-done.21 = f32[64,512]{1,0:T(8,128)S(1)} collective-permute-done((f32[64,512]{1,0:T(8,128)S(1)}, f32[64,512]{1,0:T(8,128)S(1)}, u32[]{:S(2)}, u32[]{:S(2)}) %collective-permute-start.21) | collective-permute-done | bytes 131104 | tf_op jit(solution)/shard_map/ppermute | solution.py:46
  66.4 5.6 %collective-permute-start.11 = (f32[64,512]{1,0:T(8,128)S(1)}, f32[64,512]{1,0:T(8,128)S(1)}, u32[]{:S(2)}, u32[]{:S(2)}) collective-permute-start(f32[64,512]{1,0:T(8,128)S(1)} %add.228), channel_id=1, source_target_pairs={{0,4},{1,5},{2,6},{3,7},{4,0},{5,1},{6,2},{7,3},{8,12},{9,13},{10,... | collective-permute-start | bytes 393224 | tf_op jit(solution)/shard_map/ppermute | solution.py:49
  73.4 3.5 %collective-permute-start.23 = (f32[64,512]{1,0:T(8,128)S(1)}, f32[64,512]{1,0:T(8,128)S(1)}, u32[]{:S(2)}, u32[]{:S(2)}) collective-permute-start(f32[64,512]{1,0:T(8,128)S(1)} %add.244), channel_id=1, source_target_pairs={{0,8},{8,0},{16,24},{24,16},{1,9},{9,1},{17,25},{25,17},{2,10},{10... | collective-permute-start | bytes 393224 | tf_op jit(solution)/shard_map/ppermute | solution.py:49
  78.2 3.2 %collective-permute-done.17 = f32[64,512]{1,0:T(8,128)S(1)} collective-permute-done((f32[64,512]{1,0:T(8,128)S(1)}, f32[64,512]{1,0:T(8,128)S(1)}, u32[]{:S(2)}, u32[]{:S(2)}) %collective-permute-start.17) | collective-permute-done | bytes 131104 | tf_op jit(solution)/shard_map/ppermute | solution.py:49
  82.5 2.3 %collective-permute-start.13 = (bf16[128,512]{1,0:T(8,128)(2,1)S(1)}, bf16[128,512]{1,0:T(8,128)(2,1)S(1)}, u32[]{:S(2)}, u32[]{:S(2)}) collective-permute-start(bf16[128,512]{1,0:T(8,128)(2,1)S(1)} %pad_maximum_fusion.8), channel_id=1, source_target_pairs={{0,2},{1,3},{2,0},{3,1},{4,6},{5,7},{6,4},{7,5},{8,10},{9,11},{10,... | collective-permute-start | bytes 393224 | tf_op jit(solution)/shard_map/ppermute | solution.py:56
  88.8 2.0 %collective-permute-done.25 = bf16[128,512]{1,0:T(8,128)(2,1)S(1)} collective-permute-done((bf16[128,512]{1,0:T(8,128)(2,1)S(1)}, bf16[128,512]{1,0:T(8,128)(2,1)S(1)}, u32[]{:S(2)}, u32[]{:S(2)}) %collective-permute-start.25) | collective-permute-done | bytes 131104 | tf_op jit(solution)/shard_map/ppermute | solution.py:56
  90.9 7.0 %collective-permute-start.26 = (bf16[768,512]{1,0:T(8,128)(2,1)S(1)}, bf16[768,512]{1,0:T(8,128)(2,1)S(1)}, u32[]{:S(2)}, u32[]{:S(2)}) collective-permute-start(bf16[768,512]{1,0:T(8,128)(2,1)S(1)} %select_dynamic-update-slice_fusion), channel_id=1, source_target_pairs={{0,1},{1,0},{2,3},{3,2},{4,5},{5,4},{6,7},{7,6},{8,9},{9,8},{10,11... | collective-permute-start | bytes 2359304 | tf_op jit(solution)/shard_map/ppermute | solution.py:77
  99.1 1.5 %fusion.99 = bf16[4,32,128]{2,1,0:T(8,128)(2,1)} fusion(f32[8,36,128]{2,1,0:T(8,128)S(1)} %get-tuple-element.16, f32[8,36,128]{2,1,0:T(8,128)} %get-tuple-element.36), kind=kLoop, calls=%fused_computation.196 | loop fusion | flops 32768 | bytes 163840 | tf_op jit(solution)/shard_map/convert_element_type | solution.py:175
  102.1 2.0 %maximum_convert_fusion = f32[1440,512]{1,0:T(8,128)} fusion(bf16[672,512]{1,0:T(8,128)(2,1)S(1)} %slice.446, bf16[768,512]{1,0:T(8,128)(2,1)S(1)} %get-tuple-element.19), kind=kLoop, calls=%fused_computation.5 | loop fusion | flops 2949120 | bytes 4423680 | tf_op jit(solution)/shard_map/convert_element_type | solution.py:81
  (187 shorter events, 32.7 us)
Async XLA Ops:
  4.2 9.3 %collective-permute-start.1 = (bf16[4,32,832]{2,1,0:T(8,128)(2,1)S(1)}, bf16[4,32,832]{2,1,0:T(8,128)(2,1)S(1)}, u32[]{:S(2)}, u32[]{:S(2)}) collective-permute-start(bf16[4,32,832]{2,1,0:T(8,128)(2,1)S(1)} %concatenate.104), channel_id=1, source_target_pairs={{8,0},{16,8},{24,16},{9,1},{17,9},{25,17},{10,2},{18,10},{26,18},{... | collective-permute-start | bytes 638984 | tf_op jit(solution)/shard_map/ppermute | solution.py:114
  5.5 8.8 %collective-permute-start = (bf16[4,32,832]{2,1,0:T(8,128)(2,1)S(1)}, bf16[4,32,832]{2,1,0:T(8,128)(2,1)S(1)}, u32[]{:S(2)}, u32[]{:S(2)}) collective-permute-start(bf16[4,32,832]{2,1,0:T(8,128)(2,1)S(1)} %concatenate.104), channel_id=1, source_target_pairs={{0,8},{8,16},{16,24},{1,9},{9,17},{17,25},{2,10},{10,18},{18,26},{... | collective-permute-start | bytes 638984 | tf_op jit(solution)/shard_map/ppermute | solution.py:113
  14.4 7.3 %collective-permute-start.2 = (bf16[12,4,832]{2,1,0:T(4,128)(2,1)S(1)}, bf16[12,4,832]{2,1,0:T(4,128)(2,1)S(1)}, u32[]{:S(2)}, u32[]{:S(2)}) collective-permute-start(bf16[12,4,832]{2,1,0:T(4,128)(2,1)S(1)} %get-tuple-element.30), channel_id=1, source_target_pairs={{0,1},{1,2},{2,3},{3,4},{4,5},{5,6},{6,7},{8,9},{9,10},{10,11},{11... | collective-permute-start | bytes 239624 | tf_op jit(solution)/shard_map/ppermute | solution.py:113
  19.2 5.8 %collective-permute-start.3 = (bf16[12,4,832]{2,1,0:T(4,128)(2,1)S(1)}, bf16[12,4,832]{2,1,0:T(4,128)(2,1)S(1)}, u32[]{:S(2)}, u32[]{:S(2)}) collective-permute-start(bf16[12,4,832]{2,1,0:T(4,128)(2,1)S(1)} %get-tuple-element.31), channel_id=1, source_target_pairs={{1,0},{2,1},{3,2},{4,3},{5,4},{6,5},{7,6},{9,8},{10,9},{11,10},{12... | collective-permute-start | bytes 239624 | tf_op jit(solution)/shard_map/ppermute | solution.py:114
  31.9 10.7 %collective-permute-start.5 = (bf16[6,34,160]{2,1,0:T(8,128)(2,1)}, bf16[6,34,160]{2,1,0:T(8,128)(2,1)S(1)}, u32[]{:S(2)}, u32[]{:S(2)}) collective-permute-start(bf16[6,34,160]{2,1,0:T(8,128)(2,1)} %fusion.82), channel_id=1, source_target_pairs={{0,1},{1,0},{2,3},{3,2},{4,5},{5,4},{6,7},{7,6},{8,9},{9,8},{10,11... | collective-permute-start | bytes 195848 | tf_op jit(solution)/shard_map/ppermute | solution.py:263
  31.9 11.1 %collective-permute-start.4 = (bf16[6,34,160]{2,1,0:T(8,128)(2,1)}, bf16[6,34,160]{2,1,0:T(8,128)(2,1)S(1)}, u32[]{:S(2)}, u32[]{:S(2)}) collective-permute-start(bf16[6,34,160]{2,1,0:T(8,128)(2,1)} %slice.422), channel_id=1, source_target_pairs={{0,1},{1,0},{2,3},{3,2},{4,5},{5,4},{6,7},{7,6},{8,9},{9,8},{10,11... | collective-permute-start | bytes 195848 | tf_op jit(solution)/shard_map/ppermute | solution.py:263
  37.3 6.1 %collective-permute-start.6 = (bf16[128,512]{1,0:T(8,128)(2,1)}, bf16[128,512]{1,0:T(8,128)(2,1)}, u32[]{:S(2)}, u32[]{:S(2)}) collective-permute-start(bf16[128,512]{1,0:T(8,128)(2,1)} %bitcast.32), channel_id=1, source_target_pairs={{0,1},{1,0},{2,3},{3,2},{4,5},{5,4},{6,7},{7,6},{8,9},{9,8},{10,11... | collective-permute-start | bytes 393224 | tf_op jit(solution)/shard_map/ppermute | solution.py:264
  45.3 7.7 %collective-permute-start.8 = (f32[128,512]{1,0:T(8,128)S(1)}, f32[128,512]{1,0:T(8,128)S(1)}, u32[]{:S(2)}, u32[]{:S(2)}) collective-permute-start(f32[128,512]{1,0:T(8,128)S(1)} %constant_dynamic-slice_fusion.5), channel_id=1, source_target_pairs={{0,2},{1,3},{2,0},{3,1},{4,6},{5,7},{6,4},{7,5},{8,10},{9,11},{10,... | collective-permute-start | bytes 786440 | tf_op jit(solution)/shard_map/ppermute | solution.py:46
  46.8 9.4 %collective-permute-start.14 = (f32[128,512]{1,0:T(8,128)S(1)}, f32[128,512]{1,0:T(8,128)S(1)}, u32[]{:S(2)}, u32[]{:S(2)}) collective-permute-start(f32[128,512]{1,0:T(8,128)S(1)} %constant_dynamic-slice_fusion.3), channel_id=1, source_target_pairs={{0,8},{8,0},{16,24},{24,16},{1,9},{9,1},{17,25},{25,17},{2,10},{10... | collective-permute-start | bytes 786440 | tf_op jit(solution)/shard_map/ppermute | solution.py:46
  49.9 9.5 %collective-permute-start.20 = (f32[128,512]{1,0:T(8,128)S(1)}, f32[128,512]{1,0:T(8,128)S(1)}, u32[]{:S(2)}, u32[]{:S(2)}) collective-permute-start(f32[128,512]{1,0:T(8,128)S(1)} %constant_dynamic-slice_fusion.1), channel_id=1, source_target_pairs={{0,16},{8,24},{16,0},{24,8},{1,17},{9,25},{17,1},{25,9},{2,18},{10... | collective-permute-start | bytes 786440 | tf_op jit(solution)/shard_map/ppermute | solution.py:46
  53.2 8.7 %collective-permute-start.9 = (f32[64,512]{1,0:T(8,128)S(1)}, f32[64,512]{1,0:T(8,128)S(1)}, u32[]{:S(2)}, u32[]{:S(2)}) collective-permute-start(f32[64,512]{1,0:T(8,128)S(1)} %constant_dynamic-slice_fusion.4), channel_id=1, source_target_pairs={{0,8},{8,0},{16,24},{24,16},{1,9},{9,1},{17,25},{25,17},{2,10},{10... | collective-permute-start | bytes 393224 | tf_op jit(solution)/shard_map/ppermute | solution.py:46
  56.2 5.8 %collective-permute-start.15 = (f32[64,512]{1,0:T(8,128)S(1)}, f32[64,512]{1,0:T(8,128)S(1)}, u32[]{:S(2)}, u32[]{:S(2)}) collective-permute-start(f32[64,512]{1,0:T(8,128)S(1)} %constant_dynamic-slice_fusion.2), channel_id=1, source_target_pairs={{0,16},{8,24},{16,0},{24,8},{1,17},{9,25},{17,1},{25,9},{2,18},{10... | collective-permute-start | bytes 393224 | tf_op jit(solution)/shard_map/ppermute | solution.py:46
  59.5 6.7 %collective-permute-start.21 = (f32[64,512]{1,0:T(8,128)S(1)}, f32[64,512]{1,0:T(8,128)S(1)}, u32[]{:S(2)}, u32[]{:S(2)}) collective-permute-start(f32[64,512]{1,0:T(8,128)S(1)} %constant_dynamic-slice_fusion), channel_id=1, source_target_pairs={{0,4},{1,5},{2,6},{3,7},{4,0},{5,1},{6,2},{7,3},{8,12},{9,13},{10,... | collective-permute-start | bytes 393224 | tf_op jit(solution)/shard_map/ppermute | solution.py:46
  61.9 4.4 %collective-permute-start.10 = (f32[64,512]{1,0:T(8,128)S(1)}, f32[64,512]{1,0:T(8,128)S(1)}, u32[]{:S(2)}, u32[]{:S(2)}) collective-permute-start(f32[64,512]{1,0:T(8,128)S(1)} %dynamic-slice_add_fusion.5), channel_id=1, source_target_pairs={{0,16},{8,24},{16,0},{24,8},{1,17},{9,25},{17,1},{25,9},{2,18},{10... | collective-permute-start | bytes 393224 | tf_op jit(solution)/shard_map/ppermute | solution.py:49
  62.1 11.2 %collective-permute-start.16 = (f32[64,512]{1,0:T(8,128)S(1)}, f32[64,512]{1,0:T(8,128)S(1)}, u32[]{:S(2)}, u32[]{:S(2)}) collective-permute-start(f32[64,512]{1,0:T(8,128)S(1)} %dynamic-slice_add_fusion.4), channel_id=1, source_target_pairs={{0,4},{1,5},{2,6},{3,7},{4,0},{5,1},{6,2},{7,3},{8,12},{9,13},{10,... | collective-permute-start | bytes 393224 | tf_op jit(solution)/shard_map/ppermute | solution.py:49
  66.2 7.1 %collective-permute-start.22 = (f32[64,512]{1,0:T(8,128)S(1)}, f32[64,512]{1,0:T(8,128)S(1)}, u32[]{:S(2)}, u32[]{:S(2)}) collective-permute-start(f32[64,512]{1,0:T(8,128)S(1)} %dynamic-slice_add_fusion.3), channel_id=1, source_target_pairs={{0,2},{1,3},{2,0},{3,1},{4,6},{5,7},{6,4},{7,5},{8,10},{9,11},{10,... | collective-permute-start | bytes 393224 | tf_op jit(solution)/shard_map/ppermute | solution.py:49
  66.4 10.7 %collective-permute-start.11 = (f32[64,512]{1,0:T(8,128)S(1)}, f32[64,512]{1,0:T(8,128)S(1)}, u32[]{:S(2)}, u32[]{:S(2)}) collective-permute-start(f32[64,512]{1,0:T(8,128)S(1)} %add.228), channel_id=1, source_target_pairs={{0,4},{1,5},{2,6},{3,7},{4,0},{5,1},{6,2},{7,3},{8,12},{9,13},{10,... | collective-permute-start | bytes 393224 | tf_op jit(solution)/shard_map/ppermute | solution.py:49
  73.3 8.1 %collective-permute-start.17 = (f32[64,512]{1,0:T(8,128)S(1)}, f32[64,512]{1,0:T(8,128)S(1)}, u32[]{:S(2)}, u32[]{:S(2)}) collective-permute-start(f32[64,512]{1,0:T(8,128)S(1)} %add.236), channel_id=1, source_target_pairs={{0,2},{1,3},{2,0},{3,1},{4,6},{5,7},{6,4},{7,5},{8,10},{9,11},{10,... | collective-permute-start | bytes 393224 | tf_op jit(solution)/shard_map/ppermute | solution.py:49
  73.4 8.8 %collective-permute-start.23 = (f32[64,512]{1,0:T(8,128)S(1)}, f32[64,512]{1,0:T(8,128)S(1)}, u32[]{:S(2)}, u32[]{:S(2)}) collective-permute-start(f32[64,512]{1,0:T(8,128)S(1)} %add.244), channel_id=1, source_target_pairs={{0,8},{8,0},{16,24},{24,16},{1,9},{9,1},{17,25},{25,17},{2,10},{10... | collective-permute-start | bytes 393224 | tf_op jit(solution)/shard_map/ppermute | solution.py:49
  77.1 5.4 %collective-permute-start.12 = (bf16[64,512]{1,0:T(8,128)(2,1)S(1)}, bf16[64,512]{1,0:T(8,128)(2,1)S(1)}, u32[]{:S(2)}, u32[]{:S(2)}) collective-permute-start(bf16[64,512]{1,0:T(8,128)(2,1)S(1)} %add_convert_fusion.2), channel_id=1, source_target_pairs={{0,8},{8,0},{16,24},{24,16},{1,9},{9,1},{17,25},{25,17},{2,10},{10... | collective-permute-start | bytes 196616 | tf_op jit(solution)/shard_map/ppermute | solution.py:56
  82.2 4.7 %collective-permute-start.24 = (bf16[64,512]{1,0:T(8,128)(2,1)S(1)}, bf16[64,512]{1,0:T(8,128)(2,1)S(1)}, u32[]{:S(2)}, u32[]{:S(2)}) collective-permute-start(bf16[64,512]{1,0:T(8,128)(2,1)S(1)} %add_convert_fusion), channel_id=1, source_target_pairs={{0,4},{1,5},{2,6},{3,7},{4,0},{5,1},{6,2},{7,3},{8,12},{9,13},{10,... | collective-permute-start | bytes 196616 | tf_op jit(solution)/shard_map/ppermute | solution.py:56
  82.5 5.5 %collective-permute-start.13 = (bf16[128,512]{1,0:T(8,128)(2,1)S(1)}, bf16[128,512]{1,0:T(8,128)(2,1)S(1)}, u32[]{:S(2)}, u32[]{:S(2)}) collective-permute-start(bf16[128,512]{1,0:T(8,128)(2,1)S(1)} %pad_maximum_fusion.8), channel_id=1, source_target_pairs={{0,2},{1,3},{2,0},{3,1},{4,6},{5,7},{6,4},{7,5},{8,10},{9,11},{10,... | collective-permute-start | bytes 393224 | tf_op jit(solution)/shard_map/ppermute | solution.py:56
  84.9 3.9 %collective-permute-start.19 = (bf16[128,512]{1,0:T(8,128)(2,1)S(1)}, bf16[128,512]{1,0:T(8,128)(2,1)S(1)}, u32[]{:S(2)}, u32[]{:S(2)}) collective-permute-start(bf16[128,512]{1,0:T(8,128)(2,1)S(1)} %pad_maximum_fusion.9), channel_id=1, source_target_pairs={{0,8},{8,0},{16,24},{24,16},{1,9},{9,1},{17,25},{25,17},{2,10},{10... | collective-permute-start | bytes 393224 | tf_op jit(solution)/shard_map/ppermute | solution.py:56
  90.9 10.4 %collective-permute-start.26 = (bf16[768,512]{1,0:T(8,128)(2,1)S(1)}, bf16[768,512]{1,0:T(8,128)(2,1)S(1)}, u32[]{:S(2)}, u32[]{:S(2)}) collective-permute-start(bf16[768,512]{1,0:T(8,128)(2,1)S(1)} %select_dynamic-update-slice_fusion), channel_id=1, source_target_pairs={{0,1},{1,0},{2,3},{3,2},{4,5},{5,4},{6,7},{7,6},{8,9},{9,8},{10,11... | collective-permute-start | bytes 2359304 | tf_op jit(solution)/shard_map/ppermute | solution.py:77
  (23 other events, 71.3 us)

commit v9 on v8

--- a/solution.py
+++ b/solution.py
@@ -260,8 +260,9 @@
     axis, bit = first[0]
     pairs = flip_pairs(axis, bit)
     upper = (lax.axis_index(axis) >> bit) & 1
-    near = near + [lax.ppermute(s, axis, pairs) for s in near]
-    grads_seen = grads_seen + [lax.ppermute(g, axis, pairs) for g in grads_seen]
+    theirs = lax.ppermute(jnp.concatenate(near, axis=-1), axis, pairs)
+    near = near + [theirs[..., :chans], theirs[..., chans:]]
+    grads_seen = grads_seen + [lax.ppermute(jnp.concatenate(grads_seen, axis=0), axis, pairs)]
     lifted = []
     for stacked in near:
         patches = tap_columns(stacked, rows_dev, cols_dev, False)

time: 105 us -> 106 us (level)
  waiting for transfers between devices: 16.7 us -> 22.8 us
  starting transfers between devices: 54.8 us -> 49.5 us
  other arithmetic: 14.9 us -> 13.3 us
  local copies, waits for them, and re-layouts: 10.3 us -> 11.9 us
    ppermute x6, starting transfers between devices: 11.7 us -> 7.23 us  [halve(): part = part + lax.ppermute(part, axis, flip_pairs(axis, bit))]
    ppermute x6, waiting for transfers between devices: 4.3 us -> 8.56 us  [halve(): part = part + lax.ppermute(part, axis, flip_pairs(axis, bit))]
    convert_element_type x1 -> x0, other arithmetic: 1.52 us -> none  [cell_step(): hidden = (gate_out * jnp.tanh(cell)).astype(jnp.bfloat16)]
    concatenate x2, other arithmetic: 1.37 us -> 0.09 us  [cell_grads(): jnp.concatenate([pre_in, pre_forget, pre_cand, pre_out], axis=-1)]
    ppermute x1, starting transfers between devices: 7.01 us -> 5.83 us  [sum_everywhere(): got = lax.ppermute(piece, axis, flip_pairs(axis, bit))]
    ppermute x6, waiting for transfers between devices: 3.73 us -> 4.83 us  [double(): got = lax.ppermute(piece, axis, flip_pairs(axis, bit))]
    unnamed x43 -> x45, local copies, waits for them, and re-layouts: 2.35 us -> 3.01 us
  transfers between devices with their start and end apart: 27 -> 25, of which waited for: 10 -> 11; matrix products, arithmetic and copies ran while one was open for 15% -> 14% of each run, Pallas kernels for 0% -> 0%
where the time goes in v9:
time: 106 us; the launch traced here: 105 us
  starting transfers between devices  49.5 us (47%)
  waiting for transfers between devices  22.8 us (22%)
  other arithmetic  13.3 us (13%)
  local copies, waits for them, and re-layouts  11.9 us (11%)
  matrix products  5.81 us (5%)
  between operations  1.6 us (2%)
    ppermute x6, starting transfers between devices, halve(): part = keep + lax.ppermute(send, axis, flip_pairs(axis, bit))  16.3 us
    ppermute x2, starting transfers between devices, widen(): lax.ppermute(tail, axis, [(i, i + dist) for i in range(count - dist)])  9.47 us
    ppermute x6, waiting for transfers between devices, halve(): part = part + lax.ppermute(part, axis, flip_pairs(axis, bit))  8.56 us
    ppermute x6, starting transfers between devices, halve(): part = part + lax.ppermute(part, axis, flip_pairs(axis, bit))  7.23 us
    ppermute x6, starting transfers between devices, double(): got = lax.ppermute(piece, axis, flip_pairs(axis, bit))  6.95 us
    ppermute x2, waiting for transfers between devices, widen(): lax.ppermute(head, axis, [(i + dist, i) for i in range(count - dist)])  6.49 us
    ppermute x1, starting transfers between devices, sum_everywhere(): got = lax.ppermute(piece, axis, flip_pairs(axis, bit))  5.83 us
    ppermute x6, waiting for transfers between devices, double(): got = lax.ppermute(piece, axis, flip_pairs(axis, bit))  4.83 us
  transfers between devices with their start and end apart: 25, of which 11 were waited for; matrix products, arithmetic and copies ran while one was open for 14% of the time, Pallas kernels for 0%

profile of v9, /device:TPU:1, one launch (start us, length us, event | category | flops | bytes accessed | tf_op | source)
XLA Modules:
  0.0 104.9 jit_solution(10719784817610747614)
XLA Ops:
  5.5 4.6 %collective-permute-start = (bf16[4,32,832]{2,1,0:T(8,128)(2,1)S(1)}, bf16[4,32,832]{2,1,0:T(8,128)(2,1)S(1)}, u32[]{:S(2)}, u32[]{:S(2)}) collective-permute-start(bf16[4,32,832]{2,1,0:T(8,128)(2,1)S(1)} %concatenate.110), channel_id=1, source_target_pairs={{0,8},{8,16},{16,24},{1,9},{9,17},{17,25},{2,10},{10,18},{18,26},{... | collective-permute-start | bytes 638984 | tf_op jit(solution)/shard_map/ppermute | solution.py:113
  10.3 3.1 %collective-permute-done.1 = bf16[4,32,832]{2,1,0:T(8,128)(2,1)S(1)} collective-permute-done((bf16[4,32,832]{2,1,0:T(8,128)(2,1)S(1)}, bf16[4,32,832]{2,1,0:T(8,128)(2,1)S(1)}, u32[]{:S(2)}, u32[]{:S(2)}) %collective-permute-start.1) | collective-permute-done | bytes 213024 | tf_op jit(solution)/shard_map/ppermute | solution.py:114
  14.4 4.9 %collective-permute-start.2 = (bf16[12,4,832]{2,1,0:T(4,128)(2,1)S(1)}, bf16[12,4,832]{2,1,0:T(4,128)(2,1)S(1)}, u32[]{:S(2)}, u32[]{:S(2)}) collective-permute-start(bf16[12,4,832]{2,1,0:T(4,128)(2,1)S(1)} %get-tuple-element.30), channel_id=1, source_target_pairs={{0,1},{1,2},{2,3},{3,4},{4,5},{5,6},{6,7},{8,9},{9,10},{10,11},{11... | collective-permute-start | bytes 239624 | tf_op jit(solution)/shard_map/ppermute | solution.py:113
  19.2 1.9 %collective-permute-start.3 = (bf16[12,4,832]{2,1,0:T(4,128)(2,1)S(1)}, bf16[12,4,832]{2,1,0:T(4,128)(2,1)S(1)}, u32[]{:S(2)}, u32[]{:S(2)}) collective-permute-start(bf16[12,4,832]{2,1,0:T(4,128)(2,1)S(1)} %get-tuple-element.31), channel_id=1, source_target_pairs={{1,0},{2,1},{3,2},{4,3},{5,4},{6,5},{7,6},{9,8},{10,9},{11,10},{12... | collective-permute-start | bytes 239624 | tf_op jit(solution)/shard_map/ppermute | solution.py:114
  21.7 3.4 %collective-permute-done.3 = bf16[12,4,832]{2,1,0:T(4,128)(2,1)S(1)} collective-permute-done((bf16[12,4,832]{2,1,0:T(4,128)(2,1)S(1)}, bf16[12,4,832]{2,1,0:T(4,128)(2,1)S(1)}, u32[]{:S(2)}, u32[]{:S(2)}) %collective-permute-start.3) | collective-permute-done | bytes 79904 | tf_op jit(solution)/shard_map/ppermute | solution.py:114
  32.3 2.1 %convolution_select_fusion.1 = f32[8,8,5,512]{3,1,2,0:T(8,128)S(1)} fusion(bf16[3,3,160,512]{3,2,1,0:T(8,128)(2,1)} %bitcast.92, pred[8,5]{0,1:T(8,128)(4,1)S(1)} %copy-done.19, bf16[10,1,7,2,160]{4,2,3,0,1:T(8,128)(2,1)S(1)} %slice.391, bf16[10,1,8,5,160]{4,2,3,0,1:T(8,128)(2,1)S(1)} %copy.16), kind=kOutput, calls=%fused_computation.7 | convolution fusion | flops 472560640 | bytes 2302760 | tf_op jit(solution)/shard_map/conv_general_dilated | solution.py:161
  44.5 1.6 %convolution_multiply_fusion = f32[768,512]{1,0:T(8,128)S(1)} fusion(s32[]{:T(128)S(6)} %select_n.147, bf16[128,1536]{1,0:T(8,128)(2,1)S(1)} %concatenate.126, bf16[128,1536]{1,0:T(8,128)(2,1)S(1)} %concatenate.128, bf16[128,1536]{1,0:T(8,128)(2,1)S(1)} %concatenate.131, bf16[128,1536]{1,0:T(8,128)(2,1)S(1)} %concatenate.133, ...), kind=kOutput, calls=%fused_computation.4 | convolution fusion | flops 407764992 | bytes 3670020 | tf_op jit(solution)/shard_map/dot_general | solution.py:283
  47.6 3.1 %collective-permute-start.12 = (f32[128,512]{1,0:T(8,128)S(1)}, f32[128,512]{1,0:T(8,128)S(1)}, u32[]{:S(2)}, u32[]{:S(2)}) collective-permute-start(f32[128,512]{1,0:T(8,128)S(1)} %constant_dynamic-slice_fusion.3), channel_id=1, source_target_pairs={{0,8},{8,0},{16,24},{24,16},{1,9},{9,1},{17,25},{25,17},{2,10},{10... | collective-permute-start | bytes 786440 | tf_op jit(solution)/shard_map/ppermute | solution.py:46
  50.7 3.2 %collective-permute-start.18 = (f32[128,512]{1,0:T(8,128)S(1)}, f32[128,512]{1,0:T(8,128)S(1)}, u32[]{:S(2)}, u32[]{:S(2)}) collective-permute-start(f32[128,512]{1,0:T(8,128)S(1)} %constant_dynamic-slice_fusion.1), channel_id=1, source_target_pairs={{0,16},{8,24},{16,0},{24,8},{1,17},{9,25},{17,1},{25,9},{2,18},{10... | collective-permute-start | bytes 786440 | tf_op jit(solution)/shard_map/ppermute | solution.py:46
  54.1 3.1 %collective-permute-start.7 = (f32[64,512]{1,0:T(8,128)S(1)}, f32[64,512]{1,0:T(8,128)S(1)}, u32[]{:S(2)}, u32[]{:S(2)}) collective-permute-start(f32[64,512]{1,0:T(8,128)S(1)} %constant_dynamic-slice_fusion.4), channel_id=1, source_target_pairs={{0,8},{8,0},{16,24},{24,16},{1,9},{9,1},{17,25},{25,17},{2,10},{10... | collective-permute-start | bytes 393224 | tf_op jit(solution)/shard_map/ppermute | solution.py:46
  57.3 3.2 %collective-permute-start.13 = (f32[64,512]{1,0:T(8,128)S(1)}, f32[64,512]{1,0:T(8,128)S(1)}, u32[]{:S(2)}, u32[]{:S(2)}) collective-permute-start(f32[64,512]{1,0:T(8,128)S(1)} %constant_dynamic-slice_fusion.2), channel_id=1, source_target_pairs={{0,16},{8,24},{16,0},{24,8},{1,17},{9,25},{17,1},{25,9},{2,18},{10... | collective-permute-start | bytes 393224 | tf_op jit(solution)/shard_map/ppermute | solution.py:46
  60.6 2.4 %collective-permute-start.19 = (f32[64,512]{1,0:T(8,128)S(1)}, f32[64,512]{1,0:T(8,128)S(1)}, u32[]{:S(2)}, u32[]{:S(2)}) collective-permute-start(f32[64,512]{1,0:T(8,128)S(1)} %constant_dynamic-slice_fusion), channel_id=1, source_target_pairs={{0,4},{1,5},{2,6},{3,7},{4,0},{5,1},{6,2},{7,3},{8,12},{9,13},{10,... | collective-permute-start | bytes 393224 | tf_op jit(solution)/shard_map/ppermute | solution.py:46
  63.1 2.4 %collective-permute-start.14 = (f32[64,512]{1,0:T(8,128)S(1)}, f32[64,512]{1,0:T(8,128)S(1)}, u32[]{:S(2)}, u32[]{:S(2)}) collective-permute-start(f32[64,512]{1,0:T(8,128)S(1)} %dynamic-slice_add_fusion.4), channel_id=1, source_target_pairs={{0,4},{1,5},{2,6},{3,7},{4,0},{5,1},{6,2},{7,3},{8,12},{9,13},{10,... | collective-permute-start | bytes 393224 | tf_op jit(solution)/shard_map/ppermute | solution.py:49
  65.4 1.8 %collective-permute-done.19 = f32[64,512]{1,0:T(8,128)S(1)} collective-permute-done((f32[64,512]{1,0:T(8,128)S(1)}, f32[64,512]{1,0:T(8,128)S(1)}, u32[]{:S(2)}, u32[]{:S(2)}) %collective-permute-start.19) | collective-permute-done | bytes 131104 | tf_op jit(solution)/shard_map/ppermute | solution.py:46
  67.4 2.4 %collective-permute-start.9 = (f32[64,512]{1,0:T(8,128)S(1)}, f32[64,512]{1,0:T(8,128)S(1)}, u32[]{:S(2)}, u32[]{:S(2)}) collective-permute-start(f32[64,512]{1,0:T(8,128)S(1)} %add.228), channel_id=1, source_target_pairs={{0,4},{1,5},{2,6},{3,7},{4,0},{5,1},{6,2},{7,3},{8,12},{9,13},{10,... | collective-permute-start | bytes 393224 | tf_op jit(solution)/shard_map/ppermute | solution.py:49
  69.9 5.8 %collective-permute-done.14 = f32[64,512]{1,0:T(8,128)S(1)} collective-permute-done((f32[64,512]{1,0:T(8,128)S(1)}, f32[64,512]{1,0:T(8,128)S(1)}, u32[]{:S(2)}, u32[]{:S(2)}) %collective-permute-start.14) | collective-permute-done | bytes 131104 | tf_op jit(solution)/shard_map/ppermute | solution.py:49
  75.8 2.2 %collective-permute-start.21 = (f32[64,512]{1,0:T(8,128)S(1)}, f32[64,512]{1,0:T(8,128)S(1)}, u32[]{:S(2)}, u32[]{:S(2)}) collective-permute-start(f32[64,512]{1,0:T(8,128)S(1)} %add.244), channel_id=1, source_target_pairs={{0,8},{8,0},{16,24},{24,16},{1,9},{9,1},{17,25},{25,17},{2,10},{10... | collective-permute-start | bytes 393224 | tf_op jit(solution)/shard_map/ppermute | solution.py:49
  79.6 2.8 %collective-permute-done.15 = f32[64,512]{1,0:T(8,128)S(1)} collective-permute-done((f32[64,512]{1,0:T(8,128)S(1)}, f32[64,512]{1,0:T(8,128)S(1)}, u32[]{:S(2)}, u32[]{:S(2)}) %collective-permute-start.15) | collective-permute-done | bytes 131104 | tf_op jit(solution)/shard_map/ppermute | solution.py:49
  82.4 1.9 %collective-permute-start.16 = (bf16[64,512]{1,0:T(8,128)(2,1)S(1)}, bf16[64,512]{1,0:T(8,128)(2,1)S(1)}, u32[]{:S(2)}, u32[]{:S(2)}) collective-permute-start(bf16[64,512]{1,0:T(8,128)(2,1)S(1)} %add_convert_fusion.1), channel_id=1, source_target_pairs={{0,16},{8,24},{16,0},{24,8},{1,17},{9,25},{17,1},{25,9},{2,18},{10... | collective-permute-start | bytes 196616 | tf_op jit(solution)/shard_map/ppermute | solution.py:56
  84.5 2.2 %collective-permute-start.11 = (bf16[128,512]{1,0:T(8,128)(2,1)S(1)}, bf16[128,512]{1,0:T(8,128)(2,1)S(1)}, u32[]{:S(2)}, u32[]{:S(2)}) collective-permute-start(bf16[128,512]{1,0:T(8,128)(2,1)S(1)} %pad_maximum_fusion.10), channel_id=1, source_target_pairs={{0,2},{1,3},{2,0},{3,1},{4,6},{5,7},{6,4},{7,5},{8,10},{9,11},{10,... | collective-permute-start | bytes 393224 | tf_op jit(solution)/shard_map/ppermute | solution.py:56
  90.7 2.3 %collective-permute-done.23 = bf16[128,512]{1,0:T(8,128)(2,1)S(1)} collective-permute-done((bf16[128,512]{1,0:T(8,128)(2,1)S(1)}, bf16[128,512]{1,0:T(8,128)(2,1)S(1)}, u32[]{:S(2)}, u32[]{:S(2)}) %collective-permute-start.23) | collective-permute-done | bytes 131104 | tf_op jit(solution)/shard_map/ppermute | solution.py:56
  93.1 5.8 %collective-permute-start.24 = (bf16[768,512]{1,0:T(8,128)(2,1)S(1)}, bf16[768,512]{1,0:T(8,128)(2,1)S(1)}, u32[]{:S(2)}, u32[]{:S(2)}) collective-permute-start(bf16[768,512]{1,0:T(8,128)(2,1)S(1)} %select_dynamic-update-slice_fusion), channel_id=1, source_target_pairs={{0,1},{1,0},{2,3},{3,2},{4,5},{5,4},{6,7},{7,6},{8,9},{9,8},{10,11... | collective-permute-start | bytes 2359304 | tf_op jit(solution)/shard_map/ppermute | solution.py:77
  100.6 1.6 %slice_multiply_fusion.3 = (f32[4,32,128]{2,1,0:T(8,128)}, bf16[4,32,128]{2,1,0:T(8,128)(2,1)}) fusion(f32[6,34,128]{2,1,0:T(8,128)S(1)} %copy-done.2, f32[6,34,128]{2,1,0:T(8,128)S(1)} %get-tuple-element.11, f32[8,36,128]{2,1,0:T(8,128)S(1)} %get-tuple-element.16, f32[8,36,128]{2,1,0:T(8,128)} %get-tuple-element.36), kind=kLoop, calls=%fused_computation.193 | loop fusion | flops 49152 | bytes 360448 | tf_op jit(solution)/shard_map/mul | solution.py:192
  102.9 2.0 %maximum_convert_fusion = f32[1440,512]{1,0:T(8,128)} fusion(bf16[672,512]{1,0:T(8,128)(2,1)S(1)} %slice.466, bf16[768,512]{1,0:T(8,128)(2,1)S(1)} %get-tuple-element.19), kind=kLoop, calls=%fused_computation.5 | loop fusion | flops 2949120 | bytes 4423680 | tf_op jit(solution)/shard_map/convert_element_type | solution.py:81
  (185 shorter events, 33.6 us)
Async XLA Ops:
  4.2 9.3 %collective-permute-start.1 = (bf16[4,32,832]{2,1,0:T(8,128)(2,1)S(1)}, bf16[4,32,832]{2,1,0:T(8,128)(2,1)S(1)}, u32[]{:S(2)}, u32[]{:S(2)}) collective-permute-start(bf16[4,32,832]{2,1,0:T(8,128)(2,1)S(1)} %concatenate.110), channel_id=1, source_target_pairs={{8,0},{16,8},{24,16},{9,1},{17,9},{25,17},{10,2},{18,10},{26,18},{... | collective-permute-start | bytes 638984 | tf_op jit(solution)/shard_map/ppermute | solution.py:114
  5.5 8.8 %collective-permute-start = (bf16[4,32,832]{2,1,0:T(8,128)(2,1)S(1)}, bf16[4,32,832]{2,1,0:T(8,128)(2,1)S(1)}, u32[]{:S(2)}, u32[]{:S(2)}) collective-permute-start(bf16[4,32,832]{2,1,0:T(8,128)(2,1)S(1)} %concatenate.110), channel_id=1, source_target_pairs={{0,8},{8,16},{16,24},{1,9},{9,17},{17,25},{2,10},{10,18},{18,26},{... | collective-permute-start | bytes 638984 | tf_op jit(solution)/shard_map/ppermute | solution.py:113
  14.4 7.3 %collective-permute-start.2 = (bf16[12,4,832]{2,1,0:T(4,128)(2,1)S(1)}, bf16[12,4,832]{2,1,0:T(4,128)(2,1)S(1)}, u32[]{:S(2)}, u32[]{:S(2)}) collective-permute-start(bf16[12,4,832]{2,1,0:T(4,128)(2,1)S(1)} %get-tuple-element.30), channel_id=1, source_target_pairs={{0,1},{1,2},{2,3},{3,4},{4,5},{5,6},{6,7},{8,9},{9,10},{10,11},{11... | collective-permute-start | bytes 239624 | tf_op jit(solution)/shard_map/ppermute | solution.py:113
  19.2 5.8 %collective-permute-start.3 = (bf16[12,4,832]{2,1,0:T(4,128)(2,1)S(1)}, bf16[12,4,832]{2,1,0:T(4,128)(2,1)S(1)}, u32[]{:S(2)}, u32[]{:S(2)}) collective-permute-start(bf16[12,4,832]{2,1,0:T(4,128)(2,1)S(1)} %get-tuple-element.31), channel_id=1, source_target_pairs={{1,0},{2,1},{3,2},{4,3},{5,4},{6,5},{7,6},{9,8},{10,9},{11,10},{12... | collective-permute-start | bytes 239624 | tf_op jit(solution)/shard_map/ppermute | solution.py:114
  32.1 9.9 %collective-permute-start.4 = (bf16[6,34,320]{2,1,0:T(8,128)(2,1)}, bf16[6,34,320]{2,1,0:T(8,128)(2,1)S(1)}, u32[]{:S(2)}, u32[]{:S(2)}) collective-permute-start(bf16[6,34,320]{2,1,0:T(8,128)(2,1)} %pad_maximum_fusion.3), channel_id=1, source_target_pairs={{0,1},{1,0},{2,3},{3,2},{4,5},{5,4},{6,7},{7,6},{8,9},{9,8},{10,11... | collective-permute-start | bytes 391688 | tf_op jit(solution)/shard_map/ppermute | solution.py:263
  40.3 4.2 %collective-permute-start.5 = (bf16[256,512]{1,0:T(8,128)(2,1)S(1)}, bf16[256,512]{1,0:T(8,128)(2,1)}, u32[]{:S(2)}, u32[]{:S(2)}) collective-permute-start(bf16[256,512]{1,0:T(8,128)(2,1)S(1)} %pad_maximum_fusion.2), channel_id=1, source_target_pairs={{0,1},{1,0},{2,3},{3,2},{4,5},{5,4},{6,7},{7,6},{8,9},{9,8},{10,11... | collective-permute-start | bytes 786440 | tf_op jit(solution)/shard_map/ppermute | solution.py:265
  46.3 7.8 %collective-permute-start.6 = (f32[128,512]{1,0:T(8,128)S(1)}, f32[128,512]{1,0:T(8,128)S(1)}, u32[]{:S(2)}, u32[]{:S(2)}) collective-permute-start(f32[128,512]{1,0:T(8,128)S(1)} %constant_dynamic-slice_fusion.5), channel_id=1, source_target_pairs={{0,2},{1,3},{2,0},{3,1},{4,6},{5,7},{6,4},{7,5},{8,10},{9,11},{10,... | collective-permute-start | bytes 786440 | tf_op jit(solution)/shard_map/ppermute | solution.py:46
  47.6 9.6 %collective-permute-start.12 = (f32[128,512]{1,0:T(8,128)S(1)}, f32[128,512]{1,0:T(8,128)S(1)}, u32[]{:S(2)}, u32[]{:S(2)}) collective-permute-start(f32[128,512]{1,0:T(8,128)S(1)} %constant_dynamic-slice_fusion.3), channel_id=1, source_target_pairs={{0,8},{8,0},{16,24},{24,16},{1,9},{9,1},{17,25},{25,17},{2,10},{10... | collective-permute-start | bytes 786440 | tf_op jit(solution)/shard_map/ppermute | solution.py:46
  50.7 9.8 %collective-permute-start.18 = (f32[128,512]{1,0:T(8,128)S(1)}, f32[128,512]{1,0:T(8,128)S(1)}, u32[]{:S(2)}, u32[]{:S(2)}) collective-permute-start(f32[128,512]{1,0:T(8,128)S(1)} %constant_dynamic-slice_fusion.1), channel_id=1, source_target_pairs={{0,16},{8,24},{16,0},{24,8},{1,17},{9,25},{17,1},{25,9},{2,18},{10... | collective-permute-start | bytes 786440 | tf_op jit(solution)/shard_map/ppermute | solution.py:46
  54.1 8.8 %collective-permute-start.7 = (f32[64,512]{1,0:T(8,128)S(1)}, f32[64,512]{1,0:T(8,128)S(1)}, u32[]{:S(2)}, u32[]{:S(2)}) collective-permute-start(f32[64,512]{1,0:T(8,128)S(1)} %constant_dynamic-slice_fusion.4), channel_id=1, source_target_pairs={{0,8},{8,0},{16,24},{24,16},{1,9},{9,1},{17,25},{25,17},{2,10},{10... | collective-permute-start | bytes 393224 | tf_op jit(solution)/shard_map/ppermute | solution.py:46
  57.3 5.8 %collective-permute-start.13 = (f32[64,512]{1,0:T(8,128)S(1)}, f32[64,512]{1,0:T(8,128)S(1)}, u32[]{:S(2)}, u32[]{:S(2)}) collective-permute-start(f32[64,512]{1,0:T(8,128)S(1)} %constant_dynamic-slice_fusion.2), channel_id=1, source_target_pairs={{0,16},{8,24},{16,0},{24,8},{1,17},{9,25},{17,1},{25,9},{2,18},{10... | collective-permute-start | bytes 393224 | tf_op jit(solution)/shard_map/ppermute | solution.py:46
  60.6 6.7 %collective-permute-start.19 = (f32[64,512]{1,0:T(8,128)S(1)}, f32[64,512]{1,0:T(8,128)S(1)}, u32[]{:S(2)}, u32[]{:S(2)}) collective-permute-start(f32[64,512]{1,0:T(8,128)S(1)} %constant_dynamic-slice_fusion), channel_id=1, source_target_pairs={{0,4},{1,5},{2,6},{3,7},{4,0},{5,1},{6,2},{7,3},{8,12},{9,13},{10,... | collective-permute-start | bytes 393224 | tf_op jit(solution)/shard_map/ppermute | solution.py:46
  63.0 4.4 %collective-permute-start.8 = (f32[64,512]{1,0:T(8,128)S(1)}, f32[64,512]{1,0:T(8,128)S(1)}, u32[]{:S(2)}, u32[]{:S(2)}) collective-permute-start(f32[64,512]{1,0:T(8,128)S(1)} %dynamic-slice_add_fusion.5), channel_id=1, source_target_pairs={{0,16},{8,24},{16,0},{24,8},{1,17},{9,25},{17,1},{25,9},{2,18},{10... | collective-permute-start | bytes 393224 | tf_op jit(solution)/shard_map/ppermute | solution.py:49
  63.1 12.6 %collective-permute-start.14 = (f32[64,512]{1,0:T(8,128)S(1)}, f32[64,512]{1,0:T(8,128)S(1)}, u32[]{:S(2)}, u32[]{:S(2)}) collective-permute-start(f32[64,512]{1,0:T(8,128)S(1)} %dynamic-slice_add_fusion.4), channel_id=1, source_target_pairs={{0,4},{1,5},{2,6},{3,7},{4,0},{5,1},{6,2},{7,3},{8,12},{9,13},{10,... | collective-permute-start | bytes 393224 | tf_op jit(solution)/shard_map/ppermute | solution.py:49
  67.3 8.5 %collective-permute-start.20 = (f32[64,512]{1,0:T(8,128)S(1)}, f32[64,512]{1,0:T(8,128)S(1)}, u32[]{:S(2)}, u32[]{:S(2)}) collective-permute-start(f32[64,512]{1,0:T(8,128)S(1)} %dynamic-slice_add_fusion.3), channel_id=1, source_target_pairs={{0,2},{1,3},{2,0},{3,1},{4,6},{5,7},{6,4},{7,5},{8,10},{9,11},{10,... | collective-permute-start | bytes 393224 | tf_op jit(solution)/shard_map/ppermute | solution.py:49
  67.4 10.6 %collective-permute-start.9 = (f32[64,512]{1,0:T(8,128)S(1)}, f32[64,512]{1,0:T(8,128)S(1)}, u32[]{:S(2)}, u32[]{:S(2)}) collective-permute-start(f32[64,512]{1,0:T(8,128)S(1)} %add.228), channel_id=1, source_target_pairs={{0,4},{1,5},{2,6},{3,7},{4,0},{5,1},{6,2},{7,3},{8,12},{9,13},{10,... | collective-permute-start | bytes 393224 | tf_op jit(solution)/shard_map/ppermute | solution.py:49
  75.7 6.7 %collective-permute-start.15 = (f32[64,512]{1,0:T(8,128)S(1)}, f32[64,512]{1,0:T(8,128)S(1)}, u32[]{:S(2)}, u32[]{:S(2)}) collective-permute-start(f32[64,512]{1,0:T(8,128)S(1)} %add.236), channel_id=1, source_target_pairs={{0,2},{1,3},{2,0},{3,1},{4,6},{5,7},{6,4},{7,5},{8,10},{9,11},{10,... | collective-permute-start | bytes 393224 | tf_op jit(solution)/shard_map/ppermute | solution.py:49
  75.8 8.5 %collective-permute-start.21 = (f32[64,512]{1,0:T(8,128)S(1)}, f32[64,512]{1,0:T(8,128)S(1)}, u32[]{:S(2)}, u32[]{:S(2)}) collective-permute-start(f32[64,512]{1,0:T(8,128)S(1)} %add.244), channel_id=1, source_target_pairs={{0,8},{8,0},{16,24},{24,16},{1,9},{9,1},{17,25},{25,17},{2,10},{10... | collective-permute-start | bytes 393224 | tf_op jit(solution)/shard_map/ppermute | solution.py:49
  78.1 6.3 %collective-permute-start.10 = (bf16[64,512]{1,0:T(8,128)(2,1)S(1)}, bf16[64,512]{1,0:T(8,128)(2,1)S(1)}, u32[]{:S(2)}, u32[]{:S(2)}) collective-permute-start(bf16[64,512]{1,0:T(8,128)(2,1)S(1)} %add_convert_fusion.2), channel_id=1, source_target_pairs={{0,8},{8,0},{16,24},{24,16},{1,9},{9,1},{17,25},{25,17},{2,10},{10... | collective-permute-start | bytes 196616 | tf_op jit(solution)/shard_map/ppermute | solution.py:56
  82.4 4.3 %collective-permute-start.16 = (bf16[64,512]{1,0:T(8,128)(2,1)S(1)}, bf16[64,512]{1,0:T(8,128)(2,1)S(1)}, u32[]{:S(2)}, u32[]{:S(2)}) collective-permute-start(bf16[64,512]{1,0:T(8,128)(2,1)S(1)} %add_convert_fusion.1), channel_id=1, source_target_pairs={{0,16},{8,24},{16,0},{24,8},{1,17},{9,25},{17,1},{25,9},{2,18},{10... | collective-permute-start | bytes 196616 | tf_op jit(solution)/shard_map/ppermute | solution.py:56
  84.3 4.5 %collective-permute-start.22 = (bf16[64,512]{1,0:T(8,128)(2,1)S(1)}, bf16[64,512]{1,0:T(8,128)(2,1)S(1)}, u32[]{:S(2)}, u32[]{:S(2)}) collective-permute-start(bf16[64,512]{1,0:T(8,128)(2,1)S(1)} %add_convert_fusion), channel_id=1, source_target_pairs={{0,4},{1,5},{2,6},{3,7},{4,0},{5,1},{6,2},{7,3},{8,12},{9,13},{10,... | collective-permute-start | bytes 196616 | tf_op jit(solution)/shard_map/ppermute | solution.py:56
  84.5 5.3 %collective-permute-start.11 = (bf16[128,512]{1,0:T(8,128)(2,1)S(1)}, bf16[128,512]{1,0:T(8,128)(2,1)S(1)}, u32[]{:S(2)}, u32[]{:S(2)}) collective-permute-start(bf16[128,512]{1,0:T(8,128)(2,1)S(1)} %pad_maximum_fusion.10), channel_id=1, source_target_pairs={{0,2},{1,3},{2,0},{3,1},{4,6},{5,7},{6,4},{7,5},{8,10},{9,11},{10,... | collective-permute-start | bytes 393224 | tf_op jit(solution)/shard_map/ppermute | solution.py:56
  88.8 4.2 %collective-permute-start.23 = (bf16[128,512]{1,0:T(8,128)(2,1)S(1)}, bf16[128,512]{1,0:T(8,128)(2,1)S(1)}, u32[]{:S(2)}, u32[]{:S(2)}) collective-permute-start(bf16[128,512]{1,0:T(8,128)(2,1)S(1)} %pad_maximum_fusion.12), channel_id=1, source_target_pairs={{0,16},{8,24},{16,0},{24,8},{1,17},{9,25},{17,1},{25,9},{2,18},{10... | collective-permute-start | bytes 393224 | tf_op jit(solution)/shard_map/ppermute | solution.py:56
  93.1 9.0 %collective-permute-start.24 = (bf16[768,512]{1,0:T(8,128)(2,1)S(1)}, bf16[768,512]{1,0:T(8,128)(2,1)S(1)}, u32[]{:S(2)}, u32[]{:S(2)}) collective-permute-start(bf16[768,512]{1,0:T(8,128)(2,1)S(1)} %select_dynamic-update-slice_fusion), channel_id=1, source_target_pairs={{0,1},{1,0},{2,3},{3,2},{4,5},{5,4},{6,7},{7,6},{8,9},{9,8},{10,11... | collective-permute-start | bytes 2359304 | tf_op jit(solution)/shard_map/ppermute | solution.py:77
  (22 other events, 57.4 us)

commit v10 on v8

--- a/solution.py
+++ b/solution.py
@@ -138,7 +138,7 @@
 
 
 def surround(cells, width):
-    return widen(widen(cells, "rows", 0, width), "cols", 1, width)
+    return widen(widen(cells, "cols", 1, width), "rows", 0, width)
 
 
 def inner(cells, outer, inner_width):

time: 105 us -> 105 us (level)
  waiting for transfers between devices: 16.7 us -> 23.6 us
  starting transfers between devices: 54.8 us -> 49.2 us
    ppermute x6, starting transfers between devices: 11.7 us -> 6.27 us  [halve(): part = part + lax.ppermute(part, axis, flip_pairs(axis, bit))]
    ppermute x6, waiting for transfers between devices: 1.84 us -> 4.96 us  [halve(): part = keep + lax.ppermute(send, axis, flip_pairs(axis, bit))]
    ppermute x6, waiting for transfers between devices: 4.3 us -> 6.81 us  [halve(): part = part + lax.ppermute(part, axis, flip_pairs(axis, bit))]
    ppermute x6, starting transfers between devices: 16.2 us -> 17.8 us  [halve(): part = keep + lax.ppermute(send, axis, flip_pairs(axis, bit))]
    ppermute x2, waiting for transfers between devices: 5.99 us -> 7.22 us  [widen(): lax.ppermute(head, axis, [(i + dist, i) for i in range(count - dist)])]
    unnamed x43 -> x47, local copies, waits for them, and re-layouts: 2.35 us -> 2.39 us
  transfers between devices with their start and end apart: 27 -> 27, of which waited for: 10 -> 12; matrix products, arithmetic and copies ran while one was open for 15% -> 14% of each run, Pallas kernels for 0% -> 0%
where the time goes in v10:
time: 105 us
  starting transfers between devices  49.2 us (47%)
  waiting for transfers between devices  23.6 us (22%)
  other arithmetic  14.1 us (13%)
  local copies, waits for them, and re-layouts  10.3 us (10%)
  matrix products  5.94 us (6%)
  between operations  1.55 us (1%)
    ppermute x6, starting transfers between devices, halve(): part = keep + lax.ppermute(send, axis, flip_pairs(axis, bit))  17.8 us
    ppermute x2, starting transfers between devices, widen(): lax.ppermute(tail, axis, [(i, i + dist) for i in range(count - dist)])  8.6 us
    ppermute x2, waiting for transfers between devices, widen(): lax.ppermute(head, axis, [(i + dist, i) for i in range(count - dist)])  7.22 us
    ppermute x6, waiting for transfers between devices, halve(): part = part + lax.ppermute(part, axis, flip_pairs(axis, bit))  6.81 us
    ppermute x1, starting transfers between devices, sum_everywhere(): got = lax.ppermute(piece, axis, flip_pairs(axis, bit))  6.46 us
    ppermute x6, starting transfers between devices, halve(): part = part + lax.ppermute(part, axis, flip_pairs(axis, bit))  6.27 us
    ppermute x6, starting transfers between devices, double(): got = lax.ppermute(piece, axis, flip_pairs(axis, bit))  6.05 us
    ppermute x6, waiting for transfers between devices, halve(): part = keep + lax.ppermute(send, axis, flip_pairs(axis, bit))  4.96 us
  transfers between devices with their start and end apart: 27, of which 12 were waited for; matrix products, arithmetic and copies ran while one was open for 14% of the time, Pallas kernels for 0%

profile of v10, /device:TPU:1, one launch (start us, length us, event | category | flops | bytes accessed | tf_op | source)
XLA Modules:
  0.0 104.7 jit_solution(2346443927286456382)
XLA Ops:
  4.2 4.6 %collective-permute-start = (bf16[4,4,832]{2,1,0:T(4,128)(2,1)S(1)}, bf16[4,4,832]{2,1,0:T(4,128)(2,1)S(1)}, u32[]{:S(2)}, u32[]{:S(2)}) collective-permute-start(bf16[4,4,832]{2,1,0:T(4,128)(2,1)S(1)} %get-tuple-element.44), channel_id=1, source_target_pairs={{0,1},{1,2},{2,3},{3,4},{4,5},{5,6},{6,7},{8,9},{9,10},{10,11},{11... | collective-permute-start | bytes 79880 | tf_op jit(solution)/shard_map/ppermute | solution.py:113
  8.8 1.9 %collective-permute-start.1 = (bf16[4,4,832]{2,1,0:T(4,128)(2,1)S(1)}, bf16[4,4,832]{2,1,0:T(4,128)(2,1)S(1)}, u32[]{:S(2)}, u32[]{:S(2)}) collective-permute-start(bf16[4,4,832]{2,1,0:T(4,128)(2,1)S(1)} %get-tuple-element.45), channel_id=1, source_target_pairs={{1,0},{2,1},{3,2},{4,3},{5,4},{6,5},{7,6},{9,8},{10,9},{11,10},{12... | collective-permute-start | bytes 79880 | tf_op jit(solution)/shard_map/ppermute | solution.py:114
  11.4 2.6 %collective-permute-done.1 = bf16[4,4,832]{2,1,0:T(4,128)(2,1)S(1)} collective-permute-done((bf16[4,4,832]{2,1,0:T(4,128)(2,1)S(1)}, bf16[4,4,832]{2,1,0:T(4,128)(2,1)S(1)}, u32[]{:S(2)}, u32[]{:S(2)}) %collective-permute-start.1) | collective-permute-done | bytes 26656 | tf_op jit(solution)/shard_map/ppermute | solution.py:114
  15.4 4.0 %collective-permute-start.2 = (bf16[4,40,832]{2,1,0:T(8,128)(2,1)S(1)}, bf16[4,40,832]{2,1,0:T(8,128)(2,1)S(1)}, u32[]{:S(2)}, u32[]{:S(2)}) collective-permute-start(bf16[4,40,832]{2,1,0:T(8,128)(2,1)S(1)} %pad_maximum_fusion.2), channel_id=1, source_target_pairs={{0,8},{8,16},{16,24},{1,9},{9,17},{17,25},{2,10},{10,18},{18,26},{... | collective-permute-start | bytes 798728 | tf_op jit(solution)/shard_map/ppermute | solution.py:113
  20.0 4.6 %collective-permute-done.3 = bf16[4,40,832]{2,1,0:T(8,128)(2,1)S(1)} collective-permute-done((bf16[4,40,832]{2,1,0:T(8,128)(2,1)S(1)}, bf16[4,40,832]{2,1,0:T(8,128)(2,1)S(1)}, u32[]{:S(2)}, u32[]{:S(2)}) %collective-permute-start.3) | collective-permute-done | bytes 266272 | tf_op jit(solution)/shard_map/ppermute | solution.py:114
  32.1 2.1 %convolution_select_fusion.1 = f32[8,8,5,512]{3,1,2,0:T(8,128)S(1)} fusion(bf16[3,3,160,512]{3,2,1,0:T(8,128)(2,1)} %bitcast.88, pred[8,5]{0,1:T(8,128)(4,1)S(1)} %copy-done.20, bf16[10,1,7,2,160]{4,2,3,0,1:T(8,128)(2,1)S(1)} %slice.373, bf16[10,1,8,5,160]{4,2,3,0,1:T(8,128)(2,1)S(1)} %copy.16), kind=kOutput, calls=%fused_computation.7 | convolution fusion | flops 472560640 | bytes 2302760 | tf_op jit(solution)/shard_map/conv_general_dilated | solution.py:161
  42.4 1.7 %convolution_multiply_fusion = f32[768,512]{1,0:T(8,128)S(1)} fusion(s32[]{:T(128)S(6)} %select_n.147, bf16[128,1536]{1,0:T(8,128)(2,1)S(1)} %concatenate.120, bf16[128,1536]{1,0:T(8,128)(2,1)S(1)} %concatenate.122, bf16[128,1536]{1,0:T(8,128)(2,1)S(1)} %concatenate.124, bf16[128,1536]{1,0:T(8,128)(2,1)S(1)} %concatenate.126, ...), kind=kOutput, calls=%fused_computation.4 | convolution fusion | flops 408289280 | bytes 3670020 | tf_op jit(solution)/shard_map/dot_general | solution.py:282
  44.3 2.3 %collective-permute-start.8 = (f32[128,512]{1,0:T(8,128)S(1)}, f32[128,512]{1,0:T(8,128)S(1)}, u32[]{:S(2)}, u32[]{:S(2)}) collective-permute-start(f32[128,512]{1,0:T(8,128)S(1)} %constant_dynamic-slice_fusion.5), channel_id=1, source_target_pairs={{0,2},{1,3},{2,0},{3,1},{4,6},{5,7},{6,4},{7,5},{8,10},{9,11},{10,... | collective-permute-start | bytes 786440 | tf_op jit(solution)/shard_map/ppermute | solution.py:46
  46.7 4.0 %collective-permute-start.14 = (f32[128,512]{1,0:T(8,128)S(1)}, f32[128,512]{1,0:T(8,128)S(1)}, u32[]{:S(2)}, u32[]{:S(2)}) collective-permute-start(f32[128,512]{1,0:T(8,128)S(1)} %constant_dynamic-slice_fusion.3), channel_id=1, source_target_pairs={{0,8},{8,0},{16,24},{24,16},{1,9},{9,1},{17,25},{25,17},{2,10},{10... | collective-permute-start | bytes 786440 | tf_op jit(solution)/shard_map/ppermute | solution.py:46
  50.7 2.9 %collective-permute-start.20 = (f32[128,512]{1,0:T(8,128)S(1)}, f32[128,512]{1,0:T(8,128)S(1)}, u32[]{:S(2)}, u32[]{:S(2)}) collective-permute-start(f32[128,512]{1,0:T(8,128)S(1)} %constant_dynamic-slice_fusion.1), channel_id=1, source_target_pairs={{0,16},{8,24},{16,0},{24,8},{1,17},{9,25},{17,1},{25,9},{2,18},{10... | collective-permute-start | bytes 786440 | tf_op jit(solution)/shard_map/ppermute | solution.py:46
  53.7 3.5 %collective-permute-start.9 = (f32[64,512]{1,0:T(8,128)S(1)}, f32[64,512]{1,0:T(8,128)S(1)}, u32[]{:S(2)}, u32[]{:S(2)}) collective-permute-start(f32[64,512]{1,0:T(8,128)S(1)} %constant_dynamic-slice_fusion.4), channel_id=1, source_target_pairs={{0,8},{8,0},{16,24},{24,16},{1,9},{9,1},{17,25},{25,17},{2,10},{10... | collective-permute-start | bytes 393224 | tf_op jit(solution)/shard_map/ppermute | solution.py:46
  57.3 2.9 %collective-permute-start.15 = (f32[64,512]{1,0:T(8,128)S(1)}, f32[64,512]{1,0:T(8,128)S(1)}, u32[]{:S(2)}, u32[]{:S(2)}) collective-permute-start(f32[64,512]{1,0:T(8,128)S(1)} %constant_dynamic-slice_fusion.2), channel_id=1, source_target_pairs={{0,16},{8,24},{16,0},{24,8},{1,17},{9,25},{17,1},{25,9},{2,18},{10... | collective-permute-start | bytes 393224 | tf_op jit(solution)/shard_map/ppermute | solution.py:46
  60.2 2.2 %collective-permute-start.21 = (f32[64,512]{1,0:T(8,128)S(1)}, f32[64,512]{1,0:T(8,128)S(1)}, u32[]{:S(2)}, u32[]{:S(2)}) collective-permute-start(f32[64,512]{1,0:T(8,128)S(1)} %constant_dynamic-slice_fusion), channel_id=1, source_target_pairs={{0,4},{1,5},{2,6},{3,7},{4,0},{5,1},{6,2},{7,3},{8,12},{9,13},{10,... | collective-permute-start | bytes 393224 | tf_op jit(solution)/shard_map/ppermute | solution.py:46
  63.2 1.8 %collective-permute-start.16 = (f32[64,512]{1,0:T(8,128)S(1)}, f32[64,512]{1,0:T(8,128)S(1)}, u32[]{:S(2)}, u32[]{:S(2)}) collective-permute-start(f32[64,512]{1,0:T(8,128)S(1)} %dynamic-slice_add_fusion.4), channel_id=1, source_target_pairs={{0,4},{1,5},{2,6},{3,7},{4,0},{5,1},{6,2},{7,3},{8,12},{9,13},{10,... | collective-permute-start | bytes 393224 | tf_op jit(solution)/shard_map/ppermute | solution.py:49
  65.0 4.9 %collective-permute-done.21 = f32[64,512]{1,0:T(8,128)S(1)} collective-permute-done((f32[64,512]{1,0:T(8,128)S(1)}, f32[64,512]{1,0:T(8,128)S(1)}, u32[]{:S(2)}, u32[]{:S(2)}) %collective-permute-start.21) | collective-permute-done | bytes 131104 | tf_op jit(solution)/shard_map/ppermute | solution.py:46
  70.1 2.5 %collective-permute-start.11 = (f32[64,512]{1,0:T(8,128)S(1)}, f32[64,512]{1,0:T(8,128)S(1)}, u32[]{:S(2)}, u32[]{:S(2)}) collective-permute-start(f32[64,512]{1,0:T(8,128)S(1)} %add.228), channel_id=1, source_target_pairs={{0,4},{1,5},{2,6},{3,7},{4,0},{5,1},{6,2},{7,3},{8,12},{9,13},{10,... | collective-permute-start | bytes 393224 | tf_op jit(solution)/shard_map/ppermute | solution.py:49
  74.2 2.1 %collective-permute-done.22 = f32[64,512]{1,0:T(8,128)S(1)} collective-permute-done((f32[64,512]{1,0:T(8,128)S(1)}, f32[64,512]{1,0:T(8,128)S(1)}, u32[]{:S(2)}, u32[]{:S(2)}) %collective-permute-start.22) | collective-permute-done | bytes 131104 | tf_op jit(solution)/shard_map/ppermute | solution.py:49
  79.0 3.2 %collective-permute-done.17 = f32[64,512]{1,0:T(8,128)S(1)} collective-permute-done((f32[64,512]{1,0:T(8,128)S(1)}, f32[64,512]{1,0:T(8,128)S(1)}, u32[]{:S(2)}, u32[]{:S(2)}) %collective-permute-start.17) | collective-permute-done | bytes 131104 | tf_op jit(solution)/shard_map/ppermute | solution.py:49
  83.4 2.3 %collective-permute-start.13 = (bf16[128,512]{1,0:T(8,128)(2,1)S(1)}, bf16[128,512]{1,0:T(8,128)(2,1)S(1)}, u32[]{:S(2)}, u32[]{:S(2)}) collective-permute-start(bf16[128,512]{1,0:T(8,128)(2,1)S(1)} %pad_maximum_fusion.9), channel_id=1, source_target_pairs={{0,2},{1,3},{2,0},{3,1},{4,6},{5,7},{6,4},{7,5},{8,10},{9,11},{10,... | collective-permute-start | bytes 393224 | tf_op jit(solution)/shard_map/ppermute | solution.py:56
  86.4 1.3 %collective-permute-done.24 = bf16[64,512]{1,0:T(8,128)(2,1)S(1)} collective-permute-done((bf16[64,512]{1,0:T(8,128)(2,1)S(1)}, bf16[64,512]{1,0:T(8,128)(2,1)S(1)}, u32[]{:S(2)}, u32[]{:S(2)}) %collective-permute-start.24) | collective-permute-done | bytes 65568 | tf_op jit(solution)/shard_map/ppermute | solution.py:56
  89.7 2.3 %collective-permute-done.25 = bf16[128,512]{1,0:T(8,128)(2,1)S(1)} collective-permute-done((bf16[128,512]{1,0:T(8,128)(2,1)S(1)}, bf16[128,512]{1,0:T(8,128)(2,1)S(1)}, u32[]{:S(2)}, u32[]{:S(2)}) %collective-permute-start.25) | collective-permute-done | bytes 131104 | tf_op jit(solution)/shard_map/ppermute | solution.py:56
  92.0 6.5 %collective-permute-start.26 = (bf16[768,512]{1,0:T(8,128)(2,1)S(1)}, bf16[768,512]{1,0:T(8,128)(2,1)S(1)}, u32[]{:S(2)}, u32[]{:S(2)}) collective-permute-start(bf16[768,512]{1,0:T(8,128)(2,1)S(1)} %select_dynamic-update-slice_fusion), channel_id=1, source_target_pairs={{0,1},{1,0},{2,3},{3,2},{4,5},{5,4},{6,7},{7,6},{8,9},{9,8},{10,11... | collective-permute-start | bytes 2359304 | tf_op jit(solution)/shard_map/ppermute | solution.py:77
  99.7 1.6 %fusion.99 = bf16[4,32,128]{2,1,0:T(8,128)(2,1)} fusion(f32[8,36,128]{2,1,0:T(8,128)} %copy-done.2, f32[8,36,128]{2,1,0:T(8,128)} %get-tuple-element.34), kind=kLoop, calls=%fused_computation.194 | loop fusion | flops 32768 | bytes 163840 | tf_op jit(solution)/shard_map/convert_element_type | solution.py:175
  102.7 2.0 %maximum_convert_fusion = f32[1440,512]{1,0:T(8,128)} fusion(bf16[672,512]{1,0:T(8,128)(2,1)S(1)} %slice.448, bf16[768,512]{1,0:T(8,128)(2,1)S(1)} %get-tuple-element.19), kind=kLoop, calls=%fused_computation.5 | loop fusion | flops 2949120 | bytes 4423680 | tf_op jit(solution)/shard_map/convert_element_type | solution.py:81
  (192 shorter events, 33.4 us)
Async XLA Ops:
  4.2 7.2 %collective-permute-start = (bf16[4,4,832]{2,1,0:T(4,128)(2,1)S(1)}, bf16[4,4,832]{2,1,0:T(4,128)(2,1)S(1)}, u32[]{:S(2)}, u32[]{:S(2)}) collective-permute-start(bf16[4,4,832]{2,1,0:T(4,128)(2,1)S(1)} %get-tuple-element.44), channel_id=1, source_target_pairs={{0,1},{1,2},{2,3},{3,4},{4,5},{5,6},{6,7},{8,9},{9,10},{10,11},{11... | collective-permute-start | bytes 79880 | tf_op jit(solution)/shard_map/ppermute | solution.py:113
  8.8 5.2 %collective-permute-start.1 = (bf16[4,4,832]{2,1,0:T(4,128)(2,1)S(1)}, bf16[4,4,832]{2,1,0:T(4,128)(2,1)S(1)}, u32[]{:S(2)}, u32[]{:S(2)}) collective-permute-start(bf16[4,4,832]{2,1,0:T(4,128)(2,1)S(1)} %get-tuple-element.45), channel_id=1, source_target_pairs={{1,0},{2,1},{3,2},{4,3},{5,4},{6,5},{7,6},{9,8},{10,9},{11,10},{12... | collective-permute-start | bytes 79880 | tf_op jit(solution)/shard_map/ppermute | solution.py:114
  14.1 10.5 %collective-permute-start.3 = (bf16[4,40,832]{2,1,0:T(8,128)(2,1)S(1)}, bf16[4,40,832]{2,1,0:T(8,128)(2,1)S(1)}, u32[]{:S(2)}, u32[]{:S(2)}) collective-permute-start(bf16[4,40,832]{2,1,0:T(8,128)(2,1)S(1)} %pad_maximum_fusion.2), channel_id=1, source_target_pairs={{8,0},{16,8},{24,16},{9,1},{17,9},{25,17},{10,2},{18,10},{26,18},{... | collective-permute-start | bytes 798728 | tf_op jit(solution)/shard_map/ppermute | solution.py:114
  15.4 9.3 %collective-permute-start.2 = (bf16[4,40,832]{2,1,0:T(8,128)(2,1)S(1)}, bf16[4,40,832]{2,1,0:T(8,128)(2,1)S(1)}, u32[]{:S(2)}, u32[]{:S(2)}) collective-permute-start(bf16[4,40,832]{2,1,0:T(8,128)(2,1)S(1)} %pad_maximum_fusion.2), channel_id=1, source_target_pairs={{0,8},{8,16},{16,24},{1,9},{9,17},{17,25},{2,10},{10,18},{18,26},{... | collective-permute-start | bytes 798728 | tf_op jit(solution)/shard_map/ppermute | solution.py:113
  31.4 10.2 %collective-permute-start.5 = (bf16[6,34,160]{2,1,0:T(8,128)(2,1)}, bf16[6,34,160]{2,1,0:T(8,128)(2,1)S(1)}, u32[]{:S(2)}, u32[]{:S(2)}) collective-permute-start(bf16[6,34,160]{2,1,0:T(8,128)(2,1)} %fusion.82), channel_id=1, source_target_pairs={{0,1},{1,0},{2,3},{3,2},{4,5},{5,4},{6,7},{7,6},{8,9},{9,8},{10,11... | collective-permute-start | bytes 195848 | tf_op jit(solution)/shard_map/ppermute | solution.py:263
  31.4 10.6 %collective-permute-start.4 = (bf16[6,34,160]{2,1,0:T(8,128)(2,1)}, bf16[6,34,160]{2,1,0:T(8,128)(2,1)S(1)}, u32[]{:S(2)}, u32[]{:S(2)}) collective-permute-start(bf16[6,34,160]{2,1,0:T(8,128)(2,1)} %slice.424), channel_id=1, source_target_pairs={{0,1},{1,0},{2,3},{3,2},{4,5},{5,4},{6,7},{7,6},{8,9},{9,8},{10,11... | collective-permute-start | bytes 195848 | tf_op jit(solution)/shard_map/ppermute | solution.py:263
  36.8 5.6 %collective-permute-start.6 = (bf16[128,512]{1,0:T(8,128)(2,1)}, bf16[128,512]{1,0:T(8,128)(2,1)}, u32[]{:S(2)}, u32[]{:S(2)}) collective-permute-start(bf16[128,512]{1,0:T(8,128)(2,1)} %bitcast.32), channel_id=1, source_target_pairs={{0,1},{1,0},{2,3},{3,2},{4,5},{5,4},{6,7},{7,6},{8,9},{9,8},{10,11... | collective-permute-start | bytes 393224 | tf_op jit(solution)/shard_map/ppermute | solution.py:264
  44.3 9.3 %collective-permute-start.8 = (f32[128,512]{1,0:T(8,128)S(1)}, f32[128,512]{1,0:T(8,128)S(1)}, u32[]{:S(2)}, u32[]{:S(2)}) collective-permute-start(f32[128,512]{1,0:T(8,128)S(1)} %constant_dynamic-slice_fusion.5), channel_id=1, source_target_pairs={{0,2},{1,3},{2,0},{3,1},{4,6},{5,7},{6,4},{7,5},{8,10},{9,11},{10,... | collective-permute-start | bytes 786440 | tf_op jit(solution)/shard_map/ppermute | solution.py:46
  46.7 10.5 %collective-permute-start.14 = (f32[128,512]{1,0:T(8,128)S(1)}, f32[128,512]{1,0:T(8,128)S(1)}, u32[]{:S(2)}, u32[]{:S(2)}) collective-permute-start(f32[128,512]{1,0:T(8,128)S(1)} %constant_dynamic-slice_fusion.3), channel_id=1, source_target_pairs={{0,8},{8,0},{16,24},{24,16},{1,9},{9,1},{17,25},{25,17},{2,10},{10... | collective-permute-start | bytes 786440 | tf_op jit(solution)/shard_map/ppermute | solution.py:46
  50.7 9.4 %collective-permute-start.20 = (f32[128,512]{1,0:T(8,128)S(1)}, f32[128,512]{1,0:T(8,128)S(1)}, u32[]{:S(2)}, u32[]{:S(2)}) collective-permute-start(f32[128,512]{1,0:T(8,128)S(1)} %constant_dynamic-slice_fusion.1), channel_id=1, source_target_pairs={{0,16},{8,24},{16,0},{24,8},{1,17},{9,25},{17,1},{25,9},{2,18},{10... | collective-permute-start | bytes 786440 | tf_op jit(solution)/shard_map/ppermute | solution.py:46
  53.7 8.8 %collective-permute-start.9 = (f32[64,512]{1,0:T(8,128)S(1)}, f32[64,512]{1,0:T(8,128)S(1)}, u32[]{:S(2)}, u32[]{:S(2)}) collective-permute-start(f32[64,512]{1,0:T(8,128)S(1)} %constant_dynamic-slice_fusion.4), channel_id=1, source_target_pairs={{0,8},{8,0},{16,24},{24,16},{1,9},{9,1},{17,25},{25,17},{2,10},{10... | collective-permute-start | bytes 393224 | tf_op jit(solution)/shard_map/ppermute | solution.py:46
  57.3 5.9 %collective-permute-start.15 = (f32[64,512]{1,0:T(8,128)S(1)}, f32[64,512]{1,0:T(8,128)S(1)}, u32[]{:S(2)}, u32[]{:S(2)}) collective-permute-start(f32[64,512]{1,0:T(8,128)S(1)} %constant_dynamic-slice_fusion.2), channel_id=1, source_target_pairs={{0,16},{8,24},{16,0},{24,8},{1,17},{9,25},{17,1},{25,9},{2,18},{10... | collective-permute-start | bytes 393224 | tf_op jit(solution)/shard_map/ppermute | solution.py:46
  60.2 9.7 %collective-permute-start.21 = (f32[64,512]{1,0:T(8,128)S(1)}, f32[64,512]{1,0:T(8,128)S(1)}, u32[]{:S(2)}, u32[]{:S(2)}) collective-permute-start(f32[64,512]{1,0:T(8,128)S(1)} %constant_dynamic-slice_fusion), channel_id=1, source_target_pairs={{0,4},{1,5},{2,6},{3,7},{4,0},{5,1},{6,2},{7,3},{8,12},{9,13},{10,... | collective-permute-start | bytes 393224 | tf_op jit(solution)/shard_map/ppermute | solution.py:46
  62.5 7.5 %collective-permute-start.10 = (f32[64,512]{1,0:T(8,128)S(1)}, f32[64,512]{1,0:T(8,128)S(1)}, u32[]{:S(2)}, u32[]{:S(2)}) collective-permute-start(f32[64,512]{1,0:T(8,128)S(1)} %dynamic-slice_add_fusion.5), channel_id=1, source_target_pairs={{0,16},{8,24},{16,0},{24,8},{1,17},{9,25},{17,1},{25,9},{2,18},{10... | collective-permute-start | bytes 393224 | tf_op jit(solution)/shard_map/ppermute | solution.py:49
  63.2 10.9 %collective-permute-start.16 = (f32[64,512]{1,0:T(8,128)S(1)}, f32[64,512]{1,0:T(8,128)S(1)}, u32[]{:S(2)}, u32[]{:S(2)}) collective-permute-start(f32[64,512]{1,0:T(8,128)S(1)} %dynamic-slice_add_fusion.4), channel_id=1, source_target_pairs={{0,4},{1,5},{2,6},{3,7},{4,0},{5,1},{6,2},{7,3},{8,12},{9,13},{10,... | collective-permute-start | bytes 393224 | tf_op jit(solution)/shard_map/ppermute | solution.py:49
  69.9 6.4 %collective-permute-start.22 = (f32[64,512]{1,0:T(8,128)S(1)}, f32[64,512]{1,0:T(8,128)S(1)}, u32[]{:S(2)}, u32[]{:S(2)}) collective-permute-start(f32[64,512]{1,0:T(8,128)S(1)} %dynamic-slice_add_fusion.3), channel_id=1, source_target_pairs={{0,2},{1,3},{2,0},{3,1},{4,6},{5,7},{6,4},{7,5},{8,10},{9,11},{10,... | collective-permute-start | bytes 393224 | tf_op jit(solution)/shard_map/ppermute | solution.py:49
  70.1 7.8 %collective-permute-start.11 = (f32[64,512]{1,0:T(8,128)S(1)}, f32[64,512]{1,0:T(8,128)S(1)}, u32[]{:S(2)}, u32[]{:S(2)}) collective-permute-start(f32[64,512]{1,0:T(8,128)S(1)} %add.228), channel_id=1, source_target_pairs={{0,4},{1,5},{2,6},{3,7},{4,0},{5,1},{6,2},{7,3},{8,12},{9,13},{10,... | collective-permute-start | bytes 393224 | tf_op jit(solution)/shard_map/ppermute | solution.py:49
  74.2 8.1 %collective-permute-start.17 = (f32[64,512]{1,0:T(8,128)S(1)}, f32[64,512]{1,0:T(8,128)S(1)}, u32[]{:S(2)}, u32[]{:S(2)}) collective-permute-start(f32[64,512]{1,0:T(8,128)S(1)} %add.236), channel_id=1, source_target_pairs={{0,2},{1,3},{2,0},{3,1},{4,6},{5,7},{6,4},{7,5},{8,10},{9,11},{10,... | collective-permute-start | bytes 393224 | tf_op jit(solution)/shard_map/ppermute | solution.py:49
  76.4 6.6 %collective-permute-start.23 = (f32[64,512]{1,0:T(8,128)S(1)}, f32[64,512]{1,0:T(8,128)S(1)}, u32[]{:S(2)}, u32[]{:S(2)}) collective-permute-start(f32[64,512]{1,0:T(8,128)S(1)} %add.244), channel_id=1, source_target_pairs={{0,8},{8,0},{16,24},{24,16},{1,9},{9,1},{17,25},{25,17},{2,10},{10... | collective-permute-start | bytes 393224 | tf_op jit(solution)/shard_map/ppermute | solution.py:49
  77.8 5.5 %collective-permute-start.12 = (bf16[64,512]{1,0:T(8,128)(2,1)S(1)}, bf16[64,512]{1,0:T(8,128)(2,1)S(1)}, u32[]{:S(2)}, u32[]{:S(2)}) collective-permute-start(bf16[64,512]{1,0:T(8,128)(2,1)S(1)} %add_convert_fusion.2), channel_id=1, source_target_pairs={{0,8},{8,0},{16,24},{24,16},{1,9},{9,1},{17,25},{25,17},{2,10},{10... | collective-permute-start | bytes 196616 | tf_op jit(solution)/shard_map/ppermute | solution.py:56
  83.0 4.7 %collective-permute-start.24 = (bf16[64,512]{1,0:T(8,128)(2,1)S(1)}, bf16[64,512]{1,0:T(8,128)(2,1)S(1)}, u32[]{:S(2)}, u32[]{:S(2)}) collective-permute-start(bf16[64,512]{1,0:T(8,128)(2,1)S(1)} %add_convert_fusion), channel_id=1, source_target_pairs={{0,4},{1,5},{2,6},{3,7},{4,0},{5,1},{6,2},{7,3},{8,12},{9,13},{10,... | collective-permute-start | bytes 196616 | tf_op jit(solution)/shard_map/ppermute | solution.py:56
  83.4 5.4 %collective-permute-start.13 = (bf16[128,512]{1,0:T(8,128)(2,1)S(1)}, bf16[128,512]{1,0:T(8,128)(2,1)S(1)}, u32[]{:S(2)}, u32[]{:S(2)}) collective-permute-start(bf16[128,512]{1,0:T(8,128)(2,1)S(1)} %pad_maximum_fusion.9), channel_id=1, source_target_pairs={{0,2},{1,3},{2,0},{3,1},{4,6},{5,7},{6,4},{7,5},{8,10},{9,11},{10,... | collective-permute-start | bytes 393224 | tf_op jit(solution)/shard_map/ppermute | solution.py:56
  87.8 4.2 %collective-permute-start.25 = (bf16[128,512]{1,0:T(8,128)(2,1)S(1)}, bf16[128,512]{1,0:T(8,128)(2,1)S(1)}, u32[]{:S(2)}, u32[]{:S(2)}) collective-permute-start(bf16[128,512]{1,0:T(8,128)(2,1)S(1)} %pad_maximum_fusion.11), channel_id=1, source_target_pairs={{0,16},{8,24},{16,0},{24,8},{1,17},{9,25},{17,1},{25,9},{2,18},{10... | collective-permute-start | bytes 393224 | tf_op jit(solution)/shard_map/ppermute | solution.py:56
  92.0 9.9 %collective-permute-start.26 = (bf16[768,512]{1,0:T(8,128)(2,1)S(1)}, bf16[768,512]{1,0:T(8,128)(2,1)S(1)}, u32[]{:S(2)}, u32[]{:S(2)}) collective-permute-start(bf16[768,512]{1,0:T(8,128)(2,1)S(1)} %select_dynamic-update-slice_fusion), channel_id=1, source_target_pairs={{0,1},{1,0},{2,3},{3,2},{4,5},{5,4},{6,7},{7,6},{8,9},{9,8},{10,11... | collective-permute-start | bytes 2359304 | tf_op jit(solution)/shard_map/ppermute | solution.py:77
  (25 other events, 67.0 us)

commit v11 on v8

--- a/solution.py
+++ b/solution.py
@@ -60,15 +60,11 @@
     return piece
 
 
-def sum_everywhere(part, first_halved, rest):
-    ways = min(SUM_WAYS, max(len(rest), 1))
-    width = part.shape[0] // ways
+def sum_everywhere(parts, first_halved, rest):
     pieces = []
-    for way in range(ways):
+    for way, part in enumerate(parts):
         order = rest[way:] + rest[:way]
-        chunk, halved = halve(
-            part[way * width : (way + 1) * width], order, max(len(order) - SUM_SHARED, 0)
-        )
+        chunk, halved = halve(part, order, max(len(order) - SUM_SHARED, 0))
         pieces.append(double(chunk.astype(jnp.bfloat16), halved))
     piece = jnp.concatenate(pieces, axis=0)
     if len(first_halved) == 1:
@@ -279,10 +275,19 @@
     lifted = lax.dynamic_slice_in_dim(jnp.concatenate(lifted, axis=0), upper * half, half, 1)
     total_cells = STEPS * rows_dev * lax.axis_size("rows") * cols_dev * lax.axis_size("cols")
     norm_scale = 1.0 / math.sqrt(total_cells)
-    joined = jnp.dot(
-        lifted.T, jnp.concatenate(grads_seen, axis=0), preferred_element_type=jnp.float32
-    )
-    kernel_grad, bias_grad = sum_everywhere(joined * norm_scale, first, rest)
+    grads_all = jnp.concatenate(grads_seen, axis=0)
+    ways = min(SUM_WAYS, max(len(rest), 1))
+    width = half // ways
+    parts = [
+        jnp.dot(
+            lifted[:, way * width : (way + 1) * width].T,
+            grads_all,
+            preferred_element_type=jnp.float32,
+        )
+        * norm_scale
+        for way in range(ways)
+    ]
+    kernel_grad, bias_grad = sum_everywhere(parts, first, rest)
     return (hidden_final, grad_hidden_start, grad_cell_start, kernel_grad, bias_grad)
 
 

time: 105 us -> 105 us (level)
  starting transfers between devices: 54.8 us -> 50.5 us
  waiting for transfers between devices: 16.7 us -> 19.6 us
  matrix products: 5.95 us -> 8.47 us
    ppermute x6, starting transfers between devices: 16.2 us -> 12.4 us  [halve(): part = keep + lax.ppermute(send, axis, flip_pairs(axis, bit))]
    dot_general x1 -> x3, matrix products: 1.72 us -> 4.24 us  [shards(): jnp.dot(lifted[:, way * width:(way + 1) * width].T, grads_all, preferred_...]
    ppermute x6, waiting for transfers between devices: 1.84 us -> 4.32 us  [halve(): part = keep + lax.ppermute(send, axis, flip_pairs(axis, bit))]
    ppermute x6, starting transfers between devices: 6.44 us -> 8.23 us  [double(): got = lax.ppermute(piece, axis, flip_pairs(axis, bit))]
    ppermute x6, starting transfers between devices: 11.7 us -> 10.1 us  [halve(): part = part + lax.ppermute(part, axis, flip_pairs(axis, bit))]
    unnamed x43 -> x45, local copies, waits for them, and re-layouts: 2.35 us -> 2.34 us
  transfers between devices with their start and end apart: 27 -> 27, of which waited for: 10 -> 10; matrix products, arithmetic and copies ran while one was open for 15% -> 17% of each run, Pallas kernels for 0% -> 0%
where the time goes in v11:
time: 105 us
  starting transfers between devices  50.5 us (48%)
  waiting for transfers between devices  19.6 us (19%)
  other arithmetic  14.4 us (14%)
  local copies, waits for them, and re-layouts  10.1 us (10%)
  matrix products  8.47 us (8%)
  between operations  1.6 us (2%)
    ppermute x6, starting transfers between devices, halve(): part = keep + lax.ppermute(send, axis, flip_pairs(axis, bit))  12.4 us
    ppermute x6, starting transfers between devices, halve(): part = part + lax.ppermute(part, axis, flip_pairs(axis, bit))  10.1 us
    ppermute x2, starting transfers between devices, widen(): lax.ppermute(tail, axis, [(i, i + dist) for i in range(count - dist)])  9.47 us
    ppermute x6, starting transfers between devices, double(): got = lax.ppermute(piece, axis, flip_pairs(axis, bit))  8.23 us
    ppermute x1, starting transfers between devices, sum_everywhere(): got = lax.ppermute(piece, axis, flip_pairs(axis, bit))  6.36 us
    ppermute x2, waiting for transfers between devices, widen(): lax.ppermute(head, axis, [(i + dist, i) for i in range(count - dist)])  6.35 us
    ppermute x6, waiting for transfers between devices, halve(): part = keep + lax.ppermute(send, axis, flip_pairs(axis, bit))  4.32 us
    dot_general x3, matrix products, shards(): jnp.dot(lifted[:, way * width:(way + 1) * width].T, grads_all, preferred_...  4.24 us
  transfers between devices with their start and end apart: 27, of which 10 were waited for; matrix products, arithmetic and copies ran while one was open for 17% of the time, Pallas kernels for 0%

profile of v11, /device:TPU:1, one launch (start us, length us, event | category | flops | bytes accessed | tf_op | source)
XLA Modules:
  0.0 104.7 jit_solution(15913788461536759450)
XLA Ops:
  5.5 4.6 %collective-permute-start = (bf16[4,32,832]{2,1,0:T(8,128)(2,1)S(1)}, bf16[4,32,832]{2,1,0:T(8,128)(2,1)S(1)}, u32[]{:S(2)}, u32[]{:S(2)}) collective-permute-start(bf16[4,32,832]{2,1,0:T(8,128)(2,1)S(1)} %concatenate.104), channel_id=1, source_target_pairs={{0,8},{8,16},{16,24},{1,9},{9,17},{17,25},{2,10},{10,18},{18,26},{... | collective-permute-start | bytes 638984 | tf_op jit(solution)/shard_map/ppermute | solution.py:109
  10.3 3.1 %collective-permute-done.1 = bf16[4,32,832]{2,1,0:T(8,128)(2,1)S(1)} collective-permute-done((bf16[4,32,832]{2,1,0:T(8,128)(2,1)S(1)}, bf16[4,32,832]{2,1,0:T(8,128)(2,1)S(1)}, u32[]{:S(2)}, u32[]{:S(2)}) %collective-permute-start.1) | collective-permute-done | bytes 213024 | tf_op jit(solution)/shard_map/ppermute | solution.py:110
  14.4 4.9 %collective-permute-start.2 = (bf16[12,4,832]{2,1,0:T(4,128)(2,1)S(1)}, bf16[12,4,832]{2,1,0:T(4,128)(2,1)S(1)}, u32[]{:S(2)}, u32[]{:S(2)}) collective-permute-start(bf16[12,4,832]{2,1,0:T(4,128)(2,1)S(1)} %get-tuple-element.27), channel_id=1, source_target_pairs={{0,1},{1,2},{2,3},{3,4},{4,5},{5,6},{6,7},{8,9},{9,10},{10,11},{11... | collective-permute-start | bytes 239624 | tf_op jit(solution)/shard_map/ppermute | solution.py:109
  19.2 1.9 %collective-permute-start.3 = (bf16[12,4,832]{2,1,0:T(4,128)(2,1)S(1)}, bf16[12,4,832]{2,1,0:T(4,128)(2,1)S(1)}, u32[]{:S(2)}, u32[]{:S(2)}) collective-permute-start(bf16[12,4,832]{2,1,0:T(4,128)(2,1)S(1)} %get-tuple-element.28), channel_id=1, source_target_pairs={{1,0},{2,1},{3,2},{4,3},{5,4},{6,5},{7,6},{9,8},{10,9},{11,10},{12... | collective-permute-start | bytes 239624 | tf_op jit(solution)/shard_map/ppermute | solution.py:110
  21.8 3.2 %collective-permute-done.3 = bf16[12,4,832]{2,1,0:T(4,128)(2,1)S(1)} collective-permute-done((bf16[12,4,832]{2,1,0:T(4,128)(2,1)S(1)}, bf16[12,4,832]{2,1,0:T(4,128)(2,1)S(1)}, u32[]{:S(2)}, u32[]{:S(2)}) %collective-permute-start.3) | collective-permute-done | bytes 79904 | tf_op jit(solution)/shard_map/ppermute | solution.py:110
  32.6 2.1 %convolution_select_fusion.1 = f32[8,8,5,512]{3,1,2,0:T(8,128)S(1)} fusion(bf16[3,3,160,512]{3,2,1,0:T(8,128)(2,1)} %bitcast.88, pred[8,5]{0,1:T(8,128)(4,1)S(1)} %copy-done.19, bf16[10,1,7,2,160]{4,2,3,0,1:T(8,128)(2,1)S(1)} %slice.371, bf16[10,1,8,5,160]{4,2,3,0,1:T(8,128)(2,1)S(1)} %copy.16), kind=kOutput, calls=%fused_computation.9 | convolution fusion | flops 472560640 | bytes 2302760 | tf_op jit(solution)/shard_map/conv_general_dilated | solution.py:157
  43.5 1.4 %convolution_multiply_fusion.1 = f32[256,512]{1,0:T(8,128)S(1)} fusion(bf16[512,768]{1,0:T(8,128)(2,1)S(1)} %fusion.6, bf16[128,512]{1,0:T(8,128)(2,1)} %collective-permute-done.7, bf16[128,512]{1,0:T(8,128)(2,1)} %collective-permute-done.6, bf16[128,512]{1,0:T(8,128)(2,1)} %bitcast.33, bf16[128,512]{1,0:T(8,128)(2,1)} %bitcast.32), kind=kOutput, calls=%fused_computation.7 | convolution fusion | flops 136445952 | bytes 1310720 | tf_op jit(solution)/shard_map/dot_general | solution.py:282
  45.0 3.1 %collective-permute-start.14 = (f32[128,512]{1,0:T(8,128)S(1)}, f32[128,512]{1,0:T(8,128)S(1)}, u32[]{:S(2)}, u32[]{:S(2)}) collective-permute-start(f32[128,512]{1,0:T(8,128)S(1)} %constant_dynamic-slice_fusion.3), channel_id=1, source_target_pairs={{0,8},{8,0},{16,24},{24,16},{1,9},{9,1},{17,25},{25,17},{2,10},{10... | collective-permute-start | bytes 786440 | tf_op jit(solution)/shard_map/ppermute | solution.py:46
  48.0 1.4 %convolution_multiply_fusion.2 = f32[256,512]{1,0:T(8,128)S(1)} fusion(bf16[512,768]{1,0:T(8,128)(2,1)S(1)} %fusion.6, bf16[128,512]{1,0:T(8,128)(2,1)} %collective-permute-done.7, bf16[128,512]{1,0:T(8,128)(2,1)} %collective-permute-done.6, bf16[128,512]{1,0:T(8,128)(2,1)} %bitcast.33, bf16[128,512]{1,0:T(8,128)(2,1)} %bitcast.32), kind=kOutput, calls=%fused_computation.8 | convolution fusion | flops 136445952 | bytes 1310720 | tf_op jit(solution)/shard_map/dot_general | solution.py:282
  50.9 1.4 %convolution_multiply_fusion = f32[256,512]{1,0:T(8,128)S(1)} fusion(bf16[512,768]{1,0:T(8,128)(2,1)S(1)} %fusion.6, bf16[128,512]{1,0:T(8,128)(2,1)} %collective-permute-done.7, bf16[128,512]{1,0:T(8,128)(2,1)} %collective-permute-done.6, bf16[128,512]{1,0:T(8,128)(2,1)} %bitcast.33, bf16[128,512]{1,0:T(8,128)(2,1)} %bitcast.32), kind=kOutput, calls=%fused_computation.6 | convolution fusion | flops 136445952 | bytes 1310720 | tf_op jit(solution)/shard_map/dot_general | solution.py:282
  52.3 3.2 %collective-permute-start.20 = (f32[128,512]{1,0:T(8,128)S(1)}, f32[128,512]{1,0:T(8,128)S(1)}, u32[]{:S(2)}, u32[]{:S(2)}) collective-permute-start(f32[128,512]{1,0:T(8,128)S(1)} %constant_dynamic-slice_fusion.1), channel_id=1, source_target_pairs={{0,16},{8,24},{16,0},{24,8},{1,17},{9,25},{17,1},{25,9},{2,18},{10... | collective-permute-start | bytes 786440 | tf_op jit(solution)/shard_map/ppermute | solution.py:46
  55.6 2.1 %collective-permute-start.15 = (f32[64,512]{1,0:T(8,128)S(1)}, f32[64,512]{1,0:T(8,128)S(1)}, u32[]{:S(2)}, u32[]{:S(2)}) collective-permute-start(f32[64,512]{1,0:T(8,128)S(1)} %constant_dynamic-slice_fusion.2), channel_id=1, source_target_pairs={{0,16},{8,24},{16,0},{24,8},{1,17},{9,25},{17,1},{25,9},{2,18},{10... | collective-permute-start | bytes 393224 | tf_op jit(solution)/shard_map/ppermute | solution.py:46
  59.0 2.3 %collective-permute-done.20 = f32[128,512]{1,0:T(8,128)S(1)} collective-permute-done((f32[128,512]{1,0:T(8,128)S(1)}, f32[128,512]{1,0:T(8,128)S(1)}, u32[]{:S(2)}, u32[]{:S(2)}) %collective-permute-start.20) | collective-permute-done | bytes 262176 | tf_op jit(solution)/shard_map/ppermute | solution.py:46
  67.5 4.2 %collective-permute-start.22 = (f32[64,512]{1,0:T(8,128)S(1)}, f32[64,512]{1,0:T(8,128)S(1)}, u32[]{:S(2)}, u32[]{:S(2)}) collective-permute-start(f32[64,512]{1,0:T(8,128)S(1)} %dynamic-slice_add_fusion.3), channel_id=1, source_target_pairs={{0,2},{1,3},{2,0},{3,1},{4,6},{5,7},{6,4},{7,5},{8,10},{9,11},{10,... | collective-permute-start | bytes 393224 | tf_op jit(solution)/shard_map/ppermute | solution.py:49
  71.7 3.1 %collective-permute-done.16 = f32[64,512]{1,0:T(8,128)S(1)} collective-permute-done((f32[64,512]{1,0:T(8,128)S(1)}, f32[64,512]{1,0:T(8,128)S(1)}, u32[]{:S(2)}, u32[]{:S(2)}) %collective-permute-start.16) | collective-permute-done | bytes 131104 | tf_op jit(solution)/shard_map/ppermute | solution.py:49
  75.3 2.9 %collective-permute-start.11 = (f32[64,512]{1,0:T(8,128)S(1)}, f32[64,512]{1,0:T(8,128)S(1)}, u32[]{:S(2)}, u32[]{:S(2)}) collective-permute-start(f32[64,512]{1,0:T(8,128)S(1)} %add.228), channel_id=1, source_target_pairs={{0,4},{1,5},{2,6},{3,7},{4,0},{5,1},{6,2},{7,3},{8,12},{9,13},{10,... | collective-permute-start | bytes 393224 | tf_op jit(solution)/shard_map/ppermute | solution.py:49
  79.5 2.5 %collective-permute-start.18 = (bf16[64,512]{1,0:T(8,128)(2,1)S(1)}, bf16[64,512]{1,0:T(8,128)(2,1)S(1)}, u32[]{:S(2)}, u32[]{:S(2)}) collective-permute-start(bf16[64,512]{1,0:T(8,128)(2,1)S(1)} %add_convert_fusion.1), channel_id=1, source_target_pairs={{0,16},{8,24},{16,0},{24,8},{1,17},{9,25},{17,1},{25,9},{2,18},{10... | collective-permute-start | bytes 196616 | tf_op jit(solution)/shard_map/ppermute | solution.py:56
  82.4 1.9 %collective-permute-start.24 = (bf16[64,512]{1,0:T(8,128)(2,1)S(1)}, bf16[64,512]{1,0:T(8,128)(2,1)S(1)}, u32[]{:S(2)}, u32[]{:S(2)}) collective-permute-start(bf16[64,512]{1,0:T(8,128)(2,1)S(1)} %add_convert_fusion), channel_id=1, source_target_pairs={{0,4},{1,5},{2,6},{3,7},{4,0},{5,1},{6,2},{7,3},{8,12},{9,13},{10,... | collective-permute-start | bytes 196616 | tf_op jit(solution)/shard_map/ppermute | solution.py:56
  85.8 2.1 %collective-permute-start.13 = (bf16[128,512]{1,0:T(8,128)(2,1)S(1)}, bf16[128,512]{1,0:T(8,128)(2,1)S(1)}, u32[]{:S(2)}, u32[]{:S(2)}) collective-permute-start(bf16[128,512]{1,0:T(8,128)(2,1)S(1)} %pad_maximum_fusion.9), channel_id=1, source_target_pairs={{0,2},{1,3},{2,0},{3,1},{4,6},{5,7},{6,4},{7,5},{8,10},{9,11},{10,... | collective-permute-start | bytes 393224 | tf_op jit(solution)/shard_map/ppermute | solution.py:56
  88.0 2.4 %collective-permute-done.13 = bf16[128,512]{1,0:T(8,128)(2,1)S(1)} collective-permute-done((bf16[128,512]{1,0:T(8,128)(2,1)S(1)}, bf16[128,512]{1,0:T(8,128)(2,1)S(1)}, u32[]{:S(2)}, u32[]{:S(2)}) %collective-permute-start.13) | collective-permute-done | bytes 131104 | tf_op jit(solution)/shard_map/ppermute | solution.py:56
  90.6 1.5 %collective-permute-done.25 = bf16[128,512]{1,0:T(8,128)(2,1)S(1)} collective-permute-done((bf16[128,512]{1,0:T(8,128)(2,1)S(1)}, bf16[128,512]{1,0:T(8,128)(2,1)S(1)}, u32[]{:S(2)}, u32[]{:S(2)}) %collective-permute-start.25) | collective-permute-done | bytes 131104 | tf_op jit(solution)/shard_map/ppermute | solution.py:56
  92.2 6.4 %collective-permute-start.26 = (bf16[768,512]{1,0:T(8,128)(2,1)S(1)}, bf16[768,512]{1,0:T(8,128)(2,1)S(1)}, u32[]{:S(2)}, u32[]{:S(2)}) collective-permute-start(bf16[768,512]{1,0:T(8,128)(2,1)S(1)} %select_dynamic-update-slice_fusion), channel_id=1, source_target_pairs={{0,1},{1,0},{2,3},{3,2},{4,5},{5,4},{6,7},{7,6},{8,9},{9,8},{10,11... | collective-permute-start | bytes 2359304 | tf_op jit(solution)/shard_map/ppermute | solution.py:73
  99.8 1.5 %fusion.94 = bf16[4,32,128]{2,1,0:T(8,128)(2,1)} fusion(f32[8,36,128]{2,1,0:T(8,128)S(1)} %get-tuple-element.16, f32[8,36,128]{2,1,0:T(8,128)} %get-tuple-element.33), kind=kLoop, calls=%fused_computation.195 | loop fusion | flops 32768 | bytes 163840 | tf_op jit(solution)/shard_map/convert_element_type | solution.py:171
  102.7 2.0 %maximum_convert_fusion = f32[1440,512]{1,0:T(8,128)} fusion(bf16[672,512]{1,0:T(8,128)(2,1)S(1)} %slice.446, bf16[768,512]{1,0:T(8,128)(2,1)S(1)} %get-tuple-element.19), kind=kLoop, calls=%fused_computation.4 | loop fusion | flops 2949120 | bytes 4423680 | tf_op jit(solution)/shard_map/convert_element_type | solution.py:77
  (191 shorter events, 37.8 us)
Async XLA Ops:
  4.2 9.3 %collective-permute-start.1 = (bf16[4,32,832]{2,1,0:T(8,128)(2,1)S(1)}, bf16[4,32,832]{2,1,0:T(8,128)(2,1)S(1)}, u32[]{:S(2)}, u32[]{:S(2)}) collective-permute-start(bf16[4,32,832]{2,1,0:T(8,128)(2,1)S(1)} %concatenate.104), channel_id=1, source_target_pairs={{8,0},{16,8},{24,16},{9,1},{17,9},{25,17},{10,2},{18,10},{26,18},{... | collective-permute-start | bytes 638984 | tf_op jit(solution)/shard_map/ppermute | solution.py:110
  5.5 8.8 %collective-permute-start = (bf16[4,32,832]{2,1,0:T(8,128)(2,1)S(1)}, bf16[4,32,832]{2,1,0:T(8,128)(2,1)S(1)}, u32[]{:S(2)}, u32[]{:S(2)}) collective-permute-start(bf16[4,32,832]{2,1,0:T(8,128)(2,1)S(1)} %concatenate.104), channel_id=1, source_target_pairs={{0,8},{8,16},{16,24},{1,9},{9,17},{17,25},{2,10},{10,18},{18,26},{... | collective-permute-start | bytes 638984 | tf_op jit(solution)/shard_map/ppermute | solution.py:109
  14.4 7.5 %collective-permute-start.2 = (bf16[12,4,832]{2,1,0:T(4,128)(2,1)S(1)}, bf16[12,4,832]{2,1,0:T(4,128)(2,1)S(1)}, u32[]{:S(2)}, u32[]{:S(2)}) collective-permute-start(bf16[12,4,832]{2,1,0:T(4,128)(2,1)S(1)} %get-tuple-element.27), channel_id=1, source_target_pairs={{0,1},{1,2},{2,3},{3,4},{4,5},{5,6},{6,7},{8,9},{9,10},{10,11},{11... | collective-permute-start | bytes 239624 | tf_op jit(solution)/shard_map/ppermute | solution.py:109
  19.2 5.8 %collective-permute-start.3 = (bf16[12,4,832]{2,1,0:T(4,128)(2,1)S(1)}, bf16[12,4,832]{2,1,0:T(4,128)(2,1)S(1)}, u32[]{:S(2)}, u32[]{:S(2)}) collective-permute-start(bf16[12,4,832]{2,1,0:T(4,128)(2,1)S(1)} %get-tuple-element.28), channel_id=1, source_target_pairs={{1,0},{2,1},{3,2},{4,3},{5,4},{6,5},{7,6},{9,8},{10,9},{11,10},{12... | collective-permute-start | bytes 239624 | tf_op jit(solution)/shard_map/ppermute | solution.py:110
  31.9 10.7 %collective-permute-start.5 = (bf16[6,34,160]{2,1,0:T(8,128)(2,1)}, bf16[6,34,160]{2,1,0:T(8,128)(2,1)S(1)}, u32[]{:S(2)}, u32[]{:S(2)}) collective-permute-start(bf16[6,34,160]{2,1,0:T(8,128)(2,1)} %fusion.77), channel_id=1, source_target_pairs={{0,1},{1,0},{2,3},{3,2},{4,5},{5,4},{6,7},{7,6},{8,9},{9,8},{10,11... | collective-permute-start | bytes 195848 | tf_op jit(solution)/shard_map/ppermute | solution.py:259
  31.9 11.1 %collective-permute-start.4 = (bf16[6,34,160]{2,1,0:T(8,128)(2,1)}, bf16[6,34,160]{2,1,0:T(8,128)(2,1)S(1)}, u32[]{:S(2)}, u32[]{:S(2)}) collective-permute-start(bf16[6,34,160]{2,1,0:T(8,128)(2,1)} %slice.422), channel_id=1, source_target_pairs={{0,1},{1,0},{2,3},{3,2},{4,5},{5,4},{6,7},{7,6},{8,9},{9,8},{10,11... | collective-permute-start | bytes 195848 | tf_op jit(solution)/shard_map/ppermute | solution.py:259
  37.3 6.2 %collective-permute-start.6 = (bf16[128,512]{1,0:T(8,128)(2,1)}, bf16[128,512]{1,0:T(8,128)(2,1)}, u32[]{:S(2)}, u32[]{:S(2)}) collective-permute-start(bf16[128,512]{1,0:T(8,128)(2,1)} %bitcast.32), channel_id=1, source_target_pairs={{0,1},{1,0},{2,3},{3,2},{4,5},{5,4},{6,7},{7,6},{8,9},{9,8},{10,11... | collective-permute-start | bytes 393224 | tf_op jit(solution)/shard_map/ppermute | solution.py:260
  45.0 10.5 %collective-permute-start.14 = (f32[128,512]{1,0:T(8,128)S(1)}, f32[128,512]{1,0:T(8,128)S(1)}, u32[]{:S(2)}, u32[]{:S(2)}) collective-permute-start(f32[128,512]{1,0:T(8,128)S(1)} %constant_dynamic-slice_fusion.3), channel_id=1, source_target_pairs={{0,8},{8,0},{16,24},{24,16},{1,9},{9,1},{17,25},{25,17},{2,10},{10... | collective-permute-start | bytes 786440 | tf_op jit(solution)/shard_map/ppermute | solution.py:46
  49.5 8.2 %collective-permute-start.8 = (f32[128,512]{1,0:T(8,128)S(1)}, f32[128,512]{1,0:T(8,128)S(1)}, u32[]{:S(2)}, u32[]{:S(2)}) collective-permute-start(f32[128,512]{1,0:T(8,128)S(1)} %constant_dynamic-slice_fusion.5), channel_id=1, source_target_pairs={{0,2},{1,3},{2,0},{3,1},{4,6},{5,7},{6,4},{7,5},{8,10},{9,11},{10,... | collective-permute-start | bytes 786440 | tf_op jit(solution)/shard_map/ppermute | solution.py:46
  52.3 9.0 %collective-permute-start.20 = (f32[128,512]{1,0:T(8,128)S(1)}, f32[128,512]{1,0:T(8,128)S(1)}, u32[]{:S(2)}, u32[]{:S(2)}) collective-permute-start(f32[128,512]{1,0:T(8,128)S(1)} %constant_dynamic-slice_fusion.1), channel_id=1, source_target_pairs={{0,16},{8,24},{16,0},{24,8},{1,17},{9,25},{17,1},{25,9},{2,18},{10... | collective-permute-start | bytes 786440 | tf_op jit(solution)/shard_map/ppermute | solution.py:46
  55.6 8.6 %collective-permute-start.15 = (f32[64,512]{1,0:T(8,128)S(1)}, f32[64,512]{1,0:T(8,128)S(1)}, u32[]{:S(2)}, u32[]{:S(2)}) collective-permute-start(f32[64,512]{1,0:T(8,128)S(1)} %constant_dynamic-slice_fusion.2), channel_id=1, source_target_pairs={{0,16},{8,24},{16,0},{24,8},{1,17},{9,25},{17,1},{25,9},{2,18},{10... | collective-permute-start | bytes 393224 | tf_op jit(solution)/shard_map/ppermute | solution.py:46
  57.8 7.8 %collective-permute-start.9 = (f32[64,512]{1,0:T(8,128)S(1)}, f32[64,512]{1,0:T(8,128)S(1)}, u32[]{:S(2)}, u32[]{:S(2)}) collective-permute-start(f32[64,512]{1,0:T(8,128)S(1)} %constant_dynamic-slice_fusion.4), channel_id=1, source_target_pairs={{0,8},{8,0},{16,24},{24,16},{1,9},{9,1},{17,25},{25,17},{2,10},{10... | collective-permute-start | bytes 393224 | tf_op jit(solution)/shard_map/ppermute | solution.py:46
  61.4 6.1 %collective-permute-start.21 = (f32[64,512]{1,0:T(8,128)S(1)}, f32[64,512]{1,0:T(8,128)S(1)}, u32[]{:S(2)}, u32[]{:S(2)}) collective-permute-start(f32[64,512]{1,0:T(8,128)S(1)} %constant_dynamic-slice_fusion), channel_id=1, source_target_pairs={{0,4},{1,5},{2,6},{3,7},{4,0},{5,1},{6,2},{7,3},{8,12},{9,13},{10,... | collective-permute-start | bytes 393224 | tf_op jit(solution)/shard_map/ppermute | solution.py:46
  64.2 10.7 %collective-permute-start.16 = (f32[64,512]{1,0:T(8,128)S(1)}, f32[64,512]{1,0:T(8,128)S(1)}, u32[]{:S(2)}, u32[]{:S(2)}) collective-permute-start(f32[64,512]{1,0:T(8,128)S(1)} %dynamic-slice_add_fusion.4), channel_id=1, source_target_pairs={{0,4},{1,5},{2,6},{3,7},{4,0},{5,1},{6,2},{7,3},{8,12},{9,13},{10,... | collective-permute-start | bytes 393224 | tf_op jit(solution)/shard_map/ppermute | solution.py:49
  65.6 9.7 %collective-permute-start.10 = (f32[64,512]{1,0:T(8,128)S(1)}, f32[64,512]{1,0:T(8,128)S(1)}, u32[]{:S(2)}, u32[]{:S(2)}) collective-permute-start(f32[64,512]{1,0:T(8,128)S(1)} %dynamic-slice_add_fusion.5), channel_id=1, source_target_pairs={{0,16},{8,24},{16,0},{24,8},{1,17},{9,25},{17,1},{25,9},{2,18},{10... | collective-permute-start | bytes 393224 | tf_op jit(solution)/shard_map/ppermute | solution.py:49
  67.5 10.7 %collective-permute-start.22 = (f32[64,512]{1,0:T(8,128)S(1)}, f32[64,512]{1,0:T(8,128)S(1)}, u32[]{:S(2)}, u32[]{:S(2)}) collective-permute-start(f32[64,512]{1,0:T(8,128)S(1)} %dynamic-slice_add_fusion.3), channel_id=1, source_target_pairs={{0,2},{1,3},{2,0},{3,1},{4,6},{5,7},{6,4},{7,5},{8,10},{9,11},{10,... | collective-permute-start | bytes 393224 | tf_op jit(solution)/shard_map/ppermute | solution.py:49
  74.8 4.7 %collective-permute-start.17 = (f32[64,512]{1,0:T(8,128)S(1)}, f32[64,512]{1,0:T(8,128)S(1)}, u32[]{:S(2)}, u32[]{:S(2)}) collective-permute-start(f32[64,512]{1,0:T(8,128)S(1)} %add.236), channel_id=1, source_target_pairs={{0,2},{1,3},{2,0},{3,1},{4,6},{5,7},{6,4},{7,5},{8,10},{9,11},{10,... | collective-permute-start | bytes 393224 | tf_op jit(solution)/shard_map/ppermute | solution.py:49
  75.3 6.7 %collective-permute-start.11 = (f32[64,512]{1,0:T(8,128)S(1)}, f32[64,512]{1,0:T(8,128)S(1)}, u32[]{:S(2)}, u32[]{:S(2)}) collective-permute-start(f32[64,512]{1,0:T(8,128)S(1)} %add.228), channel_id=1, source_target_pairs={{0,4},{1,5},{2,6},{3,7},{4,0},{5,1},{6,2},{7,3},{8,12},{9,13},{10,... | collective-permute-start | bytes 393224 | tf_op jit(solution)/shard_map/ppermute | solution.py:49
  78.2 4.2 %collective-permute-start.23 = (f32[64,512]{1,0:T(8,128)S(1)}, f32[64,512]{1,0:T(8,128)S(1)}, u32[]{:S(2)}, u32[]{:S(2)}) collective-permute-start(f32[64,512]{1,0:T(8,128)S(1)} %add.244), channel_id=1, source_target_pairs={{0,8},{8,0},{16,24},{24,16},{1,9},{9,1},{17,25},{25,17},{2,10},{10... | collective-permute-start | bytes 393224 | tf_op jit(solution)/shard_map/ppermute | solution.py:49
  79.5 4.8 %collective-permute-start.18 = (bf16[64,512]{1,0:T(8,128)(2,1)S(1)}, bf16[64,512]{1,0:T(8,128)(2,1)S(1)}, u32[]{:S(2)}, u32[]{:S(2)}) collective-permute-start(bf16[64,512]{1,0:T(8,128)(2,1)S(1)} %add_convert_fusion.1), channel_id=1, source_target_pairs={{0,16},{8,24},{16,0},{24,8},{1,17},{9,25},{17,1},{25,9},{2,18},{10... | collective-permute-start | bytes 196616 | tf_op jit(solution)/shard_map/ppermute | solution.py:56
  82.4 5.5 %collective-permute-start.24 = (bf16[64,512]{1,0:T(8,128)(2,1)S(1)}, bf16[64,512]{1,0:T(8,128)(2,1)S(1)}, u32[]{:S(2)}, u32[]{:S(2)}) collective-permute-start(bf16[64,512]{1,0:T(8,128)(2,1)S(1)} %add_convert_fusion), channel_id=1, source_target_pairs={{0,4},{1,5},{2,6},{3,7},{4,0},{5,1},{6,2},{7,3},{8,12},{9,13},{10,... | collective-permute-start | bytes 196616 | tf_op jit(solution)/shard_map/ppermute | solution.py:56
  84.4 6.1 %collective-permute-start.19 = (bf16[128,512]{1,0:T(8,128)(2,1)S(1)}, bf16[128,512]{1,0:T(8,128)(2,1)S(1)}, u32[]{:S(2)}, u32[]{:S(2)}) collective-permute-start(bf16[128,512]{1,0:T(8,128)(2,1)S(1)} %pad_maximum_fusion.10), channel_id=1, source_target_pairs={{0,8},{8,0},{16,24},{24,16},{1,9},{9,1},{17,25},{25,17},{2,10},{10... | collective-permute-start | bytes 393224 | tf_op jit(solution)/shard_map/ppermute | solution.py:56
  85.8 4.6 %collective-permute-start.13 = (bf16[128,512]{1,0:T(8,128)(2,1)S(1)}, bf16[128,512]{1,0:T(8,128)(2,1)S(1)}, u32[]{:S(2)}, u32[]{:S(2)}) collective-permute-start(bf16[128,512]{1,0:T(8,128)(2,1)S(1)} %pad_maximum_fusion.9), channel_id=1, source_target_pairs={{0,2},{1,3},{2,0},{3,1},{4,6},{5,7},{6,4},{7,5},{8,10},{9,11},{10,... | collective-permute-start | bytes 393224 | tf_op jit(solution)/shard_map/ppermute | solution.py:56
  92.2 9.8 %collective-permute-start.26 = (bf16[768,512]{1,0:T(8,128)(2,1)S(1)}, bf16[768,512]{1,0:T(8,128)(2,1)S(1)}, u32[]{:S(2)}, u32[]{:S(2)}) collective-permute-start(bf16[768,512]{1,0:T(8,128)(2,1)S(1)} %select_dynamic-update-slice_fusion), channel_id=1, source_target_pairs={{0,1},{1,0},{2,3},{3,2},{4,5},{5,4},{6,7},{7,6},{8,9},{9,8},{10,11... | collective-permute-start | bytes 2359304 | tf_op jit(solution)/shard_map/ppermute | solution.py:73
  (24 other events, 81.4 us)

commit v12 on v8

--- a/solution.py
+++ b/solution.py
@@ -70,18 +70,19 @@
             part[way * width : (way + 1) * width], order, max(len(order) - SUM_SHARED, 0)
         )
         pieces.append(double(chunk.astype(jnp.bfloat16), halved))
-    piece = jnp.concatenate(pieces, axis=0)
     if len(first_halved) == 1:
         axis, bit = first_halved[0]
         upper = (lax.axis_index(axis) >> bit) & 1
-        got = lax.ppermute(piece, axis, flip_pairs(axis, bit))
-        low = jnp.where(upper == 0, piece, got)
-        high = jnp.where(upper == 0, got, piece)
+        pairs = flip_pairs(axis, bit)
+        swapped = [(p, lax.ppermute(p, axis, pairs)) for p in pieces]
+        low = jnp.concatenate([jnp.where(upper == 0, p, g) for p, g in swapped], axis=0)
+        high = jnp.concatenate([jnp.where(upper == 0, g, p) for p, g in swapped], axis=0)
         split = KIN - low.shape[0]
         kernel_part = jnp.concatenate([low, high[:split]], axis=0).astype(jnp.float32)
         return kernel_part, high[split].astype(jnp.float32)
-    summed = double(piece, first_halved).astype(jnp.float32)
+    summed = double(jnp.concatenate(pieces, axis=0), first_halved).astype(jnp.float32)
     return summed[:KIN], summed[KIN]
+
 
 def tap_columns(padded, rows_dev, cols_dev, reverse):
     pieces = []

time: 105 us -> 103 us (0.981)
  waiting for transfers between devices: 16.7 us -> 15.6 us
    ppermute x2, waiting for transfers between devices: 5.99 us -> 2.56 us  [widen(): lax.ppermute(head, axis, [(i + dist, i) for i in range(count - dist)])]
    ppermute x6, starting transfers between devices: 11.7 us -> 13.6 us  [halve(): part = part + lax.ppermute(part, axis, flip_pairs(axis, bit))]
    ppermute x6, waiting for transfers between devices: 4.3 us -> 2.4 us  [halve(): part = part + lax.ppermute(part, axis, flip_pairs(axis, bit))]
    ppermute x6, starting transfers between devices: 16.2 us -> 14.3 us  [halve(): part = keep + lax.ppermute(send, axis, flip_pairs(axis, bit))]
    ppermute x6, waiting for transfers between devices: 1.84 us -> 3.55 us  [halve(): part = keep + lax.ppermute(send, axis, flip_pairs(axis, bit))]
    ppermute x2, starting transfers between devices: 3.21 us -> 4.75 us  [widen(): lax.ppermute(head, axis, [(i + dist, i) for i in range(count - dist)])]
    ppermute x2, starting transfers between devices: 9.47 us -> 7.93 us  [widen(): lax.ppermute(tail, axis, [(i, i + dist) for i in range(count - dist)])]
    ppermute x6, starting transfers between devices: 6.44 us -> 5 us  [double(): got = lax.ppermute(piece, axis, flip_pairs(axis, bit))]
  transfers between devices with their start and end apart: 27 -> 29, of which waited for: 10 -> 10; matrix products, arithmetic and copies ran while one was open for 15% -> 6% of each run, Pallas kernels for 0% -> 0%
where the time goes in v12:
time: 103 us
  starting transfers between devices  53.8 us (52%)
  waiting for transfers between devices  15.6 us (15%)
  other arithmetic  14.6 us (14%)
  local copies, waits for them, and re-layouts  11.2 us (11%)
  matrix products  5.76 us (6%)
  between operations  1.67 us (2%)
    ppermute x6, starting transfers between devices, halve(): part = keep + lax.ppermute(send, axis, flip_pairs(axis, bit))  14.3 us
    ppermute x6, starting transfers between devices, halve(): part = part + lax.ppermute(part, axis, flip_pairs(axis, bit))  13.6 us
    ppermute x2, starting transfers between devices, widen(): lax.ppermute(tail, axis, [(i, i + dist) for i in range(count - dist)])  7.93 us
    ppermute x3, starting transfers between devices, sum_everywhere(): swapped = [(p, lax.ppermute(p, axis, pairs)) for p in pieces]  7.14 us
    ppermute x6, starting transfers between devices, double(): got = lax.ppermute(piece, axis, flip_pairs(axis, bit))  5 us
    ppermute x2, starting transfers between devices, widen(): lax.ppermute(head, axis, [(i + dist, i) for i in range(count - dist)])  4.75 us
    ppermute x6, waiting for transfers between devices, double(): got = lax.ppermute(piece, axis, flip_pairs(axis, bit))  4.72 us
    conv_general_dilated x4, matrix products, convolve(): lax.conv_general_dilated(field[None], weights, (1, 1), 'VALID', dimension...  4.23 us
  transfers between devices with their start and end apart: 29, of which 10 were waited for; matrix products, arithmetic and copies ran while one was open for 6% of the time, Pallas kernels for 0%

profile of v12, /device:TPU:1, one launch (start us, length us, event | category | flops | bytes accessed | tf_op | source)
XLA Modules:
  0.0 102.5 jit_solution(13299407711933135314)
XLA Ops:
  4.2 1.3 %collective-permute-start.1 = (bf16[4,32,832]{2,1,0:T(8,128)(2,1)S(1)}, bf16[4,32,832]{2,1,0:T(8,128)(2,1)S(1)}, u32[]{:S(2)}, u32[]{:S(2)}) collective-permute-start(bf16[4,32,832]{2,1,0:T(8,128)(2,1)S(1)} %concatenate.113), channel_id=1, source_target_pairs={{8,0},{16,8},{24,16},{9,1},{17,9},{25,17},{10,2},{18,10},{26,18},{... | collective-permute-start | bytes 638984 | tf_op jit(solution)/shard_map/ppermute | solution.py:115
  5.5 4.6 %collective-permute-start = (bf16[4,32,832]{2,1,0:T(8,128)(2,1)S(1)}, bf16[4,32,832]{2,1,0:T(8,128)(2,1)S(1)}, u32[]{:S(2)}, u32[]{:S(2)}) collective-permute-start(bf16[4,32,832]{2,1,0:T(8,128)(2,1)S(1)} %concatenate.113), channel_id=1, source_target_pairs={{0,8},{8,16},{16,24},{1,9},{9,17},{17,25},{2,10},{10,18},{18,26},{... | collective-permute-start | bytes 638984 | tf_op jit(solution)/shard_map/ppermute | solution.py:114
  10.9 2.6 %collective-permute-done.1 = bf16[4,32,832]{2,1,0:T(8,128)(2,1)S(1)} collective-permute-done((bf16[4,32,832]{2,1,0:T(8,128)(2,1)S(1)}, bf16[4,32,832]{2,1,0:T(8,128)(2,1)S(1)}, u32[]{:S(2)}, u32[]{:S(2)}) %collective-permute-start.1) | collective-permute-done | bytes 213024 | tf_op jit(solution)/shard_map/ppermute | solution.py:115
  14.4 3.5 %collective-permute-start.3 = (bf16[12,4,832]{2,1,0:T(4,128)(2,1)S(1)}, bf16[12,4,832]{2,1,0:T(4,128)(2,1)S(1)}, u32[]{:S(2)}, u32[]{:S(2)}) collective-permute-start(bf16[12,4,832]{2,1,0:T(4,128)(2,1)S(1)} %get-tuple-element.29), channel_id=1, source_target_pairs={{1,0},{2,1},{3,2},{4,3},{5,4},{6,5},{7,6},{9,8},{10,9},{11,10},{12... | collective-permute-start | bytes 239624 | tf_op jit(solution)/shard_map/ppermute | solution.py:115
  17.8 3.3 %collective-permute-start.2 = (bf16[12,4,832]{2,1,0:T(4,128)(2,1)S(1)}, bf16[12,4,832]{2,1,0:T(4,128)(2,1)S(1)}, u32[]{:S(2)}, u32[]{:S(2)}) collective-permute-start(bf16[12,4,832]{2,1,0:T(4,128)(2,1)S(1)} %get-tuple-element.28), channel_id=1, source_target_pairs={{0,1},{1,2},{2,3},{3,4},{4,5},{5,6},{6,7},{8,9},{9,10},{10,11},{11... | collective-permute-start | bytes 239624 | tf_op jit(solution)/shard_map/ppermute | solution.py:114
  30.7 2.1 %convolution_select_fusion.1 = f32[8,8,5,512]{3,1,2,0:T(8,128)S(1)} fusion(bf16[3,3,160,512]{3,2,1,0:T(8,128)(2,1)} %bitcast.90, pred[8,5]{0,1:T(8,128)(4,1)S(1)} %copy-done.27, bf16[10,1,7,2,160]{4,2,3,0,1:T(8,128)(2,1)S(1)} %slice.371, bf16[10,1,8,5,160]{4,2,3,0,1:T(8,128)(2,1)S(1)} %copy.16), kind=kOutput, calls=%fused_computation.10 | convolution fusion | flops 472560640 | bytes 2302760 | tf_op jit(solution)/shard_map/conv_general_dilated | solution.py:162
  43.8 1.5 %convolution_multiply_fusion = f32[768,512]{1,0:T(8,128)S(1)} fusion(s32[]{:T(128)S(6)} %select_n.163, bf16[128,1536]{1,0:T(8,128)(2,1)S(1)} %concatenate.129, bf16[128,1536]{1,0:T(8,128)(2,1)S(1)} %concatenate.131, bf16[128,1536]{1,0:T(8,128)(2,1)S(1)} %concatenate.133, bf16[128,1536]{1,0:T(8,128)(2,1)S(1)} %concatenate.135, ...), kind=kOutput, calls=%fused_computation.4 | convolution fusion | flops 408289280 | bytes 3670020 | tf_op jit(solution)/shard_map/dot_general | solution.py:283
  45.5 5.0 %collective-permute-start.22 = (f32[128,512]{1,0:T(8,128)S(1)}, f32[128,512]{1,0:T(8,128)S(1)}, u32[]{:S(2)}, u32[]{:S(2)}) collective-permute-start(f32[128,512]{1,0:T(8,128)S(1)} %constant_dynamic-slice_fusion.1), channel_id=1, source_target_pairs={{0,16},{8,24},{16,0},{24,8},{1,17},{9,25},{17,1},{25,9},{2,18},{10... | collective-permute-start | bytes 786440 | tf_op jit(solution)/shard_map/ppermute | solution.py:46
  52.5 2.3 %collective-permute-start.8 = (f32[128,512]{1,0:T(8,128)S(1)}, f32[128,512]{1,0:T(8,128)S(1)}, u32[]{:S(2)}, u32[]{:S(2)}) collective-permute-start(f32[128,512]{1,0:T(8,128)S(1)} %constant_dynamic-slice_fusion.5), channel_id=1, source_target_pairs={{0,2},{1,3},{2,0},{3,1},{4,6},{5,7},{6,4},{7,5},{8,10},{9,11},{10,... | collective-permute-start | bytes 786440 | tf_op jit(solution)/shard_map/ppermute | solution.py:46
  54.7 2.3 %collective-permute-done.22 = f32[128,512]{1,0:T(8,128)S(1)} collective-permute-done((f32[128,512]{1,0:T(8,128)S(1)}, f32[128,512]{1,0:T(8,128)S(1)}, u32[]{:S(2)}, u32[]{:S(2)}) %collective-permute-start.22) | collective-permute-done | bytes 262176 | tf_op jit(solution)/shard_map/ppermute | solution.py:46
  57.1 3.3 %collective-permute-start.23 = (f32[64,512]{1,0:T(8,128)S(1)}, f32[64,512]{1,0:T(8,128)S(1)}, u32[]{:S(2)}, u32[]{:S(2)}) collective-permute-start(f32[64,512]{1,0:T(8,128)S(1)} %constant_dynamic-slice_fusion), channel_id=1, source_target_pairs={{0,4},{1,5},{2,6},{3,7},{4,0},{5,1},{6,2},{7,3},{8,12},{9,13},{10,... | collective-permute-start | bytes 393224 | tf_op jit(solution)/shard_map/ppermute | solution.py:46
  64.3 3.4 %collective-permute-start.24 = (f32[64,512]{1,0:T(8,128)S(1)}, f32[64,512]{1,0:T(8,128)S(1)}, u32[]{:S(2)}, u32[]{:S(2)}) collective-permute-start(f32[64,512]{1,0:T(8,128)S(1)} %dynamic-slice_add_fusion.3), channel_id=1, source_target_pairs={{0,2},{1,3},{2,0},{3,1},{4,6},{5,7},{6,4},{7,5},{8,10},{9,11},{10,... | collective-permute-start | bytes 393224 | tf_op jit(solution)/shard_map/ppermute | solution.py:49
  67.7 3.2 %collective-permute-start.17 = (f32[64,512]{1,0:T(8,128)S(1)}, f32[64,512]{1,0:T(8,128)S(1)}, u32[]{:S(2)}, u32[]{:S(2)}) collective-permute-start(f32[64,512]{1,0:T(8,128)S(1)} %dynamic-slice_add_fusion.4), channel_id=1, source_target_pairs={{0,4},{1,5},{2,6},{3,7},{4,0},{5,1},{6,2},{7,3},{8,12},{9,13},{10,... | collective-permute-start | bytes 393224 | tf_op jit(solution)/shard_map/ppermute | solution.py:49
  73.4 1.5 %fusion.101 = bf16[4,32,128]{2,1,0:T(8,128)(2,1)} fusion(f32[8,36,128]{2,1,0:T(8,128)S(1)} %get-tuple-element.16, f32[8,36,128]{2,1,0:T(8,128)} %get-tuple-element.34), kind=kLoop, calls=%fused_computation.206 | loop fusion | flops 32768 | bytes 163840 | tf_op jit(solution)/shard_map/convert_element_type | solution.py:176
  74.9 2.2 %collective-permute-start.18 = (f32[64,512]{1,0:T(8,128)S(1)}, f32[64,512]{1,0:T(8,128)S(1)}, u32[]{:S(2)}, u32[]{:S(2)}) collective-permute-start(f32[64,512]{1,0:T(8,128)S(1)} %add.236), channel_id=1, source_target_pairs={{0,2},{1,3},{2,0},{3,1},{4,6},{5,7},{6,4},{7,5},{8,10},{9,11},{10,... | collective-permute-start | bytes 393224 | tf_op jit(solution)/shard_map/ppermute | solution.py:49
  77.2 2.4 %collective-permute-start.11 = (f32[64,512]{1,0:T(8,128)S(1)}, f32[64,512]{1,0:T(8,128)S(1)}, u32[]{:S(2)}, u32[]{:S(2)}) collective-permute-start(f32[64,512]{1,0:T(8,128)S(1)} %add.228), channel_id=1, source_target_pairs={{0,4},{1,5},{2,6},{3,7},{4,0},{5,1},{6,2},{7,3},{8,12},{9,13},{10,... | collective-permute-start | bytes 393224 | tf_op jit(solution)/shard_map/ppermute | solution.py:49
  80.9 2.4 %collective-permute-done.11 = f32[64,512]{1,0:T(8,128)S(1)} collective-permute-done((f32[64,512]{1,0:T(8,128)S(1)}, f32[64,512]{1,0:T(8,128)S(1)}, u32[]{:S(2)}, u32[]{:S(2)}) %collective-permute-start.11) | collective-permute-done | bytes 131104 | tf_op jit(solution)/shard_map/ppermute | solution.py:49
  84.5 3.4 %collective-permute-done.26 = bf16[64,512]{1,0:T(8,128)(2,1)S(1)} collective-permute-done((bf16[64,512]{1,0:T(8,128)(2,1)S(1)}, bf16[64,512]{1,0:T(8,128)(2,1)S(1)}, u32[]{:S(2)}, u32[]{:S(2)}) %collective-permute-start.26) | collective-permute-done | bytes 65568 | tf_op jit(solution)/shard_map/ppermute | solution.py:56
  89.1 1.3 %collective-permute-start.20 = (bf16[128,512]{1,0:T(8,128)(2,1)S(1)}, bf16[128,512]{1,0:T(8,128)(2,1)S(1)}, u32[]{:S(2)}, u32[]{:S(2)}) collective-permute-start(bf16[128,512]{1,0:T(8,128)(2,1)S(1)} %pad_maximum_fusion.14), channel_id=1, source_target_pairs={{0,8},{8,0},{16,24},{24,16},{1,9},{9,1},{17,25},{25,17},{2,10},{10... | collective-permute-start | bytes 393224 | tf_op jit(solution)/shard_map/ppermute | solution.py:56
  90.6 1.3 %collective-permute-done.27 = bf16[128,512]{1,0:T(8,128)(2,1)S(1)} collective-permute-done((bf16[128,512]{1,0:T(8,128)(2,1)S(1)}, bf16[128,512]{1,0:T(8,128)(2,1)S(1)}, u32[]{:S(2)}, u32[]{:S(2)}) %collective-permute-start.27) | collective-permute-done | bytes 131104 | tf_op jit(solution)/shard_map/ppermute | solution.py:56
  91.9 3.8 %collective-permute-start.28 = (bf16[256,512]{1,0:T(8,128)(2,1)S(1)}, bf16[256,512]{1,0:T(8,128)(2,1)S(1)}, u32[]{:S(2)}, u32[]{:S(2)}) collective-permute-start(bf16[256,512]{1,0:T(8,128)(2,1)S(1)} %pad_maximum_fusion.6), channel_id=1, source_target_pairs={{0,1},{1,0},{2,3},{3,2},{4,5},{5,4},{6,7},{7,6},{8,9},{9,8},{10,11... | collective-permute-start | bytes 786440 | tf_op jit(solution)/shard_map/ppermute | solution.py:77
  95.8 1.4 %collective-permute-start.21 = (bf16[256,512]{1,0:T(8,128)(2,1)S(1)}, bf16[256,512]{1,0:T(8,128)(2,1)S(1)}, u32[]{:S(2)}, u32[]{:S(2)}) collective-permute-start(bf16[256,512]{1,0:T(8,128)(2,1)S(1)} %pad_maximum_fusion.5), channel_id=1, source_target_pairs={{0,1},{1,0},{2,3},{3,2},{4,5},{5,4},{6,7},{7,6},{8,9},{9,8},{10,11... | collective-permute-start | bytes 786440 | tf_op jit(solution)/shard_map/ppermute | solution.py:77
  97.3 1.9 %collective-permute-start.14 = (bf16[256,512]{1,0:T(8,128)(2,1)S(1)}, bf16[256,512]{1,0:T(8,128)(2,1)S(1)}, u32[]{:S(2)}, u32[]{:S(2)}) collective-permute-start(bf16[256,512]{1,0:T(8,128)(2,1)S(1)} %pad_maximum_fusion.4), channel_id=1, source_target_pairs={{0,1},{1,0},{2,3},{3,2},{4,5},{5,4},{6,7},{7,6},{8,9},{9,8},{10,11... | collective-permute-start | bytes 786440 | tf_op jit(solution)/shard_map/ppermute | solution.py:77
  100.5 2.0 %fusion.1 = f32[1440,512]{1,0:T(8,128)} fusion(bf16[256,512]{1,0:T(8,128)(2,1)S(1)} %get-tuple-element.40, bf16[256,512]{1,0:T(8,128)(2,1)S(1)} %get-tuple-element.38, bf16[256,512]{1,0:T(8,128)(2,1)S(1)} %get-tuple-element.36, bf16[256,512]{1,0:T(8,128)(2,1)S(1)} %get-tuple-element.39, bf16[256,512]{1,0:T(8,128)(2,1)S(1)} %get-tuple-element.37, ...), kind=kLoop, calls=%fused_computation.7 | loop fusion | flops 8847360 | bytes 4521984 | tf_op jit(solution)/shard_map/convert_element_type | solution.py:81
  (210 shorter events, 38.9 us)
Async XLA Ops:
  4.2 9.3 %collective-permute-start.1 = (bf16[4,32,832]{2,1,0:T(8,128)(2,1)S(1)}, bf16[4,32,832]{2,1,0:T(8,128)(2,1)S(1)}, u32[]{:S(2)}, u32[]{:S(2)}) collective-permute-start(bf16[4,32,832]{2,1,0:T(8,128)(2,1)S(1)} %concatenate.113), channel_id=1, source_target_pairs={{8,0},{16,8},{24,16},{9,1},{17,9},{25,17},{10,2},{18,10},{26,18},{... | collective-permute-start | bytes 638984 | tf_op jit(solution)/shard_map/ppermute | solution.py:115
  5.5 8.8 %collective-permute-start = (bf16[4,32,832]{2,1,0:T(8,128)(2,1)S(1)}, bf16[4,32,832]{2,1,0:T(8,128)(2,1)S(1)}, u32[]{:S(2)}, u32[]{:S(2)}) collective-permute-start(bf16[4,32,832]{2,1,0:T(8,128)(2,1)S(1)} %concatenate.113), channel_id=1, source_target_pairs={{0,8},{8,16},{16,24},{1,9},{9,17},{17,25},{2,10},{10,18},{18,26},{... | collective-permute-start | bytes 638984 | tf_op jit(solution)/shard_map/ppermute | solution.py:114
  14.4 7.5 %collective-permute-start.3 = (bf16[12,4,832]{2,1,0:T(4,128)(2,1)S(1)}, bf16[12,4,832]{2,1,0:T(4,128)(2,1)S(1)}, u32[]{:S(2)}, u32[]{:S(2)}) collective-permute-start(bf16[12,4,832]{2,1,0:T(4,128)(2,1)S(1)} %get-tuple-element.29), channel_id=1, source_target_pairs={{1,0},{2,1},{3,2},{4,3},{5,4},{6,5},{7,6},{9,8},{10,9},{11,10},{12... | collective-permute-start | bytes 239624 | tf_op jit(solution)/shard_map/ppermute | solution.py:115
  17.8 4.9 %collective-permute-start.2 = (bf16[12,4,832]{2,1,0:T(4,128)(2,1)S(1)}, bf16[12,4,832]{2,1,0:T(4,128)(2,1)S(1)}, u32[]{:S(2)}, u32[]{:S(2)}) collective-permute-start(bf16[12,4,832]{2,1,0:T(4,128)(2,1)S(1)} %get-tuple-element.28), channel_id=1, source_target_pairs={{0,1},{1,2},{2,3},{3,4},{4,5},{5,6},{6,7},{8,9},{9,10},{10,11},{11... | collective-permute-start | bytes 239624 | tf_op jit(solution)/shard_map/ppermute | solution.py:114
  45.5 11.5 %collective-permute-start.22 = (f32[128,512]{1,0:T(8,128)S(1)}, f32[128,512]{1,0:T(8,128)S(1)}, u32[]{:S(2)}, u32[]{:S(2)}) collective-permute-start(f32[128,512]{1,0:T(8,128)S(1)} %constant_dynamic-slice_fusion.1), channel_id=1, source_target_pairs={{0,16},{8,24},{16,0},{24,8},{1,17},{9,25},{17,1},{25,9},{2,18},{10... | collective-permute-start | bytes 786440 | tf_op jit(solution)/shard_map/ppermute | solution.py:46
  51.2 9.2 %collective-permute-start.15 = (f32[128,512]{1,0:T(8,128)S(1)}, f32[128,512]{1,0:T(8,128)S(1)}, u32[]{:S(2)}, u32[]{:S(2)}) collective-permute-start(f32[128,512]{1,0:T(8,128)S(1)} %constant_dynamic-slice_fusion.3), channel_id=1, source_target_pairs={{0,8},{8,0},{16,24},{24,16},{1,9},{9,1},{17,25},{25,17},{2,10},{10... | collective-permute-start | bytes 786440 | tf_op jit(solution)/shard_map/ppermute | solution.py:46
  52.5 9.2 %collective-permute-start.8 = (f32[128,512]{1,0:T(8,128)S(1)}, f32[128,512]{1,0:T(8,128)S(1)}, u32[]{:S(2)}, u32[]{:S(2)}) collective-permute-start(f32[128,512]{1,0:T(8,128)S(1)} %constant_dynamic-slice_fusion.5), channel_id=1, source_target_pairs={{0,2},{1,3},{2,0},{3,1},{4,6},{5,7},{6,4},{7,5},{8,10},{9,11},{10,... | collective-permute-start | bytes 786440 | tf_op jit(solution)/shard_map/ppermute | solution.py:46
  57.1 7.1 %collective-permute-start.23 = (f32[64,512]{1,0:T(8,128)S(1)}, f32[64,512]{1,0:T(8,128)S(1)}, u32[]{:S(2)}, u32[]{:S(2)}) collective-permute-start(f32[64,512]{1,0:T(8,128)S(1)} %constant_dynamic-slice_fusion), channel_id=1, source_target_pairs={{0,4},{1,5},{2,6},{3,7},{4,0},{5,1},{6,2},{7,3},{8,12},{9,13},{10,... | collective-permute-start | bytes 393224 | tf_op jit(solution)/shard_map/ppermute | solution.py:46
  60.5 7.2 %collective-permute-start.16 = (f32[64,512]{1,0:T(8,128)S(1)}, f32[64,512]{1,0:T(8,128)S(1)}, u32[]{:S(2)}, u32[]{:S(2)}) collective-permute-start(f32[64,512]{1,0:T(8,128)S(1)} %constant_dynamic-slice_fusion.2), channel_id=1, source_target_pairs={{0,16},{8,24},{16,0},{24,8},{1,17},{9,25},{17,1},{25,9},{2,18},{10... | collective-permute-start | bytes 393224 | tf_op jit(solution)/shard_map/ppermute | solution.py:46
  61.7 9.1 %collective-permute-start.9 = (f32[64,512]{1,0:T(8,128)S(1)}, f32[64,512]{1,0:T(8,128)S(1)}, u32[]{:S(2)}, u32[]{:S(2)}) collective-permute-start(f32[64,512]{1,0:T(8,128)S(1)} %constant_dynamic-slice_fusion.4), channel_id=1, source_target_pairs={{0,8},{8,0},{16,24},{24,16},{1,9},{9,1},{17,25},{25,17},{2,10},{10... | collective-permute-start | bytes 393224 | tf_op jit(solution)/shard_map/ppermute | solution.py:46
  64.3 7.8 %collective-permute-start.24 = (f32[64,512]{1,0:T(8,128)S(1)}, f32[64,512]{1,0:T(8,128)S(1)}, u32[]{:S(2)}, u32[]{:S(2)}) collective-permute-start(f32[64,512]{1,0:T(8,128)S(1)} %dynamic-slice_add_fusion.3), channel_id=1, source_target_pairs={{0,2},{1,3},{2,0},{3,1},{4,6},{5,7},{6,4},{7,5},{8,10},{9,11},{10,... | collective-permute-start | bytes 393224 | tf_op jit(solution)/shard_map/ppermute | solution.py:49
  67.7 7.2 %collective-permute-start.17 = (f32[64,512]{1,0:T(8,128)S(1)}, f32[64,512]{1,0:T(8,128)S(1)}, u32[]{:S(2)}, u32[]{:S(2)}) collective-permute-start(f32[64,512]{1,0:T(8,128)S(1)} %dynamic-slice_add_fusion.4), channel_id=1, source_target_pairs={{0,4},{1,5},{2,6},{3,7},{4,0},{5,1},{6,2},{7,3},{8,12},{9,13},{10,... | collective-permute-start | bytes 393224 | tf_op jit(solution)/shard_map/ppermute | solution.py:49
  70.9 6.3 %collective-permute-start.10 = (f32[64,512]{1,0:T(8,128)S(1)}, f32[64,512]{1,0:T(8,128)S(1)}, u32[]{:S(2)}, u32[]{:S(2)}) collective-permute-start(f32[64,512]{1,0:T(8,128)S(1)} %dynamic-slice_add_fusion.5), channel_id=1, source_target_pairs={{0,16},{8,24},{16,0},{24,8},{1,17},{9,25},{17,1},{25,9},{2,18},{10... | collective-permute-start | bytes 393224 | tf_op jit(solution)/shard_map/ppermute | solution.py:49
  72.1 7.5 %collective-permute-start.25 = (f32[64,512]{1,0:T(8,128)S(1)}, f32[64,512]{1,0:T(8,128)S(1)}, u32[]{:S(2)}, u32[]{:S(2)}) collective-permute-start(f32[64,512]{1,0:T(8,128)S(1)} %add.244), channel_id=1, source_target_pairs={{0,8},{8,0},{16,24},{24,16},{1,9},{9,1},{17,25},{25,17},{2,10},{10... | collective-permute-start | bytes 393224 | tf_op jit(solution)/shard_map/ppermute | solution.py:49
  74.9 4.8 %collective-permute-start.18 = (f32[64,512]{1,0:T(8,128)S(1)}, f32[64,512]{1,0:T(8,128)S(1)}, u32[]{:S(2)}, u32[]{:S(2)}) collective-permute-start(f32[64,512]{1,0:T(8,128)S(1)} %add.236), channel_id=1, source_target_pairs={{0,2},{1,3},{2,0},{3,1},{4,6},{5,7},{6,4},{7,5},{8,10},{9,11},{10,... | collective-permute-start | bytes 393224 | tf_op jit(solution)/shard_map/ppermute | solution.py:49
  77.2 6.1 %collective-permute-start.11 = (f32[64,512]{1,0:T(8,128)S(1)}, f32[64,512]{1,0:T(8,128)S(1)}, u32[]{:S(2)}, u32[]{:S(2)}) collective-permute-start(f32[64,512]{1,0:T(8,128)S(1)} %add.228), channel_id=1, source_target_pairs={{0,4},{1,5},{2,6},{3,7},{4,0},{5,1},{6,2},{7,3},{8,12},{9,13},{10,... | collective-permute-start | bytes 393224 | tf_op jit(solution)/shard_map/ppermute | solution.py:49
  79.6 8.4 %collective-permute-start.26 = (bf16[64,512]{1,0:T(8,128)(2,1)S(1)}, bf16[64,512]{1,0:T(8,128)(2,1)S(1)}, u32[]{:S(2)}, u32[]{:S(2)}) collective-permute-start(bf16[64,512]{1,0:T(8,128)(2,1)S(1)} %add_convert_fusion), channel_id=1, source_target_pairs={{0,4},{1,5},{2,6},{3,7},{4,0},{5,1},{6,2},{7,3},{8,12},{9,13},{10,... | collective-permute-start | bytes 196616 | tf_op jit(solution)/shard_map/ppermute | solution.py:56
  79.7 9.4 %collective-permute-start.19 = (bf16[64,512]{1,0:T(8,128)(2,1)S(1)}, bf16[64,512]{1,0:T(8,128)(2,1)S(1)}, u32[]{:S(2)}, u32[]{:S(2)}) collective-permute-start(bf16[64,512]{1,0:T(8,128)(2,1)S(1)} %add_convert_fusion.1), channel_id=1, source_target_pairs={{0,16},{8,24},{16,0},{24,8},{1,17},{9,25},{17,1},{25,9},{2,18},{10... | collective-permute-start | bytes 196616 | tf_op jit(solution)/shard_map/ppermute | solution.py:56
  83.3 7.2 %collective-permute-start.12 = (bf16[64,512]{1,0:T(8,128)(2,1)S(1)}, bf16[64,512]{1,0:T(8,128)(2,1)S(1)}, u32[]{:S(2)}, u32[]{:S(2)}) collective-permute-start(bf16[64,512]{1,0:T(8,128)(2,1)S(1)} %add_convert_fusion.2), channel_id=1, source_target_pairs={{0,8},{8,0},{16,24},{24,16},{1,9},{9,1},{17,25},{25,17},{2,10},{10... | collective-permute-start | bytes 196616 | tf_op jit(solution)/shard_map/ppermute | solution.py:56
  88.0 3.9 %collective-permute-start.27 = (bf16[128,512]{1,0:T(8,128)(2,1)S(1)}, bf16[128,512]{1,0:T(8,128)(2,1)S(1)}, u32[]{:S(2)}, u32[]{:S(2)}) collective-permute-start(bf16[128,512]{1,0:T(8,128)(2,1)S(1)} %pad_maximum_fusion.15), channel_id=1, source_target_pairs={{0,16},{8,24},{16,0},{24,8},{1,17},{9,25},{17,1},{25,9},{2,18},{10... | collective-permute-start | bytes 393224 | tf_op jit(solution)/shard_map/ppermute | solution.py:56
  89.1 6.6 %collective-permute-start.20 = (bf16[128,512]{1,0:T(8,128)(2,1)S(1)}, bf16[128,512]{1,0:T(8,128)(2,1)S(1)}, u32[]{:S(2)}, u32[]{:S(2)}) collective-permute-start(bf16[128,512]{1,0:T(8,128)(2,1)S(1)} %pad_maximum_fusion.14), channel_id=1, source_target_pairs={{0,8},{8,0},{16,24},{24,16},{1,9},{9,1},{17,25},{25,17},{2,10},{10... | collective-permute-start | bytes 393224 | tf_op jit(solution)/shard_map/ppermute | solution.py:56
  90.5 6.7 %collective-permute-start.13 = (bf16[128,512]{1,0:T(8,128)(2,1)S(1)}, bf16[128,512]{1,0:T(8,128)(2,1)S(1)}, u32[]{:S(2)}, u32[]{:S(2)}) collective-permute-start(bf16[128,512]{1,0:T(8,128)(2,1)S(1)} %pad_maximum_fusion.13), channel_id=1, source_target_pairs={{0,2},{1,3},{2,0},{3,1},{4,6},{5,7},{6,4},{7,5},{8,10},{9,11},{10,... | collective-permute-start | bytes 393224 | tf_op jit(solution)/shard_map/ppermute | solution.py:56
  91.9 7.3 %collective-permute-start.28 = (bf16[256,512]{1,0:T(8,128)(2,1)S(1)}, bf16[256,512]{1,0:T(8,128)(2,1)S(1)}, u32[]{:S(2)}, u32[]{:S(2)}) collective-permute-start(bf16[256,512]{1,0:T(8,128)(2,1)S(1)} %pad_maximum_fusion.6), channel_id=1, source_target_pairs={{0,1},{1,0},{2,3},{3,2},{4,5},{5,4},{6,7},{7,6},{8,9},{9,8},{10,11... | collective-permute-start | bytes 786440 | tf_op jit(solution)/shard_map/ppermute | solution.py:77
  95.8 4.1 %collective-permute-start.21 = (bf16[256,512]{1,0:T(8,128)(2,1)S(1)}, bf16[256,512]{1,0:T(8,128)(2,1)S(1)}, u32[]{:S(2)}, u32[]{:S(2)}) collective-permute-start(bf16[256,512]{1,0:T(8,128)(2,1)S(1)} %pad_maximum_fusion.5), channel_id=1, source_target_pairs={{0,1},{1,0},{2,3},{3,2},{4,5},{5,4},{6,7},{7,6},{8,9},{9,8},{10,11... | collective-permute-start | bytes 786440 | tf_op jit(solution)/shard_map/ppermute | solution.py:77
  (34 other events, 47.6 us)

commit v13 on v12

--- a/solution.py
+++ b/solution.py
@@ -75,11 +75,23 @@
         upper = (lax.axis_index(axis) >> bit) & 1
         pairs = flip_pairs(axis, bit)
         swapped = [(p, lax.ppermute(p, axis, pairs)) for p in pieces]
-        low = jnp.concatenate([jnp.where(upper == 0, p, g) for p, g in swapped], axis=0)
-        high = jnp.concatenate([jnp.where(upper == 0, g, p) for p, g in swapped], axis=0)
-        split = KIN - low.shape[0]
-        kernel_part = jnp.concatenate([low, high[:split]], axis=0).astype(jnp.float32)
-        return kernel_part, high[split].astype(jnp.float32)
+        half = sum(p.shape[0] for p in pieces)
+        kernel_part = jnp.zeros((KIN, GATES), jnp.float32)
+        bias_part = None
+        for way in reversed(range(len(pieces))):
+            mine, got = swapped[way]
+            start = sum(p.shape[0] for p in pieces[:way])
+            for base, rows in ((0, jnp.where(upper == 0, mine, got)),
+                               (half, jnp.where(upper == 0, got, mine))):
+                first_row = base + start
+                if first_row <= KIN < first_row + rows.shape[0]:
+                    bias_part = rows[KIN - first_row].astype(jnp.float32)
+                keep = min(rows.shape[0], KIN - first_row)
+                if keep > 0:
+                    kernel_part = lax.dynamic_update_slice_in_dim(
+                        kernel_part, rows[:keep].astype(jnp.float32), first_row, 0
+                    )
+        return kernel_part, bias_part
     summed = double(jnp.concatenate(pieces, axis=0), first_halved).astype(jnp.float32)
     return summed[:KIN], summed[KIN]
 

time: 103 us -> 100 us (0.971)
  other arithmetic: 14.6 us -> 12.3 us
  waiting for transfers between devices: 15.6 us -> 14.3 us
    ppermute x6, waiting for transfers between devices: 4.72 us -> 0.35 us  [double(): got = lax.ppermute(piece, axis, flip_pairs(axis, bit))]
    ppermute x2, waiting for transfers between devices: 2.56 us -> 6.35 us  [widen(): lax.ppermute(head, axis, [(i + dist, i) for i in range(count - dist)])]
    ppermute x6, starting transfers between devices: 13.6 us -> 11.3 us  [halve(): part = part + lax.ppermute(part, axis, flip_pairs(axis, bit))]
    convert_element_type x2 -> x1, other arithmetic: 2.6 us -> 0.58 us  [sum_everywhere(): bias_part = rows[KIN - first_row].astype(jnp.float32)]
    ppermute x6, starting transfers between devices: 5 us -> 6.99 us  [double(): got = lax.ppermute(piece, axis, flip_pairs(axis, bit))]
    ppermute x3, starting transfers between devices: 7.14 us -> 9.01 us  [sum_everywhere(): swapped = [(p, lax.ppermute(p, axis, pairs)) for p in pieces]]
    ppermute x6, starting transfers between devices: 14.3 us -> 12.5 us  [halve(): part = keep + lax.ppermute(send, axis, flip_pairs(axis, bit))]
    ppermute x2, starting transfers between devices: 7.93 us -> 9.47 us  [widen(): lax.ppermute(tail, axis, [(i, i + dist) for i in range(count - dist)])]
  transfers between devices with their start and end apart: 29 -> 29, of which waited for: 10 -> 8; matrix products, arithmetic and copies ran while one was open for 6% -> 15% of each run, Pallas kernels for 0% -> 0%
where the time goes in v13:
time: 100 us; the launch traced here: 99.6 us
  starting transfers between devices  53.3 us (53%)
  waiting for transfers between devices  14.3 us (14%)
  other arithmetic  12.3 us (12%)
  local copies, waits for them, and re-layouts  12.1 us (12%)
  matrix products  5.94 us (6%)
  between operations  1.57 us (2%)
    ppermute x6, starting transfers between devices, halve(): part = keep + lax.ppermute(send, axis, flip_pairs(axis, bit))  12.5 us
    ppermute x6, starting transfers between devices, halve(): part = part + lax.ppermute(part, axis, flip_pairs(axis, bit))  11.3 us
    ppermute x2, starting transfers between devices, widen(): lax.ppermute(tail, axis, [(i, i + dist) for i in range(count - dist)])  9.47 us
    ppermute x3, starting transfers between devices, sum_everywhere(): swapped = [(p, lax.ppermute(p, axis, pairs)) for p in pieces]  9.01 us
    ppermute x6, starting transfers between devices, double(): got = lax.ppermute(piece, axis, flip_pairs(axis, bit))  6.99 us
    ppermute x2, waiting for transfers between devices, widen(): lax.ppermute(head, axis, [(i + dist, i) for i in range(count - dist)])  6.35 us
    unnamed x39, local copies, waits for them, and re-layouts  4.24 us
    ppermute x6, waiting for transfers between devices, halve(): part = keep + lax.ppermute(send, axis, flip_pairs(axis, bit))  4.23 us
  transfers between devices with their start and end apart: 29, of which 8 were waited for; matrix products, arithmetic and copies ran while one was open for 15% of the time, Pallas kernels for 0%

profile of v13, /device:TPU:1, one launch (start us, length us, event | category | flops | bytes accessed | tf_op | source)
XLA Modules:
  0.0 99.6 jit_solution(3049865364211317140)
XLA Ops:
  4.2 1.3 %collective-permute-start.1 = (bf16[4,32,832]{2,1,0:T(8,128)(2,1)S(1)}, bf16[4,32,832]{2,1,0:T(8,128)(2,1)S(1)}, u32[]{:S(2)}, u32[]{:S(2)}) collective-permute-start(bf16[4,32,832]{2,1,0:T(8,128)(2,1)S(1)} %concatenate.107), channel_id=1, source_target_pairs={{8,0},{16,8},{24,16},{9,1},{17,9},{25,17},{10,2},{18,10},{26,18},{... | collective-permute-start | bytes 638984 | tf_op jit(solution)/shard_map/ppermute | solution.py:127
  5.5 4.6 %collective-permute-start = (bf16[4,32,832]{2,1,0:T(8,128)(2,1)S(1)}, bf16[4,32,832]{2,1,0:T(8,128)(2,1)S(1)}, u32[]{:S(2)}, u32[]{:S(2)}) collective-permute-start(bf16[4,32,832]{2,1,0:T(8,128)(2,1)S(1)} %concatenate.107), channel_id=1, source_target_pairs={{0,8},{8,16},{16,24},{1,9},{9,17},{17,25},{2,10},{10,18},{18,26},{... | collective-permute-start | bytes 638984 | tf_op jit(solution)/shard_map/ppermute | solution.py:126
  10.3 3.1 %collective-permute-done.1 = bf16[4,32,832]{2,1,0:T(8,128)(2,1)S(1)} collective-permute-done((bf16[4,32,832]{2,1,0:T(8,128)(2,1)S(1)}, bf16[4,32,832]{2,1,0:T(8,128)(2,1)S(1)}, u32[]{:S(2)}, u32[]{:S(2)}) %collective-permute-start.1) | collective-permute-done | bytes 213024 | tf_op jit(solution)/shard_map/ppermute | solution.py:127
  14.4 4.9 %collective-permute-start.2 = (bf16[12,4,832]{2,1,0:T(4,128)(2,1)S(1)}, bf16[12,4,832]{2,1,0:T(4,128)(2,1)S(1)}, u32[]{:S(2)}, u32[]{:S(2)}) collective-permute-start(bf16[12,4,832]{2,1,0:T(4,128)(2,1)S(1)} %get-tuple-element.28), channel_id=1, source_target_pairs={{0,1},{1,2},{2,3},{3,4},{4,5},{5,6},{6,7},{8,9},{9,10},{10,11},{11... | collective-permute-start | bytes 239624 | tf_op jit(solution)/shard_map/ppermute | solution.py:126
  19.2 1.9 %collective-permute-start.3 = (bf16[12,4,832]{2,1,0:T(4,128)(2,1)S(1)}, bf16[12,4,832]{2,1,0:T(4,128)(2,1)S(1)}, u32[]{:S(2)}, u32[]{:S(2)}) collective-permute-start(bf16[12,4,832]{2,1,0:T(4,128)(2,1)S(1)} %get-tuple-element.29), channel_id=1, source_target_pairs={{1,0},{2,1},{3,2},{4,3},{5,4},{6,5},{7,6},{9,8},{10,9},{11,10},{12... | collective-permute-start | bytes 239624 | tf_op jit(solution)/shard_map/ppermute | solution.py:127
  21.8 3.2 %collective-permute-done.3 = bf16[12,4,832]{2,1,0:T(4,128)(2,1)S(1)} collective-permute-done((bf16[12,4,832]{2,1,0:T(4,128)(2,1)S(1)}, bf16[12,4,832]{2,1,0:T(4,128)(2,1)S(1)}, u32[]{:S(2)}, u32[]{:S(2)}) %collective-permute-start.3) | collective-permute-done | bytes 79904 | tf_op jit(solution)/shard_map/ppermute | solution.py:127
  32.6 2.1 %convolution_select_fusion.1 = f32[8,8,5,512]{3,1,2,0:T(8,128)S(1)} fusion(bf16[3,3,160,512]{3,2,1,0:T(8,128)(2,1)} %bitcast.88, pred[8,5]{0,1:T(8,128)(4,1)S(1)} %copy-done.16, bf16[10,1,7,2,160]{4,2,3,0,1:T(8,128)(2,1)S(1)} %slice.371, bf16[10,1,8,5,160]{4,2,3,0,1:T(8,128)(2,1)S(1)} %copy.16), kind=kOutput, calls=%fused_computation.7 | convolution fusion | flops 472560640 | bytes 2302760 | tf_op jit(solution)/shard_map/conv_general_dilated | solution.py:174
  44.8 1.7 %convolution_multiply_fusion = f32[768,512]{1,0:T(8,128)S(1)} fusion(s32[]{:T(128)S(6)} %select_n.163, bf16[128,1536]{1,0:T(8,128)(2,1)S(1)} %concatenate.123, bf16[128,1536]{1,0:T(8,128)(2,1)S(1)} %concatenate.125, bf16[128,1536]{1,0:T(8,128)(2,1)S(1)} %concatenate.127, bf16[128,1536]{1,0:T(8,128)(2,1)S(1)} %concatenate.129, ...), kind=kOutput, calls=%fused_computation.4 | convolution fusion | flops 408289280 | bytes 3670020 | tf_op jit(solution)/shard_map/dot_general | solution.py:295
  46.7 5.0 %collective-permute-start.8 = (f32[128,512]{1,0:T(8,128)S(1)}, f32[128,512]{1,0:T(8,128)S(1)}, u32[]{:S(2)}, u32[]{:S(2)}) collective-permute-start(f32[128,512]{1,0:T(8,128)S(1)} %constant_dynamic-slice_fusion.5), channel_id=1, source_target_pairs={{0,16},{8,24},{16,0},{24,8},{1,17},{9,25},{17,1},{25,9},{2,18},{10... | collective-permute-start | bytes 786440 | tf_op jit(solution)/shard_map/ppermute | solution.py:46
  53.6 1.4 %collective-permute-start.22 = (f32[128,512]{1,0:T(8,128)S(1)}, f32[128,512]{1,0:T(8,128)S(1)}, u32[]{:S(2)}, u32[]{:S(2)}) collective-permute-start(f32[128,512]{1,0:T(8,128)S(1)} %constant_dynamic-slice_fusion.1), channel_id=1, source_target_pairs={{0,2},{1,3},{2,0},{3,1},{4,6},{5,7},{6,4},{7,5},{8,10},{9,11},{10,... | collective-permute-start | bytes 786440 | tf_op jit(solution)/shard_map/ppermute | solution.py:46
  55.0 3.2 %collective-permute-done.8 = f32[128,512]{1,0:T(8,128)S(1)} collective-permute-done((f32[128,512]{1,0:T(8,128)S(1)}, f32[128,512]{1,0:T(8,128)S(1)}, u32[]{:S(2)}, u32[]{:S(2)}) %collective-permute-start.8) | collective-permute-done | bytes 262176 | tf_op jit(solution)/shard_map/ppermute | solution.py:46
  58.3 2.4 %collective-permute-start.9 = (f32[64,512]{1,0:T(8,128)S(1)}, f32[64,512]{1,0:T(8,128)S(1)}, u32[]{:S(2)}, u32[]{:S(2)}) collective-permute-start(f32[64,512]{1,0:T(8,128)S(1)} %constant_dynamic-slice_fusion.4), channel_id=1, source_target_pairs={{0,4},{1,5},{2,6},{3,7},{4,0},{5,1},{6,2},{7,3},{8,12},{9,13},{10,... | collective-permute-start | bytes 393224 | tf_op jit(solution)/shard_map/ppermute | solution.py:46
  62.0 1.3 %collective-permute-start.23 = (f32[64,512]{1,0:T(8,128)S(1)}, f32[64,512]{1,0:T(8,128)S(1)}, u32[]{:S(2)}, u32[]{:S(2)}) collective-permute-start(f32[64,512]{1,0:T(8,128)S(1)} %constant_dynamic-slice_fusion), channel_id=1, source_target_pairs={{0,8},{8,0},{16,24},{24,16},{1,9},{9,1},{17,25},{25,17},{2,10},{10... | collective-permute-start | bytes 393224 | tf_op jit(solution)/shard_map/ppermute | solution.py:46
  64.3 1.9 %collective-permute-start.10 = (f32[64,512]{1,0:T(8,128)S(1)}, f32[64,512]{1,0:T(8,128)S(1)}, u32[]{:S(2)}, u32[]{:S(2)}) collective-permute-start(f32[64,512]{1,0:T(8,128)S(1)} %dynamic-slice_add_fusion.5), channel_id=1, source_target_pairs={{0,2},{1,3},{2,0},{3,1},{4,6},{5,7},{6,4},{7,5},{8,10},{9,11},{10,... | collective-permute-start | bytes 393224 | tf_op jit(solution)/shard_map/ppermute | solution.py:49
  66.2 2.6 %collective-permute-start.17 = (f32[64,512]{1,0:T(8,128)S(1)}, f32[64,512]{1,0:T(8,128)S(1)}, u32[]{:S(2)}, u32[]{:S(2)}) collective-permute-start(f32[64,512]{1,0:T(8,128)S(1)} %dynamic-slice_add_fusion.4), channel_id=1, source_target_pairs={{0,4},{1,5},{2,6},{3,7},{4,0},{5,1},{6,2},{7,3},{8,12},{9,13},{10,... | collective-permute-start | bytes 393224 | tf_op jit(solution)/shard_map/ppermute | solution.py:49
  68.9 4.6 %collective-permute-start.11 = (f32[64,512]{1,0:T(8,128)S(1)}, f32[64,512]{1,0:T(8,128)S(1)}, u32[]{:S(2)}, u32[]{:S(2)}) collective-permute-start(f32[64,512]{1,0:T(8,128)S(1)} %add.230), channel_id=1, source_target_pairs={{0,8},{8,0},{16,24},{24,16},{1,9},{9,1},{17,25},{25,17},{2,10},{10... | collective-permute-start | bytes 393224 | tf_op jit(solution)/shard_map/ppermute | solution.py:49
  73.5 1.5 %fusion.99 = bf16[4,32,128]{2,1,0:T(8,128)(2,1)} fusion(f32[8,36,128]{2,1,0:T(8,128)S(1)} %get-tuple-element.16, f32[8,36,128]{2,1,0:T(8,128)} %get-tuple-element.34), kind=kLoop, calls=%fused_computation.204 | loop fusion | flops 32768 | bytes 163840 | tf_op jit(solution)/shard_map/convert_element_type | solution.py:188
  75.2 2.2 %collective-permute-start.25 = (f32[64,512]{1,0:T(8,128)S(1)}, f32[64,512]{1,0:T(8,128)S(1)}, u32[]{:S(2)}, u32[]{:S(2)}) collective-permute-start(f32[64,512]{1,0:T(8,128)S(1)} %add.246), channel_id=1, source_target_pairs={{0,4},{1,5},{2,6},{3,7},{4,0},{5,1},{6,2},{7,3},{8,12},{9,13},{10,... | collective-permute-start | bytes 393224 | tf_op jit(solution)/shard_map/ppermute | solution.py:49
  77.7 2.5 %collective-permute-done.18 = f32[64,512]{1,0:T(8,128)S(1)} collective-permute-done((f32[64,512]{1,0:T(8,128)S(1)}, f32[64,512]{1,0:T(8,128)S(1)}, u32[]{:S(2)}, u32[]{:S(2)}) %collective-permute-start.18) | collective-permute-done | bytes 131104 | tf_op jit(solution)/shard_map/ppermute | solution.py:49
  81.4 1.8 %collective-permute-start.26 = (bf16[64,512]{1,0:T(8,128)(2,1)S(1)}, bf16[64,512]{1,0:T(8,128)(2,1)S(1)}, u32[]{:S(2)}, u32[]{:S(2)}) collective-permute-start(bf16[64,512]{1,0:T(8,128)(2,1)S(1)} %add_convert_fusion), channel_id=1, source_target_pairs={{0,8},{8,0},{16,24},{24,16},{1,9},{9,1},{17,25},{25,17},{2,10},{10... | collective-permute-start | bytes 196616 | tf_op jit(solution)/shard_map/ppermute | solution.py:56
  84.7 2.2 %collective-permute-start.20 = (bf16[128,512]{1,0:T(8,128)(2,1)S(1)}, bf16[128,512]{1,0:T(8,128)(2,1)S(1)}, u32[]{:S(2)}, u32[]{:S(2)}) collective-permute-start(bf16[128,512]{1,0:T(8,128)(2,1)S(1)} %pad_maximum_fusion.12), channel_id=1, source_target_pairs={{0,8},{8,0},{16,24},{24,16},{1,9},{9,1},{17,25},{25,17},{2,10},{10... | collective-permute-start | bytes 393224 | tf_op jit(solution)/shard_map/ppermute | solution.py:56
  87.4 5.7 %collective-permute-start.14 = (bf16[256,512]{1,0:T(8,128)(2,1)S(1)}, bf16[256,512]{1,0:T(8,128)(2,1)S(1)}, u32[]{:S(2)}, u32[]{:S(2)}) collective-permute-start(bf16[256,512]{1,0:T(8,128)(2,1)S(1)} %pad_maximum_fusion.2), channel_id=1, source_target_pairs={{0,1},{1,0},{2,3},{3,2},{4,5},{5,4},{6,7},{7,6},{8,9},{9,8},{10,11... | collective-permute-start | bytes 786440 | tf_op jit(solution)/shard_map/ppermute | solution.py:77
  94.5 2.0 %collective-permute-start.28 = (bf16[256,512]{1,0:T(8,128)(2,1)S(1)}, bf16[256,512]{1,0:T(8,128)(2,1)S(1)}, u32[]{:S(2)}, u32[]{:S(2)}) collective-permute-start(bf16[256,512]{1,0:T(8,128)(2,1)S(1)} %pad_maximum_fusion.4), channel_id=1, source_target_pairs={{0,1},{1,0},{2,3},{3,2},{4,5},{5,4},{6,7},{7,6},{8,9},{9,8},{10,11... | collective-permute-start | bytes 786440 | tf_op jit(solution)/shard_map/ppermute | solution.py:77
  98.0 1.6 %copy-done = f32[1440,512]{1,0:T(8,128)} copy-done((f32[1440,512]{1,0:T(8,128)}, f32[1440,512]{1,0:T(8,128)S(1)}, u32[]{:S(2)}) %copy-start) | copy-done | bytes 2949144
  (191 shorter events, 33.4 us)
Async XLA Ops:
  4.2 9.3 %collective-permute-start.1 = (bf16[4,32,832]{2,1,0:T(8,128)(2,1)S(1)}, bf16[4,32,832]{2,1,0:T(8,128)(2,1)S(1)}, u32[]{:S(2)}, u32[]{:S(2)}) collective-permute-start(bf16[4,32,832]{2,1,0:T(8,128)(2,1)S(1)} %concatenate.107), channel_id=1, source_target_pairs={{8,0},{16,8},{24,16},{9,1},{17,9},{25,17},{10,2},{18,10},{26,18},{... | collective-permute-start | bytes 638984 | tf_op jit(solution)/shard_map/ppermute | solution.py:127
  5.5 8.8 %collective-permute-start = (bf16[4,32,832]{2,1,0:T(8,128)(2,1)S(1)}, bf16[4,32,832]{2,1,0:T(8,128)(2,1)S(1)}, u32[]{:S(2)}, u32[]{:S(2)}) collective-permute-start(bf16[4,32,832]{2,1,0:T(8,128)(2,1)S(1)} %concatenate.107), channel_id=1, source_target_pairs={{0,8},{8,16},{16,24},{1,9},{9,17},{17,25},{2,10},{10,18},{18,26},{... | collective-permute-start | bytes 638984 | tf_op jit(solution)/shard_map/ppermute | solution.py:126
  14.4 7.5 %collective-permute-start.2 = (bf16[12,4,832]{2,1,0:T(4,128)(2,1)S(1)}, bf16[12,4,832]{2,1,0:T(4,128)(2,1)S(1)}, u32[]{:S(2)}, u32[]{:S(2)}) collective-permute-start(bf16[12,4,832]{2,1,0:T(4,128)(2,1)S(1)} %get-tuple-element.28), channel_id=1, source_target_pairs={{0,1},{1,2},{2,3},{3,4},{4,5},{5,6},{6,7},{8,9},{9,10},{10,11},{11... | collective-permute-start | bytes 239624 | tf_op jit(solution)/shard_map/ppermute | solution.py:126
  19.2 5.8 %collective-permute-start.3 = (bf16[12,4,832]{2,1,0:T(4,128)(2,1)S(1)}, bf16[12,4,832]{2,1,0:T(4,128)(2,1)S(1)}, u32[]{:S(2)}, u32[]{:S(2)}) collective-permute-start(bf16[12,4,832]{2,1,0:T(4,128)(2,1)S(1)} %get-tuple-element.29), channel_id=1, source_target_pairs={{1,0},{2,1},{3,2},{4,3},{5,4},{6,5},{7,6},{9,8},{10,9},{11,10},{12... | collective-permute-start | bytes 239624 | tf_op jit(solution)/shard_map/ppermute | solution.py:127
  31.9 12.0 %collective-permute-start.5 = (bf16[6,34,160]{2,1,0:T(8,128)(2,1)}, bf16[6,34,160]{2,1,0:T(8,128)(2,1)S(1)}, u32[]{:S(2)}, u32[]{:S(2)}) collective-permute-start(bf16[6,34,160]{2,1,0:T(8,128)(2,1)} %fusion.82), channel_id=1, source_target_pairs={{0,1},{1,0},{2,3},{3,2},{4,5},{5,4},{6,7},{7,6},{8,9},{9,8},{10,11... | collective-permute-start | bytes 195848 | tf_op jit(solution)/shard_map/ppermute | solution.py:276
  31.9 12.5 %collective-permute-start.4 = (bf16[6,34,160]{2,1,0:T(8,128)(2,1)}, bf16[6,34,160]{2,1,0:T(8,128)(2,1)S(1)}, u32[]{:S(2)}, u32[]{:S(2)}) collective-permute-start(bf16[6,34,160]{2,1,0:T(8,128)(2,1)} %slice.422), channel_id=1, source_target_pairs={{0,1},{1,0},{2,3},{3,2},{4,5},{5,4},{6,7},{7,6},{8,9},{9,8},{10,11... | collective-permute-start | bytes 195848 | tf_op jit(solution)/shard_map/ppermute | solution.py:276
  37.4 7.4 %collective-permute-start.6 = (bf16[128,512]{1,0:T(8,128)(2,1)}, bf16[128,512]{1,0:T(8,128)(2,1)}, u32[]{:S(2)}, u32[]{:S(2)}) collective-permute-start(bf16[128,512]{1,0:T(8,128)(2,1)} %bitcast.32), channel_id=1, source_target_pairs={{0,1},{1,0},{2,3},{3,2},{4,5},{5,4},{6,7},{7,6},{8,9},{9,8},{10,11... | collective-permute-start | bytes 393224 | tf_op jit(solution)/shard_map/ppermute | solution.py:277
  46.7 11.5 %collective-permute-start.8 = (f32[128,512]{1,0:T(8,128)S(1)}, f32[128,512]{1,0:T(8,128)S(1)}, u32[]{:S(2)}, u32[]{:S(2)}) collective-permute-start(f32[128,512]{1,0:T(8,128)S(1)} %constant_dynamic-slice_fusion.5), channel_id=1, source_target_pairs={{0,16},{8,24},{16,0},{24,8},{1,17},{9,25},{17,1},{25,9},{2,18},{10... | collective-permute-start | bytes 786440 | tf_op jit(solution)/shard_map/ppermute | solution.py:46
  52.3 8.3 %collective-permute-start.15 = (f32[128,512]{1,0:T(8,128)S(1)}, f32[128,512]{1,0:T(8,128)S(1)}, u32[]{:S(2)}, u32[]{:S(2)}) collective-permute-start(f32[128,512]{1,0:T(8,128)S(1)} %constant_dynamic-slice_fusion.3), channel_id=1, source_target_pairs={{0,8},{8,0},{16,24},{24,16},{1,9},{9,1},{17,25},{25,17},{2,10},{10... | collective-permute-start | bytes 786440 | tf_op jit(solution)/shard_map/ppermute | solution.py:46
  53.6 8.3 %collective-permute-start.22 = (f32[128,512]{1,0:T(8,128)S(1)}, f32[128,512]{1,0:T(8,128)S(1)}, u32[]{:S(2)}, u32[]{:S(2)}) collective-permute-start(f32[128,512]{1,0:T(8,128)S(1)} %constant_dynamic-slice_fusion.1), channel_id=1, source_target_pairs={{0,2},{1,3},{2,0},{3,1},{4,6},{5,7},{6,4},{7,5},{8,10},{9,11},{10,... | collective-permute-start | bytes 786440 | tf_op jit(solution)/shard_map/ppermute | solution.py:46
  58.3 6.0 %collective-permute-start.9 = (f32[64,512]{1,0:T(8,128)S(1)}, f32[64,512]{1,0:T(8,128)S(1)}, u32[]{:S(2)}, u32[]{:S(2)}) collective-permute-start(f32[64,512]{1,0:T(8,128)S(1)} %constant_dynamic-slice_fusion.4), channel_id=1, source_target_pairs={{0,4},{1,5},{2,6},{3,7},{4,0},{5,1},{6,2},{7,3},{8,12},{9,13},{10,... | collective-permute-start | bytes 393224 | tf_op jit(solution)/shard_map/ppermute | solution.py:46
  60.7 5.5 %collective-permute-start.16 = (f32[64,512]{1,0:T(8,128)S(1)}, f32[64,512]{1,0:T(8,128)S(1)}, u32[]{:S(2)}, u32[]{:S(2)}) collective-permute-start(f32[64,512]{1,0:T(8,128)S(1)} %constant_dynamic-slice_fusion.2), channel_id=1, source_target_pairs={{0,16},{8,24},{16,0},{24,8},{1,17},{9,25},{17,1},{25,9},{2,18},{10... | collective-permute-start | bytes 393224 | tf_op jit(solution)/shard_map/ppermute | solution.py:46
  62.0 6.8 %collective-permute-start.23 = (f32[64,512]{1,0:T(8,128)S(1)}, f32[64,512]{1,0:T(8,128)S(1)}, u32[]{:S(2)}, u32[]{:S(2)}) collective-permute-start(f32[64,512]{1,0:T(8,128)S(1)} %constant_dynamic-slice_fusion), channel_id=1, source_target_pairs={{0,8},{8,0},{16,24},{24,16},{1,9},{9,1},{17,25},{25,17},{2,10},{10... | collective-permute-start | bytes 393224 | tf_op jit(solution)/shard_map/ppermute | solution.py:46
  64.3 4.6 %collective-permute-start.10 = (f32[64,512]{1,0:T(8,128)S(1)}, f32[64,512]{1,0:T(8,128)S(1)}, u32[]{:S(2)}, u32[]{:S(2)}) collective-permute-start(f32[64,512]{1,0:T(8,128)S(1)} %dynamic-slice_add_fusion.5), channel_id=1, source_target_pairs={{0,2},{1,3},{2,0},{3,1},{4,6},{5,7},{6,4},{7,5},{8,10},{9,11},{10,... | collective-permute-start | bytes 393224 | tf_op jit(solution)/shard_map/ppermute | solution.py:49
  66.2 8.8 %collective-permute-start.17 = (f32[64,512]{1,0:T(8,128)S(1)}, f32[64,512]{1,0:T(8,128)S(1)}, u32[]{:S(2)}, u32[]{:S(2)}) collective-permute-start(f32[64,512]{1,0:T(8,128)S(1)} %dynamic-slice_add_fusion.4), channel_id=1, source_target_pairs={{0,4},{1,5},{2,6},{3,7},{4,0},{5,1},{6,2},{7,3},{8,12},{9,13},{10,... | collective-permute-start | bytes 393224 | tf_op jit(solution)/shard_map/ppermute | solution.py:49
  68.8 6.3 %collective-permute-start.24 = (f32[64,512]{1,0:T(8,128)S(1)}, f32[64,512]{1,0:T(8,128)S(1)}, u32[]{:S(2)}, u32[]{:S(2)}) collective-permute-start(f32[64,512]{1,0:T(8,128)S(1)} %dynamic-slice_add_fusion.3), channel_id=1, source_target_pairs={{0,16},{8,24},{16,0},{24,8},{1,17},{9,25},{17,1},{25,9},{2,18},{10... | collective-permute-start | bytes 393224 | tf_op jit(solution)/shard_map/ppermute | solution.py:49
  68.9 8.4 %collective-permute-start.11 = (f32[64,512]{1,0:T(8,128)S(1)}, f32[64,512]{1,0:T(8,128)S(1)}, u32[]{:S(2)}, u32[]{:S(2)}) collective-permute-start(f32[64,512]{1,0:T(8,128)S(1)} %add.230), channel_id=1, source_target_pairs={{0,8},{8,0},{16,24},{24,16},{1,9},{9,1},{17,25},{25,17},{2,10},{10... | collective-permute-start | bytes 393224 | tf_op jit(solution)/shard_map/ppermute | solution.py:49
  75.0 5.1 %collective-permute-start.18 = (f32[64,512]{1,0:T(8,128)S(1)}, f32[64,512]{1,0:T(8,128)S(1)}, u32[]{:S(2)}, u32[]{:S(2)}) collective-permute-start(f32[64,512]{1,0:T(8,128)S(1)} %add.238), channel_id=1, source_target_pairs={{0,2},{1,3},{2,0},{3,1},{4,6},{5,7},{6,4},{7,5},{8,10},{9,11},{10,... | collective-permute-start | bytes 393224 | tf_op jit(solution)/shard_map/ppermute | solution.py:49
  75.2 6.2 %collective-permute-start.25 = (f32[64,512]{1,0:T(8,128)S(1)}, f32[64,512]{1,0:T(8,128)S(1)}, u32[]{:S(2)}, u32[]{:S(2)}) collective-permute-start(f32[64,512]{1,0:T(8,128)S(1)} %add.246), channel_id=1, source_target_pairs={{0,4},{1,5},{2,6},{3,7},{4,0},{5,1},{6,2},{7,3},{8,12},{9,13},{10,... | collective-permute-start | bytes 393224 | tf_op jit(solution)/shard_map/ppermute | solution.py:49
  77.3 6.0 %collective-permute-start.12 = (bf16[64,512]{1,0:T(8,128)(2,1)S(1)}, bf16[64,512]{1,0:T(8,128)(2,1)S(1)}, u32[]{:S(2)}, u32[]{:S(2)}) collective-permute-start(bf16[64,512]{1,0:T(8,128)(2,1)S(1)} %add_convert_fusion.2), channel_id=1, source_target_pairs={{0,4},{1,5},{2,6},{3,7},{4,0},{5,1},{6,2},{7,3},{8,12},{9,13},{10,... | collective-permute-start | bytes 196616 | tf_op jit(solution)/shard_map/ppermute | solution.py:56
  81.4 5.5 %collective-permute-start.26 = (bf16[64,512]{1,0:T(8,128)(2,1)S(1)}, bf16[64,512]{1,0:T(8,128)(2,1)S(1)}, u32[]{:S(2)}, u32[]{:S(2)}) collective-permute-start(bf16[64,512]{1,0:T(8,128)(2,1)S(1)} %add_convert_fusion), channel_id=1, source_target_pairs={{0,8},{8,0},{16,24},{24,16},{1,9},{9,1},{17,25},{25,17},{2,10},{10... | collective-permute-start | bytes 196616 | tf_op jit(solution)/shard_map/ppermute | solution.py:56
  84.7 8.5 %collective-permute-start.20 = (bf16[128,512]{1,0:T(8,128)(2,1)S(1)}, bf16[128,512]{1,0:T(8,128)(2,1)S(1)}, u32[]{:S(2)}, u32[]{:S(2)}) collective-permute-start(bf16[128,512]{1,0:T(8,128)(2,1)S(1)} %pad_maximum_fusion.12), channel_id=1, source_target_pairs={{0,8},{8,0},{16,24},{24,16},{1,9},{9,1},{17,25},{25,17},{2,10},{10... | collective-permute-start | bytes 393224 | tf_op jit(solution)/shard_map/ppermute | solution.py:56
  87.0 7.5 %collective-permute-start.27 = (bf16[128,512]{1,0:T(8,128)(2,1)S(1)}, bf16[128,512]{1,0:T(8,128)(2,1)S(1)}, u32[]{:S(2)}, u32[]{:S(2)}) collective-permute-start(bf16[128,512]{1,0:T(8,128)(2,1)S(1)} %pad_maximum_fusion.13), channel_id=1, source_target_pairs={{0,2},{1,3},{2,0},{3,1},{4,6},{5,7},{6,4},{7,5},{8,10},{9,11},{10,... | collective-permute-start | bytes 393224 | tf_op jit(solution)/shard_map/ppermute | solution.py:56
  87.4 9.2 %collective-permute-start.14 = (bf16[256,512]{1,0:T(8,128)(2,1)S(1)}, bf16[256,512]{1,0:T(8,128)(2,1)S(1)}, u32[]{:S(2)}, u32[]{:S(2)}) collective-permute-start(bf16[256,512]{1,0:T(8,128)(2,1)S(1)} %pad_maximum_fusion.2), channel_id=1, source_target_pairs={{0,1},{1,0},{2,3},{3,2},{4,5},{5,4},{6,7},{7,6},{8,9},{9,8},{10,11... | collective-permute-start | bytes 786440 | tf_op jit(solution)/shard_map/ppermute | solution.py:77
  (23 other events, 40.7 us)

commit v14 on v13

--- a/solution.py
+++ b/solution.py
@@ -78,7 +78,7 @@
         half = sum(p.shape[0] for p in pieces)
         kernel_part = jnp.zeros((KIN, GATES), jnp.float32)
         bias_part = None
-        for way in reversed(range(len(pieces))):
+        for way in range(len(pieces)):
             mine, got = swapped[way]
             start = sum(p.shape[0] for p in pieces[:way])
             for base, rows in ((0, jnp.where(upper == 0, mine, got)),

time: 100 us -> 104 us (1.040)
  starting transfers between devices: 53.3 us -> 54.4 us
    ppermute x6, starting transfers between devices: 12.5 us -> 16.7 us  [halve(): part = keep + lax.ppermute(send, axis, flip_pairs(axis, bit))]
    ppermute x2, waiting for transfers between devices: 6.35 us -> 2.56 us  [widen(): lax.ppermute(head, axis, [(i + dist, i) for i in range(count - dist)])]
    ppermute x6, waiting for transfers between devices: 0.35 us -> 2.4 us  [double(): got = lax.ppermute(piece, axis, flip_pairs(axis, bit))]
    ppermute x2, starting transfers between devices: 9.47 us -> 7.93 us  [widen(): lax.ppermute(tail, axis, [(i, i + dist) for i in range(count - dist)])]
    ppermute x2, starting transfers between devices: 3.21 us -> 4.75 us  [widen(): lax.ppermute(head, axis, [(i + dist, i) for i in range(count - dist)])]
    ppermute x6, starting transfers between devices: 6.99 us -> 5.52 us  [double(): got = lax.ppermute(piece, axis, flip_pairs(axis, bit))]
    ppermute x3, starting transfers between devices: 9.01 us -> 7.61 us  [sum_everywhere(): swapped = [(p, lax.ppermute(p, axis, pairs)) for p in pieces]]
    ppermute x6, waiting for transfers between devices: 4.23 us -> 5.49 us  [halve(): part = keep + lax.ppermute(send, axis, flip_pairs(axis, bit))]
  transfers between devices with their start and end apart: 29 -> 29, of which waited for: 8 -> 13; matrix products, arithmetic and copies ran while one was open for 15% -> 6% of each run, Pallas kernels for 0% -> 0%
where the time goes in v14:
time: 104 us; the launch traced here: 103 us
  starting transfers between devices  54.4 us (52%)
  waiting for transfers between devices  14.9 us (14%)
  other arithmetic  13.1 us (13%)
  local copies, waits for them, and re-layouts  12.8 us (12%)
  matrix products  5.76 us (6%)
  between operations  1.73 us (2%)
    ppermute x6, starting transfers between devices, halve(): part = keep + lax.ppermute(send, axis, flip_pairs(axis, bit))  16.7 us
    ppermute x6, starting transfers between devices, halve(): part = part + lax.ppermute(part, axis, flip_pairs(axis, bit))  10.9 us
    ppermute x2, starting transfers between devices, widen(): lax.ppermute(tail, axis, [(i, i + dist) for i in range(count - dist)])  7.93 us
    ppermute x3, starting transfers between devices, sum_everywhere(): swapped = [(p, lax.ppermute(p, axis, pairs)) for p in pieces]  7.61 us
    ppermute x6, starting transfers between devices, double(): got = lax.ppermute(piece, axis, flip_pairs(axis, bit))  5.52 us
    ppermute x6, waiting for transfers between devices, halve(): part = keep + lax.ppermute(send, axis, flip_pairs(axis, bit))  5.49 us
    unnamed x63, local copies, waits for them, and re-layouts  4.91 us
    ppermute x2, starting transfers between devices, widen(): lax.ppermute(head, axis, [(i + dist, i) for i in range(count - dist)])  4.75 us
  transfers between devices with their start and end apart: 29, of which 13 were waited for; matrix products, arithmetic and copies ran while one was open for 6% of the time, Pallas kernels for 0%

profile of v14, /device:TPU:1, one launch (start us, length us, event | category | flops | bytes accessed | tf_op | source)
XLA Modules:
  0.0 102.6 jit_solution(290044298478345988)
XLA Ops:
  5.5 4.6 %collective-permute-start = (bf16[4,32,832]{2,1,0:T(8,128)(2,1)S(1)}, bf16[4,32,832]{2,1,0:T(8,128)(2,1)S(1)}, u32[]{:S(2)}, u32[]{:S(2)}) collective-permute-start(bf16[4,32,832]{2,1,0:T(8,128)(2,1)S(1)} %concatenate.107), channel_id=1, source_target_pairs={{0,8},{8,16},{16,24},{1,9},{9,17},{17,25},{2,10},{10,18},{18,26},{... | collective-permute-start | bytes 638984 | tf_op jit(solution)/shard_map/ppermute | solution.py:126
  10.9 2.6 %collective-permute-done.1 = bf16[4,32,832]{2,1,0:T(8,128)(2,1)S(1)} collective-permute-done((bf16[4,32,832]{2,1,0:T(8,128)(2,1)S(1)}, bf16[4,32,832]{2,1,0:T(8,128)(2,1)S(1)}, u32[]{:S(2)}, u32[]{:S(2)}) %collective-permute-start.1) | collective-permute-done | bytes 213024 | tf_op jit(solution)/shard_map/ppermute | solution.py:127
  14.4 3.5 %collective-permute-start.3 = (bf16[12,4,832]{2,1,0:T(4,128)(2,1)S(1)}, bf16[12,4,832]{2,1,0:T(4,128)(2,1)S(1)}, u32[]{:S(2)}, u32[]{:S(2)}) collective-permute-start(bf16[12,4,832]{2,1,0:T(4,128)(2,1)S(1)} %get-tuple-element.29), channel_id=1, source_target_pairs={{1,0},{2,1},{3,2},{4,3},{5,4},{6,5},{7,6},{9,8},{10,9},{11,10},{12... | collective-permute-start | bytes 239624 | tf_op jit(solution)/shard_map/ppermute | solution.py:127
  17.8 3.3 %collective-permute-start.2 = (bf16[12,4,832]{2,1,0:T(4,128)(2,1)S(1)}, bf16[12,4,832]{2,1,0:T(4,128)(2,1)S(1)}, u32[]{:S(2)}, u32[]{:S(2)}) collective-permute-start(bf16[12,4,832]{2,1,0:T(4,128)(2,1)S(1)} %get-tuple-element.28), channel_id=1, source_target_pairs={{0,1},{1,2},{2,3},{3,4},{4,5},{5,6},{6,7},{8,9},{9,10},{10,11},{11... | collective-permute-start | bytes 239624 | tf_op jit(solution)/shard_map/ppermute | solution.py:126
  30.7 2.1 %convolution_select_fusion.1 = f32[8,8,5,512]{3,1,2,0:T(8,128)S(1)} fusion(bf16[3,3,160,512]{3,2,1,0:T(8,128)(2,1)} %bitcast.90, pred[8,5]{0,1:T(8,128)(4,1)S(1)} %copy-done.28, bf16[10,1,7,2,160]{4,2,3,0,1:T(8,128)(2,1)S(1)} %slice.371, bf16[10,1,8,5,160]{4,2,3,0,1:T(8,128)(2,1)S(1)} %copy.16), kind=kOutput, calls=%fused_computation.7 | convolution fusion | flops 472560640 | bytes 2302760 | tf_op jit(solution)/shard_map/conv_general_dilated | solution.py:174
  43.8 1.5 %convolution_multiply_fusion = f32[768,512]{1,0:T(8,128)S(1)} fusion(s32[]{:T(128)S(6)} %select_n.163, bf16[128,1536]{1,0:T(8,128)(2,1)S(1)} %concatenate.123, bf16[128,1536]{1,0:T(8,128)(2,1)S(1)} %concatenate.125, bf16[128,1536]{1,0:T(8,128)(2,1)S(1)} %concatenate.127, bf16[128,1536]{1,0:T(8,128)(2,1)S(1)} %concatenate.129, ...), kind=kOutput, calls=%fused_computation.4 | convolution fusion | flops 408289280 | bytes 3670020 | tf_op jit(solution)/shard_map/dot_general | solution.py:295
  45.5 2.3 %collective-permute-start.8 = (f32[128,512]{1,0:T(8,128)S(1)}, f32[128,512]{1,0:T(8,128)S(1)}, u32[]{:S(2)}, u32[]{:S(2)}) collective-permute-start(f32[128,512]{1,0:T(8,128)S(1)} %constant_dynamic-slice_fusion.5), channel_id=1, source_target_pairs={{0,2},{1,3},{2,0},{3,1},{4,6},{5,7},{6,4},{7,5},{8,10},{9,11},{10,... | collective-permute-start | bytes 786440 | tf_op jit(solution)/shard_map/ppermute | solution.py:46
  48.5 3.1 %collective-permute-start.15 = (f32[128,512]{1,0:T(8,128)S(1)}, f32[128,512]{1,0:T(8,128)S(1)}, u32[]{:S(2)}, u32[]{:S(2)}) collective-permute-start(f32[128,512]{1,0:T(8,128)S(1)} %constant_dynamic-slice_fusion.3), channel_id=1, source_target_pairs={{0,8},{8,0},{16,24},{24,16},{1,9},{9,1},{17,25},{25,17},{2,10},{10... | collective-permute-start | bytes 786440 | tf_op jit(solution)/shard_map/ppermute | solution.py:46
  51.6 3.2 %collective-permute-start.22 = (f32[128,512]{1,0:T(8,128)S(1)}, f32[128,512]{1,0:T(8,128)S(1)}, u32[]{:S(2)}, u32[]{:S(2)}) collective-permute-start(f32[128,512]{1,0:T(8,128)S(1)} %constant_dynamic-slice_fusion.1), channel_id=1, source_target_pairs={{0,16},{8,24},{16,0},{24,8},{1,17},{9,25},{17,1},{25,9},{2,18},{10... | collective-permute-start | bytes 786440 | tf_op jit(solution)/shard_map/ppermute | solution.py:46
  54.8 2.6 %collective-permute-start.9 = (f32[64,512]{1,0:T(8,128)S(1)}, f32[64,512]{1,0:T(8,128)S(1)}, u32[]{:S(2)}, u32[]{:S(2)}) collective-permute-start(f32[64,512]{1,0:T(8,128)S(1)} %constant_dynamic-slice_fusion.4), channel_id=1, source_target_pairs={{0,8},{8,0},{16,24},{24,16},{1,9},{9,1},{17,25},{25,17},{2,10},{10... | collective-permute-start | bytes 393224 | tf_op jit(solution)/shard_map/ppermute | solution.py:46
  57.8 3.1 %collective-permute-start.16 = (f32[64,512]{1,0:T(8,128)S(1)}, f32[64,512]{1,0:T(8,128)S(1)}, u32[]{:S(2)}, u32[]{:S(2)}) collective-permute-start(f32[64,512]{1,0:T(8,128)S(1)} %constant_dynamic-slice_fusion.2), channel_id=1, source_target_pairs={{0,16},{8,24},{16,0},{24,8},{1,17},{9,25},{17,1},{25,9},{2,18},{10... | collective-permute-start | bytes 393224 | tf_op jit(solution)/shard_map/ppermute | solution.py:46
  61.0 2.4 %collective-permute-start.23 = (f32[64,512]{1,0:T(8,128)S(1)}, f32[64,512]{1,0:T(8,128)S(1)}, u32[]{:S(2)}, u32[]{:S(2)}) collective-permute-start(f32[64,512]{1,0:T(8,128)S(1)} %constant_dynamic-slice_fusion), channel_id=1, source_target_pairs={{0,4},{1,5},{2,6},{3,7},{4,0},{5,1},{6,2},{7,3},{8,12},{9,13},{10,... | collective-permute-start | bytes 393224 | tf_op jit(solution)/shard_map/ppermute | solution.py:46
  64.3 1.3 %collective-permute-start.17 = (f32[64,512]{1,0:T(8,128)S(1)}, f32[64,512]{1,0:T(8,128)S(1)}, u32[]{:S(2)}, u32[]{:S(2)}) collective-permute-start(f32[64,512]{1,0:T(8,128)S(1)} %dynamic-slice_add_fusion.4), channel_id=1, source_target_pairs={{0,4},{1,5},{2,6},{3,7},{4,0},{5,1},{6,2},{7,3},{8,12},{9,13},{10,... | collective-permute-start | bytes 393224 | tf_op jit(solution)/shard_map/ppermute | solution.py:49
  65.7 5.2 %collective-permute-done.23 = f32[64,512]{1,0:T(8,128)S(1)} collective-permute-done((f32[64,512]{1,0:T(8,128)S(1)}, f32[64,512]{1,0:T(8,128)S(1)}, u32[]{:S(2)}, u32[]{:S(2)}) %collective-permute-start.23) | collective-permute-done | bytes 131104 | tf_op jit(solution)/shard_map/ppermute | solution.py:46
  71.2 4.6 %collective-permute-start.11 = (f32[64,512]{1,0:T(8,128)S(1)}, f32[64,512]{1,0:T(8,128)S(1)}, u32[]{:S(2)}, u32[]{:S(2)}) collective-permute-start(f32[64,512]{1,0:T(8,128)S(1)} %add.230), channel_id=1, source_target_pairs={{0,4},{1,5},{2,6},{3,7},{4,0},{5,1},{6,2},{7,3},{8,12},{9,13},{10,... | collective-permute-start | bytes 393224 | tf_op jit(solution)/shard_map/ppermute | solution.py:49
  75.8 1.5 %fusion.99 = bf16[4,32,128]{2,1,0:T(8,128)(2,1)} fusion(f32[8,36,128]{2,1,0:T(8,128)S(1)} %get-tuple-element.16, f32[8,36,128]{2,1,0:T(8,128)} %get-tuple-element.34), kind=kLoop, calls=%fused_computation.204 | loop fusion | flops 32768 | bytes 163840 | tf_op jit(solution)/shard_map/convert_element_type | solution.py:188
  78.5 3.7 %collective-permute-start.25 = (f32[64,512]{1,0:T(8,128)S(1)}, f32[64,512]{1,0:T(8,128)S(1)}, u32[]{:S(2)}, u32[]{:S(2)}) collective-permute-start(f32[64,512]{1,0:T(8,128)S(1)} %add.246), channel_id=1, source_target_pairs={{0,8},{8,0},{16,24},{24,16},{1,9},{9,1},{17,25},{25,17},{2,10},{10... | collective-permute-start | bytes 393224 | tf_op jit(solution)/shard_map/ppermute | solution.py:49
  82.7 1.6 %collective-permute-start.19 = (bf16[64,512]{1,0:T(8,128)(2,1)S(1)}, bf16[64,512]{1,0:T(8,128)(2,1)S(1)}, u32[]{:S(2)}, u32[]{:S(2)}) collective-permute-start(bf16[64,512]{1,0:T(8,128)(2,1)S(1)} %add_convert_fusion.1), channel_id=1, source_target_pairs={{0,16},{8,24},{16,0},{24,8},{1,17},{9,25},{17,1},{25,9},{2,18},{10... | collective-permute-start | bytes 196616 | tf_op jit(solution)/shard_map/ppermute | solution.py:56
  86.2 2.2 %collective-permute-start.13 = (bf16[128,512]{1,0:T(8,128)(2,1)S(1)}, bf16[128,512]{1,0:T(8,128)(2,1)S(1)}, u32[]{:S(2)}, u32[]{:S(2)}) collective-permute-start(bf16[128,512]{1,0:T(8,128)(2,1)S(1)} %pad_maximum_fusion.11), channel_id=1, source_target_pairs={{0,2},{1,3},{2,0},{3,1},{4,6},{5,7},{6,4},{7,5},{8,10},{9,11},{10,... | collective-permute-start | bytes 393224 | tf_op jit(solution)/shard_map/ppermute | solution.py:56
  89.4 1.6 %collective-permute-done.13 = bf16[128,512]{1,0:T(8,128)(2,1)S(1)} collective-permute-done((bf16[128,512]{1,0:T(8,128)(2,1)S(1)}, bf16[128,512]{1,0:T(8,128)(2,1)S(1)}, u32[]{:S(2)}, u32[]{:S(2)}) %collective-permute-start.13) | collective-permute-done | bytes 131104 | tf_op jit(solution)/shard_map/ppermute | solution.py:56
  91.1 3.9 %collective-permute-start.14 = (bf16[256,512]{1,0:T(8,128)(2,1)S(1)}, bf16[256,512]{1,0:T(8,128)(2,1)S(1)}, u32[]{:S(2)}, u32[]{:S(2)}) collective-permute-start(bf16[256,512]{1,0:T(8,128)(2,1)S(1)} %pad_maximum_fusion.2), channel_id=1, source_target_pairs={{0,1},{1,0},{2,3},{3,2},{4,5},{5,4},{6,7},{7,6},{8,9},{9,8},{10,11... | collective-permute-start | bytes 786440 | tf_op jit(solution)/shard_map/ppermute | solution.py:77
  95.0 1.9 %collective-permute-start.21 = (bf16[256,512]{1,0:T(8,128)(2,1)S(1)}, bf16[256,512]{1,0:T(8,128)(2,1)S(1)}, u32[]{:S(2)}, u32[]{:S(2)}) collective-permute-start(bf16[256,512]{1,0:T(8,128)(2,1)S(1)} %pad_maximum_fusion.3), channel_id=1, source_target_pairs={{0,1},{1,0},{2,3},{3,2},{4,5},{5,4},{6,7},{7,6},{8,9},{9,8},{10,11... | collective-permute-start | bytes 786440 | tf_op jit(solution)/shard_map/ppermute | solution.py:77
  97.0 1.8 %collective-permute-start.28 = (bf16[256,512]{1,0:T(8,128)(2,1)S(1)}, bf16[256,512]{1,0:T(8,128)(2,1)S(1)}, u32[]{:S(2)}, u32[]{:S(2)}) collective-permute-start(bf16[256,512]{1,0:T(8,128)(2,1)S(1)} %pad_maximum_fusion.4), channel_id=1, source_target_pairs={{0,1},{1,0},{2,3},{3,2},{4,5},{5,4},{6,7},{7,6},{8,9},{9,8},{10,11... | collective-permute-start | bytes 786440 | tf_op jit(solution)/shard_map/ppermute | solution.py:77
  101.0 1.6 %copy-done = f32[1440,512]{1,0:T(8,128)} copy-done((f32[1440,512]{1,0:T(8,128)}, f32[1440,512]{1,0:T(8,128)S(1)}, u32[]{:S(2)}) %copy-start) | copy-done | bytes 2949144
  (216 shorter events, 35.7 us)
Async XLA Ops:
  4.2 9.3 %collective-permute-start.1 = (bf16[4,32,832]{2,1,0:T(8,128)(2,1)S(1)}, bf16[4,32,832]{2,1,0:T(8,128)(2,1)S(1)}, u32[]{:S(2)}, u32[]{:S(2)}) collective-permute-start(bf16[4,32,832]{2,1,0:T(8,128)(2,1)S(1)} %concatenate.107), channel_id=1, source_target_pairs={{8,0},{16,8},{24,16},{9,1},{17,9},{25,17},{10,2},{18,10},{26,18},{... | collective-permute-start | bytes 638984 | tf_op jit(solution)/shard_map/ppermute | solution.py:127
  5.5 8.8 %collective-permute-start = (bf16[4,32,832]{2,1,0:T(8,128)(2,1)S(1)}, bf16[4,32,832]{2,1,0:T(8,128)(2,1)S(1)}, u32[]{:S(2)}, u32[]{:S(2)}) collective-permute-start(bf16[4,32,832]{2,1,0:T(8,128)(2,1)S(1)} %concatenate.107), channel_id=1, source_target_pairs={{0,8},{8,16},{16,24},{1,9},{9,17},{17,25},{2,10},{10,18},{18,26},{... | collective-permute-start | bytes 638984 | tf_op jit(solution)/shard_map/ppermute | solution.py:126
  14.4 7.5 %collective-permute-start.3 = (bf16[12,4,832]{2,1,0:T(4,128)(2,1)S(1)}, bf16[12,4,832]{2,1,0:T(4,128)(2,1)S(1)}, u32[]{:S(2)}, u32[]{:S(2)}) collective-permute-start(bf16[12,4,832]{2,1,0:T(4,128)(2,1)S(1)} %get-tuple-element.29), channel_id=1, source_target_pairs={{1,0},{2,1},{3,2},{4,3},{5,4},{6,5},{7,6},{9,8},{10,9},{11,10},{12... | collective-permute-start | bytes 239624 | tf_op jit(solution)/shard_map/ppermute | solution.py:127
  17.8 4.9 %collective-permute-start.2 = (bf16[12,4,832]{2,1,0:T(4,128)(2,1)S(1)}, bf16[12,4,832]{2,1,0:T(4,128)(2,1)S(1)}, u32[]{:S(2)}, u32[]{:S(2)}) collective-permute-start(bf16[12,4,832]{2,1,0:T(4,128)(2,1)S(1)} %get-tuple-element.28), channel_id=1, source_target_pairs={{0,1},{1,2},{2,3},{3,4},{4,5},{5,6},{6,7},{8,9},{9,10},{10,11},{11... | collective-permute-start | bytes 239624 | tf_op jit(solution)/shard_map/ppermute | solution.py:126
  45.5 9.2 %collective-permute-start.8 = (f32[128,512]{1,0:T(8,128)S(1)}, f32[128,512]{1,0:T(8,128)S(1)}, u32[]{:S(2)}, u32[]{:S(2)}) collective-permute-start(f32[128,512]{1,0:T(8,128)S(1)} %constant_dynamic-slice_fusion.5), channel_id=1, source_target_pairs={{0,2},{1,3},{2,0},{3,1},{4,6},{5,7},{6,4},{7,5},{8,10},{9,11},{10,... | collective-permute-start | bytes 786440 | tf_op jit(solution)/shard_map/ppermute | solution.py:46
  48.5 9.2 %collective-permute-start.15 = (f32[128,512]{1,0:T(8,128)S(1)}, f32[128,512]{1,0:T(8,128)S(1)}, u32[]{:S(2)}, u32[]{:S(2)}) collective-permute-start(f32[128,512]{1,0:T(8,128)S(1)} %constant_dynamic-slice_fusion.3), channel_id=1, source_target_pairs={{0,8},{8,0},{16,24},{24,16},{1,9},{9,1},{17,25},{25,17},{2,10},{10... | collective-permute-start | bytes 786440 | tf_op jit(solution)/shard_map/ppermute | solution.py:46
  51.6 9.4 %collective-permute-start.22 = (f32[128,512]{1,0:T(8,128)S(1)}, f32[128,512]{1,0:T(8,128)S(1)}, u32[]{:S(2)}, u32[]{:S(2)}) collective-permute-start(f32[128,512]{1,0:T(8,128)S(1)} %constant_dynamic-slice_fusion.1), channel_id=1, source_target_pairs={{0,16},{8,24},{16,0},{24,8},{1,17},{9,25},{17,1},{25,9},{2,18},{10... | collective-permute-start | bytes 786440 | tf_op jit(solution)/shard_map/ppermute | solution.py:46
  54.8 8.5 %collective-permute-start.9 = (f32[64,512]{1,0:T(8,128)S(1)}, f32[64,512]{1,0:T(8,128)S(1)}, u32[]{:S(2)}, u32[]{:S(2)}) collective-permute-start(f32[64,512]{1,0:T(8,128)S(1)} %constant_dynamic-slice_fusion.4), channel_id=1, source_target_pairs={{0,8},{8,0},{16,24},{24,16},{1,9},{9,1},{17,25},{25,17},{2,10},{10... | collective-permute-start | bytes 393224 | tf_op jit(solution)/shard_map/ppermute | solution.py:46
  57.8 6.5 %collective-permute-start.16 = (f32[64,512]{1,0:T(8,128)S(1)}, f32[64,512]{1,0:T(8,128)S(1)}, u32[]{:S(2)}, u32[]{:S(2)}) collective-permute-start(f32[64,512]{1,0:T(8,128)S(1)} %constant_dynamic-slice_fusion.2), channel_id=1, source_target_pairs={{0,16},{8,24},{16,0},{24,8},{1,17},{9,25},{17,1},{25,9},{2,18},{10... | collective-permute-start | bytes 393224 | tf_op jit(solution)/shard_map/ppermute | solution.py:46
  61.0 9.9 %collective-permute-start.23 = (f32[64,512]{1,0:T(8,128)S(1)}, f32[64,512]{1,0:T(8,128)S(1)}, u32[]{:S(2)}, u32[]{:S(2)}) collective-permute-start(f32[64,512]{1,0:T(8,128)S(1)} %constant_dynamic-slice_fusion), channel_id=1, source_target_pairs={{0,4},{1,5},{2,6},{3,7},{4,0},{5,1},{6,2},{7,3},{8,12},{9,13},{10,... | collective-permute-start | bytes 393224 | tf_op jit(solution)/shard_map/ppermute | solution.py:46
  63.4 7.8 %collective-permute-start.10 = (f32[64,512]{1,0:T(8,128)S(1)}, f32[64,512]{1,0:T(8,128)S(1)}, u32[]{:S(2)}, u32[]{:S(2)}) collective-permute-start(f32[64,512]{1,0:T(8,128)S(1)} %dynamic-slice_add_fusion.5), channel_id=1, source_target_pairs={{0,16},{8,24},{16,0},{24,8},{1,17},{9,25},{17,1},{25,9},{2,18},{10... | collective-permute-start | bytes 393224 | tf_op jit(solution)/shard_map/ppermute | solution.py:49
  64.3 13.0 %collective-permute-start.17 = (f32[64,512]{1,0:T(8,128)S(1)}, f32[64,512]{1,0:T(8,128)S(1)}, u32[]{:S(2)}, u32[]{:S(2)}) collective-permute-start(f32[64,512]{1,0:T(8,128)S(1)} %dynamic-slice_add_fusion.4), channel_id=1, source_target_pairs={{0,4},{1,5},{2,6},{3,7},{4,0},{5,1},{6,2},{7,3},{8,12},{9,13},{10,... | collective-permute-start | bytes 393224 | tf_op jit(solution)/shard_map/ppermute | solution.py:49
  70.9 7.6 %collective-permute-start.24 = (f32[64,512]{1,0:T(8,128)S(1)}, f32[64,512]{1,0:T(8,128)S(1)}, u32[]{:S(2)}, u32[]{:S(2)}) collective-permute-start(f32[64,512]{1,0:T(8,128)S(1)} %dynamic-slice_add_fusion.3), channel_id=1, source_target_pairs={{0,2},{1,3},{2,0},{3,1},{4,6},{5,7},{6,4},{7,5},{8,10},{9,11},{10,... | collective-permute-start | bytes 393224 | tf_op jit(solution)/shard_map/ppermute | solution.py:49
  71.2 11.1 %collective-permute-start.11 = (f32[64,512]{1,0:T(8,128)S(1)}, f32[64,512]{1,0:T(8,128)S(1)}, u32[]{:S(2)}, u32[]{:S(2)}) collective-permute-start(f32[64,512]{1,0:T(8,128)S(1)} %add.230), channel_id=1, source_target_pairs={{0,4},{1,5},{2,6},{3,7},{4,0},{5,1},{6,2},{7,3},{8,12},{9,13},{10,... | collective-permute-start | bytes 393224 | tf_op jit(solution)/shard_map/ppermute | solution.py:49
  77.3 5.3 %collective-permute-start.18 = (f32[64,512]{1,0:T(8,128)S(1)}, f32[64,512]{1,0:T(8,128)S(1)}, u32[]{:S(2)}, u32[]{:S(2)}) collective-permute-start(f32[64,512]{1,0:T(8,128)S(1)} %add.238), channel_id=1, source_target_pairs={{0,2},{1,3},{2,0},{3,1},{4,6},{5,7},{6,4},{7,5},{8,10},{9,11},{10,... | collective-permute-start | bytes 393224 | tf_op jit(solution)/shard_map/ppermute | solution.py:49
  78.5 6.1 %collective-permute-start.25 = (f32[64,512]{1,0:T(8,128)S(1)}, f32[64,512]{1,0:T(8,128)S(1)}, u32[]{:S(2)}, u32[]{:S(2)}) collective-permute-start(f32[64,512]{1,0:T(8,128)S(1)} %add.246), channel_id=1, source_target_pairs={{0,8},{8,0},{16,24},{24,16},{1,9},{9,1},{17,25},{25,17},{2,10},{10... | collective-permute-start | bytes 393224 | tf_op jit(solution)/shard_map/ppermute | solution.py:49
  82.3 3.9 %collective-permute-start.12 = (bf16[64,512]{1,0:T(8,128)(2,1)S(1)}, bf16[64,512]{1,0:T(8,128)(2,1)S(1)}, u32[]{:S(2)}, u32[]{:S(2)}) collective-permute-start(bf16[64,512]{1,0:T(8,128)(2,1)S(1)} %add_convert_fusion.2), channel_id=1, source_target_pairs={{0,8},{8,0},{16,24},{24,16},{1,9},{9,1},{17,25},{25,17},{2,10},{10... | collective-permute-start | bytes 196616 | tf_op jit(solution)/shard_map/ppermute | solution.py:56
  82.7 5.7 %collective-permute-start.19 = (bf16[64,512]{1,0:T(8,128)(2,1)S(1)}, bf16[64,512]{1,0:T(8,128)(2,1)S(1)}, u32[]{:S(2)}, u32[]{:S(2)}) collective-permute-start(bf16[64,512]{1,0:T(8,128)(2,1)S(1)} %add_convert_fusion.1), channel_id=1, source_target_pairs={{0,16},{8,24},{16,0},{24,8},{1,17},{9,25},{17,1},{25,9},{2,18},{10... | collective-permute-start | bytes 196616 | tf_op jit(solution)/shard_map/ppermute | solution.py:56
  84.6 4.1 %collective-permute-start.26 = (bf16[64,512]{1,0:T(8,128)(2,1)S(1)}, bf16[64,512]{1,0:T(8,128)(2,1)S(1)}, u32[]{:S(2)}, u32[]{:S(2)}) collective-permute-start(bf16[64,512]{1,0:T(8,128)(2,1)S(1)} %add_convert_fusion), channel_id=1, source_target_pairs={{0,4},{1,5},{2,6},{3,7},{4,0},{5,1},{6,2},{7,3},{8,12},{9,13},{10,... | collective-permute-start | bytes 196616 | tf_op jit(solution)/shard_map/ppermute | solution.py:56
  86.2 4.8 %collective-permute-start.13 = (bf16[128,512]{1,0:T(8,128)(2,1)S(1)}, bf16[128,512]{1,0:T(8,128)(2,1)S(1)}, u32[]{:S(2)}, u32[]{:S(2)}) collective-permute-start(bf16[128,512]{1,0:T(8,128)(2,1)S(1)} %pad_maximum_fusion.11), channel_id=1, source_target_pairs={{0,2},{1,3},{2,0},{3,1},{4,6},{5,7},{6,4},{7,5},{8,10},{9,11},{10,... | collective-permute-start | bytes 393224 | tf_op jit(solution)/shard_map/ppermute | solution.py:56
  88.4 6.5 %collective-permute-start.20 = (bf16[128,512]{1,0:T(8,128)(2,1)S(1)}, bf16[128,512]{1,0:T(8,128)(2,1)S(1)}, u32[]{:S(2)}, u32[]{:S(2)}) collective-permute-start(bf16[128,512]{1,0:T(8,128)(2,1)S(1)} %pad_maximum_fusion.12), channel_id=1, source_target_pairs={{0,8},{8,0},{16,24},{24,16},{1,9},{9,1},{17,25},{25,17},{2,10},{10... | collective-permute-start | bytes 393224 | tf_op jit(solution)/shard_map/ppermute | solution.py:56
  88.7 8.2 %collective-permute-start.27 = (bf16[128,512]{1,0:T(8,128)(2,1)S(1)}, bf16[128,512]{1,0:T(8,128)(2,1)S(1)}, u32[]{:S(2)}, u32[]{:S(2)}) collective-permute-start(bf16[128,512]{1,0:T(8,128)(2,1)S(1)} %pad_maximum_fusion.13), channel_id=1, source_target_pairs={{0,16},{8,24},{16,0},{24,8},{1,17},{9,25},{17,1},{25,9},{2,18},{10... | collective-permute-start | bytes 393224 | tf_op jit(solution)/shard_map/ppermute | solution.py:56
  91.1 7.8 %collective-permute-start.14 = (bf16[256,512]{1,0:T(8,128)(2,1)S(1)}, bf16[256,512]{1,0:T(8,128)(2,1)S(1)}, u32[]{:S(2)}, u32[]{:S(2)}) collective-permute-start(bf16[256,512]{1,0:T(8,128)(2,1)S(1)} %pad_maximum_fusion.2), channel_id=1, source_target_pairs={{0,1},{1,0},{2,3},{3,2},{4,5},{5,4},{6,7},{7,6},{8,9},{9,8},{10,11... | collective-permute-start | bytes 786440 | tf_op jit(solution)/shard_map/ppermute | solution.py:77
  95.0 5.7 %collective-permute-start.21 = (bf16[256,512]{1,0:T(8,128)(2,1)S(1)}, bf16[256,512]{1,0:T(8,128)(2,1)S(1)}, u32[]{:S(2)}, u32[]{:S(2)}) collective-permute-start(bf16[256,512]{1,0:T(8,128)(2,1)S(1)} %pad_maximum_fusion.3), channel_id=1, source_target_pairs={{0,1},{1,0},{2,3},{3,2},{4,5},{5,4},{6,7},{7,6},{8,9},{9,8},{10,11... | collective-permute-start | bytes 786440 | tf_op jit(solution)/shard_map/ppermute | solution.py:77
  (35 other events, 49.1 us)

commit v15 on v13

--- a/solution.py
+++ b/solution.py
@@ -292,9 +292,11 @@
     lifted = lax.dynamic_slice_in_dim(jnp.concatenate(lifted, axis=0), upper * half, half, 1)
     total_cells = STEPS * rows_dev * lax.axis_size("rows") * cols_dev * lax.axis_size("cols")
     norm_scale = 1.0 / math.sqrt(total_cells)
+    early = (len(grads_seen) - 1) * cells
+    grads_all = jnp.concatenate(grads_seen, axis=0)
     joined = jnp.dot(
-        lifted.T, jnp.concatenate(grads_seen, axis=0), preferred_element_type=jnp.float32
-    )
+        lifted[:early].T, grads_all[:early], preferred_element_type=jnp.float32
+    ) + jnp.dot(lifted[early:].T, grads_all[early:], preferred_element_type=jnp.float32)
     kernel_grad, bias_grad = sum_everywhere(joined * norm_scale, first, rest)
     return (hidden_final, grad_hidden_start, grad_cell_start, kernel_grad, bias_grad)
 

time: 100 us -> 101 us (1.010)
  waiting for transfers between devices: 14.3 us -> 16.5 us
  starting transfers between devices: 53.3 us -> 51.1 us
  matrix products: 5.94 us -> 7.08 us
    ppermute x6, waiting for transfers between devices: 0.35 us -> 2.62 us  [double(): got = lax.ppermute(piece, axis, flip_pairs(axis, bit))]
    ppermute x6, starting transfers between devices: 6.99 us -> 5.05 us  [double(): got = lax.ppermute(piece, axis, flip_pairs(axis, bit))]
    dot_general x1 -> x2, matrix products: 1.72 us -> 2.85 us  [the longest x1 1.57 us: shards(): jnp.dot(lifted[:early].T, grads_all[:early], preferred_element_type=jnp.f...]
  transfers between devices with their start and end apart: 29 -> 29, of which waited for: 8 -> 8; matrix products, arithmetic and copies ran while one was open for 15% -> 16% of each run, Pallas kernels for 0% -> 0%
where the time goes in v15:
time: 101 us; the launch traced here: 100 us
  starting transfers between devices  51.1 us (51%)
  waiting for transfers between devices  16.5 us (16%)
  local copies, waits for them, and re-layouts  12.1 us (12%)
  other arithmetic  11.7 us (12%)
  matrix products  7.08 us (7%)
  between operations  1.59 us (2%)
    ppermute x6, starting transfers between devices, halve(): part = keep + lax.ppermute(send, axis, flip_pairs(axis, bit))  12.5 us
    ppermute x6, starting transfers between devices, halve(): part = part + lax.ppermute(part, axis, flip_pairs(axis, bit))  11.4 us
    ppermute x2, starting transfers between devices, widen(): lax.ppermute(tail, axis, [(i, i + dist) for i in range(count - dist)])  9.47 us
    ppermute x3, starting transfers between devices, sum_everywhere(): swapped = [(p, lax.ppermute(p, axis, pairs)) for p in pieces]  8.65 us
    ppermute x2, waiting for transfers between devices, widen(): lax.ppermute(head, axis, [(i + dist, i) for i in range(count - dist)])  6.35 us
    ppermute x6, starting transfers between devices, double(): got = lax.ppermute(piece, axis, flip_pairs(axis, bit))  5.05 us
    unnamed x39, local copies, waits for them, and re-layouts  4.24 us
    conv_general_dilated x4, matrix products, convolve(): lax.conv_general_dilated(field[None], weights, (1, 1), 'VALID', dimension...  4.23 us
  transfers between devices with their start and end apart: 29, of which 8 were waited for; matrix products, arithmetic and copies ran while one was open for 16% of the time, Pallas kernels for 0%

profile of v15, /device:TPU:1, one launch (start us, length us, event | category | flops | bytes accessed | tf_op | source)
XLA Modules:
  0.0 100.1 jit_solution(4822386062680691164)
XLA Ops:
  4.2 1.3 %collective-permute-start.1 = (bf16[4,32,832]{2,1,0:T(8,128)(2,1)S(1)}, bf16[4,32,832]{2,1,0:T(8,128)(2,1)S(1)}, u32[]{:S(2)}, u32[]{:S(2)}) collective-permute-start(bf16[4,32,832]{2,1,0:T(8,128)(2,1)S(1)} %concatenate.107), channel_id=1, source_target_pairs={{8,0},{16,8},{24,16},{9,1},{17,9},{25,17},{10,2},{18,10},{26,18},{... | collective-permute-start | bytes 638984 | tf_op jit(solution)/shard_map/ppermute | solution.py:127
  5.5 4.6 %collective-permute-start = (bf16[4,32,832]{2,1,0:T(8,128)(2,1)S(1)}, bf16[4,32,832]{2,1,0:T(8,128)(2,1)S(1)}, u32[]{:S(2)}, u32[]{:S(2)}) collective-permute-start(bf16[4,32,832]{2,1,0:T(8,128)(2,1)S(1)} %concatenate.107), channel_id=1, source_target_pairs={{0,8},{8,16},{16,24},{1,9},{9,17},{17,25},{2,10},{10,18},{18,26},{... | collective-permute-start | bytes 638984 | tf_op jit(solution)/shard_map/ppermute | solution.py:126
  10.3 3.1 %collective-permute-done.1 = bf16[4,32,832]{2,1,0:T(8,128)(2,1)S(1)} collective-permute-done((bf16[4,32,832]{2,1,0:T(8,128)(2,1)S(1)}, bf16[4,32,832]{2,1,0:T(8,128)(2,1)S(1)}, u32[]{:S(2)}, u32[]{:S(2)}) %collective-permute-start.1) | collective-permute-done | bytes 213024 | tf_op jit(solution)/shard_map/ppermute | solution.py:127
  14.4 4.9 %collective-permute-start.2 = (bf16[12,4,832]{2,1,0:T(4,128)(2,1)S(1)}, bf16[12,4,832]{2,1,0:T(4,128)(2,1)S(1)}, u32[]{:S(2)}, u32[]{:S(2)}) collective-permute-start(bf16[12,4,832]{2,1,0:T(4,128)(2,1)S(1)} %get-tuple-element.28), channel_id=1, source_target_pairs={{0,1},{1,2},{2,3},{3,4},{4,5},{5,6},{6,7},{8,9},{9,10},{10,11},{11... | collective-permute-start | bytes 239624 | tf_op jit(solution)/shard_map/ppermute | solution.py:126
  19.2 1.9 %collective-permute-start.3 = (bf16[12,4,832]{2,1,0:T(4,128)(2,1)S(1)}, bf16[12,4,832]{2,1,0:T(4,128)(2,1)S(1)}, u32[]{:S(2)}, u32[]{:S(2)}) collective-permute-start(bf16[12,4,832]{2,1,0:T(4,128)(2,1)S(1)} %get-tuple-element.29), channel_id=1, source_target_pairs={{1,0},{2,1},{3,2},{4,3},{5,4},{6,5},{7,6},{9,8},{10,9},{11,10},{12... | collective-permute-start | bytes 239624 | tf_op jit(solution)/shard_map/ppermute | solution.py:127
  21.8 3.2 %collective-permute-done.3 = bf16[12,4,832]{2,1,0:T(4,128)(2,1)S(1)} collective-permute-done((bf16[12,4,832]{2,1,0:T(4,128)(2,1)S(1)}, bf16[12,4,832]{2,1,0:T(4,128)(2,1)S(1)}, u32[]{:S(2)}, u32[]{:S(2)}) %collective-permute-start.3) | collective-permute-done | bytes 79904 | tf_op jit(solution)/shard_map/ppermute | solution.py:127
  32.6 2.1 %convolution_select_fusion.1 = f32[8,8,5,512]{3,1,2,0:T(8,128)S(1)} fusion(bf16[3,3,160,512]{3,2,1,0:T(8,128)(2,1)} %bitcast.91, pred[8,5]{0,1:T(8,128)(4,1)S(1)} %copy-done.16, bf16[10,1,7,2,160]{4,2,3,0,1:T(8,128)(2,1)S(1)} %slice.379, bf16[10,1,8,5,160]{4,2,3,0,1:T(8,128)(2,1)S(1)} %copy.16), kind=kOutput, calls=%fused_computation.7 | convolution fusion | flops 472560640 | bytes 2302760 | tf_op jit(solution)/shard_map/conv_general_dilated | solution.py:174
  45.6 1.6 %add_multiply_fusion = f32[768,512]{1,0:T(8,128)S(1)} fusion(f32[768,512]{1,0:T(8,128)S(1)} %fusion.64, bf16[512,768]{1,0:T(8,128)(2,1)S(1)} %fusion.6, bf16[128,512]{1,0:T(8,128)(2,1)} %collective-permute-done.6, bf16[128,512]{1,0:T(8,128)(2,1)S(1)} %bitcast.88, bf16[128,512]{1,0:T(8,128)(2,1)} %bitcast.32), kind=kOutput, calls=%fused_computation.4 | convolution fusion | flops 303955968 | bytes 4128768 | tf_op jit(solution)/shard_map/dot_general | solution.py:297
  47.3 5.0 %collective-permute-start.8 = (f32[128,512]{1,0:T(8,128)S(1)}, f32[128,512]{1,0:T(8,128)S(1)}, u32[]{:S(2)}, u32[]{:S(2)}) collective-permute-start(f32[128,512]{1,0:T(8,128)S(1)} %constant_dynamic-slice_fusion.5), channel_id=1, source_target_pairs={{0,16},{8,24},{16,0},{24,8},{1,17},{9,25},{17,1},{25,9},{2,18},{10... | collective-permute-start | bytes 786440 | tf_op jit(solution)/shard_map/ppermute | solution.py:46
  54.2 1.4 %collective-permute-start.22 = (f32[128,512]{1,0:T(8,128)S(1)}, f32[128,512]{1,0:T(8,128)S(1)}, u32[]{:S(2)}, u32[]{:S(2)}) collective-permute-start(f32[128,512]{1,0:T(8,128)S(1)} %constant_dynamic-slice_fusion.1), channel_id=1, source_target_pairs={{0,2},{1,3},{2,0},{3,1},{4,6},{5,7},{6,4},{7,5},{8,10},{9,11},{10,... | collective-permute-start | bytes 786440 | tf_op jit(solution)/shard_map/ppermute | solution.py:46
  55.6 3.2 %collective-permute-done.8 = f32[128,512]{1,0:T(8,128)S(1)} collective-permute-done((f32[128,512]{1,0:T(8,128)S(1)}, f32[128,512]{1,0:T(8,128)S(1)}, u32[]{:S(2)}, u32[]{:S(2)}) %collective-permute-start.8) | collective-permute-done | bytes 262176 | tf_op jit(solution)/shard_map/ppermute | solution.py:46
  58.8 2.4 %collective-permute-start.9 = (f32[64,512]{1,0:T(8,128)S(1)}, f32[64,512]{1,0:T(8,128)S(1)}, u32[]{:S(2)}, u32[]{:S(2)}) collective-permute-start(f32[64,512]{1,0:T(8,128)S(1)} %constant_dynamic-slice_fusion.4), channel_id=1, source_target_pairs={{0,4},{1,5},{2,6},{3,7},{4,0},{5,1},{6,2},{7,3},{8,12},{9,13},{10,... | collective-permute-start | bytes 393224 | tf_op jit(solution)/shard_map/ppermute | solution.py:46
  64.8 1.9 %collective-permute-start.10 = (f32[64,512]{1,0:T(8,128)S(1)}, f32[64,512]{1,0:T(8,128)S(1)}, u32[]{:S(2)}, u32[]{:S(2)}) collective-permute-start(f32[64,512]{1,0:T(8,128)S(1)} %dynamic-slice_add_fusion.5), channel_id=1, source_target_pairs={{0,2},{1,3},{2,0},{3,1},{4,6},{5,7},{6,4},{7,5},{8,10},{9,11},{10,... | collective-permute-start | bytes 393224 | tf_op jit(solution)/shard_map/ppermute | solution.py:49
  66.8 2.5 %collective-permute-start.17 = (f32[64,512]{1,0:T(8,128)S(1)}, f32[64,512]{1,0:T(8,128)S(1)}, u32[]{:S(2)}, u32[]{:S(2)}) collective-permute-start(f32[64,512]{1,0:T(8,128)S(1)} %dynamic-slice_add_fusion.4), channel_id=1, source_target_pairs={{0,4},{1,5},{2,6},{3,7},{4,0},{5,1},{6,2},{7,3},{8,12},{9,13},{10,... | collective-permute-start | bytes 393224 | tf_op jit(solution)/shard_map/ppermute | solution.py:49
  69.5 4.6 %collective-permute-start.11 = (f32[64,512]{1,0:T(8,128)S(1)}, f32[64,512]{1,0:T(8,128)S(1)}, u32[]{:S(2)}, u32[]{:S(2)}) collective-permute-start(f32[64,512]{1,0:T(8,128)S(1)} %add.234), channel_id=1, source_target_pairs={{0,8},{8,0},{16,24},{24,16},{1,9},{9,1},{17,25},{25,17},{2,10},{10... | collective-permute-start | bytes 393224 | tf_op jit(solution)/shard_map/ppermute | solution.py:49
  74.1 1.5 %fusion.99 = bf16[4,32,128]{2,1,0:T(8,128)(2,1)} fusion(f32[8,36,128]{2,1,0:T(8,128)S(1)} %get-tuple-element.16, f32[8,36,128]{2,1,0:T(8,128)} %get-tuple-element.34), kind=kLoop, calls=%fused_computation.205 | loop fusion | flops 32768 | bytes 163840 | tf_op jit(solution)/shard_map/convert_element_type | solution.py:188
  75.7 2.2 %collective-permute-start.25 = (f32[64,512]{1,0:T(8,128)S(1)}, f32[64,512]{1,0:T(8,128)S(1)}, u32[]{:S(2)}, u32[]{:S(2)}) collective-permute-start(f32[64,512]{1,0:T(8,128)S(1)} %add.250), channel_id=1, source_target_pairs={{0,4},{1,5},{2,6},{3,7},{4,0},{5,1},{6,2},{7,3},{8,12},{9,13},{10,... | collective-permute-start | bytes 393224 | tf_op jit(solution)/shard_map/ppermute | solution.py:49
  78.2 2.5 %collective-permute-done.18 = f32[64,512]{1,0:T(8,128)S(1)} collective-permute-done((f32[64,512]{1,0:T(8,128)S(1)}, f32[64,512]{1,0:T(8,128)S(1)}, u32[]{:S(2)}, u32[]{:S(2)}) %collective-permute-start.18) | collective-permute-done | bytes 131104 | tf_op jit(solution)/shard_map/ppermute | solution.py:49
  82.6 1.4 %collective-permute-done.12 = bf16[64,512]{1,0:T(8,128)(2,1)S(1)} collective-permute-done((bf16[64,512]{1,0:T(8,128)(2,1)S(1)}, bf16[64,512]{1,0:T(8,128)(2,1)S(1)}, u32[]{:S(2)}, u32[]{:S(2)}) %collective-permute-start.12) | collective-permute-done | bytes 65568 | tf_op jit(solution)/shard_map/ppermute | solution.py:56
  85.3 1.6 %collective-permute-start.20 = (bf16[128,512]{1,0:T(8,128)(2,1)S(1)}, bf16[128,512]{1,0:T(8,128)(2,1)S(1)}, u32[]{:S(2)}, u32[]{:S(2)}) collective-permute-start(bf16[128,512]{1,0:T(8,128)(2,1)S(1)} %pad_maximum_fusion.12), channel_id=1, source_target_pairs={{0,8},{8,0},{16,24},{24,16},{1,9},{9,1},{17,25},{25,17},{2,10},{10... | collective-permute-start | bytes 393224 | tf_op jit(solution)/shard_map/ppermute | solution.py:56
  88.3 5.2 %collective-permute-start.14 = (bf16[256,512]{1,0:T(8,128)(2,1)S(1)}, bf16[256,512]{1,0:T(8,128)(2,1)S(1)}, u32[]{:S(2)}, u32[]{:S(2)}) collective-permute-start(bf16[256,512]{1,0:T(8,128)(2,1)S(1)} %pad_maximum_fusion.2), channel_id=1, source_target_pairs={{0,1},{1,0},{2,3},{3,2},{4,5},{5,4},{6,7},{7,6},{8,9},{9,8},{10,11... | collective-permute-start | bytes 786440 | tf_op jit(solution)/shard_map/ppermute | solution.py:77
  93.6 1.5 %collective-permute-start.21 = (bf16[256,512]{1,0:T(8,128)(2,1)S(1)}, bf16[256,512]{1,0:T(8,128)(2,1)S(1)}, u32[]{:S(2)}, u32[]{:S(2)}) collective-permute-start(bf16[256,512]{1,0:T(8,128)(2,1)S(1)} %pad_maximum_fusion.3), channel_id=1, source_target_pairs={{0,1},{1,0},{2,3},{3,2},{4,5},{5,4},{6,7},{7,6},{8,9},{9,8},{10,11... | collective-permute-start | bytes 786440 | tf_op jit(solution)/shard_map/ppermute | solution.py:77
  95.1 2.0 %collective-permute-start.28 = (bf16[256,512]{1,0:T(8,128)(2,1)S(1)}, bf16[256,512]{1,0:T(8,128)(2,1)S(1)}, u32[]{:S(2)}, u32[]{:S(2)}) collective-permute-start(bf16[256,512]{1,0:T(8,128)(2,1)S(1)} %pad_maximum_fusion.4), channel_id=1, source_target_pairs={{0,1},{1,0},{2,3},{3,2},{4,5},{5,4},{6,7},{7,6},{8,9},{9,8},{10,11... | collective-permute-start | bytes 786440 | tf_op jit(solution)/shard_map/ppermute | solution.py:77
  98.6 1.6 %copy-done = f32[1440,512]{1,0:T(8,128)} copy-done((f32[1440,512]{1,0:T(8,128)}, f32[1440,512]{1,0:T(8,128)S(1)}, u32[]{:S(2)}) %copy-start) | copy-done | bytes 2949144
  (193 shorter events, 35.5 us)
Async XLA Ops:
  4.2 9.3 %collective-permute-start.1 = (bf16[4,32,832]{2,1,0:T(8,128)(2,1)S(1)}, bf16[4,32,832]{2,1,0:T(8,128)(2,1)S(1)}, u32[]{:S(2)}, u32[]{:S(2)}) collective-permute-start(bf16[4,32,832]{2,1,0:T(8,128)(2,1)S(1)} %concatenate.107), channel_id=1, source_target_pairs={{8,0},{16,8},{24,16},{9,1},{17,9},{25,17},{10,2},{18,10},{26,18},{... | collective-permute-start | bytes 638984 | tf_op jit(solution)/shard_map/ppermute | solution.py:127
  5.5 8.8 %collective-permute-start = (bf16[4,32,832]{2,1,0:T(8,128)(2,1)S(1)}, bf16[4,32,832]{2,1,0:T(8,128)(2,1)S(1)}, u32[]{:S(2)}, u32[]{:S(2)}) collective-permute-start(bf16[4,32,832]{2,1,0:T(8,128)(2,1)S(1)} %concatenate.107), channel_id=1, source_target_pairs={{0,8},{8,16},{16,24},{1,9},{9,17},{17,25},{2,10},{10,18},{18,26},{... | collective-permute-start | bytes 638984 | tf_op jit(solution)/shard_map/ppermute | solution.py:126
  14.4 7.5 %collective-permute-start.2 = (bf16[12,4,832]{2,1,0:T(4,128)(2,1)S(1)}, bf16[12,4,832]{2,1,0:T(4,128)(2,1)S(1)}, u32[]{:S(2)}, u32[]{:S(2)}) collective-permute-start(bf16[12,4,832]{2,1,0:T(4,128)(2,1)S(1)} %get-tuple-element.28), channel_id=1, source_target_pairs={{0,1},{1,2},{2,3},{3,4},{4,5},{5,6},{6,7},{8,9},{9,10},{10,11},{11... | collective-permute-start | bytes 239624 | tf_op jit(solution)/shard_map/ppermute | solution.py:126
  19.2 5.8 %collective-permute-start.3 = (bf16[12,4,832]{2,1,0:T(4,128)(2,1)S(1)}, bf16[12,4,832]{2,1,0:T(4,128)(2,1)S(1)}, u32[]{:S(2)}, u32[]{:S(2)}) collective-permute-start(bf16[12,4,832]{2,1,0:T(4,128)(2,1)S(1)} %get-tuple-element.29), channel_id=1, source_target_pairs={{1,0},{2,1},{3,2},{4,3},{5,4},{6,5},{7,6},{9,8},{10,9},{11,10},{12... | collective-permute-start | bytes 239624 | tf_op jit(solution)/shard_map/ppermute | solution.py:127
  31.9 11.4 %collective-permute-start.5 = (bf16[6,34,160]{2,1,0:T(8,128)(2,1)}, bf16[6,34,160]{2,1,0:T(8,128)(2,1)S(1)}, u32[]{:S(2)}, u32[]{:S(2)}) collective-permute-start(bf16[6,34,160]{2,1,0:T(8,128)(2,1)} %fusion.82), channel_id=1, source_target_pairs={{0,1},{1,0},{2,3},{3,2},{4,5},{5,4},{6,7},{7,6},{8,9},{9,8},{10,11... | collective-permute-start | bytes 195848 | tf_op jit(solution)/shard_map/ppermute | solution.py:276
  31.9 11.8 %collective-permute-start.4 = (bf16[6,34,160]{2,1,0:T(8,128)(2,1)}, bf16[6,34,160]{2,1,0:T(8,128)(2,1)S(1)}, u32[]{:S(2)}, u32[]{:S(2)}) collective-permute-start(bf16[6,34,160]{2,1,0:T(8,128)(2,1)} %slice.430), channel_id=1, source_target_pairs={{0,1},{1,0},{2,3},{3,2},{4,5},{5,4},{6,7},{7,6},{8,9},{9,8},{10,11... | collective-permute-start | bytes 195848 | tf_op jit(solution)/shard_map/ppermute | solution.py:276
  37.3 8.2 %collective-permute-start.6 = (bf16[128,512]{1,0:T(8,128)(2,1)}, bf16[128,512]{1,0:T(8,128)(2,1)}, u32[]{:S(2)}, u32[]{:S(2)}) collective-permute-start(bf16[128,512]{1,0:T(8,128)(2,1)} %bitcast.32), channel_id=1, source_target_pairs={{0,1},{1,0},{2,3},{3,2},{4,5},{5,4},{6,7},{7,6},{8,9},{9,8},{10,11... | collective-permute-start | bytes 393224 | tf_op jit(solution)/shard_map/ppermute | solution.py:277
  47.3 11.5 %collective-permute-start.8 = (f32[128,512]{1,0:T(8,128)S(1)}, f32[128,512]{1,0:T(8,128)S(1)}, u32[]{:S(2)}, u32[]{:S(2)}) collective-permute-start(f32[128,512]{1,0:T(8,128)S(1)} %constant_dynamic-slice_fusion.5), channel_id=1, source_target_pairs={{0,16},{8,24},{16,0},{24,8},{1,17},{9,25},{17,1},{25,9},{2,18},{10... | collective-permute-start | bytes 786440 | tf_op jit(solution)/shard_map/ppermute | solution.py:46
  52.9 8.3 %collective-permute-start.15 = (f32[128,512]{1,0:T(8,128)S(1)}, f32[128,512]{1,0:T(8,128)S(1)}, u32[]{:S(2)}, u32[]{:S(2)}) collective-permute-start(f32[128,512]{1,0:T(8,128)S(1)} %constant_dynamic-slice_fusion.3), channel_id=1, source_target_pairs={{0,8},{8,0},{16,24},{24,16},{1,9},{9,1},{17,25},{25,17},{2,10},{10... | collective-permute-start | bytes 786440 | tf_op jit(solution)/shard_map/ppermute | solution.py:46
  54.2 8.3 %collective-permute-start.22 = (f32[128,512]{1,0:T(8,128)S(1)}, f32[128,512]{1,0:T(8,128)S(1)}, u32[]{:S(2)}, u32[]{:S(2)}) collective-permute-start(f32[128,512]{1,0:T(8,128)S(1)} %constant_dynamic-slice_fusion.1), channel_id=1, source_target_pairs={{0,2},{1,3},{2,0},{3,1},{4,6},{5,7},{6,4},{7,5},{8,10},{9,11},{10,... | collective-permute-start | bytes 786440 | tf_op jit(solution)/shard_map/ppermute | solution.py:46
  58.8 6.0 %collective-permute-start.9 = (f32[64,512]{1,0:T(8,128)S(1)}, f32[64,512]{1,0:T(8,128)S(1)}, u32[]{:S(2)}, u32[]{:S(2)}) collective-permute-start(f32[64,512]{1,0:T(8,128)S(1)} %constant_dynamic-slice_fusion.4), channel_id=1, source_target_pairs={{0,4},{1,5},{2,6},{3,7},{4,0},{5,1},{6,2},{7,3},{8,12},{9,13},{10,... | collective-permute-start | bytes 393224 | tf_op jit(solution)/shard_map/ppermute | solution.py:46
  61.3 5.5 %collective-permute-start.16 = (f32[64,512]{1,0:T(8,128)S(1)}, f32[64,512]{1,0:T(8,128)S(1)}, u32[]{:S(2)}, u32[]{:S(2)}) collective-permute-start(f32[64,512]{1,0:T(8,128)S(1)} %constant_dynamic-slice_fusion.2), channel_id=1, source_target_pairs={{0,16},{8,24},{16,0},{24,8},{1,17},{9,25},{17,1},{25,9},{2,18},{10... | collective-permute-start | bytes 393224 | tf_op jit(solution)/shard_map/ppermute | solution.py:46
  62.6 6.8 %collective-permute-start.23 = (f32[64,512]{1,0:T(8,128)S(1)}, f32[64,512]{1,0:T(8,128)S(1)}, u32[]{:S(2)}, u32[]{:S(2)}) collective-permute-start(f32[64,512]{1,0:T(8,128)S(1)} %constant_dynamic-slice_fusion), channel_id=1, source_target_pairs={{0,8},{8,0},{16,24},{24,16},{1,9},{9,1},{17,25},{25,17},{2,10},{10... | collective-permute-start | bytes 393224 | tf_op jit(solution)/shard_map/ppermute | solution.py:46
  64.8 4.6 %collective-permute-start.10 = (f32[64,512]{1,0:T(8,128)S(1)}, f32[64,512]{1,0:T(8,128)S(1)}, u32[]{:S(2)}, u32[]{:S(2)}) collective-permute-start(f32[64,512]{1,0:T(8,128)S(1)} %dynamic-slice_add_fusion.5), channel_id=1, source_target_pairs={{0,2},{1,3},{2,0},{3,1},{4,6},{5,7},{6,4},{7,5},{8,10},{9,11},{10,... | collective-permute-start | bytes 393224 | tf_op jit(solution)/shard_map/ppermute | solution.py:49
  66.8 8.8 %collective-permute-start.17 = (f32[64,512]{1,0:T(8,128)S(1)}, f32[64,512]{1,0:T(8,128)S(1)}, u32[]{:S(2)}, u32[]{:S(2)}) collective-permute-start(f32[64,512]{1,0:T(8,128)S(1)} %dynamic-slice_add_fusion.4), channel_id=1, source_target_pairs={{0,4},{1,5},{2,6},{3,7},{4,0},{5,1},{6,2},{7,3},{8,12},{9,13},{10,... | collective-permute-start | bytes 393224 | tf_op jit(solution)/shard_map/ppermute | solution.py:49
  69.4 6.3 %collective-permute-start.24 = (f32[64,512]{1,0:T(8,128)S(1)}, f32[64,512]{1,0:T(8,128)S(1)}, u32[]{:S(2)}, u32[]{:S(2)}) collective-permute-start(f32[64,512]{1,0:T(8,128)S(1)} %dynamic-slice_add_fusion.3), channel_id=1, source_target_pairs={{0,16},{8,24},{16,0},{24,8},{1,17},{9,25},{17,1},{25,9},{2,18},{10... | collective-permute-start | bytes 393224 | tf_op jit(solution)/shard_map/ppermute | solution.py:49
  69.5 8.4 %collective-permute-start.11 = (f32[64,512]{1,0:T(8,128)S(1)}, f32[64,512]{1,0:T(8,128)S(1)}, u32[]{:S(2)}, u32[]{:S(2)}) collective-permute-start(f32[64,512]{1,0:T(8,128)S(1)} %add.234), channel_id=1, source_target_pairs={{0,8},{8,0},{16,24},{24,16},{1,9},{9,1},{17,25},{25,17},{2,10},{10... | collective-permute-start | bytes 393224 | tf_op jit(solution)/shard_map/ppermute | solution.py:49
  75.6 5.1 %collective-permute-start.18 = (f32[64,512]{1,0:T(8,128)S(1)}, f32[64,512]{1,0:T(8,128)S(1)}, u32[]{:S(2)}, u32[]{:S(2)}) collective-permute-start(f32[64,512]{1,0:T(8,128)S(1)} %add.242), channel_id=1, source_target_pairs={{0,2},{1,3},{2,0},{3,1},{4,6},{5,7},{6,4},{7,5},{8,10},{9,11},{10,... | collective-permute-start | bytes 393224 | tf_op jit(solution)/shard_map/ppermute | solution.py:49
  75.7 6.2 %collective-permute-start.25 = (f32[64,512]{1,0:T(8,128)S(1)}, f32[64,512]{1,0:T(8,128)S(1)}, u32[]{:S(2)}, u32[]{:S(2)}) collective-permute-start(f32[64,512]{1,0:T(8,128)S(1)} %add.250), channel_id=1, source_target_pairs={{0,4},{1,5},{2,6},{3,7},{4,0},{5,1},{6,2},{7,3},{8,12},{9,13},{10,... | collective-permute-start | bytes 393224 | tf_op jit(solution)/shard_map/ppermute | solution.py:49
  77.9 6.0 %collective-permute-start.12 = (bf16[64,512]{1,0:T(8,128)(2,1)S(1)}, bf16[64,512]{1,0:T(8,128)(2,1)S(1)}, u32[]{:S(2)}, u32[]{:S(2)}) collective-permute-start(bf16[64,512]{1,0:T(8,128)(2,1)S(1)} %add_convert_fusion.2), channel_id=1, source_target_pairs={{0,4},{1,5},{2,6},{3,7},{4,0},{5,1},{6,2},{7,3},{8,12},{9,13},{10,... | collective-permute-start | bytes 196616 | tf_op jit(solution)/shard_map/ppermute | solution.py:56
  82.0 4.9 %collective-permute-start.26 = (bf16[64,512]{1,0:T(8,128)(2,1)S(1)}, bf16[64,512]{1,0:T(8,128)(2,1)S(1)}, u32[]{:S(2)}, u32[]{:S(2)}) collective-permute-start(bf16[64,512]{1,0:T(8,128)(2,1)S(1)} %add_convert_fusion), channel_id=1, source_target_pairs={{0,8},{8,0},{16,24},{24,16},{1,9},{9,1},{17,25},{25,17},{2,10},{10... | collective-permute-start | bytes 196616 | tf_op jit(solution)/shard_map/ppermute | solution.py:56
  85.3 8.2 %collective-permute-start.20 = (bf16[128,512]{1,0:T(8,128)(2,1)S(1)}, bf16[128,512]{1,0:T(8,128)(2,1)S(1)}, u32[]{:S(2)}, u32[]{:S(2)}) collective-permute-start(bf16[128,512]{1,0:T(8,128)(2,1)S(1)} %pad_maximum_fusion.12), channel_id=1, source_target_pairs={{0,8},{8,0},{16,24},{24,16},{1,9},{9,1},{17,25},{25,17},{2,10},{10... | collective-permute-start | bytes 393224 | tf_op jit(solution)/shard_map/ppermute | solution.py:56
  86.9 8.1 %collective-permute-start.27 = (bf16[128,512]{1,0:T(8,128)(2,1)S(1)}, bf16[128,512]{1,0:T(8,128)(2,1)S(1)}, u32[]{:S(2)}, u32[]{:S(2)}) collective-permute-start(bf16[128,512]{1,0:T(8,128)(2,1)S(1)} %pad_maximum_fusion.13), channel_id=1, source_target_pairs={{0,2},{1,3},{2,0},{3,1},{4,6},{5,7},{6,4},{7,5},{8,10},{9,11},{10,... | collective-permute-start | bytes 393224 | tf_op jit(solution)/shard_map/ppermute | solution.py:56
  88.3 8.8 %collective-permute-start.14 = (bf16[256,512]{1,0:T(8,128)(2,1)S(1)}, bf16[256,512]{1,0:T(8,128)(2,1)S(1)}, u32[]{:S(2)}, u32[]{:S(2)}) collective-permute-start(bf16[256,512]{1,0:T(8,128)(2,1)S(1)} %pad_maximum_fusion.2), channel_id=1, source_target_pairs={{0,1},{1,0},{2,3},{3,2},{4,5},{5,4},{6,7},{7,6},{8,9},{9,8},{10,11... | collective-permute-start | bytes 786440 | tf_op jit(solution)/shard_map/ppermute | solution.py:77
  (23 other events, 40.7 us)

commit v16 on v13

--- a/solution.py
+++ b/solution.py
@@ -13,7 +13,7 @@
 KIN = 1440
 SUM_ROWS = 1536
 SUM_WAYS = 3
-SUM_SHARED = 2
+SUM_SHARED = 1
 
 
 def flip_pairs(axis, bit):

time: 100 us -> 100 us (level)
  waiting for transfers between devices: 14.3 us -> 16.1 us
  other arithmetic: 12.3 us -> 10.9 us
    ppermute x6 -> x3, starting transfers between devices: 11.3 us -> 2.83 us  [halve(): part = part + lax.ppermute(part, axis, flip_pairs(axis, bit))]
    ppermute x6 -> x9, starting transfers between devices: 12.5 us -> 17 us  [halve(): part = keep + lax.ppermute(send, axis, flip_pairs(axis, bit))]
    ppermute x6 -> x9, starting transfers between devices: 6.99 us -> 10.1 us  [double(): got = lax.ppermute(piece, axis, flip_pairs(axis, bit))]
    ppermute x6 -> x9, waiting for transfers between devices: 0.35 us -> 2.76 us  [double(): got = lax.ppermute(piece, axis, flip_pairs(axis, bit))]
    ppermute x6 -> x3, waiting for transfers between devices: 2.47 us -> 0.58 us  [halve(): part = part + lax.ppermute(part, axis, flip_pairs(axis, bit))]
    ppermute x6 -> x9, waiting for transfers between devices: 4.23 us -> 5.56 us  [halve(): part = keep + lax.ppermute(send, axis, flip_pairs(axis, bit))]
  transfers between devices with their start and end apart: 29 -> 32, of which waited for: 8 -> 11; matrix products, arithmetic and copies ran while one was open for 15% -> 14% of each run, Pallas kernels for 0% -> 0%
where the time goes in v16:
time: 100 us; the launch traced here: 99.4 us
  starting transfers between devices  52.7 us (53%)
  waiting for transfers between devices  16.1 us (16%)
  local copies, waits for them, and re-layouts  12.1 us (12%)
  other arithmetic  10.9 us (11%)
  matrix products  5.95 us (6%)
  between operations  1.62 us (2%)
    ppermute x9, starting transfers between devices, halve(): part = keep + lax.ppermute(send, axis, flip_pairs(axis, bit))  17 us
    ppermute x9, starting transfers between devices, double(): got = lax.ppermute(piece, axis, flip_pairs(axis, bit))  10.1 us
    ppermute x2, starting transfers between devices, widen(): lax.ppermute(tail, axis, [(i, i + dist) for i in range(count - dist)])  9.47 us
    ppermute x3, starting transfers between devices, sum_everywhere(): swapped = [(p, lax.ppermute(p, axis, pairs)) for p in pieces]  9.23 us
    ppermute x2, waiting for transfers between devices, widen(): lax.ppermute(head, axis, [(i + dist, i) for i in range(count - dist)])  6.35 us
    ppermute x9, waiting for transfers between devices, halve(): part = keep + lax.ppermute(send, axis, flip_pairs(axis, bit))  5.56 us
    conv_general_dilated x4, matrix products, convolve(): lax.conv_general_dilated(field[None], weights, (1, 1), 'VALID', dimension...  4.23 us
    unnamed x39, local copies, waits for them, and re-layouts  4.21 us
  transfers between devices with their start and end apart: 32, of which 11 were waited for; matrix products, arithmetic and copies ran while one was open for 14% of the time, Pallas kernels for 0%

profile of v16, /device:TPU:1, one launch (start us, length us, event | category | flops | bytes accessed | tf_op | source)
XLA Modules:
  0.0 99.4 jit_solution(1214342129907003052)
XLA Ops:
  4.2 1.3 %collective-permute-start.1 = (bf16[4,32,832]{2,1,0:T(8,128)(2,1)S(1)}, bf16[4,32,832]{2,1,0:T(8,128)(2,1)S(1)}, u32[]{:S(2)}, u32[]{:S(2)}) collective-permute-start(bf16[4,32,832]{2,1,0:T(8,128)(2,1)S(1)} %concatenate.116), channel_id=1, source_target_pairs={{8,0},{16,8},{24,16},{9,1},{17,9},{25,17},{10,2},{18,10},{26,18},{... | collective-permute-start | bytes 638984 | tf_op jit(solution)/shard_map/ppermute | solution.py:127
  5.5 4.6 %collective-permute-start = (bf16[4,32,832]{2,1,0:T(8,128)(2,1)S(1)}, bf16[4,32,832]{2,1,0:T(8,128)(2,1)S(1)}, u32[]{:S(2)}, u32[]{:S(2)}) collective-permute-start(bf16[4,32,832]{2,1,0:T(8,128)(2,1)S(1)} %concatenate.116), channel_id=1, source_target_pairs={{0,8},{8,16},{16,24},{1,9},{9,17},{17,25},{2,10},{10,18},{18,26},{... | collective-permute-start | bytes 638984 | tf_op jit(solution)/shard_map/ppermute | solution.py:126
  10.3 3.1 %collective-permute-done.1 = bf16[4,32,832]{2,1,0:T(8,128)(2,1)S(1)} collective-permute-done((bf16[4,32,832]{2,1,0:T(8,128)(2,1)S(1)}, bf16[4,32,832]{2,1,0:T(8,128)(2,1)S(1)}, u32[]{:S(2)}, u32[]{:S(2)}) %collective-permute-start.1) | collective-permute-done | bytes 213024 | tf_op jit(solution)/shard_map/ppermute | solution.py:127
  14.4 4.9 %collective-permute-start.2 = (bf16[12,4,832]{2,1,0:T(4,128)(2,1)S(1)}, bf16[12,4,832]{2,1,0:T(4,128)(2,1)S(1)}, u32[]{:S(2)}, u32[]{:S(2)}) collective-permute-start(bf16[12,4,832]{2,1,0:T(4,128)(2,1)S(1)} %get-tuple-element.28), channel_id=1, source_target_pairs={{0,1},{1,2},{2,3},{3,4},{4,5},{5,6},{6,7},{8,9},{9,10},{10,11},{11... | collective-permute-start | bytes 239624 | tf_op jit(solution)/shard_map/ppermute | solution.py:126
  19.2 1.9 %collective-permute-start.3 = (bf16[12,4,832]{2,1,0:T(4,128)(2,1)S(1)}, bf16[12,4,832]{2,1,0:T(4,128)(2,1)S(1)}, u32[]{:S(2)}, u32[]{:S(2)}) collective-permute-start(bf16[12,4,832]{2,1,0:T(4,128)(2,1)S(1)} %get-tuple-element.29), channel_id=1, source_target_pairs={{1,0},{2,1},{3,2},{4,3},{5,4},{6,5},{7,6},{9,8},{10,9},{11,10},{12... | collective-permute-start | bytes 239624 | tf_op jit(solution)/shard_map/ppermute | solution.py:127
  21.8 3.2 %collective-permute-done.3 = bf16[12,4,832]{2,1,0:T(4,128)(2,1)S(1)} collective-permute-done((bf16[12,4,832]{2,1,0:T(4,128)(2,1)S(1)}, bf16[12,4,832]{2,1,0:T(4,128)(2,1)S(1)}, u32[]{:S(2)}, u32[]{:S(2)}) %collective-permute-start.3) | collective-permute-done | bytes 79904 | tf_op jit(solution)/shard_map/ppermute | solution.py:127
  32.6 2.1 %convolution_select_fusion.1 = f32[8,8,5,512]{3,1,2,0:T(8,128)S(1)} fusion(bf16[3,3,160,512]{3,2,1,0:T(8,128)(2,1)} %bitcast.88, pred[8,5]{0,1:T(8,128)(4,1)S(1)} %copy-done.16, bf16[10,1,7,2,160]{4,2,3,0,1:T(8,128)(2,1)S(1)} %slice.371, bf16[10,1,8,5,160]{4,2,3,0,1:T(8,128)(2,1)S(1)} %copy.16), kind=kOutput, calls=%fused_computation.7 | convolution fusion | flops 472560640 | bytes 2302760 | tf_op jit(solution)/shard_map/conv_general_dilated | solution.py:174
  44.8 1.7 %convolution_multiply_fusion = f32[768,512]{1,0:T(8,128)S(1)} fusion(s32[]{:T(128)S(6)} %select_n.214, bf16[128,1536]{1,0:T(8,128)(2,1)S(1)} %concatenate.132, bf16[128,1536]{1,0:T(8,128)(2,1)S(1)} %concatenate.134, bf16[128,1536]{1,0:T(8,128)(2,1)S(1)} %concatenate.136, bf16[128,1536]{1,0:T(8,128)(2,1)S(1)} %concatenate.138, ...), kind=kOutput, calls=%fused_computation.4 | convolution fusion | flops 408289280 | bytes 3670020 | tf_op jit(solution)/shard_map/dot_general | solution.py:295
  46.7 5.0 %collective-permute-start.8 = (f32[128,512]{1,0:T(8,128)S(1)}, f32[128,512]{1,0:T(8,128)S(1)}, u32[]{:S(2)}, u32[]{:S(2)}) collective-permute-start(f32[128,512]{1,0:T(8,128)S(1)} %constant_dynamic-slice_fusion.8), channel_id=1, source_target_pairs={{0,16},{8,24},{16,0},{24,8},{1,17},{9,25},{17,1},{25,9},{2,18},{10... | collective-permute-start | bytes 786440 | tf_op jit(solution)/shard_map/ppermute | solution.py:46
  52.3 1.3 %collective-permute-start.16 = (f32[128,512]{1,0:T(8,128)S(1)}, f32[128,512]{1,0:T(8,128)S(1)}, u32[]{:S(2)}, u32[]{:S(2)}) collective-permute-start(f32[128,512]{1,0:T(8,128)S(1)} %constant_dynamic-slice_fusion.5), channel_id=1, source_target_pairs={{0,8},{8,0},{16,24},{24,16},{1,9},{9,1},{17,25},{25,17},{2,10},{10... | collective-permute-start | bytes 786440 | tf_op jit(solution)/shard_map/ppermute | solution.py:46
  53.6 1.4 %collective-permute-start.24 = (f32[128,512]{1,0:T(8,128)S(1)}, f32[128,512]{1,0:T(8,128)S(1)}, u32[]{:S(2)}, u32[]{:S(2)}) collective-permute-start(f32[128,512]{1,0:T(8,128)S(1)} %constant_dynamic-slice_fusion.2), channel_id=1, source_target_pairs={{0,2},{1,3},{2,0},{3,1},{4,6},{5,7},{6,4},{7,5},{8,10},{9,11},{10,... | collective-permute-start | bytes 786440 | tf_op jit(solution)/shard_map/ppermute | solution.py:46
  55.0 3.2 %collective-permute-done.8 = f32[128,512]{1,0:T(8,128)S(1)} collective-permute-done((f32[128,512]{1,0:T(8,128)S(1)}, f32[128,512]{1,0:T(8,128)S(1)}, u32[]{:S(2)}, u32[]{:S(2)}) %collective-permute-start.8) | collective-permute-done | bytes 262176 | tf_op jit(solution)/shard_map/ppermute | solution.py:46
  58.2 2.4 %collective-permute-start.9 = (f32[64,512]{1,0:T(8,128)S(1)}, f32[64,512]{1,0:T(8,128)S(1)}, u32[]{:S(2)}, u32[]{:S(2)}) collective-permute-start(f32[64,512]{1,0:T(8,128)S(1)} %constant_dynamic-slice_fusion.7), channel_id=1, source_target_pairs={{0,4},{1,5},{2,6},{3,7},{4,0},{5,1},{6,2},{7,3},{8,12},{9,13},{10,... | collective-permute-start | bytes 393224 | tf_op jit(solution)/shard_map/ppermute | solution.py:46
  62.0 1.3 %collective-permute-start.25 = (f32[64,512]{1,0:T(8,128)S(1)}, f32[64,512]{1,0:T(8,128)S(1)}, u32[]{:S(2)}, u32[]{:S(2)}) collective-permute-start(f32[64,512]{1,0:T(8,128)S(1)} %constant_dynamic-slice_fusion.1), channel_id=1, source_target_pairs={{0,8},{8,0},{16,24},{24,16},{1,9},{9,1},{17,25},{25,17},{2,10},{10... | collective-permute-start | bytes 393224 | tf_op jit(solution)/shard_map/ppermute | solution.py:46
  64.3 1.9 %collective-permute-start.10 = (f32[32,512]{1,0:T(8,128)S(1)}, f32[32,512]{1,0:T(8,128)S(1)}, u32[]{:S(2)}, u32[]{:S(2)}) collective-permute-start(f32[32,512]{1,0:T(8,128)S(1)} %constant_dynamic-slice_fusion.6), channel_id=1, source_target_pairs={{0,2},{1,3},{2,0},{3,1},{4,6},{5,7},{6,4},{7,5},{8,10},{9,11},{10,... | collective-permute-start | bytes 196616 | tf_op jit(solution)/shard_map/ppermute | solution.py:46
  66.2 2.6 %collective-permute-start.18 = (f32[32,512]{1,0:T(8,128)S(1)}, f32[32,512]{1,0:T(8,128)S(1)}, u32[]{:S(2)}, u32[]{:S(2)}) collective-permute-start(f32[32,512]{1,0:T(8,128)S(1)} %constant_dynamic-slice_fusion.3), channel_id=1, source_target_pairs={{0,4},{1,5},{2,6},{3,7},{4,0},{5,1},{6,2},{7,3},{8,12},{9,13},{10,... | collective-permute-start | bytes 196616 | tf_op jit(solution)/shard_map/ppermute | solution.py:46
  69.0 1.9 %collective-permute-start.11 = (f32[32,512]{1,0:T(8,128)S(1)}, f32[32,512]{1,0:T(8,128)S(1)}, u32[]{:S(2)}, u32[]{:S(2)}) collective-permute-start(f32[32,512]{1,0:T(8,128)S(1)} %dynamic-slice_add_fusion.8), channel_id=1, source_target_pairs={{0,8},{8,0},{16,24},{24,16},{1,9},{9,1},{17,25},{25,17},{2,10},{10... | collective-permute-start | bytes 196616 | tf_op jit(solution)/shard_map/ppermute | solution.py:49
  73.2 1.5 %collective-permute-start.12 = (bf16[32,512]{1,0:T(8,128)(2,1)S(1)}, bf16[32,512]{1,0:T(8,128)(2,1)S(1)}, u32[]{:S(2)}, u32[]{:S(2)}) collective-permute-start(bf16[32,512]{1,0:T(8,128)(2,1)S(1)} %add_convert_fusion.2), channel_id=1, source_target_pairs={{0,2},{1,3},{2,0},{3,1},{4,6},{5,7},{6,4},{7,5},{8,10},{9,11},{10,... | collective-permute-start | bytes 98312 | tf_op jit(solution)/shard_map/ppermute | solution.py:56
  74.7 1.8 %collective-permute-start.20 = (bf16[32,512]{1,0:T(8,128)(2,1)S(1)}, bf16[32,512]{1,0:T(8,128)(2,1)S(1)}, u32[]{:S(2)}, u32[]{:S(2)}) collective-permute-start(bf16[32,512]{1,0:T(8,128)(2,1)S(1)} %add_convert_fusion.1), channel_id=1, source_target_pairs={{0,4},{1,5},{2,6},{3,7},{4,0},{5,1},{6,2},{7,3},{8,12},{9,13},{10,... | collective-permute-start | bytes 98312 | tf_op jit(solution)/shard_map/ppermute | solution.py:56
  77.1 1.4 %collective-permute-start.28 = (bf16[32,512]{1,0:T(8,128)(2,1)S(1)}, bf16[32,512]{1,0:T(8,128)(2,1)S(1)}, u32[]{:S(2)}, u32[]{:S(2)}) collective-permute-start(bf16[32,512]{1,0:T(8,128)(2,1)S(1)} %add_convert_fusion), channel_id=1, source_target_pairs={{0,16},{8,24},{16,0},{24,8},{1,17},{9,25},{17,1},{25,9},{2,18},{10... | collective-permute-start | bytes 98312 | tf_op jit(solution)/shard_map/ppermute | solution.py:56
  80.3 1.7 %collective-permute-start.29 = (bf16[64,512]{1,0:T(8,128)(2,1)S(1)}, bf16[64,512]{1,0:T(8,128)(2,1)S(1)}, u32[]{:S(2)}, u32[]{:S(2)}) collective-permute-start(bf16[64,512]{1,0:T(8,128)(2,1)S(1)} %pad_maximum_fusion.20), channel_id=1, source_target_pairs={{0,8},{8,0},{16,24},{24,16},{1,9},{9,1},{17,25},{25,17},{2,10},{10... | collective-permute-start | bytes 196616 | tf_op jit(solution)/shard_map/ppermute | solution.py:56
  85.5 1.5 %collective-permute-done.14 = bf16[128,512]{1,0:T(8,128)(2,1)S(1)} collective-permute-done((bf16[128,512]{1,0:T(8,128)(2,1)S(1)}, bf16[128,512]{1,0:T(8,128)(2,1)S(1)}, u32[]{:S(2)}, u32[]{:S(2)}) %collective-permute-start.14) | collective-permute-done | bytes 131104 | tf_op jit(solution)/shard_map/ppermute | solution.py:56
  87.0 7.9 %collective-permute-start.15 = (bf16[256,512]{1,0:T(8,128)(2,1)S(1)}, bf16[256,512]{1,0:T(8,128)(2,1)S(1)}, u32[]{:S(2)}, u32[]{:S(2)}) collective-permute-start(bf16[256,512]{1,0:T(8,128)(2,1)S(1)} %pad_maximum_fusion.2), channel_id=1, source_target_pairs={{0,1},{1,0},{2,3},{3,2},{4,5},{5,4},{6,7},{7,6},{8,9},{9,8},{10,11... | collective-permute-start | bytes 786440 | tf_op jit(solution)/shard_map/ppermute | solution.py:77
  97.8 1.6 %copy-done = f32[1440,512]{1,0:T(8,128)} copy-done((f32[1440,512]{1,0:T(8,128)}, f32[1440,512]{1,0:T(8,128)S(1)}, u32[]{:S(2)}) %copy-start) | copy-done | bytes 2949144
  (206 shorter events, 36.8 us)
Async XLA Ops:
  4.2 9.3 %collective-permute-start.1 = (bf16[4,32,832]{2,1,0:T(8,128)(2,1)S(1)}, bf16[4,32,832]{2,1,0:T(8,128)(2,1)S(1)}, u32[]{:S(2)}, u32[]{:S(2)}) collective-permute-start(bf16[4,32,832]{2,1,0:T(8,128)(2,1)S(1)} %concatenate.116), channel_id=1, source_target_pairs={{8,0},{16,8},{24,16},{9,1},{17,9},{25,17},{10,2},{18,10},{26,18},{... | collective-permute-start | bytes 638984 | tf_op jit(solution)/shard_map/ppermute | solution.py:127
  5.5 8.8 %collective-permute-start = (bf16[4,32,832]{2,1,0:T(8,128)(2,1)S(1)}, bf16[4,32,832]{2,1,0:T(8,128)(2,1)S(1)}, u32[]{:S(2)}, u32[]{:S(2)}) collective-permute-start(bf16[4,32,832]{2,1,0:T(8,128)(2,1)S(1)} %concatenate.116), channel_id=1, source_target_pairs={{0,8},{8,16},{16,24},{1,9},{9,17},{17,25},{2,10},{10,18},{18,26},{... | collective-permute-start | bytes 638984 | tf_op jit(solution)/shard_map/ppermute | solution.py:126
  14.4 7.5 %collective-permute-start.2 = (bf16[12,4,832]{2,1,0:T(4,128)(2,1)S(1)}, bf16[12,4,832]{2,1,0:T(4,128)(2,1)S(1)}, u32[]{:S(2)}, u32[]{:S(2)}) collective-permute-start(bf16[12,4,832]{2,1,0:T(4,128)(2,1)S(1)} %get-tuple-element.28), channel_id=1, source_target_pairs={{0,1},{1,2},{2,3},{3,4},{4,5},{5,6},{6,7},{8,9},{9,10},{10,11},{11... | collective-permute-start | bytes 239624 | tf_op jit(solution)/shard_map/ppermute | solution.py:126
  19.2 5.8 %collective-permute-start.3 = (bf16[12,4,832]{2,1,0:T(4,128)(2,1)S(1)}, bf16[12,4,832]{2,1,0:T(4,128)(2,1)S(1)}, u32[]{:S(2)}, u32[]{:S(2)}) collective-permute-start(bf16[12,4,832]{2,1,0:T(4,128)(2,1)S(1)} %get-tuple-element.29), channel_id=1, source_target_pairs={{1,0},{2,1},{3,2},{4,3},{5,4},{6,5},{7,6},{9,8},{10,9},{11,10},{12... | collective-permute-start | bytes 239624 | tf_op jit(solution)/shard_map/ppermute | solution.py:127
  31.9 12.0 %collective-permute-start.5 = (bf16[6,34,160]{2,1,0:T(8,128)(2,1)}, bf16[6,34,160]{2,1,0:T(8,128)(2,1)S(1)}, u32[]{:S(2)}, u32[]{:S(2)}) collective-permute-start(bf16[6,34,160]{2,1,0:T(8,128)(2,1)} %fusion.82), channel_id=1, source_target_pairs={{0,1},{1,0},{2,3},{3,2},{4,5},{5,4},{6,7},{7,6},{8,9},{9,8},{10,11... | collective-permute-start | bytes 195848 | tf_op jit(solution)/shard_map/ppermute | solution.py:276
  31.9 12.4 %collective-permute-start.4 = (bf16[6,34,160]{2,1,0:T(8,128)(2,1)}, bf16[6,34,160]{2,1,0:T(8,128)(2,1)S(1)}, u32[]{:S(2)}, u32[]{:S(2)}) collective-permute-start(bf16[6,34,160]{2,1,0:T(8,128)(2,1)} %slice.422), channel_id=1, source_target_pairs={{0,1},{1,0},{2,3},{3,2},{4,5},{5,4},{6,7},{7,6},{8,9},{9,8},{10,11... | collective-permute-start | bytes 195848 | tf_op jit(solution)/shard_map/ppermute | solution.py:276
  37.3 7.4 %collective-permute-start.6 = (bf16[128,512]{1,0:T(8,128)(2,1)}, bf16[128,512]{1,0:T(8,128)(2,1)}, u32[]{:S(2)}, u32[]{:S(2)}) collective-permute-start(bf16[128,512]{1,0:T(8,128)(2,1)} %bitcast.32), channel_id=1, source_target_pairs={{0,1},{1,0},{2,3},{3,2},{4,5},{5,4},{6,7},{7,6},{8,9},{9,8},{10,11... | collective-permute-start | bytes 393224 | tf_op jit(solution)/shard_map/ppermute | solution.py:277
  46.7 11.5 %collective-permute-start.8 = (f32[128,512]{1,0:T(8,128)S(1)}, f32[128,512]{1,0:T(8,128)S(1)}, u32[]{:S(2)}, u32[]{:S(2)}) collective-permute-start(f32[128,512]{1,0:T(8,128)S(1)} %constant_dynamic-slice_fusion.8), channel_id=1, source_target_pairs={{0,16},{8,24},{16,0},{24,8},{1,17},{9,25},{17,1},{25,9},{2,18},{10... | collective-permute-start | bytes 786440 | tf_op jit(solution)/shard_map/ppermute | solution.py:46
  52.3 8.3 %collective-permute-start.16 = (f32[128,512]{1,0:T(8,128)S(1)}, f32[128,512]{1,0:T(8,128)S(1)}, u32[]{:S(2)}, u32[]{:S(2)}) collective-permute-start(f32[128,512]{1,0:T(8,128)S(1)} %constant_dynamic-slice_fusion.5), channel_id=1, source_target_pairs={{0,8},{8,0},{16,24},{24,16},{1,9},{9,1},{17,25},{25,17},{2,10},{10... | collective-permute-start | bytes 786440 | tf_op jit(solution)/shard_map/ppermute | solution.py:46
  53.6 8.3 %collective-permute-start.24 = (f32[128,512]{1,0:T(8,128)S(1)}, f32[128,512]{1,0:T(8,128)S(1)}, u32[]{:S(2)}, u32[]{:S(2)}) collective-permute-start(f32[128,512]{1,0:T(8,128)S(1)} %constant_dynamic-slice_fusion.2), channel_id=1, source_target_pairs={{0,2},{1,3},{2,0},{3,1},{4,6},{5,7},{6,4},{7,5},{8,10},{9,11},{10,... | collective-permute-start | bytes 786440 | tf_op jit(solution)/shard_map/ppermute | solution.py:46
  58.2 6.0 %collective-permute-start.9 = (f32[64,512]{1,0:T(8,128)S(1)}, f32[64,512]{1,0:T(8,128)S(1)}, u32[]{:S(2)}, u32[]{:S(2)}) collective-permute-start(f32[64,512]{1,0:T(8,128)S(1)} %constant_dynamic-slice_fusion.7), channel_id=1, source_target_pairs={{0,4},{1,5},{2,6},{3,7},{4,0},{5,1},{6,2},{7,3},{8,12},{9,13},{10,... | collective-permute-start | bytes 393224 | tf_op jit(solution)/shard_map/ppermute | solution.py:46
  60.7 5.5 %collective-permute-start.17 = (f32[64,512]{1,0:T(8,128)S(1)}, f32[64,512]{1,0:T(8,128)S(1)}, u32[]{:S(2)}, u32[]{:S(2)}) collective-permute-start(f32[64,512]{1,0:T(8,128)S(1)} %constant_dynamic-slice_fusion.4), channel_id=1, source_target_pairs={{0,16},{8,24},{16,0},{24,8},{1,17},{9,25},{17,1},{25,9},{2,18},{10... | collective-permute-start | bytes 393224 | tf_op jit(solution)/shard_map/ppermute | solution.py:46
  62.0 6.8 %collective-permute-start.25 = (f32[64,512]{1,0:T(8,128)S(1)}, f32[64,512]{1,0:T(8,128)S(1)}, u32[]{:S(2)}, u32[]{:S(2)}) collective-permute-start(f32[64,512]{1,0:T(8,128)S(1)} %constant_dynamic-slice_fusion.1), channel_id=1, source_target_pairs={{0,8},{8,0},{16,24},{24,16},{1,9},{9,1},{17,25},{25,17},{2,10},{10... | collective-permute-start | bytes 393224 | tf_op jit(solution)/shard_map/ppermute | solution.py:46
  64.3 4.6 %collective-permute-start.10 = (f32[32,512]{1,0:T(8,128)S(1)}, f32[32,512]{1,0:T(8,128)S(1)}, u32[]{:S(2)}, u32[]{:S(2)}) collective-permute-start(f32[32,512]{1,0:T(8,128)S(1)} %constant_dynamic-slice_fusion.6), channel_id=1, source_target_pairs={{0,2},{1,3},{2,0},{3,1},{4,6},{5,7},{6,4},{7,5},{8,10},{9,11},{10,... | collective-permute-start | bytes 196616 | tf_op jit(solution)/shard_map/ppermute | solution.py:46
  66.2 4.9 %collective-permute-start.18 = (f32[32,512]{1,0:T(8,128)S(1)}, f32[32,512]{1,0:T(8,128)S(1)}, u32[]{:S(2)}, u32[]{:S(2)}) collective-permute-start(f32[32,512]{1,0:T(8,128)S(1)} %constant_dynamic-slice_fusion.3), channel_id=1, source_target_pairs={{0,4},{1,5},{2,6},{3,7},{4,0},{5,1},{6,2},{7,3},{8,12},{9,13},{10,... | collective-permute-start | bytes 196616 | tf_op jit(solution)/shard_map/ppermute | solution.py:46
  69.0 4.2 %collective-permute-start.11 = (f32[32,512]{1,0:T(8,128)S(1)}, f32[32,512]{1,0:T(8,128)S(1)}, u32[]{:S(2)}, u32[]{:S(2)}) collective-permute-start(f32[32,512]{1,0:T(8,128)S(1)} %dynamic-slice_add_fusion.8), channel_id=1, source_target_pairs={{0,8},{8,0},{16,24},{24,16},{1,9},{9,1},{17,25},{25,17},{2,10},{10... | collective-permute-start | bytes 196616 | tf_op jit(solution)/shard_map/ppermute | solution.py:49
  72.3 4.8 %collective-permute-start.27 = (f32[32,512]{1,0:T(8,128)S(1)}, f32[32,512]{1,0:T(8,128)S(1)}, u32[]{:S(2)}, u32[]{:S(2)}) collective-permute-start(f32[32,512]{1,0:T(8,128)S(1)} %dynamic-slice_add_fusion.6), channel_id=1, source_target_pairs={{0,4},{1,5},{2,6},{3,7},{4,0},{5,1},{6,2},{7,3},{8,12},{9,13},{10,... | collective-permute-start | bytes 196616 | tf_op jit(solution)/shard_map/ppermute | solution.py:49
  73.2 5.3 %collective-permute-start.12 = (bf16[32,512]{1,0:T(8,128)(2,1)S(1)}, bf16[32,512]{1,0:T(8,128)(2,1)S(1)}, u32[]{:S(2)}, u32[]{:S(2)}) collective-permute-start(bf16[32,512]{1,0:T(8,128)(2,1)S(1)} %add_convert_fusion.2), channel_id=1, source_target_pairs={{0,2},{1,3},{2,0},{3,1},{4,6},{5,7},{6,4},{7,5},{8,10},{9,11},{10,... | collective-permute-start | bytes 98312 | tf_op jit(solution)/shard_map/ppermute | solution.py:56
  78.9 4.8 %collective-permute-start.21 = (bf16[64,512]{1,0:T(8,128)(2,1)S(1)}, bf16[64,512]{1,0:T(8,128)(2,1)S(1)}, u32[]{:S(2)}, u32[]{:S(2)}) collective-permute-start(bf16[64,512]{1,0:T(8,128)(2,1)S(1)} %pad_maximum_fusion.19), channel_id=1, source_target_pairs={{0,16},{8,24},{16,0},{24,8},{1,17},{9,25},{17,1},{25,9},{2,18},{10... | collective-permute-start | bytes 196616 | tf_op jit(solution)/shard_map/ppermute | solution.py:56
  80.3 4.6 %collective-permute-start.29 = (bf16[64,512]{1,0:T(8,128)(2,1)S(1)}, bf16[64,512]{1,0:T(8,128)(2,1)S(1)}, u32[]{:S(2)}, u32[]{:S(2)}) collective-permute-start(bf16[64,512]{1,0:T(8,128)(2,1)S(1)} %pad_maximum_fusion.20), channel_id=1, source_target_pairs={{0,8},{8,0},{16,24},{24,16},{1,9},{9,1},{17,25},{25,17},{2,10},{10... | collective-permute-start | bytes 196616 | tf_op jit(solution)/shard_map/ppermute | solution.py:56
  82.7 4.2 %collective-permute-start.14 = (bf16[128,512]{1,0:T(8,128)(2,1)S(1)}, bf16[128,512]{1,0:T(8,128)(2,1)S(1)}, u32[]{:S(2)}, u32[]{:S(2)}) collective-permute-start(bf16[128,512]{1,0:T(8,128)(2,1)S(1)} %pad_maximum_fusion.11), channel_id=1, source_target_pairs={{0,16},{8,24},{16,0},{24,8},{1,17},{9,25},{17,1},{25,9},{2,18},{10... | collective-permute-start | bytes 393224 | tf_op jit(solution)/shard_map/ppermute | solution.py:56
  83.7 11.2 %collective-permute-start.22 = (bf16[128,512]{1,0:T(8,128)(2,1)S(1)}, bf16[128,512]{1,0:T(8,128)(2,1)S(1)}, u32[]{:S(2)}, u32[]{:S(2)}) collective-permute-start(bf16[128,512]{1,0:T(8,128)(2,1)S(1)} %pad_maximum_fusion.12), channel_id=1, source_target_pairs={{0,8},{8,0},{16,24},{24,16},{1,9},{9,1},{17,25},{25,17},{2,10},{10... | collective-permute-start | bytes 393224 | tf_op jit(solution)/shard_map/ppermute | solution.py:56
  85.0 10.2 %collective-permute-start.30 = (bf16[128,512]{1,0:T(8,128)(2,1)S(1)}, bf16[128,512]{1,0:T(8,128)(2,1)S(1)}, u32[]{:S(2)}, u32[]{:S(2)}) collective-permute-start(bf16[128,512]{1,0:T(8,128)(2,1)S(1)} %pad_maximum_fusion.13), channel_id=1, source_target_pairs={{0,2},{1,3},{2,0},{3,1},{4,6},{5,7},{6,4},{7,5},{8,10},{9,11},{10,... | collective-permute-start | bytes 393224 | tf_op jit(solution)/shard_map/ppermute | solution.py:56
  87.0 9.4 %collective-permute-start.15 = (bf16[256,512]{1,0:T(8,128)(2,1)S(1)}, bf16[256,512]{1,0:T(8,128)(2,1)S(1)}, u32[]{:S(2)}, u32[]{:S(2)}) collective-permute-start(bf16[256,512]{1,0:T(8,128)(2,1)S(1)} %pad_maximum_fusion.2), channel_id=1, source_target_pairs={{0,1},{1,0},{2,3},{3,2},{4,5},{5,4},{6,7},{7,6},{8,9},{9,8},{10,11... | collective-permute-start | bytes 786440 | tf_op jit(solution)/shard_map/ppermute | solution.py:77
  (26 other events, 47.7 us)

commit v17 on v16

--- a/solution.py
+++ b/solution.py
@@ -13,7 +13,7 @@
 KIN = 1440
 SUM_ROWS = 1536
 SUM_WAYS = 3
-SUM_SHARED = 1
+SUM_SHARED = 0
 
 
 def flip_pairs(axis, bit):

time: 100 us -> 104 us (1.040)
  starting transfers between devices: 52.7 us -> 54.9 us
  waiting for transfers between devices: 16.1 us -> 17.7 us
    ppermute x9 -> x12, starting transfers between devices: 17 us -> 20.1 us  [halve(): part = keep + lax.ppermute(send, axis, flip_pairs(axis, bit))]
    ppermute x3 -> x0, starting transfers between devices: 2.83 us -> none  [halve(): part = part + lax.ppermute(part, axis, flip_pairs(axis, bit))]
    ppermute x9 -> x12, waiting for transfers between devices: 2.76 us -> 5.19 us  [double(): got = lax.ppermute(piece, axis, flip_pairs(axis, bit))]
    ppermute x9 -> x12, starting transfers between devices: 10.1 us -> 11.9 us  [double(): got = lax.ppermute(piece, axis, flip_pairs(axis, bit))]
    ppermute x9 -> x12, waiting for transfers between devices: 5.56 us -> 5.28 us  [halve(): part = keep + lax.ppermute(send, axis, flip_pairs(axis, bit))]
  transfers between devices with their start and end apart: 32 -> 35, of which waited for: 11 -> 11; matrix products, arithmetic and copies ran while one was open for 14% -> 14% of each run, Pallas kernels for 0% -> 0%
where the time goes in v17:
time: 104 us; the launch traced here: 103 us
  starting transfers between devices  54.9 us (53%)
  waiting for transfers between devices  17.7 us (17%)
  local copies, waits for them, and re-layouts  12.2 us (12%)
  other arithmetic  10.9 us (10%)
  matrix products  5.94 us (6%)
  between operations  1.67 us (2%)
    ppermute x12, starting transfers between devices, halve(): part = keep + lax.ppermute(send, axis, flip_pairs(axis, bit))  20.1 us
    ppermute x12, starting transfers between devices, double(): got = lax.ppermute(piece, axis, flip_pairs(axis, bit))  11.9 us
    ppermute x3, starting transfers between devices, sum_everywhere(): swapped = [(p, lax.ppermute(p, axis, pairs)) for p in pieces]  9.49 us
    ppermute x2, starting transfers between devices, widen(): lax.ppermute(tail, axis, [(i, i + dist) for i in range(count - dist)])  9.47 us
    ppermute x2, waiting for transfers between devices, widen(): lax.ppermute(head, axis, [(i + dist, i) for i in range(count - dist)])  6.35 us
    ppermute x12, waiting for transfers between devices, halve(): part = keep + lax.ppermute(send, axis, flip_pairs(axis, bit))  5.28 us
    ppermute x12, waiting for transfers between devices, double(): got = lax.ppermute(piece, axis, flip_pairs(axis, bit))  5.19 us
    unnamed x39, local copies, waits for them, and re-layouts  4.23 us
  transfers between devices with their start and end apart: 35, of which 11 were waited for; matrix products, arithmetic and copies ran while one was open for 14% of the time, Pallas kernels for 0%

profile of v17, /device:TPU:1, one launch (start us, length us, event | category | flops | bytes accessed | tf_op | source)
XLA Modules:
  0.0 103.4 jit_solution(5883807932234920334)
XLA Ops:
  4.2 1.3 %collective-permute-start.1 = (bf16[4,32,832]{2,1,0:T(8,128)(2,1)S(1)}, bf16[4,32,832]{2,1,0:T(8,128)(2,1)S(1)}, u32[]{:S(2)}, u32[]{:S(2)}) collective-permute-start(bf16[4,32,832]{2,1,0:T(8,128)(2,1)S(1)} %concatenate.125), channel_id=1, source_target_pairs={{8,0},{16,8},{24,16},{9,1},{17,9},{25,17},{10,2},{18,10},{26,18},{... | collective-permute-start | bytes 638984 | tf_op jit(solution)/shard_map/ppermute | solution.py:127
  5.5 4.6 %collective-permute-start = (bf16[4,32,832]{2,1,0:T(8,128)(2,1)S(1)}, bf16[4,32,832]{2,1,0:T(8,128)(2,1)S(1)}, u32[]{:S(2)}, u32[]{:S(2)}) collective-permute-start(bf16[4,32,832]{2,1,0:T(8,128)(2,1)S(1)} %concatenate.125), channel_id=1, source_target_pairs={{0,8},{8,16},{16,24},{1,9},{9,17},{17,25},{2,10},{10,18},{18,26},{... | collective-permute-start | bytes 638984 | tf_op jit(solution)/shard_map/ppermute | solution.py:126
  10.3 3.1 %collective-permute-done.1 = bf16[4,32,832]{2,1,0:T(8,128)(2,1)S(1)} collective-permute-done((bf16[4,32,832]{2,1,0:T(8,128)(2,1)S(1)}, bf16[4,32,832]{2,1,0:T(8,128)(2,1)S(1)}, u32[]{:S(2)}, u32[]{:S(2)}) %collective-permute-start.1) | collective-permute-done | bytes 213024 | tf_op jit(solution)/shard_map/ppermute | solution.py:127
  14.4 4.9 %collective-permute-start.2 = (bf16[12,4,832]{2,1,0:T(4,128)(2,1)S(1)}, bf16[12,4,832]{2,1,0:T(4,128)(2,1)S(1)}, u32[]{:S(2)}, u32[]{:S(2)}) collective-permute-start(bf16[12,4,832]{2,1,0:T(4,128)(2,1)S(1)} %get-tuple-element.28), channel_id=1, source_target_pairs={{0,1},{1,2},{2,3},{3,4},{4,5},{5,6},{6,7},{8,9},{9,10},{10,11},{11... | collective-permute-start | bytes 239624 | tf_op jit(solution)/shard_map/ppermute | solution.py:126
  19.2 1.9 %collective-permute-start.3 = (bf16[12,4,832]{2,1,0:T(4,128)(2,1)S(1)}, bf16[12,4,832]{2,1,0:T(4,128)(2,1)S(1)}, u32[]{:S(2)}, u32[]{:S(2)}) collective-permute-start(bf16[12,4,832]{2,1,0:T(4,128)(2,1)S(1)} %get-tuple-element.29), channel_id=1, source_target_pairs={{1,0},{2,1},{3,2},{4,3},{5,4},{6,5},{7,6},{9,8},{10,9},{11,10},{12... | collective-permute-start | bytes 239624 | tf_op jit(solution)/shard_map/ppermute | solution.py:127
  21.8 3.2 %collective-permute-done.3 = bf16[12,4,832]{2,1,0:T(4,128)(2,1)S(1)} collective-permute-done((bf16[12,4,832]{2,1,0:T(4,128)(2,1)S(1)}, bf16[12,4,832]{2,1,0:T(4,128)(2,1)S(1)}, u32[]{:S(2)}, u32[]{:S(2)}) %collective-permute-start.3) | collective-permute-done | bytes 79904 | tf_op jit(solution)/shard_map/ppermute | solution.py:127
  32.7 2.1 %convolution_select_fusion.1 = f32[8,8,5,512]{3,1,2,0:T(8,128)S(1)} fusion(bf16[3,3,160,512]{3,2,1,0:T(8,128)(2,1)} %bitcast.88, pred[8,5]{0,1:T(8,128)(4,1)S(1)} %copy-done.16, bf16[10,1,7,2,160]{4,2,3,0,1:T(8,128)(2,1)S(1)} %slice.371, bf16[10,1,8,5,160]{4,2,3,0,1:T(8,128)(2,1)S(1)} %copy.16), kind=kOutput, calls=%fused_computation.7 | convolution fusion | flops 472560640 | bytes 2302760 | tf_op jit(solution)/shard_map/conv_general_dilated | solution.py:174
  44.8 1.7 %convolution_multiply_fusion = f32[768,512]{1,0:T(8,128)S(1)} fusion(s32[]{:T(128)S(6)} %select_n.265, bf16[128,1536]{1,0:T(8,128)(2,1)S(1)} %concatenate.141, bf16[128,1536]{1,0:T(8,128)(2,1)S(1)} %concatenate.143, bf16[128,1536]{1,0:T(8,128)(2,1)S(1)} %concatenate.145, bf16[128,1536]{1,0:T(8,128)(2,1)S(1)} %concatenate.147, ...), kind=kOutput, calls=%fused_computation.4 | convolution fusion | flops 408289280 | bytes 3670020 | tf_op jit(solution)/shard_map/dot_general | solution.py:295
  46.7 5.0 %collective-permute-start.8 = (f32[128,512]{1,0:T(8,128)S(1)}, f32[128,512]{1,0:T(8,128)S(1)}, u32[]{:S(2)}, u32[]{:S(2)}) collective-permute-start(f32[128,512]{1,0:T(8,128)S(1)} %constant_dynamic-slice_fusion.11), channel_id=1, source_target_pairs={{0,16},{8,24},{16,0},{24,8},{1,17},{9,25},{17,1},{25,9},{2,18},{10... | collective-permute-start | bytes 786440 | tf_op jit(solution)/shard_map/ppermute | solution.py:46
  52.3 1.3 %collective-permute-start.17 = (f32[128,512]{1,0:T(8,128)S(1)}, f32[128,512]{1,0:T(8,128)S(1)}, u32[]{:S(2)}, u32[]{:S(2)}) collective-permute-start(f32[128,512]{1,0:T(8,128)S(1)} %constant_dynamic-slice_fusion.7), channel_id=1, source_target_pairs={{0,8},{8,0},{16,24},{24,16},{1,9},{9,1},{17,25},{25,17},{2,10},{10... | collective-permute-start | bytes 786440 | tf_op jit(solution)/shard_map/ppermute | solution.py:46
  53.6 1.4 %collective-permute-start.26 = (f32[128,512]{1,0:T(8,128)S(1)}, f32[128,512]{1,0:T(8,128)S(1)}, u32[]{:S(2)}, u32[]{:S(2)}) collective-permute-start(f32[128,512]{1,0:T(8,128)S(1)} %constant_dynamic-slice_fusion.3), channel_id=1, source_target_pairs={{0,2},{1,3},{2,0},{3,1},{4,6},{5,7},{6,4},{7,5},{8,10},{9,11},{10,... | collective-permute-start | bytes 786440 | tf_op jit(solution)/shard_map/ppermute | solution.py:46
  55.0 3.2 %collective-permute-done.8 = f32[128,512]{1,0:T(8,128)S(1)} collective-permute-done((f32[128,512]{1,0:T(8,128)S(1)}, f32[128,512]{1,0:T(8,128)S(1)}, u32[]{:S(2)}, u32[]{:S(2)}) %collective-permute-start.8) | collective-permute-done | bytes 262176 | tf_op jit(solution)/shard_map/ppermute | solution.py:46
  58.3 2.4 %collective-permute-start.9 = (f32[64,512]{1,0:T(8,128)S(1)}, f32[64,512]{1,0:T(8,128)S(1)}, u32[]{:S(2)}, u32[]{:S(2)}) collective-permute-start(f32[64,512]{1,0:T(8,128)S(1)} %constant_dynamic-slice_fusion.10), channel_id=1, source_target_pairs={{0,4},{1,5},{2,6},{3,7},{4,0},{5,1},{6,2},{7,3},{8,12},{9,13},{10,... | collective-permute-start | bytes 393224 | tf_op jit(solution)/shard_map/ppermute | solution.py:46
  64.3 1.9 %collective-permute-start.10 = (f32[32,512]{1,0:T(8,128)S(1)}, f32[32,512]{1,0:T(8,128)S(1)}, u32[]{:S(2)}, u32[]{:S(2)}) collective-permute-start(f32[32,512]{1,0:T(8,128)S(1)} %constant_dynamic-slice_fusion.9), channel_id=1, source_target_pairs={{0,2},{1,3},{2,0},{3,1},{4,6},{5,7},{6,4},{7,5},{8,10},{9,11},{10,... | collective-permute-start | bytes 196616 | tf_op jit(solution)/shard_map/ppermute | solution.py:46
  66.3 2.5 %collective-permute-start.19 = (f32[32,512]{1,0:T(8,128)S(1)}, f32[32,512]{1,0:T(8,128)S(1)}, u32[]{:S(2)}, u32[]{:S(2)}) collective-permute-start(f32[32,512]{1,0:T(8,128)S(1)} %constant_dynamic-slice_fusion.5), channel_id=1, source_target_pairs={{0,4},{1,5},{2,6},{3,7},{4,0},{5,1},{6,2},{7,3},{8,12},{9,13},{10,... | collective-permute-start | bytes 196616 | tf_op jit(solution)/shard_map/ppermute | solution.py:46
  68.9 2.0 %collective-permute-start.11 = (f32[16,512]{1,0:T(8,128)S(1)}, f32[16,512]{1,0:T(8,128)S(1)}, u32[]{:S(2)}, u32[]{:S(2)}) collective-permute-start(f32[16,512]{1,0:T(8,128)S(1)} %constant_dynamic-slice_fusion.8), channel_id=1, source_target_pairs={{0,8},{8,0},{16,24},{24,16},{1,9},{9,1},{17,25},{25,17},{2,10},{10... | collective-permute-start | bytes 98312 | tf_op jit(solution)/shard_map/ppermute | solution.py:46
  74.5 1.5 %collective-permute-start.21 = (bf16[16,512]{1,0:T(8,128)(2,1)S(1)}, bf16[16,512]{1,0:T(8,128)(2,1)S(1)}, u32[]{:S(2)}, u32[]{:S(2)}) collective-permute-start(bf16[16,512]{1,0:T(8,128)(2,1)S(1)} %add_convert_fusion.1), channel_id=1, source_target_pairs={{0,2},{1,3},{2,0},{3,1},{4,6},{5,7},{6,4},{7,5},{8,10},{9,11},{10,... | collective-permute-start | bytes 49160 | tf_op jit(solution)/shard_map/ppermute | solution.py:56
  77.0 1.6 %collective-permute-start.13 = (bf16[32,512]{1,0:T(8,128)(2,1)S(1)}, bf16[32,512]{1,0:T(8,128)(2,1)S(1)}, u32[]{:S(2)}, u32[]{:S(2)}) collective-permute-start(bf16[32,512]{1,0:T(8,128)(2,1)S(1)} %pad_maximum_fusion.22), channel_id=1, source_target_pairs={{0,2},{1,3},{2,0},{3,1},{4,6},{5,7},{6,4},{7,5},{8,10},{9,11},{10,... | collective-permute-start | bytes 98312 | tf_op jit(solution)/shard_map/ppermute | solution.py:56
  80.6 1.3 %collective-permute-start.31 = (bf16[32,512]{1,0:T(8,128)(2,1)S(1)}, bf16[32,512]{1,0:T(8,128)(2,1)S(1)}, u32[]{:S(2)}, u32[]{:S(2)}) collective-permute-start(bf16[32,512]{1,0:T(8,128)(2,1)S(1)} %pad_maximum_fusion.24), channel_id=1, source_target_pairs={{0,16},{8,24},{16,0},{24,8},{1,17},{9,25},{17,1},{25,9},{2,18},{10... | collective-permute-start | bytes 98312 | tf_op jit(solution)/shard_map/ppermute | solution.py:56
  84.6 1.9 %collective-permute-done.14 = bf16[64,512]{1,0:T(8,128)(2,1)S(1)} collective-permute-done((bf16[64,512]{1,0:T(8,128)(2,1)S(1)}, bf16[64,512]{1,0:T(8,128)(2,1)S(1)}, u32[]{:S(2)}, u32[]{:S(2)}) %collective-permute-start.14) | collective-permute-done | bytes 65568 | tf_op jit(solution)/shard_map/ppermute | solution.py:56
  88.6 2.1 %collective-permute-done.15 = bf16[128,512]{1,0:T(8,128)(2,1)S(1)} collective-permute-done((bf16[128,512]{1,0:T(8,128)(2,1)S(1)}, bf16[128,512]{1,0:T(8,128)(2,1)S(1)}, u32[]{:S(2)}, u32[]{:S(2)}) %collective-permute-start.15) | collective-permute-done | bytes 131104 | tf_op jit(solution)/shard_map/ppermute | solution.py:56
  90.7 8.0 %collective-permute-start.16 = (bf16[256,512]{1,0:T(8,128)(2,1)S(1)}, bf16[256,512]{1,0:T(8,128)(2,1)S(1)}, u32[]{:S(2)}, u32[]{:S(2)}) collective-permute-start(bf16[256,512]{1,0:T(8,128)(2,1)S(1)} %pad_maximum_fusion.2), channel_id=1, source_target_pairs={{0,1},{1,0},{2,3},{3,2},{4,5},{5,4},{6,7},{7,6},{8,9},{9,8},{10,11... | collective-permute-start | bytes 786440 | tf_op jit(solution)/shard_map/ppermute | solution.py:77
  99.0 1.4 %collective-permute-start.34 = (bf16[256,512]{1,0:T(8,128)(2,1)S(1)}, bf16[256,512]{1,0:T(8,128)(2,1)S(1)}, u32[]{:S(2)}, u32[]{:S(2)}) collective-permute-start(bf16[256,512]{1,0:T(8,128)(2,1)S(1)} %pad_maximum_fusion.4), channel_id=1, source_target_pairs={{0,1},{1,0},{2,3},{3,2},{4,5},{5,4},{6,7},{7,6},{8,9},{9,8},{10,11... | collective-permute-start | bytes 786440 | tf_op jit(solution)/shard_map/ppermute | solution.py:77
  101.8 1.6 %copy-done = f32[1440,512]{1,0:T(8,128)} copy-done((f32[1440,512]{1,0:T(8,128)}, f32[1440,512]{1,0:T(8,128)S(1)}, u32[]{:S(2)}) %copy-start) | copy-done | bytes 2949144
  (221 shorter events, 40.0 us)
Async XLA Ops:
  4.2 9.3 %collective-permute-start.1 = (bf16[4,32,832]{2,1,0:T(8,128)(2,1)S(1)}, bf16[4,32,832]{2,1,0:T(8,128)(2,1)S(1)}, u32[]{:S(2)}, u32[]{:S(2)}) collective-permute-start(bf16[4,32,832]{2,1,0:T(8,128)(2,1)S(1)} %concatenate.125), channel_id=1, source_target_pairs={{8,0},{16,8},{24,16},{9,1},{17,9},{25,17},{10,2},{18,10},{26,18},{... | collective-permute-start | bytes 638984 | tf_op jit(solution)/shard_map/ppermute | solution.py:127
  5.5 8.8 %collective-permute-start = (bf16[4,32,832]{2,1,0:T(8,128)(2,1)S(1)}, bf16[4,32,832]{2,1,0:T(8,128)(2,1)S(1)}, u32[]{:S(2)}, u32[]{:S(2)}) collective-permute-start(bf16[4,32,832]{2,1,0:T(8,128)(2,1)S(1)} %concatenate.125), channel_id=1, source_target_pairs={{0,8},{8,16},{16,24},{1,9},{9,17},{17,25},{2,10},{10,18},{18,26},{... | collective-permute-start | bytes 638984 | tf_op jit(solution)/shard_map/ppermute | solution.py:126
  14.4 7.5 %collective-permute-start.2 = (bf16[12,4,832]{2,1,0:T(4,128)(2,1)S(1)}, bf16[12,4,832]{2,1,0:T(4,128)(2,1)S(1)}, u32[]{:S(2)}, u32[]{:S(2)}) collective-permute-start(bf16[12,4,832]{2,1,0:T(4,128)(2,1)S(1)} %get-tuple-element.28), channel_id=1, source_target_pairs={{0,1},{1,2},{2,3},{3,4},{4,5},{5,6},{6,7},{8,9},{9,10},{10,11},{11... | collective-permute-start | bytes 239624 | tf_op jit(solution)/shard_map/ppermute | solution.py:126
  19.2 5.8 %collective-permute-start.3 = (bf16[12,4,832]{2,1,0:T(4,128)(2,1)S(1)}, bf16[12,4,832]{2,1,0:T(4,128)(2,1)S(1)}, u32[]{:S(2)}, u32[]{:S(2)}) collective-permute-start(bf16[12,4,832]{2,1,0:T(4,128)(2,1)S(1)} %get-tuple-element.29), channel_id=1, source_target_pairs={{1,0},{2,1},{3,2},{4,3},{5,4},{6,5},{7,6},{9,8},{10,9},{11,10},{12... | collective-permute-start | bytes 239624 | tf_op jit(solution)/shard_map/ppermute | solution.py:127
  31.9 12.0 %collective-permute-start.5 = (bf16[6,34,160]{2,1,0:T(8,128)(2,1)}, bf16[6,34,160]{2,1,0:T(8,128)(2,1)S(1)}, u32[]{:S(2)}, u32[]{:S(2)}) collective-permute-start(bf16[6,34,160]{2,1,0:T(8,128)(2,1)} %fusion.82), channel_id=1, source_target_pairs={{0,1},{1,0},{2,3},{3,2},{4,5},{5,4},{6,7},{7,6},{8,9},{9,8},{10,11... | collective-permute-start | bytes 195848 | tf_op jit(solution)/shard_map/ppermute | solution.py:276
  31.9 12.4 %collective-permute-start.4 = (bf16[6,34,160]{2,1,0:T(8,128)(2,1)}, bf16[6,34,160]{2,1,0:T(8,128)(2,1)S(1)}, u32[]{:S(2)}, u32[]{:S(2)}) collective-permute-start(bf16[6,34,160]{2,1,0:T(8,128)(2,1)} %slice.422), channel_id=1, source_target_pairs={{0,1},{1,0},{2,3},{3,2},{4,5},{5,4},{6,7},{7,6},{8,9},{9,8},{10,11... | collective-permute-start | bytes 195848 | tf_op jit(solution)/shard_map/ppermute | solution.py:276
  37.4 7.4 %collective-permute-start.6 = (bf16[128,512]{1,0:T(8,128)(2,1)}, bf16[128,512]{1,0:T(8,128)(2,1)}, u32[]{:S(2)}, u32[]{:S(2)}) collective-permute-start(bf16[128,512]{1,0:T(8,128)(2,1)} %bitcast.32), channel_id=1, source_target_pairs={{0,1},{1,0},{2,3},{3,2},{4,5},{5,4},{6,7},{7,6},{8,9},{9,8},{10,11... | collective-permute-start | bytes 393224 | tf_op jit(solution)/shard_map/ppermute | solution.py:277
  46.7 11.5 %collective-permute-start.8 = (f32[128,512]{1,0:T(8,128)S(1)}, f32[128,512]{1,0:T(8,128)S(1)}, u32[]{:S(2)}, u32[]{:S(2)}) collective-permute-start(f32[128,512]{1,0:T(8,128)S(1)} %constant_dynamic-slice_fusion.11), channel_id=1, source_target_pairs={{0,16},{8,24},{16,0},{24,8},{1,17},{9,25},{17,1},{25,9},{2,18},{10... | collective-permute-start | bytes 786440 | tf_op jit(solution)/shard_map/ppermute | solution.py:46
  52.3 8.3 %collective-permute-start.17 = (f32[128,512]{1,0:T(8,128)S(1)}, f32[128,512]{1,0:T(8,128)S(1)}, u32[]{:S(2)}, u32[]{:S(2)}) collective-permute-start(f32[128,512]{1,0:T(8,128)S(1)} %constant_dynamic-slice_fusion.7), channel_id=1, source_target_pairs={{0,8},{8,0},{16,24},{24,16},{1,9},{9,1},{17,25},{25,17},{2,10},{10... | collective-permute-start | bytes 786440 | tf_op jit(solution)/shard_map/ppermute | solution.py:46
  53.6 8.3 %collective-permute-start.26 = (f32[128,512]{1,0:T(8,128)S(1)}, f32[128,512]{1,0:T(8,128)S(1)}, u32[]{:S(2)}, u32[]{:S(2)}) collective-permute-start(f32[128,512]{1,0:T(8,128)S(1)} %constant_dynamic-slice_fusion.3), channel_id=1, source_target_pairs={{0,2},{1,3},{2,0},{3,1},{4,6},{5,7},{6,4},{7,5},{8,10},{9,11},{10,... | collective-permute-start | bytes 786440 | tf_op jit(solution)/shard_map/ppermute | solution.py:46
  58.3 6.0 %collective-permute-start.9 = (f32[64,512]{1,0:T(8,128)S(1)}, f32[64,512]{1,0:T(8,128)S(1)}, u32[]{:S(2)}, u32[]{:S(2)}) collective-permute-start(f32[64,512]{1,0:T(8,128)S(1)} %constant_dynamic-slice_fusion.10), channel_id=1, source_target_pairs={{0,4},{1,5},{2,6},{3,7},{4,0},{5,1},{6,2},{7,3},{8,12},{9,13},{10,... | collective-permute-start | bytes 393224 | tf_op jit(solution)/shard_map/ppermute | solution.py:46
  60.7 5.5 %collective-permute-start.18 = (f32[64,512]{1,0:T(8,128)S(1)}, f32[64,512]{1,0:T(8,128)S(1)}, u32[]{:S(2)}, u32[]{:S(2)}) collective-permute-start(f32[64,512]{1,0:T(8,128)S(1)} %constant_dynamic-slice_fusion.6), channel_id=1, source_target_pairs={{0,16},{8,24},{16,0},{24,8},{1,17},{9,25},{17,1},{25,9},{2,18},{10... | collective-permute-start | bytes 393224 | tf_op jit(solution)/shard_map/ppermute | solution.py:46
  62.0 6.8 %collective-permute-start.27 = (f32[64,512]{1,0:T(8,128)S(1)}, f32[64,512]{1,0:T(8,128)S(1)}, u32[]{:S(2)}, u32[]{:S(2)}) collective-permute-start(f32[64,512]{1,0:T(8,128)S(1)} %constant_dynamic-slice_fusion.2), channel_id=1, source_target_pairs={{0,8},{8,0},{16,24},{24,16},{1,9},{9,1},{17,25},{25,17},{2,10},{10... | collective-permute-start | bytes 393224 | tf_op jit(solution)/shard_map/ppermute | solution.py:46
  64.3 4.6 %collective-permute-start.10 = (f32[32,512]{1,0:T(8,128)S(1)}, f32[32,512]{1,0:T(8,128)S(1)}, u32[]{:S(2)}, u32[]{:S(2)}) collective-permute-start(f32[32,512]{1,0:T(8,128)S(1)} %constant_dynamic-slice_fusion.9), channel_id=1, source_target_pairs={{0,2},{1,3},{2,0},{3,1},{4,6},{5,7},{6,4},{7,5},{8,10},{9,11},{10,... | collective-permute-start | bytes 196616 | tf_op jit(solution)/shard_map/ppermute | solution.py:46
  66.3 4.9 %collective-permute-start.19 = (f32[32,512]{1,0:T(8,128)S(1)}, f32[32,512]{1,0:T(8,128)S(1)}, u32[]{:S(2)}, u32[]{:S(2)}) collective-permute-start(f32[32,512]{1,0:T(8,128)S(1)} %constant_dynamic-slice_fusion.5), channel_id=1, source_target_pairs={{0,4},{1,5},{2,6},{3,7},{4,0},{5,1},{6,2},{7,3},{8,12},{9,13},{10,... | collective-permute-start | bytes 196616 | tf_op jit(solution)/shard_map/ppermute | solution.py:46
  68.9 4.3 %collective-permute-start.11 = (f32[16,512]{1,0:T(8,128)S(1)}, f32[16,512]{1,0:T(8,128)S(1)}, u32[]{:S(2)}, u32[]{:S(2)}) collective-permute-start(f32[16,512]{1,0:T(8,128)S(1)} %constant_dynamic-slice_fusion.8), channel_id=1, source_target_pairs={{0,8},{8,0},{16,24},{24,16},{1,9},{9,1},{17,25},{25,17},{2,10},{10... | collective-permute-start | bytes 98312 | tf_op jit(solution)/shard_map/ppermute | solution.py:46
  76.0 4.5 %collective-permute-start.30 = (bf16[16,512]{1,0:T(8,128)(2,1)S(1)}, bf16[16,512]{1,0:T(8,128)(2,1)S(1)}, u32[]{:S(2)}, u32[]{:S(2)}) collective-permute-start(bf16[16,512]{1,0:T(8,128)(2,1)S(1)} %add_convert_fusion), channel_id=1, source_target_pairs={{0,4},{1,5},{2,6},{3,7},{4,0},{5,1},{6,2},{7,3},{8,12},{9,13},{10,... | collective-permute-start | bytes 49160 | tf_op jit(solution)/shard_map/ppermute | solution.py:56
  77.0 4.9 %collective-permute-start.13 = (bf16[32,512]{1,0:T(8,128)(2,1)S(1)}, bf16[32,512]{1,0:T(8,128)(2,1)S(1)}, u32[]{:S(2)}, u32[]{:S(2)}) collective-permute-start(bf16[32,512]{1,0:T(8,128)(2,1)S(1)} %pad_maximum_fusion.22), channel_id=1, source_target_pairs={{0,2},{1,3},{2,0},{3,1},{4,6},{5,7},{6,4},{7,5},{8,10},{9,11},{10,... | collective-permute-start | bytes 98312 | tf_op jit(solution)/shard_map/ppermute | solution.py:56
  81.9 4.6 %collective-permute-start.14 = (bf16[64,512]{1,0:T(8,128)(2,1)S(1)}, bf16[64,512]{1,0:T(8,128)(2,1)S(1)}, u32[]{:S(2)}, u32[]{:S(2)}) collective-permute-start(bf16[64,512]{1,0:T(8,128)(2,1)S(1)} %pad_maximum_fusion.18), channel_id=1, source_target_pairs={{0,4},{1,5},{2,6},{3,7},{4,0},{5,1},{6,2},{7,3},{8,12},{9,13},{10,... | collective-permute-start | bytes 196616 | tf_op jit(solution)/shard_map/ppermute | solution.py:56
  82.6 4.6 %collective-permute-start.23 = (bf16[64,512]{1,0:T(8,128)(2,1)S(1)}, bf16[64,512]{1,0:T(8,128)(2,1)S(1)}, u32[]{:S(2)}, u32[]{:S(2)}) collective-permute-start(bf16[64,512]{1,0:T(8,128)(2,1)S(1)} %pad_maximum_fusion.19), channel_id=1, source_target_pairs={{0,16},{8,24},{16,0},{24,8},{1,17},{9,25},{17,1},{25,9},{2,18},{10... | collective-permute-start | bytes 196616 | tf_op jit(solution)/shard_map/ppermute | solution.py:56
  83.6 4.8 %collective-permute-start.32 = (bf16[64,512]{1,0:T(8,128)(2,1)S(1)}, bf16[64,512]{1,0:T(8,128)(2,1)S(1)}, u32[]{:S(2)}, u32[]{:S(2)}) collective-permute-start(bf16[64,512]{1,0:T(8,128)(2,1)S(1)} %pad_maximum_fusion.20), channel_id=1, source_target_pairs={{0,8},{8,0},{16,24},{24,16},{1,9},{9,1},{17,25},{25,17},{2,10},{10... | collective-permute-start | bytes 196616 | tf_op jit(solution)/shard_map/ppermute | solution.py:56
  87.3 11.4 %collective-permute-start.24 = (bf16[128,512]{1,0:T(8,128)(2,1)S(1)}, bf16[128,512]{1,0:T(8,128)(2,1)S(1)}, u32[]{:S(2)}, u32[]{:S(2)}) collective-permute-start(bf16[128,512]{1,0:T(8,128)(2,1)S(1)} %pad_maximum_fusion.12), channel_id=1, source_target_pairs={{0,8},{8,0},{16,24},{24,16},{1,9},{9,1},{17,25},{25,17},{2,10},{10... | collective-permute-start | bytes 393224 | tf_op jit(solution)/shard_map/ppermute | solution.py:56
  88.5 10.4 %collective-permute-start.33 = (bf16[128,512]{1,0:T(8,128)(2,1)S(1)}, bf16[128,512]{1,0:T(8,128)(2,1)S(1)}, u32[]{:S(2)}, u32[]{:S(2)}) collective-permute-start(bf16[128,512]{1,0:T(8,128)(2,1)S(1)} %pad_maximum_fusion.13), channel_id=1, source_target_pairs={{0,2},{1,3},{2,0},{3,1},{4,6},{5,7},{6,4},{7,5},{8,10},{9,11},{10,... | collective-permute-start | bytes 393224 | tf_op jit(solution)/shard_map/ppermute | solution.py:56
  90.7 9.7 %collective-permute-start.16 = (bf16[256,512]{1,0:T(8,128)(2,1)S(1)}, bf16[256,512]{1,0:T(8,128)(2,1)S(1)}, u32[]{:S(2)}, u32[]{:S(2)}) collective-permute-start(bf16[256,512]{1,0:T(8,128)(2,1)S(1)} %pad_maximum_fusion.2), channel_id=1, source_target_pairs={{0,1},{1,0},{2,3},{3,2},{4,5},{5,4},{6,7},{7,6},{8,9},{9,8},{10,11... | collective-permute-start | bytes 786440 | tf_op jit(solution)/shard_map/ppermute | solution.py:77
  (29 other events, 59.2 us)

commit v18 on v16

--- a/solution.py
+++ b/solution.py
@@ -12,7 +12,7 @@
 GATES = 512
 KIN = 1440
 SUM_ROWS = 1536
-SUM_WAYS = 3
+SUM_WAYS = 2
 SUM_SHARED = 1
 
 

time: 100 us -> 102 us (1.020)
  starting transfers between devices: 52.7 us -> 43.3 us
  waiting for transfers between devices: 16.1 us -> 25 us
  other arithmetic: 10.9 us -> 12.4 us
    ppermute x9 -> x6, starting transfers between devices: 17 us -> 12.4 us  [halve(): part = keep + lax.ppermute(send, axis, flip_pairs(axis, bit))]
    ppermute x9 -> x6, waiting for transfers between devices: 5.56 us -> 9.75 us  [halve(): part = keep + lax.ppermute(send, axis, flip_pairs(axis, bit))]
    ppermute x9 -> x6, starting transfers between devices: 10.1 us -> 6.69 us  [double(): got = lax.ppermute(piece, axis, flip_pairs(axis, bit))]
    ppermute x9 -> x6, waiting for transfers between devices: 2.76 us -> 5.14 us  [double(): got = lax.ppermute(piece, axis, flip_pairs(axis, bit))]
    ppermute x3 -> x2, waiting for transfers between devices: 0.58 us -> 2.75 us  [halve(): part = part + lax.ppermute(part, axis, flip_pairs(axis, bit))]
    ppermute x3 -> x2, starting transfers between devices: 2.83 us -> 2.08 us  [halve(): part = part + lax.ppermute(part, axis, flip_pairs(axis, bit))]
    ppermute x3 -> x2, starting transfers between devices: 9.23 us -> 8.58 us  [sum_everywhere(): swapped = [(p, lax.ppermute(p, axis, pairs)) for p in pieces]]
    unnamed x39 -> x41, local copies, waits for them, and re-layouts: 4.21 us -> 4.2 us
  transfers between devices with their start and end apart: 32 -> 24, of which waited for: 11 -> 14; matrix products, arithmetic and copies ran while one was open for 14% -> 16% of each run, Pallas kernels for 0% -> 0%
where the time goes in v18:
time: 102 us; the launch traced here: 101 us
  starting transfers between devices  43.3 us (42%)
  waiting for transfers between devices  25 us (25%)
  other arithmetic  12.4 us (12%)
  local copies, waits for them, and re-layouts  12.1 us (12%)
  matrix products  6.58 us (6%)
  between operations  1.46 us (1%)
    ppermute x6, starting transfers between devices, halve(): part = keep + lax.ppermute(send, axis, flip_pairs(axis, bit))  12.4 us
    ppermute x6, waiting for transfers between devices, halve(): part = keep + lax.ppermute(send, axis, flip_pairs(axis, bit))  9.75 us
    ppermute x2, starting transfers between devices, widen(): lax.ppermute(tail, axis, [(i, i + dist) for i in range(count - dist)])  9.47 us
    ppermute x2, starting transfers between devices, sum_everywhere(): swapped = [(p, lax.ppermute(p, axis, pairs)) for p in pieces]  8.58 us
    ppermute x6, starting transfers between devices, double(): got = lax.ppermute(piece, axis, flip_pairs(axis, bit))  6.69 us
    ppermute x2, waiting for transfers between devices, widen(): lax.ppermute(head, axis, [(i + dist, i) for i in range(count - dist)])  6.35 us
    ppermute x6, waiting for transfers between devices, double(): got = lax.ppermute(piece, axis, flip_pairs(axis, bit))  5.14 us
    conv_general_dilated x4, matrix products, convolve(): lax.conv_general_dilated(field[None], weights, (1, 1), 'VALID', dimension...  4.86 us
  transfers between devices with their start and end apart: 24, of which 14 were waited for; matrix products, arithmetic and copies ran while one was open for 16% of the time, Pallas kernels for 0%

profile of v18, /device:TPU:1, one launch (start us, length us, event | category | flops | bytes accessed | tf_op | source)
XLA Modules:
  0.0 100.9 jit_solution(13191267224255876718)
XLA Ops:
  4.2 1.3 %collective-permute-start.1 = (bf16[4,32,832]{2,1,0:T(8,128)(2,1)S(1)}, bf16[4,32,832]{2,1,0:T(8,128)(2,1)S(1)}, u32[]{:S(2)}, u32[]{:S(2)}) collective-permute-start(bf16[4,32,832]{2,1,0:T(8,128)(2,1)S(1)} %concatenate.107), channel_id=1, source_target_pairs={{8,0},{16,8},{24,16},{9,1},{17,9},{25,17},{10,2},{18,10},{26,18},{... | collective-permute-start | bytes 638984 | tf_op jit(solution)/shard_map/ppermute | solution.py:127
  5.5 4.6 %collective-permute-start = (bf16[4,32,832]{2,1,0:T(8,128)(2,1)S(1)}, bf16[4,32,832]{2,1,0:T(8,128)(2,1)S(1)}, u32[]{:S(2)}, u32[]{:S(2)}) collective-permute-start(bf16[4,32,832]{2,1,0:T(8,128)(2,1)S(1)} %concatenate.107), channel_id=1, source_target_pairs={{0,8},{8,16},{16,24},{1,9},{9,17},{17,25},{2,10},{10,18},{18,26},{... | collective-permute-start | bytes 638984 | tf_op jit(solution)/shard_map/ppermute | solution.py:126
  10.3 3.1 %collective-permute-done.1 = bf16[4,32,832]{2,1,0:T(8,128)(2,1)S(1)} collective-permute-done((bf16[4,32,832]{2,1,0:T(8,128)(2,1)S(1)}, bf16[4,32,832]{2,1,0:T(8,128)(2,1)S(1)}, u32[]{:S(2)}, u32[]{:S(2)}) %collective-permute-start.1) | collective-permute-done | bytes 213024 | tf_op jit(solution)/shard_map/ppermute | solution.py:127
  14.4 4.9 %collective-permute-start.2 = (bf16[12,4,832]{2,1,0:T(4,128)(2,1)S(1)}, bf16[12,4,832]{2,1,0:T(4,128)(2,1)S(1)}, u32[]{:S(2)}, u32[]{:S(2)}) collective-permute-start(bf16[12,4,832]{2,1,0:T(4,128)(2,1)S(1)} %get-tuple-element.29), channel_id=1, source_target_pairs={{0,1},{1,2},{2,3},{3,4},{4,5},{5,6},{6,7},{8,9},{9,10},{10,11},{11... | collective-permute-start | bytes 239624 | tf_op jit(solution)/shard_map/ppermute | solution.py:126
  19.2 1.9 %collective-permute-start.3 = (bf16[12,4,832]{2,1,0:T(4,128)(2,1)S(1)}, bf16[12,4,832]{2,1,0:T(4,128)(2,1)S(1)}, u32[]{:S(2)}, u32[]{:S(2)}) collective-permute-start(bf16[12,4,832]{2,1,0:T(4,128)(2,1)S(1)} %get-tuple-element.30), channel_id=1, source_target_pairs={{1,0},{2,1},{3,2},{4,3},{5,4},{6,5},{7,6},{9,8},{10,9},{11,10},{12... | collective-permute-start | bytes 239624 | tf_op jit(solution)/shard_map/ppermute | solution.py:127
  21.8 3.2 %collective-permute-done.3 = bf16[12,4,832]{2,1,0:T(4,128)(2,1)S(1)} collective-permute-done((bf16[12,4,832]{2,1,0:T(4,128)(2,1)S(1)}, bf16[12,4,832]{2,1,0:T(4,128)(2,1)S(1)}, u32[]{:S(2)}, u32[]{:S(2)}) %collective-permute-start.3) | collective-permute-done | bytes 79904 | tf_op jit(solution)/shard_map/ppermute | solution.py:127
  32.6 2.1 %convolution_select_fusion.1 = f32[8,8,5,512]{3,1,2,0:T(8,128)S(1)} fusion(bf16[3,3,160,512]{3,2,1,0:T(8,128)(2,1)} %bitcast.88, pred[8,5]{0,1:T(8,128)(4,1)S(1)} %copy-done.17, bf16[10,1,7,2,160]{4,2,3,0,1:T(8,128)(2,1)S(1)} %slice.367, bf16[10,1,8,5,160]{4,2,3,0,1:T(8,128)(2,1)S(1)} %copy.16), kind=kOutput, calls=%fused_computation.7 | convolution fusion | flops 472560640 | bytes 2302760 | tf_op jit(solution)/shard_map/conv_general_dilated | solution.py:174
  44.7 1.7 %convolution_multiply_fusion = f32[768,512]{1,0:T(8,128)S(1)} fusion(s32[]{:T(128)S(6)} %select_n.158, bf16[128,1536]{1,0:T(8,128)(2,1)S(1)} %concatenate.123, bf16[128,1536]{1,0:T(8,128)(2,1)S(1)} %concatenate.125, bf16[128,1536]{1,0:T(8,128)(2,1)S(1)} %concatenate.127, bf16[128,1536]{1,0:T(8,128)(2,1)S(1)} %concatenate.129, ...), kind=kOutput, calls=%fused_computation.4 | convolution fusion | flops 408289280 | bytes 3670020 | tf_op jit(solution)/shard_map/dot_general | solution.py:295
  46.6 3.1 %collective-permute-start.8 = (f32[192,512]{1,0:T(8,128)S(1)}, f32[192,512]{1,0:T(8,128)S(1)}, u32[]{:S(2)}, u32[]{:S(2)}) collective-permute-start(f32[192,512]{1,0:T(8,128)S(1)} %constant_dynamic-slice_fusion.5), channel_id=1, source_target_pairs={{0,8},{8,0},{16,24},{24,16},{1,9},{9,1},{17,25},{25,17},{2,10},{10... | collective-permute-start | bytes 1179656 | tf_op jit(solution)/shard_map/ppermute | solution.py:46
  50.3 1.4 %collective-permute-start.16 = (f32[192,512]{1,0:T(8,128)S(1)}, f32[192,512]{1,0:T(8,128)S(1)}, u32[]{:S(2)}, u32[]{:S(2)}) collective-permute-start(f32[192,512]{1,0:T(8,128)S(1)} %constant_dynamic-slice_fusion.2), channel_id=1, source_target_pairs={{0,2},{1,3},{2,0},{3,1},{4,6},{5,7},{6,4},{7,5},{8,10},{9,11},{10,... | collective-permute-start | bytes 1179656 | tf_op jit(solution)/shard_map/ppermute | solution.py:46
  51.7 1.5 %fusion.99 = bf16[4,32,128]{2,1,0:T(8,128)(2,1)} fusion(f32[8,36,128]{2,1,0:T(8,128)S(1)} %get-tuple-element.16, f32[8,36,128]{2,1,0:T(8,128)} %get-tuple-element.35), kind=kLoop, calls=%fused_computation.203 | loop fusion | flops 32768 | bytes 163840 | tf_op jit(solution)/shard_map/convert_element_type | solution.py:188
  53.2 5.7 %collective-permute-done.8 = f32[192,512]{1,0:T(8,128)S(1)} collective-permute-done((f32[192,512]{1,0:T(8,128)S(1)}, f32[192,512]{1,0:T(8,128)S(1)}, u32[]{:S(2)}, u32[]{:S(2)}) %collective-permute-start.8) | collective-permute-done | bytes 393248 | tf_op jit(solution)/shard_map/ppermute | solution.py:46
  59.1 3.1 %collective-permute-start.9 = (f32[96,512]{1,0:T(8,128)S(1)}, f32[96,512]{1,0:T(8,128)S(1)}, u32[]{:S(2)}, u32[]{:S(2)}) collective-permute-start(f32[96,512]{1,0:T(8,128)S(1)} %constant_dynamic-slice_fusion.4), channel_id=1, source_target_pairs={{0,16},{8,24},{16,0},{24,8},{1,17},{9,25},{17,1},{25,9},{2,18},{10... | collective-permute-start | bytes 589832 | tf_op jit(solution)/shard_map/ppermute | solution.py:46
  63.6 2.8 %collective-permute-done.9 = f32[96,512]{1,0:T(8,128)S(1)} collective-permute-done((f32[96,512]{1,0:T(8,128)S(1)}, f32[96,512]{1,0:T(8,128)S(1)}, u32[]{:S(2)}, u32[]{:S(2)}) %collective-permute-start.9) | collective-permute-done | bytes 196640 | tf_op jit(solution)/shard_map/ppermute | solution.py:46
  66.4 2.4 %collective-permute-start.10 = (f32[48,512]{1,0:T(8,128)S(1)}, f32[48,512]{1,0:T(8,128)S(1)}, u32[]{:S(2)}, u32[]{:S(2)}) collective-permute-start(f32[48,512]{1,0:T(8,128)S(1)} %constant_dynamic-slice_fusion.3), channel_id=1, source_target_pairs={{0,4},{1,5},{2,6},{3,7},{4,0},{5,1},{6,2},{7,3},{8,12},{9,13},{10,... | collective-permute-start | bytes 294920 | tf_op jit(solution)/shard_map/ppermute | solution.py:46
  70.9 1.4 %collective-permute-start.11 = (f32[48,512]{1,0:T(8,128)S(1)}, f32[48,512]{1,0:T(8,128)S(1)}, u32[]{:S(2)}, u32[]{:S(2)}) collective-permute-start(f32[48,512]{1,0:T(8,128)S(1)} %dynamic-slice_add_fusion.5), channel_id=1, source_target_pairs={{0,2},{1,3},{2,0},{3,1},{4,6},{5,7},{6,4},{7,5},{8,10},{9,11},{10,... | collective-permute-start | bytes 294920 | tf_op jit(solution)/shard_map/ppermute | solution.py:49
  73.4 1.3 %collective-permute-done.11 = f32[48,512]{1,0:T(8,128)S(1)} collective-permute-done((f32[48,512]{1,0:T(8,128)S(1)}, f32[48,512]{1,0:T(8,128)S(1)}, u32[]{:S(2)}, u32[]{:S(2)}) %collective-permute-start.11) | collective-permute-done | bytes 98336 | tf_op jit(solution)/shard_map/ppermute | solution.py:49
  74.7 2.1 %collective-permute-start.12 = (bf16[48,512]{1,0:T(8,128)(2,1)S(1)}, bf16[48,512]{1,0:T(8,128)(2,1)S(1)}, u32[]{:S(2)}, u32[]{:S(2)}) collective-permute-start(bf16[48,512]{1,0:T(8,128)(2,1)S(1)} %add_convert_fusion.1), channel_id=1, source_target_pairs={{0,4},{1,5},{2,6},{3,7},{4,0},{5,1},{6,2},{7,3},{8,12},{9,13},{10,... | collective-permute-start | bytes 147464 | tf_op jit(solution)/shard_map/ppermute | solution.py:56
  76.8 1.4 %collective-permute-done.19 = f32[48,512]{1,0:T(8,128)S(1)} collective-permute-done((f32[48,512]{1,0:T(8,128)S(1)}, f32[48,512]{1,0:T(8,128)S(1)}, u32[]{:S(2)}, u32[]{:S(2)}) %collective-permute-start.19) | collective-permute-done | bytes 98336 | tf_op jit(solution)/shard_map/ppermute | solution.py:49
  80.1 1.5 %collective-permute-done.20 = bf16[48,512]{1,0:T(8,128)(2,1)S(1)} collective-permute-done((bf16[48,512]{1,0:T(8,128)(2,1)S(1)}, bf16[48,512]{1,0:T(8,128)(2,1)S(1)}, u32[]{:S(2)}, u32[]{:S(2)}) %collective-permute-start.20) | collective-permute-done | bytes 49184 | tf_op jit(solution)/shard_map/ppermute | solution.py:56
  85.5 2.7 %collective-permute-done.14 = bf16[192,512]{1,0:T(8,128)(2,1)S(1)} collective-permute-done((bf16[192,512]{1,0:T(8,128)(2,1)S(1)}, bf16[192,512]{1,0:T(8,128)(2,1)S(1)}, u32[]{:S(2)}, u32[]{:S(2)}) %collective-permute-start.14) | collective-permute-done | bytes 196640 | tf_op jit(solution)/shard_map/ppermute | solution.py:56
  88.3 7.2 %collective-permute-start.15 = (bf16[384,512]{1,0:T(8,128)(2,1)S(1)}, bf16[384,512]{1,0:T(8,128)(2,1)S(1)}, u32[]{:S(2)}, u32[]{:S(2)}) collective-permute-start(bf16[384,512]{1,0:T(8,128)(2,1)S(1)} %pad_maximum_fusion.2), channel_id=1, source_target_pairs={{0,1},{1,0},{2,3},{3,2},{4,5},{5,4},{6,7},{7,6},{8,9},{9,8},{10,11... | collective-permute-start | bytes 1179656 | tf_op jit(solution)/shard_map/ppermute | solution.py:77
  96.3 1.4 %collective-permute-start.23 = (bf16[384,512]{1,0:T(8,128)(2,1)S(1)}, bf16[384,512]{1,0:T(8,128)(2,1)S(1)}, u32[]{:S(2)}, u32[]{:S(2)}) collective-permute-start(bf16[384,512]{1,0:T(8,128)(2,1)S(1)} %pad_maximum_fusion.3), channel_id=1, source_target_pairs={{0,1},{1,0},{2,3},{3,2},{4,5},{5,4},{6,7},{7,6},{8,9},{9,8},{10,11... | collective-permute-start | bytes 1179656 | tf_op jit(solution)/shard_map/ppermute | solution.py:77
  99.3 1.6 %copy-done = f32[1440,512]{1,0:T(8,128)} copy-done((f32[1440,512]{1,0:T(8,128)}, f32[1440,512]{1,0:T(8,128)S(1)}, u32[]{:S(2)}) %copy-start) | copy-done | bytes 2949144
  (177 shorter events, 35.9 us)
Async XLA Ops:
  4.2 9.3 %collective-permute-start.1 = (bf16[4,32,832]{2,1,0:T(8,128)(2,1)S(1)}, bf16[4,32,832]{2,1,0:T(8,128)(2,1)S(1)}, u32[]{:S(2)}, u32[]{:S(2)}) collective-permute-start(bf16[4,32,832]{2,1,0:T(8,128)(2,1)S(1)} %concatenate.107), channel_id=1, source_target_pairs={{8,0},{16,8},{24,16},{9,1},{17,9},{25,17},{10,2},{18,10},{26,18},{... | collective-permute-start | bytes 638984 | tf_op jit(solution)/shard_map/ppermute | solution.py:127
  5.5 8.8 %collective-permute-start = (bf16[4,32,832]{2,1,0:T(8,128)(2,1)S(1)}, bf16[4,32,832]{2,1,0:T(8,128)(2,1)S(1)}, u32[]{:S(2)}, u32[]{:S(2)}) collective-permute-start(bf16[4,32,832]{2,1,0:T(8,128)(2,1)S(1)} %concatenate.107), channel_id=1, source_target_pairs={{0,8},{8,16},{16,24},{1,9},{9,17},{17,25},{2,10},{10,18},{18,26},{... | collective-permute-start | bytes 638984 | tf_op jit(solution)/shard_map/ppermute | solution.py:126
  14.4 7.5 %collective-permute-start.2 = (bf16[12,4,832]{2,1,0:T(4,128)(2,1)S(1)}, bf16[12,4,832]{2,1,0:T(4,128)(2,1)S(1)}, u32[]{:S(2)}, u32[]{:S(2)}) collective-permute-start(bf16[12,4,832]{2,1,0:T(4,128)(2,1)S(1)} %get-tuple-element.29), channel_id=1, source_target_pairs={{0,1},{1,2},{2,3},{3,4},{4,5},{5,6},{6,7},{8,9},{9,10},{10,11},{11... | collective-permute-start | bytes 239624 | tf_op jit(solution)/shard_map/ppermute | solution.py:126
  19.2 5.8 %collective-permute-start.3 = (bf16[12,4,832]{2,1,0:T(4,128)(2,1)S(1)}, bf16[12,4,832]{2,1,0:T(4,128)(2,1)S(1)}, u32[]{:S(2)}, u32[]{:S(2)}) collective-permute-start(bf16[12,4,832]{2,1,0:T(4,128)(2,1)S(1)} %get-tuple-element.30), channel_id=1, source_target_pairs={{1,0},{2,1},{3,2},{4,3},{5,4},{6,5},{7,6},{9,8},{10,9},{11,10},{12... | collective-permute-start | bytes 239624 | tf_op jit(solution)/shard_map/ppermute | solution.py:127
  31.9 11.9 %collective-permute-start.5 = (bf16[6,34,160]{2,1,0:T(8,128)(2,1)}, bf16[6,34,160]{2,1,0:T(8,128)(2,1)S(1)}, u32[]{:S(2)}, u32[]{:S(2)}) collective-permute-start(bf16[6,34,160]{2,1,0:T(8,128)(2,1)} %fusion.82), channel_id=1, source_target_pairs={{0,1},{1,0},{2,3},{3,2},{4,5},{5,4},{6,7},{7,6},{8,9},{9,8},{10,11... | collective-permute-start | bytes 195848 | tf_op jit(solution)/shard_map/ppermute | solution.py:276
  31.9 12.3 %collective-permute-start.4 = (bf16[6,34,160]{2,1,0:T(8,128)(2,1)}, bf16[6,34,160]{2,1,0:T(8,128)(2,1)S(1)}, u32[]{:S(2)}, u32[]{:S(2)}) collective-permute-start(bf16[6,34,160]{2,1,0:T(8,128)(2,1)} %slice.418), channel_id=1, source_target_pairs={{0,1},{1,0},{2,3},{3,2},{4,5},{5,4},{6,7},{7,6},{8,9},{9,8},{10,11... | collective-permute-start | bytes 195848 | tf_op jit(solution)/shard_map/ppermute | solution.py:276
  37.3 7.3 %collective-permute-start.6 = (bf16[128,512]{1,0:T(8,128)(2,1)}, bf16[128,512]{1,0:T(8,128)(2,1)}, u32[]{:S(2)}, u32[]{:S(2)}) collective-permute-start(bf16[128,512]{1,0:T(8,128)(2,1)} %bitcast.32), channel_id=1, source_target_pairs={{0,1},{1,0},{2,3},{3,2},{4,5},{5,4},{6,7},{7,6},{8,9},{9,8},{10,11... | collective-permute-start | bytes 393224 | tf_op jit(solution)/shard_map/ppermute | solution.py:277
  40.5 4.1 %collective-permute-start.7 = (bf16[128,512]{1,0:T(8,128)(2,1)}, bf16[128,512]{1,0:T(8,128)(2,1)}, u32[]{:S(2)}, u32[]{:S(2)}) collective-permute-start(bf16[128,512]{1,0:T(8,128)(2,1)} %bitcast.33), channel_id=1, source_target_pairs={{0,1},{1,0},{2,3},{3,2},{4,5},{5,4},{6,7},{7,6},{8,9},{9,8},{10,11... | collective-permute-start | bytes 393224 | tf_op jit(solution)/shard_map/ppermute | solution.py:277
  46.6 12.4 %collective-permute-start.8 = (f32[192,512]{1,0:T(8,128)S(1)}, f32[192,512]{1,0:T(8,128)S(1)}, u32[]{:S(2)}, u32[]{:S(2)}) collective-permute-start(f32[192,512]{1,0:T(8,128)S(1)} %constant_dynamic-slice_fusion.5), channel_id=1, source_target_pairs={{0,8},{8,0},{16,24},{24,16},{1,9},{9,1},{17,25},{25,17},{2,10},{10... | collective-permute-start | bytes 1179656 | tf_op jit(solution)/shard_map/ppermute | solution.py:46
  50.3 11.9 %collective-permute-start.16 = (f32[192,512]{1,0:T(8,128)S(1)}, f32[192,512]{1,0:T(8,128)S(1)}, u32[]{:S(2)}, u32[]{:S(2)}) collective-permute-start(f32[192,512]{1,0:T(8,128)S(1)} %constant_dynamic-slice_fusion.2), channel_id=1, source_target_pairs={{0,2},{1,3},{2,0},{3,1},{4,6},{5,7},{6,4},{7,5},{8,10},{9,11},{10,... | collective-permute-start | bytes 1179656 | tf_op jit(solution)/shard_map/ppermute | solution.py:46
  59.1 7.3 %collective-permute-start.9 = (f32[96,512]{1,0:T(8,128)S(1)}, f32[96,512]{1,0:T(8,128)S(1)}, u32[]{:S(2)}, u32[]{:S(2)}) collective-permute-start(f32[96,512]{1,0:T(8,128)S(1)} %constant_dynamic-slice_fusion.4), channel_id=1, source_target_pairs={{0,16},{8,24},{16,0},{24,8},{1,17},{9,25},{17,1},{25,9},{2,18},{10... | collective-permute-start | bytes 589832 | tf_op jit(solution)/shard_map/ppermute | solution.py:46
  62.3 6.5 %collective-permute-start.17 = (f32[96,512]{1,0:T(8,128)S(1)}, f32[96,512]{1,0:T(8,128)S(1)}, u32[]{:S(2)}, u32[]{:S(2)}) collective-permute-start(f32[96,512]{1,0:T(8,128)S(1)} %constant_dynamic-slice_fusion.1), channel_id=1, source_target_pairs={{0,8},{8,0},{16,24},{24,16},{1,9},{9,1},{17,25},{25,17},{2,10},{10... | collective-permute-start | bytes 589832 | tf_op jit(solution)/shard_map/ppermute | solution.py:46
  66.4 4.4 %collective-permute-start.10 = (f32[48,512]{1,0:T(8,128)S(1)}, f32[48,512]{1,0:T(8,128)S(1)}, u32[]{:S(2)}, u32[]{:S(2)}) collective-permute-start(f32[48,512]{1,0:T(8,128)S(1)} %constant_dynamic-slice_fusion.3), channel_id=1, source_target_pairs={{0,4},{1,5},{2,6},{3,7},{4,0},{5,1},{6,2},{7,3},{8,12},{9,13},{10,... | collective-permute-start | bytes 294920 | tf_op jit(solution)/shard_map/ppermute | solution.py:46
  68.9 3.8 %collective-permute-start.18 = (f32[48,512]{1,0:T(8,128)S(1)}, f32[48,512]{1,0:T(8,128)S(1)}, u32[]{:S(2)}, u32[]{:S(2)}) collective-permute-start(f32[48,512]{1,0:T(8,128)S(1)} %constant_dynamic-slice_fusion), channel_id=1, source_target_pairs={{0,16},{8,24},{16,0},{24,8},{1,17},{9,25},{17,1},{25,9},{2,18},{10... | collective-permute-start | bytes 294920 | tf_op jit(solution)/shard_map/ppermute | solution.py:46
  70.9 3.8 %collective-permute-start.11 = (f32[48,512]{1,0:T(8,128)S(1)}, f32[48,512]{1,0:T(8,128)S(1)}, u32[]{:S(2)}, u32[]{:S(2)}) collective-permute-start(f32[48,512]{1,0:T(8,128)S(1)} %dynamic-slice_add_fusion.5), channel_id=1, source_target_pairs={{0,2},{1,3},{2,0},{3,1},{4,6},{5,7},{6,4},{7,5},{8,10},{9,11},{10,... | collective-permute-start | bytes 294920 | tf_op jit(solution)/shard_map/ppermute | solution.py:49
  72.7 5.6 %collective-permute-start.19 = (f32[48,512]{1,0:T(8,128)S(1)}, f32[48,512]{1,0:T(8,128)S(1)}, u32[]{:S(2)}, u32[]{:S(2)}) collective-permute-start(f32[48,512]{1,0:T(8,128)S(1)} %dynamic-slice_add_fusion.4), channel_id=1, source_target_pairs={{0,4},{1,5},{2,6},{3,7},{4,0},{5,1},{6,2},{7,3},{8,12},{9,13},{10,... | collective-permute-start | bytes 294920 | tf_op jit(solution)/shard_map/ppermute | solution.py:49
  74.7 4.8 %collective-permute-start.12 = (bf16[48,512]{1,0:T(8,128)(2,1)S(1)}, bf16[48,512]{1,0:T(8,128)(2,1)S(1)}, u32[]{:S(2)}, u32[]{:S(2)}) collective-permute-start(bf16[48,512]{1,0:T(8,128)(2,1)S(1)} %add_convert_fusion.1), channel_id=1, source_target_pairs={{0,4},{1,5},{2,6},{3,7},{4,0},{5,1},{6,2},{7,3},{8,12},{9,13},{10,... | collective-permute-start | bytes 147464 | tf_op jit(solution)/shard_map/ppermute | solution.py:56
  78.3 3.3 %collective-permute-start.20 = (bf16[48,512]{1,0:T(8,128)(2,1)S(1)}, bf16[48,512]{1,0:T(8,128)(2,1)S(1)}, u32[]{:S(2)}, u32[]{:S(2)}) collective-permute-start(bf16[48,512]{1,0:T(8,128)(2,1)S(1)} %add_convert_fusion), channel_id=1, source_target_pairs={{0,16},{8,24},{16,0},{24,8},{1,17},{9,25},{17,1},{25,9},{2,18},{10... | collective-permute-start | bytes 147464 | tf_op jit(solution)/shard_map/ppermute | solution.py:56
  79.6 3.7 %collective-permute-start.13 = (bf16[96,512]{1,0:T(8,128)(2,1)S(1)}, bf16[96,512]{1,0:T(8,128)(2,1)S(1)}, u32[]{:S(2)}, u32[]{:S(2)}) collective-permute-start(bf16[96,512]{1,0:T(8,128)(2,1)S(1)} %pad_maximum_fusion.12), channel_id=1, source_target_pairs={{0,16},{8,24},{16,0},{24,8},{1,17},{9,25},{17,1},{25,9},{2,18},{10... | collective-permute-start | bytes 294920 | tf_op jit(solution)/shard_map/ppermute | solution.py:56
  81.6 3.5 %collective-permute-start.21 = (bf16[96,512]{1,0:T(8,128)(2,1)S(1)}, bf16[96,512]{1,0:T(8,128)(2,1)S(1)}, u32[]{:S(2)}, u32[]{:S(2)}) collective-permute-start(bf16[96,512]{1,0:T(8,128)(2,1)S(1)} %pad_maximum_fusion.13), channel_id=1, source_target_pairs={{0,8},{8,0},{16,24},{24,16},{1,9},{9,1},{17,25},{25,17},{2,10},{10... | collective-permute-start | bytes 294920 | tf_op jit(solution)/shard_map/ppermute | solution.py:56
  83.3 4.9 %collective-permute-start.14 = (bf16[192,512]{1,0:T(8,128)(2,1)S(1)}, bf16[192,512]{1,0:T(8,128)(2,1)S(1)}, u32[]{:S(2)}, u32[]{:S(2)}) collective-permute-start(bf16[192,512]{1,0:T(8,128)(2,1)S(1)} %pad_maximum_fusion.4), channel_id=1, source_target_pairs={{0,8},{8,0},{16,24},{24,16},{1,9},{9,1},{17,25},{25,17},{2,10},{10... | collective-permute-start | bytes 589832 | tf_op jit(solution)/shard_map/ppermute | solution.py:56
  85.2 10.9 %collective-permute-start.22 = (bf16[192,512]{1,0:T(8,128)(2,1)S(1)}, bf16[192,512]{1,0:T(8,128)(2,1)S(1)}, u32[]{:S(2)}, u32[]{:S(2)}) collective-permute-start(bf16[192,512]{1,0:T(8,128)(2,1)S(1)} %pad_maximum_fusion.5), channel_id=1, source_target_pairs={{0,2},{1,3},{2,0},{3,1},{4,6},{5,7},{6,4},{7,5},{8,10},{9,11},{10,... | collective-permute-start | bytes 589832 | tf_op jit(solution)/shard_map/ppermute | solution.py:56
  88.3 9.3 %collective-permute-start.15 = (bf16[384,512]{1,0:T(8,128)(2,1)S(1)}, bf16[384,512]{1,0:T(8,128)(2,1)S(1)}, u32[]{:S(2)}, u32[]{:S(2)}) collective-permute-start(bf16[384,512]{1,0:T(8,128)(2,1)S(1)} %pad_maximum_fusion.2), channel_id=1, source_target_pairs={{0,1},{1,0},{2,3},{3,2},{4,5},{5,4},{6,7},{7,6},{8,9},{9,8},{10,11... | collective-permute-start | bytes 1179656 | tf_op jit(solution)/shard_map/ppermute | solution.py:77
  96.3 2.7 %collective-permute-start.23 = (bf16[384,512]{1,0:T(8,128)(2,1)S(1)}, bf16[384,512]{1,0:T(8,128)(2,1)S(1)}, u32[]{:S(2)}, u32[]{:S(2)}) collective-permute-start(bf16[384,512]{1,0:T(8,128)(2,1)S(1)} %pad_maximum_fusion.3), channel_id=1, source_target_pairs={{0,1},{1,0},{2,3},{3,2},{4,5},{5,4},{6,7},{7,6},{8,9},{9,8},{10,11... | collective-permute-start | bytes 1179656 | tf_op jit(solution)/shard_map/ppermute | solution.py:77
  (19 other events, 28.3 us)
